TPU v7x, 32 devices: a whole 2x2x4 slice. The times are simulated.
32 devices in a mesh: seq: 2 (over y), fsdp: 16 (over z, x, core).
Axes of the slice: x: 2, y: 2, z: 4, core: 2. Of those that a mesh axis runs over, the one named last changes fastest.
Arguments:
- layer_input: bfloat16 [16, 256, 8192], P('fsdp', 'seq'), may hold values from -6 to 6
- queries: bfloat16 [16, 256, 4096], P('fsdp', 'seq'), may hold values from -24 to 24
- key_states: bfloat16 [16, 256, 512], P('fsdp', 'seq'), may hold values from -24 to 24
- out_grad: bfloat16 [16, 256, 4096], P('fsdp', 'seq'), may hold values from -6 to 6
- doc_positions: int32 [16, 256], P('fsdp'), may hold values from 0 to 127, as said below
- drop_seed: int32 [], replicated, may hold values from 0 to 2147483646
- value_weight: bfloat16 [8192, 512], P(('seq', 'fsdp')), may hold values from -0.0625 to 0.0625
Outputs:
- query_grad: bfloat16 [16, 256, 4096], P('fsdp', 'seq')
- key_grad: bfloat16 [16, 256, 512], P('fsdp', 'seq')
- input_grad: bfloat16 [16, 256, 8192], P('fsdp', 'seq')
- weight_grad: bfloat16 [8192, 512], P(('seq', 'fsdp'))
Inputs may be any that keep to these rules, and one draw needn't show every extreme that they name: `doc_positions`: the value at a token is its distance from the first token of its document; documents are runs of consecutive tokens of at most 128 tokens, and each sequence has one of exactly 128.
All inputs are finite; a program needn't handle non-finite values.
Results may differ from a plain program's by a relative error of at most 0.0078.
Values may be sent and summed in bfloat16 or wider, within the bound.
No kernel may reach another device: no remote copies, remote signals or barrier semaphores. Data moves between devices by JAX's collectives and lax.ppermute only.
A program may use at most 128 MiB of HBM per device.

v0:
```python
import math

import jax
import jax.numpy as jnp
from jax import lax
from jax.sharding import PartitionSpec as P

HD = 128
QH = 32
KVH = 4


drop_cut = 1677722
keep_scale = 1.0 / 0.9


def mixing(state):
    state = state ^ lax.shift_right_logical(state, jnp.full_like(state, 16))
    state = state * 2146121005
    state = state ^ lax.shift_right_logical(state, jnp.full_like(state, 15))
    state = state * 739982445
    state = state ^ lax.shift_right_logical(state, jnp.full_like(state, 16))
    return state


def head_pass(query_h, grad_h, key_h, value_h, visible, cells, head_seed):
    inverse_root = 1.0 / math.sqrt(query_h.shape[1])
    last_dims = (((1,), (1,)), ((), ()))
    first_dims = (((0,), (0,)), ((), ()))
    scores = (
        lax.dot_general(query_h, key_h, last_dims, preferred_element_type=jnp.float32)
        * inverse_root
    )
    masked = jnp.where(visible, scores, -jnp.inf)
    row_max = jnp.max(masked, axis=1, keepdims=True)
    exp_terms = jnp.where(visible, jnp.exp(scores - row_max), 0.0)
    attn_probs = exp_terms / jnp.sum(exp_terms, axis=1, keepdims=True)
    kept_mask = mixing(cells + head_seed) & 16777215 >= drop_cut
    dropped = jnp.where(kept_mask, attn_probs * keep_scale, 0.0).astype(jnp.bfloat16)
    raw_grad = lax.dot_general(grad_h, value_h, last_dims, preferred_element_type=jnp.float32)
    prob_grad = jnp.where(kept_mask, raw_grad * keep_scale, 0.0)
    row_delta = jnp.sum(attn_probs * prob_grad, axis=1, keepdims=True)
    score_grad = (attn_probs * (prob_grad - row_delta)).astype(jnp.bfloat16)
    query_part = jnp.dot(score_grad, key_h, preferred_element_type=jnp.float32) * inverse_root
    key_part = (
        lax.dot_general(score_grad, query_h, first_dims, preferred_element_type=jnp.float32)
        * inverse_root
    )
    value_part = lax.dot_general(dropped, grad_h, first_dims, preferred_element_type=jnp.float32)
    return (query_part, key_part, value_part)


def per_device(layer_input, queries, key_states, out_grad, doc_positions, drop_seed, value_weight):
    seq_devices = lax.axis_size("seq")
    seq_index = lax.axis_index("seq")
    batch_index = lax.axis_index("fsdp")
    tok_rows = layer_input.shape[1]
    seq_len = tok_rows * seq_devices
    local_input = layer_input[0]
    copies_total = max(KVH, seq_devices)
    copies_dev = copies_total // seq_devices
    per_copy = QH // copies_total
    heads_dev = QH // seq_devices
    full_weight = lax.all_gather(value_weight, ("seq", "fsdp"), axis=0, tiled=True)
    values_loc = jnp.dot(local_input, full_weight, preferred_element_type=jnp.float32).astype(
        jnp.bfloat16
    )
    repeat_count = copies_total // KVH
    key_rep = jnp.repeat(key_states[0].reshape(tok_rows, KVH, HD), repeat_count, axis=1).reshape(
        tok_rows, copies_total * HD
    )
    value_rep = jnp.repeat(values_loc.reshape(tok_rows, KVH, HD), repeat_count, axis=1).reshape(
        tok_rows, copies_total * HD
    )
    query_dev, grad_dev, key_dev, value_dev = (
        lax.all_to_all(queries[0], "seq", split_axis=1, concat_axis=0, tiled=True),
        lax.all_to_all(out_grad[0], "seq", split_axis=1, concat_axis=0, tiled=True),
        lax.all_to_all(key_rep, "seq", split_axis=1, concat_axis=0, tiled=True),
        lax.all_to_all(value_rep, "seq", split_axis=1, concat_axis=0, tiled=True),
    )

    def pair_for(local_head):
        offset = local_head // per_copy * HD
        return (
            lax.dynamic_slice_in_dim(key_dev, offset, HD, 1),
            lax.dynamic_slice_in_dim(value_dev, offset, HD, 1),
        )

    position_row = doc_positions[0]
    rows_idx = lax.broadcasted_iota(jnp.int32, (seq_len, seq_len), 0)
    cols_idx = lax.broadcasted_iota(jnp.int32, (seq_len, seq_len), 1)
    visible = (cols_idx <= rows_idx) & (rows_idx - cols_idx <= position_row[:, None])
    cells = rows_idx * seq_len + cols_idx
    base_seed = mixing(drop_seed + batch_index * 1000003)

    def one_head(carry, local_head):
        key_acc, value_acc = carry
        global_head = seq_index * heads_dev + local_head
        head_seed = mixing(base_seed ^ global_head * 1640531527)
        query_h = lax.dynamic_slice_in_dim(query_dev, local_head * HD, HD, 1)
        grad_h = lax.dynamic_slice_in_dim(grad_dev, local_head * HD, HD, 1)
        key_h, value_h = pair_for(local_head)
        query_part, key_part, value_part = head_pass(
            query_h, grad_h, key_h, value_h, visible, cells, head_seed
        )
        offset = local_head // per_copy * HD
        key_acc = lax.dynamic_update_slice_in_dim(
            key_acc, lax.dynamic_slice_in_dim(key_acc, offset, HD, 1) + key_part, offset, 1
        )
        value_acc = lax.dynamic_update_slice_in_dim(
            value_acc, lax.dynamic_slice_in_dim(value_acc, offset, HD, 1) + value_part, offset, 1
        )
        return ((key_acc, value_acc), query_part.astype(jnp.bfloat16))

    start_acc = jnp.zeros((seq_len, copies_dev * HD), jnp.float32)
    head_ids = jnp.arange(heads_dev, dtype=jnp.int32)
    (key_acc, value_acc), query_parts = lax.scan(one_head, (start_acc, start_acc), head_ids)
    query_grad_dev = jnp.transpose(query_parts, (1, 0, 2)).reshape(seq_len, heads_dev * HD)
    query_grad = lax.all_to_all(query_grad_dev, "seq", split_axis=0, concat_axis=1, tiled=True)
    key_back, value_back = (
        lax.all_to_all(
            key_acc.astype(jnp.bfloat16), "seq", split_axis=0, concat_axis=1, tiled=True
        ).astype(key_acc.dtype),
        lax.all_to_all(
            value_acc.astype(jnp.bfloat16), "seq", split_axis=0, concat_axis=1, tiled=True
        ).astype(value_acc.dtype),
    )
    key_grad = (
        jnp.sum(key_back.reshape(tok_rows, KVH, copies_total // KVH, HD), axis=2)
        .reshape(tok_rows, KVH * HD)
        .astype(jnp.bfloat16)
    )
    value_grad = (
        jnp.sum(value_back.reshape(tok_rows, KVH, copies_total // KVH, HD), axis=2)
        .reshape(tok_rows, KVH * HD)
        .astype(jnp.bfloat16)
    )
    last_dims = (((1,), (1,)), ((), ()))
    input_grad = lax.dot_general(
        value_grad, full_weight, last_dims, preferred_element_type=jnp.float32
    ).astype(jnp.bfloat16)
    summed = lax.psum_scatter(
        lax.dot_general(
            local_input, value_grad, (((0,), (0,)), ((), ())), preferred_element_type=jnp.float32
        ),
        ("seq", "fsdp"),
        scatter_dimension=0,
        tiled=True,
    )
    weight_grad = (summed * (1.0 / math.sqrt(lax.axis_size("fsdp") * seq_len))).astype(jnp.bfloat16)
    return (query_grad[None], key_grad[None], input_grad[None], weight_grad)


def solution(mesh):
    return jax.shard_map(
        per_device,
        mesh=mesh,
        in_specs=(
            P("fsdp", "seq", None),
            P("fsdp", "seq", None),
            P("fsdp", "seq", None),
            P("fsdp", "seq", None),
            P("fsdp", None),
            P(),
            P(("seq", "fsdp"), None),
        ),
        out_specs=(
            P("fsdp", "seq", None),
            P("fsdp", "seq", None),
            P("fsdp", "seq", None),
            P(("seq", "fsdp"), None),
        ),
        check_vma=False,
    )
```

profile of v0, /device:TPU:10, one launch (start us, length us, event | category | flops | bytes accessed | tf_op | source)
XLA Modules:
  0.0 484.5 jit_solution(4034488465177212748)
XLA Ops:
  9.5 3.4 all-to-all-start.1
  12.9 1.8 all_to_all.96
  14.8 1.3 copy.43
  16.1 1.3 all-to-all-done.1
  17.4 4.4 all-to-all-start
  22.5 1.8 all_to_all.104
  24.3 1.4 copy.45
  25.7 10.8 %all-to-all-done = bf16[128,2,2048]{2,0,1:T(8,128)(2,1)} async-done(((bf16[128,2,2048]{2,0,1:T(8,128)(2,1)}), bf16[128,2,2048]{2,0,1:T(8,128)(2,1)}, u32[]{:S(2)}, u32[]{:S(2)}) %all-to-all-start) | async-done | bytes 1048608 | tf_op jit(solution)/shard_map/all_to_all | solution.py:76
  36.5 3.6 all-to-all-start.2
  40.1 51.4 %all-gather.2.cloned.1.call-done = bf16[8192,512]{1,0:T(8,128)(2,1)} async-done(((bf16[256,512]{1,0:T(8,128)(2,1)}), bf16[8192,512]{1,0:T(8,128)(2,1)}) %all-gather.2.cloned.1.call-update) | async-done | bytes 8388624 | tf_op jit(solution)/shard_map/all_gather | solution.py:64
  91.5 4.6 fusion.46
  96.8 3.4 all-to-all-start.3
  100.3 4.4 all-to-all-done.3
  106.1 170.9 %while.17 = (s32[]{:T(128)}, f32[256,256]{1,0:T(8,128)S(1)}, f32[256,256]{1,0:T(8,128)}, bf16[16,256,128]{2,1,0:T(8,128)(2,1)}, s32[16]{0:T(128)S(1)}, /*index=5...) while((s32[]{:T(128)}, f32[256,256]{1,0:T(8,128)S(1)}, ...), condition=%wide.region_4.5_spmd.clone, body=%wide.region_0.4_spmd.clone.sunk | while | flops 88571160 | bytes 3295903 | solution.py:117
  110.6 1.1 select_reduce_fusion.2
  111.7 1.9 fusion.71
  113.6 1.2 multiply_reduce_fusion.2
  121.3 1.1 select_reduce_fusion.2
  122.4 1.9 fusion.71
  124.3 1.2 multiply_reduce_fusion.2
  131.9 1.1 select_reduce_fusion.2
  133.1 1.9 fusion.71
  135.0 1.2 multiply_reduce_fusion.2
  142.6 1.1 select_reduce_fusion.2
  143.8 1.9 fusion.71
  145.6 1.1 multiply_reduce_fusion.2
  153.3 1.1 select_reduce_fusion.2
  154.4 1.9 fusion.71
  156.3 1.2 multiply_reduce_fusion.2
  165.1 1.9 fusion.71
  167.0 1.2 multiply_reduce_fusion.2
  175.8 1.9 fusion.71
  177.7 1.2 multiply_reduce_fusion.2
  186.5 1.9 fusion.71
  188.3 1.2 multiply_reduce_fusion.2
  197.1 1.9 fusion.71
  199.0 1.2 multiply_reduce_fusion.2
  207.8 1.9 fusion.71
  209.7 1.1 multiply_reduce_fusion.2
  218.5 1.9 fusion.71
  220.4 1.1 multiply_reduce_fusion.2
  229.2 1.9 fusion.71
  231.1 1.2 multiply_reduce_fusion.2
  239.9 1.9 fusion.71
  241.7 1.2 multiply_reduce_fusion.2
  249.4 1.1 select_reduce_fusion.2
  250.5 1.9 fusion.71
  252.4 1.2 multiply_reduce_fusion.2
  261.2 1.9 fusion.71
  263.1 1.2 multiply_reduce_fusion.2
  271.9 1.9 fusion.71
  273.8 1.2 multiply_reduce_fusion.2
  277.9 6.8 %all_to_all.130 = bf16[2,128,256]{2,1,0:T(8,128)(2,1)S(1)} all-to-all(bf16[2,128,256]{2,1,0:T(8,128)(2,1)S(1)} %bitcast.65), channel_id=1, replica_groups=mesh['seq'=2,'fsdp'=16] {'seq'}, dimensions={0} | all-to-all | bytes 262144 | tf_op jit(solution)/shard_map/all_to_all | solution.py:124
  284.9 8.1 %convolution_bitcast_fusion = f32[8192,512]{0,1:T(8,128)} fusion(bf16[128,512]{0,1:T(8,128)(2,1)S(1)} %bitcast.60, bf16[1,128,8192]{2,1,0:T(8,128)(2,1)S(1)} %copy-done), kind=kOutput, calls=%fused_computation.54 | convolution fusion | flops 1073741824 | bytes 19005440 | tf_op jit(solution)/shard_map/dot_general | solution.py:143
  293.6 3.4 all-to-all-start.5
  297.0 2.1 copy.47
  299.2 1.3 all_to_all.112
  301.5 3.6 all-to-all-start.4
  306.0 7.5 %fusion.42 = bf16[1,128,8192]{2,1,0:T(8,128)(2,1)} fusion(bf16[128,512]{0,1:T(8,128)(2,1)S(1)} %bitcast.61, bf16[8192,512]{1,0:T(8,128)(2,1)} %all-gather.2.cloned.1.call-done), kind=kOutput, calls=%fused_computation.56 | convolution fusion | flops 1074790400 | bytes 10616832 | tf_op jit(solution)/shard_map/dot_general | solution.py:139
  313.5 2.4 all-to-all-done.4
  315.9 1.3 copy.48
  317.2 2.3 copy.51
  319.5 156.3 %reduce-scatter.2.cloned.1.call-done = f32[256,512]{0,1:T(8,128)} async-done(((f32[8192,512]{0,1:T(8,128)}), f32[256,512]{0,1:T(8,128)}) %reduce-scatter.2.cloned.1.call-update) | async-done | bytes 524304 | tf_op jit(solution)/shard_map/reduce_scatter | solution.py:142
  475.7 1.1 multiply_convert_fusion.1
  (116 shorter events, 62.1 us)
Async XLA Ops:
  7.2 84.3 %copy-start = (bf16[1,128,8192]{2,1,0:T(8,128)(2,1)S(1)}, bf16[1,128,8192]{2,1,0:T(8,128)(2,1)}, u32[]{:S(2)}) copy-start(bf16[1,128,8192]{2,1,0:T(8,128)(2,1)} %param.9) | copy-start | bytes 6291460
  7.2 84.3 %all-gather.2.cloned.1.call-start = ((), (), s32[]{:S(2)}) async-start(), calls=%async_computation.8 | async-start | bytes 8650752 | tf_op jit(solution)/shard_map/all_gather | solution.py:64
  9.5 7.8 %all-to-all-start.1 = ((bf16[128,2,256]{2,0,1:T(8,128)(2,1)}), bf16[128,2,256]{2,0,1:T(8,128)(2,1)S(1)}, u32[]{:S(2)}, u32[]{:S(2)}) async-start(bf16[128,2,256]{2,0,1:T(8,128)(2,1)} %copy.44), calls=%async_computation.1 | async-start | bytes 262144 | tf_op jit(solution)/shard_map/all_to_all | solution.py:78
  17.4 19.1 %all-to-all-start = ((bf16[128,2,2048]{2,0,1:T(8,128)(2,1)}), bf16[128,2,2048]{2,0,1:T(8,128)(2,1)}, u32[]{:S(2)}, u32[]{:S(2)}) async-start(bf16[128,2,2048]{2,0,1:T(8,128)(2,1)} %copy.43), calls=%async_computation | async-start | bytes 2097152 | tf_op jit(solution)/shard_map/all_to_all | solution.py:76
  36.5 60.3 %all-to-all-start.2 = ((bf16[128,2,2048]{2,0,1:T(8,128)(2,1)}), bf16[128,2,2048]{2,0,1:T(8,128)(2,1)S(1)}, u32[]{:S(2)}, u32[]{:S(2)}) async-start(bf16[128,2,2048]{2,0,1:T(8,128)(2,1)} %copy.45), calls=%async_computation.2 | async-start | bytes 2097152 | tf_op jit(solution)/shard_map/all_to_all | solution.py:77
  40.1 66.0 %copy-start.2 = (s32[1,256]{1,0:T(1,128)S(1)}, s32[1,256]{1,0:T(1,128)}, u32[]{:S(2)}) copy-start(s32[1,256]{1,0:T(1,128)} %param.13) | copy-start | bytes 3076
  96.8 7.8 %all-to-all-start.3 = ((bf16[128,2,256]{2,0,1:T(8,128)(2,1)}), bf16[128,2,256]{2,0,1:T(8,128)(2,1)S(1)}, u32[]{:S(2)}, u32[]{:S(2)}) async-start(bf16[128,2,256]{2,0,1:T(8,128)(2,1)} %bitcast.48), calls=%async_computation.3 | async-start | bytes 262144 | tf_op jit(solution)/shard_map/all_to_all | solution.py:79
  100.2 375.5 %reduce-scatter.2.cloned.1.call-start = ((), (), s32[]{:S(2)}) async-start(), calls=%async_computation.9 | async-start | bytes 17301504 | tf_op jit(solution)/shard_map/reduce_scatter | solution.py:142
  104.7 0.7 copy-start.1
  293.6 7.8 %all-to-all-start.5 = ((bf16[2,128,256]{2,1,0:T(8,128)(2,1)}), bf16[2,128,256]{2,1,0:T(8,128)(2,1)S(1)}, u32[]{:S(2)}, u32[]{:S(2)}) async-start(bf16[2,128,256]{2,1,0:T(8,128)(2,1)} %bitcast.13), calls=%async_computation.5 | async-start | bytes 262144 | tf_op jit(solution)/shard_map/all_to_all | solution.py:121
  301.5 14.4 %all-to-all-start.4 = ((bf16[2,128,2048]{2,1,0:T(8,128)(2,1)}), bf16[2,128,2048]{2,1,0:T(8,128)(2,1)S(1)}, u32[]{:S(2)}, u32[]{:S(2)}) async-start(bf16[2,128,2048]{2,1,0:T(8,128)(2,1)} %all_to_all.112), calls=%async_computation.4 | async-start | bytes 2097152 | tf_op jit(solution)/shard_map/all_to_all | solution.py:119
Sparse Core Ops, SparseCore 0:
  10.9 80.5 all-gather.1
  293.1 182.6 reduce-scatter.1
where the time goes:
time: 490 us; the launch traced here: 484 us
  waiting for transfers between devices  228 us (47%)
  matrix products  116 us (24%)
  loops' own time  62.9 us (13%)
  local copies, waits for them, and re-layouts  28.2 us (6%)
  starting transfers between devices  21.8 us (4%)
  between operations  14.8 us (3%)
  blocking collectives  6.85 us (1%)
  other arithmetic  5.65 us (1%)
    reduce_scatter x1, waiting for transfers between devices, per_device(): lax.psum_scatter(lax.dot_general(local_input, value_grad, (((0,), (0,)),...  156 us
    another operation x1, loops' own time, per_device(): lax.scan(one_head, (start_acc, start_acc), head_ids)  62.9 us
    all_gather x1, waiting for transfers between devices, per_device(): lax.all_gather(value_weight, ('seq', 'fsdp'), axis=0, tiled=True)  51.4 us
    dot_general x16, matrix products, head_pass(): lax.dot_general(dropped, grad_h, first_dims, preferred_element_type=jnp.f...  30.1 us
    dot_general x16, matrix products, head_pass(): lax.dot_general(grad_h, value_h, last_dims, preferred_element_type=jnp.fl...  18.4 us
    dot_general x16, matrix products, head_pass(): lax.dot_general(query_h, key_h, last_dims, preferred_element_type=jnp.flo...  17.1 us
    dot_general x16, matrix products, head_pass(): lax.dot_general(score_grad, query_h, first_dims, preferred_element_type=j...  16.3 us
    dot_general x16, matrix products, head_pass(): jnp.dot(score_grad, key_h, preferred_element_type=jnp.float32)  13.9 us
  transfers between devices with their start and end apart: 8, of which 7 were waited for; matrix products, arithmetic and copies ran while one was open for 5% of the time, Pallas kernels for 0%

commit v1 on v0

v1 whole, which is shorter than its diff:
```python
import functools
import math

import jax
import jax.numpy as jnp
from jax import lax
from jax.experimental import pallas as pl
from jax.experimental.pallas import tpu as pltpu
from jax.sharding import PartitionSpec as P

HD = 128
QH = 32
KVH = 4
ROWS = 128


drop_cut = 1677722
keep_scale = 1.0 / 0.9


def mixing(state):
    state = state ^ lax.shift_right_logical(state, jnp.full_like(state, 16))
    state = state * 2146121005
    state = state ^ lax.shift_right_logical(state, jnp.full_like(state, 15))
    state = state * 739982445
    state = state ^ lax.shift_right_logical(state, jnp.full_like(state, 16))
    return state


def attention_kernel(seeds_ref, pos_ref, q_ref, do_ref, k_ref, v_ref, dq_ref, dk_ref, dv_ref, *,
                     seq_len, per_copy):
    c = pl.program_id(0)
    h = pl.program_id(1)
    head_seed = seeds_ref[c * per_copy + h]
    inverse_root = 1.0 / math.sqrt(HD)
    last_dims = (((1,), (1,)), ((), ()))
    first_dims = (((0,), (0,)), ((), ()))

    @pl.when(h == 0)
    def _():
        dk_ref[...] = jnp.zeros_like(dk_ref)
        dv_ref[...] = jnp.zeros_like(dv_ref)

    for r in range(seq_len // ROWS):
        width = (r + 1) * ROWS
        lo = r * ROWS
        q = q_ref[lo:lo + ROWS, :]
        do = do_ref[lo:lo + ROWS, :]
        k = k_ref[0:width, :]
        v = v_ref[0:width, :]
        pos = pos_ref[lo:lo + ROWS, :]
        scores = lax.dot_general(q, k, last_dims, preferred_element_type=jnp.float32) * inverse_root
        rows = lax.broadcasted_iota(jnp.int32, (ROWS, width), 0) + lo
        cols = lax.broadcasted_iota(jnp.int32, (ROWS, width), 1)
        visible = (cols <= rows) & (rows - cols <= pos)
        masked = jnp.where(visible, scores, -jnp.inf)
        row_max = jnp.max(masked, axis=1, keepdims=True)
        exp_terms = jnp.where(visible, jnp.exp(scores - row_max), 0.0)
        probs = exp_terms / jnp.sum(exp_terms, axis=1, keepdims=True)
        kept = (mixing(rows * seq_len + cols + head_seed) & 16777215) >= drop_cut
        dropped = jnp.where(kept, probs * keep_scale, 0.0).astype(jnp.bfloat16)
        raw = lax.dot_general(do, v, last_dims, preferred_element_type=jnp.float32)
        prob_grad = jnp.where(kept, raw * keep_scale, 0.0)
        row_delta = jnp.sum(probs * prob_grad, axis=1, keepdims=True)
        score_grad = (probs * (prob_grad - row_delta)).astype(jnp.bfloat16)
        dq = jnp.dot(score_grad, k, preferred_element_type=jnp.float32) * inverse_root
        dq_ref[lo:lo + ROWS, :] = dq.astype(dq_ref.dtype)
        dk_ref[0:width, :] += (
            lax.dot_general(score_grad, q, first_dims, preferred_element_type=jnp.float32)
            * inverse_root
        )
        dv_ref[0:width, :] += lax.dot_general(
            dropped, do, first_dims, preferred_element_type=jnp.float32
        )


def attention(seeds, pos, query_dev, grad_dev, key_dev, value_dev, copies_dev, per_copy):
    seq_len = query_dev.shape[0]
    head_map = lambda c, h, s: (0, c * per_copy + h)
    copy_map = lambda c, h, s: (0, c)
    whole_map = lambda c, h, s: (0, 0)
    kernel = functools.partial(attention_kernel, seq_len=seq_len, per_copy=per_copy)
    return pl.pallas_call(
        kernel,
        grid_spec=pltpu.PrefetchScalarGridSpec(
            num_scalar_prefetch=1,
            grid=(copies_dev, per_copy),
            in_specs=[
                pl.BlockSpec((seq_len, 1), whole_map),
                pl.BlockSpec((seq_len, HD), head_map),
                pl.BlockSpec((seq_len, HD), head_map),
                pl.BlockSpec((seq_len, HD), copy_map),
                pl.BlockSpec((seq_len, HD), copy_map),
            ],
            out_specs=[
                pl.BlockSpec((seq_len, HD), head_map),
                pl.BlockSpec((seq_len, HD), copy_map),
                pl.BlockSpec((seq_len, HD), copy_map),
            ],
        ),
        out_shape=[
            jax.ShapeDtypeStruct(query_dev.shape, jnp.bfloat16),
            jax.ShapeDtypeStruct(key_dev.shape, jnp.float32),
            jax.ShapeDtypeStruct(key_dev.shape, jnp.float32),
        ],
        compiler_params=pltpu.CompilerParams(
            dimension_semantics=("arbitrary", "arbitrary"),
            vmem_limit_bytes=48 * 1024 * 1024,
        ),
    )(seeds, pos, query_dev, grad_dev, key_dev, value_dev)


def per_device(layer_input, queries, key_states, out_grad, doc_positions, drop_seed, value_weight):
    seq_devices = lax.axis_size("seq")
    fsdp_devices = lax.axis_size("fsdp")
    seq_index = lax.axis_index("seq")
    batch_index = lax.axis_index("fsdp")
    tok_rows = layer_input.shape[1]
    seq_len = tok_rows * seq_devices
    local_input = layer_input[0]
    copies_total = max(KVH, seq_devices)
    copies_dev = copies_total // seq_devices
    per_copy = QH // copies_total
    heads_dev = QH // seq_devices
    repeat_count = copies_total // KVH
    full_weight = lax.all_gather(value_weight, ("seq", "fsdp"), axis=0, tiled=True)
    values_loc = jnp.dot(local_input, full_weight, preferred_element_type=jnp.float32).astype(
        jnp.bfloat16
    )
    key_rep = jnp.repeat(key_states[0].reshape(tok_rows, KVH, HD), repeat_count, axis=1).reshape(
        tok_rows, copies_total * HD
    )
    value_rep = jnp.repeat(values_loc.reshape(tok_rows, KVH, HD), repeat_count, axis=1).reshape(
        tok_rows, copies_total * HD
    )
    query_dev, grad_dev, key_dev, value_dev = (
        lax.all_to_all(queries[0], "seq", split_axis=1, concat_axis=0, tiled=True),
        lax.all_to_all(out_grad[0], "seq", split_axis=1, concat_axis=0, tiled=True),
        lax.all_to_all(key_rep, "seq", split_axis=1, concat_axis=0, tiled=True),
        lax.all_to_all(value_rep, "seq", split_axis=1, concat_axis=0, tiled=True),
    )
    base_seed = mixing(drop_seed + batch_index * 1000003)
    global_heads = seq_index * heads_dev + jnp.arange(heads_dev, dtype=jnp.int32)
    seeds = mixing(base_seed ^ global_heads * 1640531527)
    pos = doc_positions[0][:, None]
    dq, dk, dv = attention(seeds, pos, query_dev, grad_dev, key_dev, value_dev, copies_dev, per_copy)

    query_grad = lax.all_to_all(dq, "seq", split_axis=0, concat_axis=1, tiled=True)
    key_back = lax.all_to_all(
        dk.astype(jnp.bfloat16), "seq", split_axis=0, concat_axis=1, tiled=True
    ).astype(jnp.float32)
    key_grad = (
        jnp.sum(key_back.reshape(tok_rows, KVH, repeat_count, HD), axis=2)
        .reshape(tok_rows, KVH * HD)
        .astype(jnp.bfloat16)
    )

    last_dims = (((1,), (1,)), ((), ()))
    total_tokens = fsdp_devices * seq_len
    if total_tokens * 2 <= full_weight.shape[0] * 4:
        vg_all = lax.all_gather(dv.astype(jnp.bfloat16), ("seq", "fsdp"), axis=0, tiled=False)
        vg_all = vg_all.reshape(seq_devices, fsdp_devices, seq_len, copies_dev, HD)
        vg_tok = jnp.transpose(vg_all, (1, 2, 0, 3, 4)).reshape(
            fsdp_devices, seq_len, KVH, repeat_count, HD
        )
        vg_tok = jnp.sum(vg_tok.astype(jnp.float32), axis=3).astype(jnp.bfloat16).reshape(
            fsdp_devices, seq_devices, tok_rows, KVH * HD
        )
        value_grad = lax.dynamic_index_in_dim(
            lax.dynamic_index_in_dim(vg_tok, batch_index, 0, keepdims=False),
            seq_index,
            0,
            keepdims=False,
        )
        input_cols = lax.all_to_all(
            local_input, ("seq", "fsdp"), split_axis=1, concat_axis=0, tiled=True
        )
        cols_in = input_cols.reshape(seq_devices, fsdp_devices, tok_rows, input_cols.shape[1])
        summed = lax.dot_general(
            cols_in,
            vg_tok,
            (((0, 1, 2), (1, 0, 2)), ((), ())),
            preferred_element_type=jnp.float32,
        )
    else:
        value_back = lax.all_to_all(
            dv.astype(jnp.bfloat16), "seq", split_axis=0, concat_axis=1, tiled=True
        ).astype(jnp.float32)
        value_grad = (
            jnp.sum(value_back.reshape(tok_rows, KVH, repeat_count, HD), axis=2)
            .reshape(tok_rows, KVH * HD)
            .astype(jnp.bfloat16)
        )
        summed = lax.psum_scatter(
            lax.dot_general(
                local_input, value_grad, (((0,), (0,)), ((), ())),
                preferred_element_type=jnp.float32,
            ),
            ("seq", "fsdp"),
            scatter_dimension=0,
            tiled=True,
        )
    input_grad = lax.dot_general(
        value_grad, full_weight, last_dims, preferred_element_type=jnp.float32
    ).astype(jnp.bfloat16)
    weight_grad = (summed * (1.0 / math.sqrt(fsdp_devices * seq_len))).astype(jnp.bfloat16)
    return (query_grad[None], key_grad[None], input_grad[None], weight_grad)


def solution(mesh):
    return jax.shard_map(
        per_device,
        mesh=mesh,
        in_specs=(
            P("fsdp", "seq", None),
            P("fsdp", "seq", None),
            P("fsdp", "seq", None),
            P("fsdp", "seq", None),
            P("fsdp", None),
            P(),
            P(("seq", "fsdp"), None),
        ),
        out_specs=(
            P("fsdp", "seq", None),
            P("fsdp", "seq", None),
            P("fsdp", "seq", None),
            P(("seq", "fsdp"), None),
        ),
        check_vma=False,
    )
```

time: 490 us -> 247 us (0.50)
  waiting for transfers between devices: 228 us -> 125 us
  matrix products: 116 us -> 17 us
  loops' own time: 62.9 us -> 0 us
  Pallas kernels: 0 us -> 19.9 us
  local copies, waits for them, and re-layouts: 28.2 us -> 36.5 us
  other arithmetic: 5.65 us -> 0.7 us
    reduce_scatter x1 -> x0, waiting for transfers between devices: 156 us -> none  [per_device(): lax.psum_scatter(lax.dot_general(local_input, value_grad, (((0,), (0,)),...]
    dot_general x81 -> x1, matrix products: 104 us -> 4.16 us  [per_device(): lax.dot_general(cols_in, vg_tok, (((0, 1, 2), (1, 0, 2)), ((), ())), pref...]
    another operation x1 -> x0, loops' own time: 62.9 us -> none  [per_device(): lax.scan(one_head, (start_acc, start_acc), head_ids)]
    all_gather x0 -> x1, waiting for transfers between devices: none -> 44.6 us  [per_device(): lax.all_gather(dv.astype(jnp.bfloat16), ('seq', 'fsdp'), axis=0, tiled=Fa...]
    reshape x0 -> x3, local copies, waits for them, and re-layouts: none -> 21.3 us  [the longest x2 14.1 us: per_device(): vg_all = vg_all.reshape(seq_devices, fsdp_devices, seq_len, copies_dev, HD)]
    pallas_call x0 -> x1, Pallas kernels: none -> 19.9 us  [attention(): pl.pallas_call(kernel, grid_spec=pltpu.PrefetchScalarGridSpec(num_scalar_...]
    dynamic_slice x16 -> x0, local copies, waits for them, and re-layouts: 9.32 us -> none  [per_device(): lax.scan(one_head, (start_acc, start_acc), head_ids)]
    all_to_all x2, waiting for transfers between devices: 3.44 us -> 8.88 us  [the longest x1 8.87 us: per_device(): lax.all_to_all(dq, 'seq', split_axis=0, concat_axis=1, tiled=True)]
  transfers between devices with their start and end apart: 8 -> 8, of which waited for: 7 -> 6; matrix products, arithmetic and copies ran while one was open for 5% -> 15% of each run, Pallas kernels for 0% -> 0%
where the time goes in v1:
time: 247 us; the launch traced here: 242 us
  waiting for transfers between devices  125 us (51%)
  local copies, waits for them, and re-layouts  36.5 us (15%)
  starting transfers between devices  22 us (9%)
  Pallas kernels  19.9 us (8%)
  matrix products  17 us (7%)
  between operations  14.9 us (6%)
  blocking collectives  6.85 us (3%)
    all_gather x1, waiting for transfers between devices, per_device(): lax.all_gather(value_weight, ('seq', 'fsdp'), axis=0, tiled=True)  53.1 us
    all_gather x1, waiting for transfers between devices, per_device(): lax.all_gather(dv.astype(jnp.bfloat16), ('seq', 'fsdp'), axis=0, tiled=Fa...  44.6 us
    pallas_call x1, Pallas kernels, attention(): pl.pallas_call(kernel, grid_spec=pltpu.PrefetchScalarGridSpec(num_scalar_...  19.9 us
    reshape x2, local copies, waits for them, and re-layouts, per_device(): vg_all = vg_all.reshape(seq_devices, fsdp_devices, seq_len, copies_dev, HD)  14.1 us
    all_to_all x1, waiting for transfers between devices, per_device(): lax.all_to_all(queries[0], 'seq', split_axis=1, concat_axis=0, tiled=True)  11.6 us
    all_to_all x1, waiting for transfers between devices, per_device(): lax.all_to_all(dq, 'seq', split_axis=0, concat_axis=1, tiled=True)  8.87 us
    dot_general x1, matrix products, per_device(): lax.dot_general(value_grad, full_weight, last_dims, preferred_element_typ...  7.59 us
    reshape x1, local copies, waits for them, and re-layouts, per_device(): jnp.transpose(vg_all, (1, 2, 0, 3, 4))  7.19 us
  transfers between devices with their start and end apart: 8, of which 6 were waited for; matrix products, arithmetic and copies ran while one was open for 15% of the time, Pallas kernels for 0%

profile of v1, /device:TPU:10, one launch (start us, length us, event | category | flops | bytes accessed | tf_op | source)
XLA Modules:
  0.0 242.4 jit_solution(1988797615500715687)
XLA Ops:
  7.2 0.0 copy-start.2
  7.2 0.0 copy-start.1
  7.2 0.0 all-gather.4.cloned.1.call-start
  7.2 0.7 all-gather.4.cloned.1.call-update
  7.9 0.9 all_to_all.102
  8.9 0.7 copy.21
  9.5 3.4 %all-to-all-start.2 = ((bf16[128,2,256]{2,0,1:T(8,128)(2,1)}), bf16[128,2,256]{2,0,1:T(8,128)(2,1)S(1)}, u32[]{:S(2)}, u32[]{:S(2)}) async-start(bf16[128,2,256]{2,0,1:T(8,128)(2,1)} %copy.21), calls=%async_computation.2 | async-start | bytes 262144 | tf_op jit(solution)/shard_map/all_to_all | solution.py:139
  12.9 1.8 all_to_all.94
  14.8 1.3 copy.19
  16.1 1.3 all-to-all-done.2
  17.4 3.6 %all-to-all-start = ((bf16[128,2,2048]{2,0,1:T(8,128)(2,1)}), bf16[128,2,2048]{2,0,1:T(8,128)(2,1)S(1)}, u32[]{:S(2)}, u32[]{:S(2)}) async-start(bf16[128,2,2048]{2,0,1:T(8,128)(2,1)} %copy.19), calls=%async_computation | async-start | bytes 2097152 | tf_op jit(solution)/shard_map/all_to_all | solution.py:137
  21.6 0.0 copy-done.2
  21.7 0.1 copy.23.pos_ref
  21.8 0.0 copy-done.1
  21.8 0.8 all_to_all.98
  22.6 1.3 copy.20
  23.9 11.6 %all-to-all-done = bf16[128,2,2048]{2,0,1:T(8,128)(2,1)S(1)} async-done(((bf16[128,2,2048]{2,0,1:T(8,128)(2,1)}), bf16[128,2,2048]{2,0,1:T(8,128)(2,1)S(1)}, u32[]{:S(2)}, u32[]{:S(2)}) %all-to-all-start) | async-done | bytes 1048608 | tf_op jit(solution)/shard_map/all_to_all | solution.py:137
  35.5 3.6 %all-to-all-start.1 = ((bf16[128,2,2048]{2,0,1:T(8,128)(2,1)}), bf16[128,2,2048]{2,0,1:T(8,128)(2,1)S(1)}, u32[]{:S(2)}, u32[]{:S(2)}) async-start(bf16[128,2,2048]{2,0,1:T(8,128)(2,1)} %copy.20), calls=%async_computation.1 | async-start | bytes 2097152 | tf_op jit(solution)/shard_map/all_to_all | solution.py:138
  39.1 53.1 %all-gather.4.cloned.1.call-done = bf16[8192,512]{1,0:T(8,128)(2,1)} async-done(((bf16[256,512]{1,0:T(8,128)(2,1)}), bf16[8192,512]{1,0:T(8,128)(2,1)}) %all-gather.4.cloned.1.call-update) | async-done | bytes 8388624 | tf_op jit(solution)/shard_map/all_gather | solution.py:126
  92.2 5.3 %fusion.17 = bf16[128,512]{1,0:T(8,128)(2,1)S(1)} fusion(bf16[8192,512]{1,0:T(8,128)(2,1)} %all-gather.4.cloned.1.call-done, bf16[1,128,8192]{2,1,0:T(8,128)(2,1)} %param.7), kind=kOutput, calls=%fused_computation.11 | convolution fusion | flops 1073807360 | bytes 10616832 | tf_op jit(solution)/shard_map/dot_general | solution.py:127
  97.5 0.7 copy.48
  98.2 0.0 all-to-all-done.1
  98.2 3.4 %all-to-all-start.3 = ((bf16[128,2,256]{2,0,1:T(8,128)(2,1)}), bf16[128,2,256]{2,0,1:T(8,128)(2,1)S(1)}, u32[]{:S(2)}, u32[]{:S(2)}) async-start(bf16[128,2,256]{2,0,1:T(8,128)(2,1)} %bitcast.54), calls=%async_computation.3 | async-start | bytes 262144 | tf_op jit(solution)/shard_map/all_to_all | solution.py:140
  101.5 0.0 all-gather.6.cloned.1.call-start
  101.6 4.4 %all-to-all-done.3 = bf16[128,2,256]{2,0,1:T(8,128)(2,1)S(1)} async-done(((bf16[128,2,256]{2,0,1:T(8,128)(2,1)}), bf16[128,2,256]{2,0,1:T(8,128)(2,1)S(1)}, u32[]{:S(2)}, u32[]{:S(2)}) %all-to-all-start.3) | async-done | bytes 131104 | tf_op jit(solution)/shard_map/all_to_all | solution.py:140
  106.0 19.9 %shard_map.102 = (bf16[256,2048]{1,0:T(8,128)(2,1)}, f32[256,256]{1,0:T(8,128)S(1)}, f32[256,256]{1,0:T(8,128)S(1)}) custom-call(s32[16]{0:T(128)S(1)} %shift-right-logical_xor_fusion.seeds_ref, s32[256,1]{1,0:T(8,128)S(1)} %copy.23.pos_ref, bf16[256,2048]{1,0:T(8,128)(2,1)S(1)} %bitcast.55, bf16[256,2048]{1,0:T(8,128)(2,1)S(1)} %bitcast.56, ...), custom_call_target="tpu_custom_call" | custom-call | tf_op jit(solution)/shard_map/pallas_call | solution.py:83
  125.9 0.0 copy-start
  125.9 0.7 convert_element_type.33
  126.6 0.0 all-gather.6.cloned.1.call-update
  126.6 6.8 %all_to_all.127 = bf16[2,128,256]{2,1,0:T(8,128)(2,1)S(1)} all-to-all(bf16[2,128,256]{2,1,0:T(8,128)(2,1)S(1)} %bitcast.64), channel_id=1, replica_groups=mesh['seq'=2,'fsdp'=16] {'seq'}, dimensions={0} | all-to-all | bytes 262144 | tf_op jit(solution)/shard_map/all_to_all | solution.py:149
  133.5 3.6 %all-to-all-start.4 = ((bf16[2,128,2048]{2,1,0:T(8,128)(2,1)}), bf16[2,128,2048]{2,1,0:T(8,128)(2,1)S(1)}, u32[]{:S(2)}, u32[]{:S(2)}) async-start(bf16[2,128,2048]{2,1,0:T(8,128)(2,1)} %bitcast.10), calls=%async_computation.4 | async-start | bytes 2097152 | tf_op jit(solution)/shard_map/all_to_all | solution.py:148
  137.1 0.0 copy-done
  137.1 0.6 copy.34
  137.7 2.5 %copy.27 = bf16[128,32,256]{2,0,1:T(8,128)(2,1)} copy(bf16[128,32,256]{2,1,0:T(8,128)(2,1)S(1)} %bitcast.61) | data formatting | bytes 4194304 | tf_op jit(solution)/shard_map/all_to_all | solution.py:175
  140.2 8.9 %all-to-all-done.4 = bf16[2,128,2048]{2,1,0:T(8,128)(2,1)S(1)} async-done(((bf16[2,128,2048]{2,1,0:T(8,128)(2,1)}), bf16[2,128,2048]{2,1,0:T(8,128)(2,1)S(1)}, u32[]{:S(2)}, u32[]{:S(2)}) %all-to-all-start.4) | async-done | bytes 1048608 | tf_op jit(solution)/shard_map/all_to_all | solution.py:148
  149.1 4.4 %all-to-all-start.6 = ((bf16[128,32,256]{2,0,1:T(8,128)(2,1)}), bf16[128,32,256]{2,0,1:T(8,128)(2,1)}, u32[]{:S(2)}, u32[]{:S(2)}) async-start(bf16[128,32,256]{2,0,1:T(8,128)(2,1)} %copy.27), calls=%async_computation.6 | async-start | bytes 4194304 | tf_op jit(solution)/shard_map/all_to_all | solution.py:175
  153.5 0.1 copy.25
  153.6 0.7 all_to_all.116
  154.4 1.1 copy.24
  155.5 1.6 broadcast_in_dim.7
  157.1 44.6 %all-gather.6.cloned.1.call-done = bf16[8192,256]{1,0:T(8,128)(2,1)} async-done(((bf16[256,256]{1,0:T(8,128)(2,1)}), bf16[8192,256]{1,0:T(8,128)(2,1)}) %all-gather.6.cloned.1.call-update) | async-done | bytes 4194320 | tf_op jit(solution)/shard_map/all_gather | solution.py:161
  201.7 6.9 %reshape.60 = bf16[2,16,256,2,128]{4,3,2,1,0:T(2,128)(2,1)} reshape(bf16[8192,256]{1,0:T(8,128)(2,1)} %all-gather.6.cloned.1.call-done) | data formatting | bytes 8388608 | tf_op jit(solution)/shard_map/reshape | solution.py:162
  208.6 7.2 %copy.47 = bf16[2,16,256,2,128]{4,3,0,2,1:T(2,128)(2,1)} copy(bf16[2,16,256,2,128]{4,3,2,1,0:T(2,128)(2,1)} %reshape.60) | data formatting | bytes 8388608 | tf_op jit(solution)/shard_map/reshape | solution.py:162
  215.8 7.2 %reshape.61 = bf16[16,2,128,512]{3,2,1,0:T(8,128)(2,1)} reshape(bf16[16,256,2,2,128]{4,3,2,1,0:T(2,128)(2,1)} %bitcast.59) | data formatting | bytes 8388608 | tf_op jit(solution)/shard_map/reshape | solution.py:163
  223.0 0.0 all-to-all-done.6
  223.0 4.2 %fusion.14 = bf16[256,512]{0,1:T(8,128)(2,1)S(1)} fusion(bf16[2,16,128,256]{3,2,1,0:T(8,128)(2,1)} %bitcast.18, bf16[16,2,128,512]{3,2,1,0:T(8,128)(2,1)} %reshape.61), kind=kOutput, calls=%fused_computation.10 | convolution fusion | flops 1074003968 | bytes 6553600 | tf_op jit(solution)/shard_map/dot_general | solution.py:179
  227.2 0.8 copy.29
  228.0 7.6 %fusion = bf16[1,128,8192]{2,1,0:T(8,128)(2,1)} fusion(bf16[8192,512]{1,0:T(8,128)(2,1)} %all-gather.4.cloned.1.call-done, bf16[16,2,128,512]{3,2,1,0:T(8,128)(2,1)} %reshape.61, s32[]{:T(128)S(6)} %select_n.13, s32[]{:T(128)S(6)} %select_n.15), kind=kOutput, calls=%fused_computation.1 | convolution fusion | flops 1074790400 | bytes 10616840 | tf_op jit(solution)/shard_map/dot_general | solution.py:203
  (2 shorter events, 0.0 us)
Async XLA Ops:
  7.2 14.5 %copy-start.2 = (s32[1,256]{1,0:T(1,128)S(1)}, s32[1,256]{1,0:T(1,128)}, u32[]{:S(2)}) copy-start(s32[1,256]{1,0:T(1,128)} %param.11) | copy-start | bytes 3076
  7.2 14.6 %copy-start.1 = (bf16[1,128,4096]{2,1,0:T(8,128)(2,1)S(1)}, bf16[1,128,4096]{2,1,0:T(8,128)(2,1)}, u32[]{:S(2)}) copy-start(bf16[1,128,4096]{2,1,0:T(8,128)(2,1)} %param.10) | copy-start | bytes 3145732
  7.2 85.0 %all-gather.4.cloned.1.call-start = ((), (), s32[]{:S(2)}) async-start(), calls=%async_computation.7 | async-start | bytes 8650752 | tf_op jit(solution)/shard_map/all_gather | solution.py:126
  9.5 7.8 %all-to-all-start.2 = ((bf16[128,2,256]{2,0,1:T(8,128)(2,1)}), bf16[128,2,256]{2,0,1:T(8,128)(2,1)S(1)}, u32[]{:S(2)}, u32[]{:S(2)}) async-start(bf16[128,2,256]{2,0,1:T(8,128)(2,1)} %copy.21), calls=%async_computation.2 | async-start | bytes 262144 | tf_op jit(solution)/shard_map/all_to_all | solution.py:139
  17.4 18.2 %all-to-all-start = ((bf16[128,2,2048]{2,0,1:T(8,128)(2,1)}), bf16[128,2,2048]{2,0,1:T(8,128)(2,1)S(1)}, u32[]{:S(2)}, u32[]{:S(2)}) async-start(bf16[128,2,2048]{2,0,1:T(8,128)(2,1)} %copy.19), calls=%async_computation | async-start | bytes 2097152 | tf_op jit(solution)/shard_map/all_to_all | solution.py:137
  35.5 62.6 %all-to-all-start.1 = ((bf16[128,2,2048]{2,0,1:T(8,128)(2,1)}), bf16[128,2,2048]{2,0,1:T(8,128)(2,1)S(1)}, u32[]{:S(2)}, u32[]{:S(2)}) async-start(bf16[128,2,2048]{2,0,1:T(8,128)(2,1)} %copy.20), calls=%async_computation.1 | async-start | bytes 2097152 | tf_op jit(solution)/shard_map/all_to_all | solution.py:138
  98.2 7.8 %all-to-all-start.3 = ((bf16[128,2,256]{2,0,1:T(8,128)(2,1)}), bf16[128,2,256]{2,0,1:T(8,128)(2,1)S(1)}, u32[]{:S(2)}, u32[]{:S(2)}) async-start(bf16[128,2,256]{2,0,1:T(8,128)(2,1)} %bitcast.54), calls=%async_computation.3 | async-start | bytes 262144 | tf_op jit(solution)/shard_map/all_to_all | solution.py:140
  101.5 100.1 %all-gather.6.cloned.1.call-start = ((), (), s32[]{:S(2)}) async-start(), calls=%async_computation.8 | async-start | bytes 4325376 | tf_op jit(solution)/shard_map/all_gather | solution.py:161
  125.9 11.2 %copy-start = (bf16[1,128,8192]{2,1,0:T(8,128)(2,1)S(1)}, bf16[1,128,8192]{2,1,0:T(8,128)(2,1)}, u32[]{:S(2)}) copy-start(bf16[1,128,8192]{2,1,0:T(8,128)(2,1)} %param.7) | copy-start | bytes 6291460
  133.5 15.6 %all-to-all-start.4 = ((bf16[2,128,2048]{2,1,0:T(8,128)(2,1)}), bf16[2,128,2048]{2,1,0:T(8,128)(2,1)S(1)}, u32[]{:S(2)}, u32[]{:S(2)}) async-start(bf16[2,128,2048]{2,1,0:T(8,128)(2,1)} %bitcast.10), calls=%async_computation.4 | async-start | bytes 2097152 | tf_op jit(solution)/shard_map/all_to_all | solution.py:148
  149.1 73.9 %all-to-all-start.6 = ((bf16[128,32,256]{2,0,1:T(8,128)(2,1)}), bf16[128,32,256]{2,0,1:T(8,128)(2,1)}, u32[]{:S(2)}, u32[]{:S(2)}) async-start(bf16[128,32,256]{2,0,1:T(8,128)(2,1)} %copy.27), calls=%async_computation.6 | async-start | bytes 4194304 | tf_op jit(solution)/shard_map/all_to_all | solution.py:175
Sparse Core Ops, SparseCore 0:
  10.9 81.3 all-gather.3
  126.7 74.9 all-gather.5

commit v2 on v1

v2 whole, which is shorter than its diff:
```python
import functools
import math

import jax
import jax.numpy as jnp
from jax import lax
from jax.experimental import pallas as pl
from jax.experimental.pallas import tpu as pltpu
from jax.sharding import PartitionSpec as P

HD = 128
QH = 32
KVH = 4
ROWS = 128


drop_cut = 1677722
keep_scale = 1.0 / 0.9


def mixing(state):
    state = state ^ lax.shift_right_logical(state, jnp.full_like(state, 16))
    state = state * 2146121005
    state = state ^ lax.shift_right_logical(state, jnp.full_like(state, 15))
    state = state * 739982445
    state = state ^ lax.shift_right_logical(state, jnp.full_like(state, 16))
    return state


def attention_kernel(seeds_ref, pos_ref, q_ref, do_ref, k_ref, *refs, seq_len, per_copy, first):
    if first:
        (dv_ref,) = refs
    else:
        v_ref, dq_ref, dk_ref = refs
    c = pl.program_id(0)
    h = pl.program_id(1)
    head_seed = seeds_ref[c * per_copy + h]
    inverse_root = 1.0 / math.sqrt(HD)
    last_dims = (((1,), (1,)), ((), ()))
    first_dims = (((0,), (0,)), ((), ()))

    acc_ref = dv_ref if first else dk_ref

    @pl.when(h == 0)
    def _():
        acc_ref[...] = jnp.zeros_like(acc_ref)

    for r in range(seq_len // ROWS):
        width = (r + 1) * ROWS
        lo = r * ROWS
        q = q_ref[lo:lo + ROWS, :]
        do = do_ref[lo:lo + ROWS, :]
        k = k_ref[0:width, :]
        pos = pos_ref[lo:lo + ROWS, :]
        scores = lax.dot_general(q, k, last_dims, preferred_element_type=jnp.float32) * inverse_root
        rows = lax.broadcasted_iota(jnp.int32, (ROWS, width), 0) + lo
        cols = lax.broadcasted_iota(jnp.int32, (ROWS, width), 1)
        visible = (cols <= rows) & (rows - cols <= pos)
        masked = jnp.where(visible, scores, -jnp.inf)
        row_max = jnp.max(masked, axis=1, keepdims=True)
        exp_terms = jnp.where(visible, jnp.exp(scores - row_max), 0.0)
        probs = exp_terms / jnp.sum(exp_terms, axis=1, keepdims=True)
        kept = (mixing(rows * seq_len + cols + head_seed) & 16777215) >= drop_cut
        if first:
            dropped = jnp.where(kept, probs * keep_scale, 0.0).astype(jnp.bfloat16)
            dv_ref[0:width, :] += lax.dot_general(
                dropped, do, first_dims, preferred_element_type=jnp.float32
            )
            continue
        v = v_ref[0:width, :]
        raw = lax.dot_general(do, v, last_dims, preferred_element_type=jnp.float32)
        prob_grad = jnp.where(kept, raw * keep_scale, 0.0)
        row_delta = jnp.sum(probs * prob_grad, axis=1, keepdims=True)
        score_grad = (probs * (prob_grad - row_delta)).astype(jnp.bfloat16)
        dq = jnp.dot(score_grad, k, preferred_element_type=jnp.float32) * inverse_root
        dq_ref[lo:lo + ROWS, :] = dq.astype(dq_ref.dtype)
        dk_ref[0:width, :] += (
            lax.dot_general(score_grad, q, first_dims, preferred_element_type=jnp.float32)
            * inverse_root
        )


def attention(seeds, pos, query_dev, grad_dev, key_dev, value_dev, copies_dev, per_copy):
    seq_len = query_dev.shape[0]
    head_map = lambda c, h, s: (0, c * per_copy + h)
    copy_map = lambda c, h, s: (0, c)
    whole_map = lambda c, h, s: (0, 0)
    first = value_dev is None
    kernel = functools.partial(
        attention_kernel, seq_len=seq_len, per_copy=per_copy, first=first
    )
    in_specs = [
        pl.BlockSpec((seq_len, 1), whole_map),
        pl.BlockSpec((seq_len, HD), head_map),
        pl.BlockSpec((seq_len, HD), head_map),
        pl.BlockSpec((seq_len, HD), copy_map),
    ]
    operands = [seeds, pos, query_dev, grad_dev, key_dev]
    acc = jax.ShapeDtypeStruct(key_dev.shape, jnp.float32)
    if first:
        out_specs = [pl.BlockSpec((seq_len, HD), copy_map)]
        out_shape = [acc]
    else:
        in_specs.append(pl.BlockSpec((seq_len, HD), copy_map))
        operands.append(value_dev)
        out_specs = [pl.BlockSpec((seq_len, HD), head_map), pl.BlockSpec((seq_len, HD), copy_map)]
        out_shape = [jax.ShapeDtypeStruct(query_dev.shape, jnp.bfloat16), acc]
    return pl.pallas_call(
        kernel,
        grid_spec=pltpu.PrefetchScalarGridSpec(
            num_scalar_prefetch=1,
            grid=(copies_dev, per_copy),
            in_specs=in_specs,
            out_specs=out_specs,
        ),
        out_shape=out_shape,
        compiler_params=pltpu.CompilerParams(
            dimension_semantics=("arbitrary", "arbitrary"),
            vmem_limit_bytes=48 * 1024 * 1024,
        ),
    )(*operands)


def per_device(layer_input, queries, key_states, out_grad, doc_positions, drop_seed, value_weight):
    seq_devices = lax.axis_size("seq")
    fsdp_devices = lax.axis_size("fsdp")
    seq_index = lax.axis_index("seq")
    batch_index = lax.axis_index("fsdp")
    tok_rows = layer_input.shape[1]
    seq_len = tok_rows * seq_devices
    local_input = layer_input[0]
    copies_total = max(KVH, seq_devices)
    copies_dev = copies_total // seq_devices
    per_copy = QH // copies_total
    heads_dev = QH // seq_devices
    repeat_count = copies_total // KVH
    full_weight = lax.all_gather(value_weight, ("seq", "fsdp"), axis=0, tiled=True)
    block_rows = value_weight.shape[0]
    input_cols = lax.all_to_all(
        local_input.reshape(tok_rows, seq_devices, fsdp_devices, block_rows),
        "fsdp",
        split_axis=2,
        concat_axis=0,
        tiled=True,
    ).reshape(fsdp_devices * tok_rows, seq_devices * block_rows)
    key_rep = jnp.repeat(key_states[0].reshape(tok_rows, KVH, HD), repeat_count, axis=1).reshape(
        tok_rows, copies_total * HD
    )
    query_dev, grad_dev, key_dev = (
        lax.all_to_all(queries[0], "seq", split_axis=1, concat_axis=0, tiled=True),
        lax.all_to_all(out_grad[0], "seq", split_axis=1, concat_axis=0, tiled=True),
        lax.all_to_all(key_rep, "seq", split_axis=1, concat_axis=0, tiled=True),
    )
    base_seed = mixing(drop_seed + batch_index * 1000003)
    global_heads = seq_index * heads_dev + jnp.arange(heads_dev, dtype=jnp.int32)
    seeds = mixing(base_seed ^ global_heads * 1640531527)
    pos = doc_positions[0][:, None]
    (dv,) = attention(seeds, pos, query_dev, grad_dev, key_dev, None, copies_dev, per_copy)
    dv, full_weight = lax.optimization_barrier((dv, full_weight))
    value_back = lax.all_to_all(
        dv.astype(jnp.bfloat16), "seq", split_axis=0, concat_axis=1, tiled=True
    ).astype(jnp.float32)
    value_grad = (
        jnp.sum(value_back.reshape(tok_rows, KVH, repeat_count, HD), axis=2)
        .reshape(tok_rows, KVH * HD)
        .astype(jnp.bfloat16)
    )
    value_grads = lax.all_gather(value_grad, "fsdp", axis=0, tiled=True)

    values_loc = jnp.dot(local_input, full_weight, preferred_element_type=jnp.float32).astype(
        jnp.bfloat16
    )
    value_rep = jnp.repeat(values_loc.reshape(tok_rows, KVH, HD), repeat_count, axis=1).reshape(
        tok_rows, copies_total * HD
    )
    value_dev = lax.all_to_all(value_rep, "seq", split_axis=1, concat_axis=0, tiled=True)
    dq, dk = attention(seeds, pos, query_dev, grad_dev, key_dev, value_dev, copies_dev, per_copy)
    value_grads, input_cols, dq, dk = lax.optimization_barrier((value_grads, input_cols, dq, dk))
    partial = lax.dot_general(
        input_cols, value_grads, (((0,), (0,)), ((), ())), preferred_element_type=jnp.float32
    )
    summed = lax.psum_scatter(partial, "seq", scatter_dimension=0, tiled=True)
    weight_grad = (summed * (1.0 / math.sqrt(fsdp_devices * seq_len))).astype(jnp.bfloat16)
    query_grad = lax.all_to_all(dq, "seq", split_axis=0, concat_axis=1, tiled=True)
    key_back = lax.all_to_all(
        dk.astype(jnp.bfloat16), "seq", split_axis=0, concat_axis=1, tiled=True
    ).astype(jnp.float32)
    key_grad = (
        jnp.sum(key_back.reshape(tok_rows, KVH, repeat_count, HD), axis=2)
        .reshape(tok_rows, KVH * HD)
        .astype(jnp.bfloat16)
    )
    last_dims = (((1,), (1,)), ((), ()))
    input_grad = lax.dot_general(
        value_grad, full_weight, last_dims, preferred_element_type=jnp.float32
    ).astype(jnp.bfloat16)
    return (query_grad[None], key_grad[None], input_grad[None], weight_grad)


def solution(mesh):
    return jax.shard_map(
        per_device,
        mesh=mesh,
        in_specs=(
            P("fsdp", "seq", None),
            P("fsdp", "seq", None),
            P("fsdp", "seq", None),
            P("fsdp", "seq", None),
            P("fsdp", None),
            P(),
            P(("seq", "fsdp"), None),
        ),
        out_specs=(
            P("fsdp", "seq", None),
            P("fsdp", "seq", None),
            P("fsdp", "seq", None),
            P(("seq", "fsdp"), None),
        ),
        check_vma=False,
    )
```

time: 247 us -> 242 us (0.980); the launches traced: 242 us -> 241 us
  Pallas kernels: 19.9 us -> 35.2 us
  waiting for transfers between devices: 125 us -> 112 us
  local copies, waits for them, and re-layouts: 36.5 us -> 24.8 us
  starting transfers between devices: 22 us -> 26 us
    all_to_all x1 -> x2, waiting for transfers between devices: 0.01 us -> 49.1 us  [the longest x1 49.1 us: per_device(): lax.all_to_all(local_input.reshape(tok_rows, seq_devices, fsdp_devices, b...]
    all_gather x1, waiting for transfers between devices: 44.6 us -> 0.01 us  [per_device(): value_grads = lax.all_gather(value_grad, 'fsdp', axis=0, tiled=True)]
    all_gather x1, waiting for transfers between devices: 53.1 us -> 20.2 us  [per_device(): lax.all_gather(value_weight, ('seq', 'fsdp'), axis=0, tiled=True)]
    reshape x3 -> x0, local copies, waits for them, and re-layouts: 21.3 us -> none  [the longest x2 14.1 us: per_device(): vg_all = vg_all.reshape(seq_devices, fsdp_devices, seq_len, copies_dev, HD)]
    all_to_all x1, waiting for transfers between devices: 0.01 us -> 15.8 us  [per_device(): lax.all_to_all(out_grad[0], 'seq', split_axis=1, concat_axis=0, tiled=True)]
    pallas_call x1 -> x2, Pallas kernels: 19.9 us -> 35.2 us  [attention(): pl.pallas_call(kernel, grid_spec=pltpu.PrefetchScalarGridSpec(num_scalar_...]
    unnamed x8 -> x10, local copies, waits for them, and re-layouts: 1.45 us -> 6.6 us
    all_to_all x1, waiting for transfers between devices: 4.39 us -> 0.01 us  [per_device(): lax.all_to_all(value_rep, 'seq', split_axis=1, concat_axis=0, tiled=True)]
  transfers between devices with their start and end apart: 8 -> 10, of which waited for: 6 -> 6; matrix products, arithmetic and copies ran while one was open for 15% -> 14% of each run, Pallas kernels for 0% -> 15%
where the time goes in v2:
time: 242 us; the launch traced here: 241 us
  waiting for transfers between devices  112 us (46%)
  Pallas kernels  35.2 us (15%)
  starting transfers between devices  26 us (11%)
  local copies, waits for them, and re-layouts  24.8 us (10%)
  matrix products  18.4 us (8%)
  between operations  14.5 us (6%)
  blocking collectives  7.7 us (3%)
    all_to_all x1, waiting for transfers between devices, per_device(): lax.all_to_all(local_input.reshape(tok_rows, seq_devices, fsdp_devices, b...  49.1 us
    pallas_call x2, Pallas kernels, attention(): pl.pallas_call(kernel, grid_spec=pltpu.PrefetchScalarGridSpec(num_scalar_...  35.2 us
    all_gather x1, waiting for transfers between devices, per_device(): lax.all_gather(value_weight, ('seq', 'fsdp'), axis=0, tiled=True)  20.2 us
    all_to_all x1, waiting for transfers between devices, per_device(): lax.all_to_all(out_grad[0], 'seq', split_axis=1, concat_axis=0, tiled=True)  15.8 us
    all_to_all x1, waiting for transfers between devices, per_device(): lax.all_to_all(queries[0], 'seq', split_axis=1, concat_axis=0, tiled=True)  12.4 us
    all_to_all x1, waiting for transfers between devices, per_device(): lax.all_to_all(dq, 'seq', split_axis=0, concat_axis=1, tiled=True)  12 us
    all_to_all x1, blocking collectives, per_device(): lax.all_to_all(dk.astype(jnp.bfloat16), 'seq', split_axis=0, concat_axis=...  7.7 us
    dot_general x1, matrix products, per_device(): lax.dot_general(value_grad, full_weight, last_dims, preferred_element_typ...  7.59 us
  transfers between devices with their start and end apart: 10, of which 6 were waited for; matrix products, arithmetic and copies ran while one was open for 14% of the time, Pallas kernels for 15%

profile of v2, /device:TPU:10, one launch (start us, length us, event | category | flops | bytes accessed | tf_op | source)
XLA Modules:
  0.0 240.7 jit_solution(6988330860585188898)
XLA Ops:
  7.2 0.0 all-gather.3.cloned.1.call-start
  7.2 0.7 all-gather.3.cloned.1.call-update
  7.9 0.9 all_to_all.115
  8.8 0.7 copy.39
  9.5 3.4 %all-to-all-start.2 = ((bf16[128,2,256]{2,0,1:T(8,128)(2,1)}), bf16[128,2,256]{2,0,1:T(8,128)(2,1)S(1)}, u32[]{:S(2)}, u32[]{:S(2)}) async-start(bf16[128,2,256]{2,0,1:T(8,128)(2,1)} %copy.39), calls=%async_computation.2 | async-start | bytes 262144 | tf_op jit(solution)/shard_map/all_to_all | solution.py:152
  12.9 1.8 all_to_all.107
  14.7 0.0 copy-start.2
  14.8 1.3 copy.37
  16.1 1.3 all-to-all-done.2
  17.4 3.6 %all-to-all-start = ((bf16[128,2,2048]{2,0,1:T(8,128)(2,1)}), bf16[128,2,2048]{2,0,1:T(8,128)(2,1)S(1)}, u32[]{:S(2)}, u32[]{:S(2)}) async-start(bf16[128,2,2048]{2,0,1:T(8,128)(2,1)} %copy.37), calls=%async_computation | async-start | bytes 2097152 | tf_op jit(solution)/shard_map/all_to_all | solution.py:150
  21.0 0.0 copy-done.2
  21.0 0.8 all_to_all.111
  21.8 0.0 copy-start.3
  21.8 1.3 copy.38
  23.1 12.4 %all-to-all-done = bf16[128,2,2048]{2,0,1:T(8,128)(2,1)S(1)} async-done(((bf16[128,2,2048]{2,0,1:T(8,128)(2,1)}), bf16[128,2,2048]{2,0,1:T(8,128)(2,1)S(1)}, u32[]{:S(2)}, u32[]{:S(2)}) %all-to-all-start) | async-done | bytes 1048608 | tf_op jit(solution)/shard_map/all_to_all | solution.py:150
  35.5 3.6 %all-to-all-start.1 = ((bf16[128,2,2048]{2,0,1:T(8,128)(2,1)}), bf16[128,2,2048]{2,0,1:T(8,128)(2,1)S(1)}, u32[]{:S(2)}, u32[]{:S(2)}) async-start(bf16[128,2,2048]{2,0,1:T(8,128)(2,1)} %copy.38), calls=%async_computation.1 | async-start | bytes 2097152 | tf_op jit(solution)/shard_map/all_to_all | solution.py:151
  39.8 0.0 copy-done.3
  39.8 0.1 copy.40.pos_ref
  39.9 15.8 %all-to-all-done.1 = bf16[128,2,2048]{2,0,1:T(8,128)(2,1)S(1)} async-done(((bf16[128,2,2048]{2,0,1:T(8,128)(2,1)}), bf16[128,2,2048]{2,0,1:T(8,128)(2,1)S(1)}, u32[]{:S(2)}, u32[]{:S(2)}) %all-to-all-start.1) | async-done | bytes 1048608 | tf_op jit(solution)/shard_map/all_to_all | solution.py:151
  55.8 16.4 %shard_map.102 = f32[256,256]{1,0:T(8,128)S(1)} custom-call(s32[16]{0:T(128)S(1)} %shift-right-logical_xor_fusion.seeds_ref, s32[256,1]{1,0:T(8,128)S(1)} %copy.40.pos_ref, bf16[256,2048]{1,0:T(8,128)(2,1)S(1)} %bitcast.47, bf16[256,2048]{1,0:T(8,128)(2,1)S(1)} %bitcast.49, bf16[256,256]{1,0:T(8,128)(2,1)S(1)} %bitcast.51), custom_call_target="tpu_custom_call" | custom-call | tf_op jit(solution)/shard_map/pallas_call | solution.py:108
  72.2 20.2 %all-gather.3.cloned.1.call-done = bf16[8192,512]{1,0:T(8,128)(2,1)} async-done(((bf16[256,512]{1,0:T(8,128)(2,1)}), bf16[8192,512]{1,0:T(8,128)(2,1)}) %all-gather.3.cloned.1.call-update) | async-done | bytes 8388624 | tf_op jit(solution)/shard_map/all_gather | solution.py:137
  92.4 0.8 copy.41
  93.1 3.4 %all-to-all-start.3 = ((bf16[2,128,256]{1,2,0:T(8,128)(2,1)}), bf16[2,128,256]{1,2,0:T(8,128)(2,1)S(1)}, u32[]{:S(2)}, u32[]{:S(2)}) async-start(bf16[2,128,256]{1,2,0:T(8,128)(2,1)} %copy.41), calls=%async_computation.3 | async-start | bytes 262144 | tf_op jit(solution)/shard_map/all_to_all | solution.py:160
  96.5 4.1 %copy.42 = bf16[1,128,8192]{1,2,0:T(8,128)(2,1)} copy(bf16[1,128,8192]{2,1,0:T(8,128)(2,1)} %param.7) | data formatting | bytes 4194304 | tf_op args[0]
  100.6 3.1 %copy.43 = bf16[128,2,16,256]{0,3,1,2:T(8,128)(2,1)} copy(bf16[128,2,16,256]{0,3,2,1:T(8,128)(2,1)} %bitcast.55) | data formatting | bytes 4194304 | tf_op jit(solution)/shard_map/reshape;squeeze | solution.py:140
  103.7 0.0 all-to-all-done.3
  103.7 0.0 copy-start
  103.7 0.7 copy-done
  104.4 4.8 %all-to-all-start.4 = ((bf16[128,2,16,256]{0,3,1,2:T(8,128)(2,1)}), bf16[128,2,16,256]{0,3,1,2:T(8,128)(2,1)}, u32[]{:S(2)}, u32[]{:S(2)}) async-start(bf16[128,2,16,256]{0,3,1,2:T(8,128)(2,1)} %copy.43), calls=%async_computation.4 | async-start | bytes 4194304 | tf_op jit(solution)/shard_map/all_to_all | solution.py:139
  109.1 0.0 all-gather.5.cloned.1.call-start
  109.2 0.7 all-gather.5.cloned.1.call-update
  109.9 6.4 %fusion.3 = bf16[512,128]{1,0:T(8,128)(2,1)S(1)} fusion(bf16[8192,512]{1,0:T(8,128)(2,1)} %all-gather.3.cloned.1.call-done, bf16[1,128,8192]{2,1,0:T(8,128)(2,1)} %param.7), kind=kOutput, calls=%fused_computation.5 | convolution fusion | flops 1073807360 | bytes 10616832 | tf_op jit(solution)/shard_map/dot_general | solution.py:170
  116.3 0.8 copy.45
  117.0 49.1 %all-to-all-done.4 = bf16[128,2,16,256]{0,3,1,2:T(8,128)(2,1)} async-done(((bf16[128,2,16,256]{0,3,1,2:T(8,128)(2,1)}), bf16[128,2,16,256]{0,3,1,2:T(8,128)(2,1)}, u32[]{:S(2)}, u32[]{:S(2)}) %all-to-all-start.4) | async-done | bytes 2097184 | tf_op jit(solution)/shard_map/all_to_all | solution.py:139
  166.2 3.5 %all-to-all-start.5 = ((bf16[128,2,256]{2,0,1:T(8,128)(2,1)}), bf16[128,2,256]{2,0,1:T(8,128)(2,1)S(1)}, u32[]{:S(2)}, u32[]{:S(2)}) async-start(bf16[128,2,256]{2,0,1:T(8,128)(2,1)} %copy.45), calls=%async_computation.5 | async-start | bytes 262144 | tf_op jit(solution)/shard_map/all_to_all | solution.py:176
  169.6 0.0 reduce-scatter.2.cloned.1.call-start
  169.6 2.9 %copy.44 = bf16[16,128,2,1,256]{1,0,4,2,3:T(8,128)(2,1)S(1)} copy(bf16[16,128,2,1,256]{1,4,2,0,3:T(8,128)(2,1)} %bitcast.12) | data formatting | bytes 4194304 | tf_op jit(solution)/shard_map/all_to_all | solution.py:139
  172.6 1.9 copy.51
  174.4 0.0 all-to-all-done.5
  174.4 18.8 %shard_map.103 = (bf16[256,2048]{1,0:T(8,128)(2,1)}, f32[256,256]{1,0:T(8,128)S(1)}) custom-call(s32[16]{0:T(128)S(1)} %shift-right-logical_xor_fusion.seeds_ref, s32[256,1]{1,0:T(8,128)S(1)} %copy.40.pos_ref, bf16[256,2048]{1,0:T(8,128)(2,1)S(1)} %bitcast.48, bf16[256,2048]{1,0:T(8,128)(2,1)S(1)} %bitcast.50, bf16[256,256]{1,0:T(8,128)(2,1)S(1)} %bitcast.52, ...), custom_call_target="tpu_custom_call" | custom-call | tf_op jit(solution)/shard_map/pallas_call | solution.py:108
  193.3 0.0 all-gather.5.cloned.1.call-done
  193.3 4.5 %fusion.8 = f32[512,512]{1,0:T(8,128)} fusion(bf16[2048,512]{0,1:T(8,128)(2,1)} %bitcast.57, bf16[2048,512]{0,1:T(8,128)(2,1)} %all-gather.5.cloned.1.call-done), kind=kOutput, calls=%fused_computation.12 | convolution fusion | flops 1073741824 | bytes 5242880 | tf_op jit(solution)/shard_map/dot_general | solution.py:179
  197.8 0.0 copy-start.1
  197.8 0.0 reduce-scatter.2.cloned.1.call-update
  197.8 7.7 %all_to_all.145 = bf16[2,128,256]{2,1,0:T(8,128)(2,1)S(1)} all-to-all(bf16[2,128,256]{2,1,0:T(8,128)(2,1)S(1)} %bitcast.61), channel_id=1, replica_groups=mesh['seq'=2,'fsdp'=16] {'seq'}, dimensions={0} | all-to-all | bytes 262144 | tf_op jit(solution)/shard_map/all_to_all | solution.py:185
  205.5 3.8 %all-to-all-start.6 = ((bf16[2,128,2048]{2,1,0:T(8,128)(2,1)}), bf16[2,128,2048]{2,1,0:T(8,128)(2,1)S(1)}, u32[]{:S(2)}, u32[]{:S(2)}) async-start(bf16[2,128,2048]{2,1,0:T(8,128)(2,1)} %bitcast.21), calls=%async_computation.6 | async-start | bytes 2097152 | tf_op jit(solution)/shard_map/all_to_all | solution.py:184
  209.3 0.0 copy-done.1
  209.3 7.6 %fusion = bf16[1,128,8192]{2,1,0:T(8,128)(2,1)} fusion(bf16[128,512]{0,1:T(8,128)(2,1)S(1)} %bitcast.59, bf16[8192,512]{1,0:T(8,128)(2,1)} %all-gather.3.cloned.1.call-done), kind=kOutput, calls=%fused_computation.1 | convolution fusion | flops 1074790400 | bytes 10616832 | tf_op jit(solution)/shard_map/dot_general | solution.py:194
  216.9 0.1 copy.48
  217.0 0.7 all_to_all.136
  217.8 12.0 %all-to-all-done.6 = bf16[2,128,2048]{2,1,0:T(8,128)(2,1)S(1)} async-done(((bf16[2,128,2048]{2,1,0:T(8,128)(2,1)}), bf16[2,128,2048]{2,1,0:T(8,128)(2,1)S(1)}, u32[]{:S(2)}, u32[]{:S(2)}) %all-to-all-start.6) | async-done | bytes 1048608 | tf_op jit(solution)/shard_map/all_to_all | solution.py:184
  229.7 1.1 copy.47
  230.8 1.6 broadcast_in_dim.7
  232.4 0.0 reduce-scatter.2.cloned.1.call-done
  232.4 1.8 multiply_convert_fusion
  (3 shorter events, 0.0 us)
Async XLA Ops:
  7.2 85.2 %all-gather.3.cloned.1.call-start = ((), (), s32[]{:S(2)}) async-start(), calls=%async_computation.9 | async-start | bytes 8650752 | tf_op jit(solution)/shard_map/all_gather | solution.py:137
  9.5 7.8 %all-to-all-start.2 = ((bf16[128,2,256]{2,0,1:T(8,128)(2,1)}), bf16[128,2,256]{2,0,1:T(8,128)(2,1)S(1)}, u32[]{:S(2)}, u32[]{:S(2)}) async-start(bf16[128,2,256]{2,0,1:T(8,128)(2,1)} %copy.39), calls=%async_computation.2 | async-start | bytes 262144 | tf_op jit(solution)/shard_map/all_to_all | solution.py:152
  14.7 6.2 %copy-start.2 = (bf16[1,128,4096]{2,1,0:T(8,128)(2,1)S(1)}, bf16[1,128,4096]{2,1,0:T(8,128)(2,1)}, u32[]{:S(2)}) copy-start(bf16[1,128,4096]{2,1,0:T(8,128)(2,1)} %param.10) | copy-start | bytes 3145732
  17.4 18.2 %all-to-all-start = ((bf16[128,2,2048]{2,0,1:T(8,128)(2,1)}), bf16[128,2,2048]{2,0,1:T(8,128)(2,1)S(1)}, u32[]{:S(2)}, u32[]{:S(2)}) async-start(bf16[128,2,2048]{2,0,1:T(8,128)(2,1)} %copy.37), calls=%async_computation | async-start | bytes 2097152 | tf_op jit(solution)/shard_map/all_to_all | solution.py:150
  21.8 18.0 %copy-start.3 = (s32[1,256]{1,0:T(1,128)S(1)}, s32[1,256]{1,0:T(1,128)}, u32[]{:S(2)}) copy-start(s32[1,256]{1,0:T(1,128)} %param.11) | copy-start | bytes 3076
  35.5 20.2 %all-to-all-start.1 = ((bf16[128,2,2048]{2,0,1:T(8,128)(2,1)}), bf16[128,2,2048]{2,0,1:T(8,128)(2,1)S(1)}, u32[]{:S(2)}, u32[]{:S(2)}) async-start(bf16[128,2,2048]{2,0,1:T(8,128)(2,1)} %copy.38), calls=%async_computation.1 | async-start | bytes 2097152 | tf_op jit(solution)/shard_map/all_to_all | solution.py:151
  93.1 10.6 %all-to-all-start.3 = ((bf16[2,128,256]{1,2,0:T(8,128)(2,1)}), bf16[2,128,256]{1,2,0:T(8,128)(2,1)S(1)}, u32[]{:S(2)}, u32[]{:S(2)}) async-start(bf16[2,128,256]{1,2,0:T(8,128)(2,1)} %copy.41), calls=%async_computation.3 | async-start | bytes 262144 | tf_op jit(solution)/shard_map/all_to_all | solution.py:160
  103.7 0.7 copy-start
  104.4 61.8 %all-to-all-start.4 = ((bf16[128,2,16,256]{0,3,1,2:T(8,128)(2,1)}), bf16[128,2,16,256]{0,3,1,2:T(8,128)(2,1)}, u32[]{:S(2)}, u32[]{:S(2)}) async-start(bf16[128,2,16,256]{0,3,1,2:T(8,128)(2,1)} %copy.43), calls=%async_computation.4 | async-start | bytes 4194304 | tf_op jit(solution)/shard_map/all_to_all | solution.py:139
  109.1 84.1 %all-gather.5.cloned.1.call-start = ((), (), s32[]{:S(2)}) async-start(), calls=%async_computation.10 | async-start | bytes 2228224 | tf_op jit(solution)/shard_map/all_gather | solution.py:168
  166.2 8.3 %all-to-all-start.5 = ((bf16[128,2,256]{2,0,1:T(8,128)(2,1)}), bf16[128,2,256]{2,0,1:T(8,128)(2,1)S(1)}, u32[]{:S(2)}, u32[]{:S(2)}) async-start(bf16[128,2,256]{2,0,1:T(8,128)(2,1)} %copy.45), calls=%async_computation.5 | async-start | bytes 262144 | tf_op jit(solution)/shard_map/all_to_all | solution.py:176
  169.6 62.8 %reduce-scatter.2.cloned.1.call-start = ((), (), s32[]{:S(2)}) async-start(), calls=%async_computation.11 | async-start | bytes 1572864 | tf_op jit(solution)/shard_map/reduce_scatter | solution.py:182
  197.8 11.5 %copy-start.1 = (bf16[2,128,256]{1,2,0:T(8,128)(2,1)S(1)}, bf16[2,128,256]{1,2,0:T(8,128)(2,1)}, u32[]{:S(2)}) copy-start(bf16[2,128,256]{1,2,0:T(8,128)(2,1)} %copy-done) | copy-start | bytes 393220
  205.5 24.2 %all-to-all-start.6 = ((bf16[2,128,2048]{2,1,0:T(8,128)(2,1)}), bf16[2,128,2048]{2,1,0:T(8,128)(2,1)S(1)}, u32[]{:S(2)}, u32[]{:S(2)}) async-start(bf16[2,128,2048]{2,1,0:T(8,128)(2,1)} %bitcast.21), calls=%async_computation.6 | async-start | bytes 2097152 | tf_op jit(solution)/shard_map/all_to_all | solution.py:184
Sparse Core Ops, SparseCore 0:
  10.8 81.4 all-gather.2
  112.7 59.7 all-gather.4
  197.9 27.8 reduce-scatter.1

commit v3 on v2

--- a/solution.py
+++ b/solution.py
@@ -156,7 +156,6 @@
     seeds = mixing(base_seed ^ global_heads * 1640531527)
     pos = doc_positions[0][:, None]
     (dv,) = attention(seeds, pos, query_dev, grad_dev, key_dev, None, copies_dev, per_copy)
-    dv, full_weight = lax.optimization_barrier((dv, full_weight))
     value_back = lax.all_to_all(
         dv.astype(jnp.bfloat16), "seq", split_axis=0, concat_axis=1, tiled=True
     ).astype(jnp.float32)
@@ -165,7 +164,26 @@
         .reshape(tok_rows, KVH * HD)
         .astype(jnp.bfloat16)
     )
-    value_grads = lax.all_gather(value_grad, "fsdp", axis=0, tiled=True)
+    value_grads = lax.all_to_all(
+        jnp.broadcast_to(value_grad[None], (fsdp_devices,) + value_grad.shape),
+        "fsdp",
+        split_axis=0,
+        concat_axis=0,
+        tiled=True,
+    ).reshape(fsdp_devices * tok_rows, KVH * HD)
+
+    partial = lax.dot_general(
+        input_cols, value_grads, (((0,), (0,)), ((), ())), preferred_element_type=jnp.float32
+    ).reshape(seq_devices, block_rows, KVH * HD)
+    summed = lax.dynamic_index_in_dim(partial, seq_index, 0, keepdims=False)
+    for shift in range(1, seq_devices):
+        piece = lax.dynamic_index_in_dim(
+            partial, (seq_index + shift) % seq_devices, 0, keepdims=False
+        )
+        summed = summed + lax.ppermute(
+            piece, "seq", [(i, (i + shift) % seq_devices) for i in range(seq_devices)]
+        )
+    weight_grad = (summed * (1.0 / math.sqrt(fsdp_devices * seq_len))).astype(jnp.bfloat16)
 
     values_loc = jnp.dot(local_input, full_weight, preferred_element_type=jnp.float32).astype(
         jnp.bfloat16
@@ -175,12 +193,6 @@
     )
     value_dev = lax.all_to_all(value_rep, "seq", split_axis=1, concat_axis=0, tiled=True)
     dq, dk = attention(seeds, pos, query_dev, grad_dev, key_dev, value_dev, copies_dev, per_copy)
-    value_grads, input_cols, dq, dk = lax.optimization_barrier((value_grads, input_cols, dq, dk))
-    partial = lax.dot_general(
-        input_cols, value_grads, (((0,), (0,)), ((), ())), preferred_element_type=jnp.float32
-    )
-    summed = lax.psum_scatter(partial, "seq", scatter_dimension=0, tiled=True)
-    weight_grad = (summed * (1.0 / math.sqrt(fsdp_devices * seq_len))).astype(jnp.bfloat16)
     query_grad = lax.all_to_all(dq, "seq", split_axis=0, concat_axis=1, tiled=True)
     key_back = lax.all_to_all(
         dk.astype(jnp.bfloat16), "seq", split_axis=0, concat_axis=1, tiled=True

time: 242 us -> 267 us (1.10)
  waiting for transfers between devices: 112 us -> 132 us
  starting transfers between devices: 26 us -> 37.8 us
  blocking collectives: 7.7 us -> 0 us
    all_to_all x0 -> x2, waiting for transfers between devices: none -> 45.7 us  [the longest x1 43.1 us: per_device(): lax.all_to_all(jnp.broadcast_to(value_grad[None], (fsdp_devices,) + value...]
    all_gather x1, waiting for transfers between devices: 20.2 us -> 0.01 us  [per_device(): lax.all_gather(value_weight, ('seq', 'fsdp'), axis=0, tiled=True)]
    all_to_all x0 -> x2, starting transfers between devices: none -> 8.44 us  [the longest x1 5.06 us: per_device(): lax.all_to_all(jnp.broadcast_to(value_grad[None], (fsdp_devices,) + value...]
    all_to_all x1, waiting for transfers between devices: 12 us -> 3.83 us  [per_device(): lax.all_to_all(dq, 'seq', split_axis=0, concat_axis=1, tiled=True)]
    all_to_all x1 -> x0, blocking collectives: 7.7 us -> none  [per_device(): lax.all_to_all(dk.astype(jnp.bfloat16), 'seq', split_axis=0, concat_axis=...]
    all_to_all x1, waiting for transfers between devices: 0.01 us -> 4.66 us  [per_device(): lax.all_to_all(value_rep, 'seq', split_axis=1, concat_axis=0, tiled=True)]
    unnamed x10 -> x7, local copies, waits for them, and re-layouts: 6.6 us -> 5.08 us
  transfers between devices with their start and end apart: 10 -> 11, of which waited for: 6 -> 8; matrix products, arithmetic and copies ran while one was open for 14% -> 14% of each run, Pallas kernels for 15% -> 13%
where the time goes in v3:
time: 267 us; the launch traced here: 266 us
  waiting for transfers between devices  132 us (49%)
  starting transfers between devices  37.8 us (14%)
  Pallas kernels  35.2 us (13%)
  local copies, waits for them, and re-layouts  27.1 us (10%)
  matrix products  16.3 us (6%)
  between operations  14.9 us (6%)
    all_to_all x1, waiting for transfers between devices, per_device(): lax.all_to_all(local_input.reshape(tok_rows, seq_devices, fsdp_devices, b...  47.3 us
    all_to_all x1, waiting for transfers between devices, per_device(): lax.all_to_all(jnp.broadcast_to(value_grad[None], (fsdp_devices,) + value...  43.1 us
    pallas_call x2, Pallas kernels, attention(): pl.pallas_call(kernel, grid_spec=pltpu.PrefetchScalarGridSpec(num_scalar_...  35.2 us
    all_to_all x1, waiting for transfers between devices, per_device(): lax.all_to_all(out_grad[0], 'seq', split_axis=1, concat_axis=0, tiled=True)  15.8 us
    all_to_all x1, waiting for transfers between devices, per_device(): lax.all_to_all(queries[0], 'seq', split_axis=1, concat_axis=0, tiled=True)  12.4 us
    dot_general x1, matrix products, per_device(): lax.dot_general(value_grad, full_weight, last_dims, preferred_element_typ...  7.59 us
    all_to_all x1, starting transfers between devices, per_device(): lax.all_to_all(local_input.reshape(tok_rows, seq_devices, fsdp_devices, b...  6.45 us
  transfers between devices with their start and end apart: 11, of which 8 were waited for; matrix products, arithmetic and copies ran while one was open for 14% of the time, Pallas kernels for 13%

profile of v3, /device:TPU:10, one launch (start us, length us, event | category | flops | bytes accessed | tf_op | source)
XLA Modules:
  0.0 265.5 jit_solution(12588534795477349423)
XLA Ops:
  7.2 0.0 all-gather.2.cloned.1.call-start
  7.2 0.7 all-gather.2.cloned.1.call-update
  7.9 0.9 all_to_all.118
  8.8 0.7 copy.41
  9.5 3.4 %all-to-all-start.2 = ((bf16[128,2,256]{2,0,1:T(8,128)(2,1)}), bf16[128,2,256]{2,0,1:T(8,128)(2,1)S(1)}, u32[]{:S(2)}, u32[]{:S(2)}) async-start(bf16[128,2,256]{2,0,1:T(8,128)(2,1)} %copy.41), calls=%async_computation.2 | async-start | bytes 262144 | tf_op jit(solution)/shard_map/all_to_all | solution.py:152
  12.9 1.8 all_to_all.110
  14.7 0.0 copy-start.1
  14.8 1.3 copy.39
  16.1 1.3 all-to-all-done.2
  17.4 3.6 %all-to-all-start = ((bf16[128,2,2048]{2,0,1:T(8,128)(2,1)}), bf16[128,2,2048]{2,0,1:T(8,128)(2,1)S(1)}, u32[]{:S(2)}, u32[]{:S(2)}) async-start(bf16[128,2,2048]{2,0,1:T(8,128)(2,1)} %copy.39), calls=%async_computation | async-start | bytes 2097152 | tf_op jit(solution)/shard_map/all_to_all | solution.py:150
  21.0 0.0 copy-done.1
  21.0 0.8 all_to_all.114
  21.8 0.0 copy-start.2
  21.8 1.3 copy.40
  23.1 12.4 %all-to-all-done = bf16[128,2,2048]{2,0,1:T(8,128)(2,1)S(1)} async-done(((bf16[128,2,2048]{2,0,1:T(8,128)(2,1)}), bf16[128,2,2048]{2,0,1:T(8,128)(2,1)S(1)}, u32[]{:S(2)}, u32[]{:S(2)}) %all-to-all-start) | async-done | bytes 1048608 | tf_op jit(solution)/shard_map/all_to_all | solution.py:150
  35.5 3.6 %all-to-all-start.1 = ((bf16[128,2,2048]{2,0,1:T(8,128)(2,1)}), bf16[128,2,2048]{2,0,1:T(8,128)(2,1)S(1)}, u32[]{:S(2)}, u32[]{:S(2)}) async-start(bf16[128,2,2048]{2,0,1:T(8,128)(2,1)} %copy.40), calls=%async_computation.1 | async-start | bytes 2097152 | tf_op jit(solution)/shard_map/all_to_all | solution.py:151
  39.8 0.0 copy-done.2
  39.8 0.1 copy.43.pos_ref
  39.9 15.8 %all-to-all-done.1 = bf16[128,2,2048]{2,0,1:T(8,128)(2,1)S(1)} async-done(((bf16[128,2,2048]{2,0,1:T(8,128)(2,1)}), bf16[128,2,2048]{2,0,1:T(8,128)(2,1)S(1)}, u32[]{:S(2)}, u32[]{:S(2)}) %all-to-all-start.1) | async-done | bytes 1048608 | tf_op jit(solution)/shard_map/all_to_all | solution.py:151
  55.8 16.4 %shard_map.103 = f32[256,256]{1,0:T(8,128)S(1)} custom-call(s32[16]{0:T(128)S(1)} %shift-right-logical_xor_fusion.seeds_ref, s32[256,1]{1,0:T(8,128)S(1)} %copy.43.pos_ref, bf16[256,2048]{1,0:T(8,128)(2,1)S(1)} %bitcast.59, bf16[256,2048]{1,0:T(8,128)(2,1)S(1)} %bitcast.61, bf16[256,256]{1,0:T(8,128)(2,1)S(1)} %bitcast.63), custom_call_target="tpu_custom_call" | custom-call | tf_op jit(solution)/shard_map/pallas_call | solution.py:108
  72.2 0.8 copy.47
  72.9 3.4 %all-to-all-start.6 = ((bf16[2,128,256]{1,2,0:T(8,128)(2,1)}), bf16[2,128,256]{1,2,0:T(8,128)(2,1)S(1)}, u32[]{:S(2)}, u32[]{:S(2)}) async-start(bf16[2,128,256]{1,2,0:T(8,128)(2,1)} %copy.47), calls=%async_computation.6 | async-start | bytes 262144 | tf_op jit(solution)/shard_map/all_to_all | solution.py:159
  76.3 4.1 %copy.49 = bf16[1,128,8192]{1,2,0:T(8,128)(2,1)} copy(bf16[1,128,8192]{2,1,0:T(8,128)(2,1)} %param.7) | data formatting | bytes 4194304 | tf_op args[0]
  80.4 3.2 %copy.50 = bf16[128,2,16,256]{0,3,1,2:T(8,128)(2,1)} copy(bf16[128,2,16,256]{0,3,2,1:T(8,128)(2,1)} %bitcast.66) | data formatting | bytes 4194304 | tf_op jit(solution)/shard_map/reshape;squeeze | solution.py:140
  83.7 0.0 all-to-all-done.6
  83.7 6.4 %all-to-all-start.8 = ((bf16[128,2,16,256]{0,3,1,2:T(8,128)(2,1)}), bf16[128,2,16,256]{0,3,1,2:T(8,128)(2,1)}, u32[]{:S(2)}, u32[]{:S(2)}) async-start(bf16[128,2,16,256]{0,3,1,2:T(8,128)(2,1)} %copy.50), calls=%async_computation.8 | async-start | bytes 4194304 | tf_op jit(solution)/shard_map/all_to_all | solution.py:139
  90.1 0.1 copy.48
  90.2 47.3 %all-to-all-done.8 = bf16[128,2,16,256]{0,3,1,2:T(8,128)(2,1)} async-done(((bf16[128,2,16,256]{0,3,1,2:T(8,128)(2,1)}), bf16[128,2,16,256]{0,3,1,2:T(8,128)(2,1)}, u32[]{:S(2)}, u32[]{:S(2)}) %all-to-all-start.8) | async-done | bytes 2097184 | tf_op jit(solution)/shard_map/all_to_all | solution.py:139
  137.5 1.5 broadcast_in_dim.15
  139.0 5.1 %all-to-all-start.7 = ((bf16[16,128,512]{2,1,0:T(8,128)(2,1)}), bf16[16,128,512]{2,1,0:T(8,128)(2,1)}, u32[]{:S(2)}, u32[]{:S(2)}) async-start(bf16[16,128,512]{2,1,0:T(8,128)(2,1)} %broadcast_in_dim.15), calls=%async_computation.7 | async-start | bytes 4194304 | tf_op jit(solution)/shard_map/all_to_all | solution.py:167
  144.1 4.3 %copy.51 = bf16[16,128,2,1,256]{1,0,4,2,3:T(8,128)(2,1)} copy(bf16[16,128,2,1,256]{1,4,2,0,3:T(8,128)(2,1)} %bitcast.25) | data formatting | bytes 4194304 | tf_op jit(solution)/shard_map/all_to_all | solution.py:139
  148.3 43.1 %all-to-all-done.7 = bf16[16,128,512]{2,1,0:T(8,128)(2,1)} async-done(((bf16[16,128,512]{2,1,0:T(8,128)(2,1)}), bf16[16,128,512]{2,1,0:T(8,128)(2,1)}, u32[]{:S(2)}, u32[]{:S(2)}) %all-to-all-start.7) | async-done | bytes 2097184 | tf_op jit(solution)/shard_map/all_to_all | solution.py:167
  191.4 3.5 %fusion.1 = f32[512,512]{0,1:T(8,128)S(1)} fusion(bf16[2048,512]{1,0:T(8,128)(2,1)} %bitcast.22, bf16[64,8,16,128]{3,2,1,0:T(8,128)(2,1)} %bitcast.68), kind=kOutput, calls=%fused_computation.2 | convolution fusion | flops 1073741824 | bytes 5242880 | tf_op jit(solution)/shard_map/dot_general | solution.py:175
  194.9 0.0 copy-start
  194.9 1.0 copy-done
  195.9 0.9 dynamic-slice_bitcast_fusion
  196.8 1.8 collective-permute-start
  198.6 0.0 all-gather.2.cloned.1.call-done
  198.6 5.3 %fusion.6 = bf16[128,512]{1,0:T(8,128)(2,1)S(1)} fusion(bf16[8192,512]{1,0:T(8,128)(2,1)} %all-gather.2.cloned.1.call-done, bf16[1,128,8192]{2,1,0:T(8,128)(2,1)} %param.7), kind=kOutput, calls=%fused_computation.7 | convolution fusion | flops 1073807360 | bytes 10616832 | tf_op jit(solution)/shard_map/dot_general | solution.py:188
  203.9 0.7 copy.59
  204.5 3.4 %all-to-all-start.3 = ((bf16[128,2,256]{2,0,1:T(8,128)(2,1)}), bf16[128,2,256]{2,0,1:T(8,128)(2,1)S(1)}, u32[]{:S(2)}, u32[]{:S(2)}) async-start(bf16[128,2,256]{2,0,1:T(8,128)(2,1)} %bitcast.58), calls=%async_computation.3 | async-start | bytes 262144 | tf_op jit(solution)/shard_map/all_to_all | solution.py:194
  207.9 4.7 %all-to-all-done.3 = bf16[128,2,256]{2,0,1:T(8,128)(2,1)S(1)} async-done(((bf16[128,2,256]{2,0,1:T(8,128)(2,1)}), bf16[128,2,256]{2,0,1:T(8,128)(2,1)S(1)}, u32[]{:S(2)}, u32[]{:S(2)}) %all-to-all-start.3) | async-done | bytes 131104 | tf_op jit(solution)/shard_map/all_to_all | solution.py:194
  212.6 18.8 %shard_map.102 = (bf16[256,2048]{1,0:T(8,128)(2,1)}, f32[256,256]{1,0:T(8,128)S(1)}) custom-call(s32[16]{0:T(128)S(1)} %shift-right-logical_xor_fusion.seeds_ref, s32[256,1]{1,0:T(8,128)S(1)} %copy.43.pos_ref, bf16[256,2048]{1,0:T(8,128)(2,1)S(1)} %bitcast.60, bf16[256,2048]{1,0:T(8,128)(2,1)S(1)} %bitcast.62, bf16[256,256]{1,0:T(8,128)(2,1)S(1)} %bitcast.64, ...), custom_call_target="tpu_custom_call" | custom-call | tf_op jit(solution)/shard_map/pallas_call | solution.py:108
  231.4 0.7 convert_element_type.28
  232.1 3.4 %all-to-all-start.5 = ((bf16[2,128,256]{2,1,0:T(8,128)(2,1)}), bf16[2,128,256]{2,1,0:T(8,128)(2,1)S(1)}, u32[]{:S(2)}, u32[]{:S(2)}) async-start(bf16[2,128,256]{2,1,0:T(8,128)(2,1)} %bitcast.12), calls=%async_computation.5 | async-start | bytes 262144 | tf_op jit(solution)/shard_map/all_to_all | solution.py:197
  235.5 0.0 collective-permute-done
  235.5 1.9 fusion.10
  237.3 2.6 all-to-all-done.5
  239.9 3.8 %all-to-all-start.4 = ((bf16[2,128,2048]{2,1,0:T(8,128)(2,1)}), bf16[2,128,2048]{2,1,0:T(8,128)(2,1)S(1)}, u32[]{:S(2)}, u32[]{:S(2)}) async-start(bf16[2,128,2048]{2,1,0:T(8,128)(2,1)} %bitcast.10), calls=%async_computation.4 | async-start | bytes 2097152 | tf_op jit(solution)/shard_map/all_to_all | solution.py:196
  243.7 7.6 %fusion = bf16[1,128,8192]{2,1,0:T(8,128)(2,1)} fusion(bf16[128,512]{0,1:T(8,128)(2,1)S(1)} %bitcast.70, bf16[8192,512]{1,0:T(8,128)(2,1)} %all-gather.2.cloned.1.call-done), kind=kOutput, calls=%fused_computation.1 | convolution fusion | flops 1074790400 | bytes 10616832 | tf_op jit(solution)/shard_map/dot_general | solution.py:206
  251.3 0.1 copy.45
  251.4 0.7 all_to_all.132
  252.2 3.8 %all-to-all-done.4 = bf16[2,128,2048]{2,1,0:T(8,128)(2,1)S(1)} async-done(((bf16[2,128,2048]{2,1,0:T(8,128)(2,1)}), bf16[2,128,2048]{2,1,0:T(8,128)(2,1)S(1)}, u32[]{:S(2)}, u32[]{:S(2)}) %all-to-all-start.4) | async-done | bytes 1048608 | tf_op jit(solution)/shard_map/all_to_all | solution.py:196
  256.0 1.1 copy.44
  257.1 1.6 broadcast_in_dim.6
  (2 shorter events, 0.0 us)
Async XLA Ops:
  7.2 191.4 %all-gather.2.cloned.1.call-start = ((), (), s32[]{:S(2)}) async-start(), calls=%async_computation.9 | async-start | bytes 8650752 | tf_op jit(solution)/shard_map/all_gather | solution.py:137
  9.5 7.8 %all-to-all-start.2 = ((bf16[128,2,256]{2,0,1:T(8,128)(2,1)}), bf16[128,2,256]{2,0,1:T(8,128)(2,1)S(1)}, u32[]{:S(2)}, u32[]{:S(2)}) async-start(bf16[128,2,256]{2,0,1:T(8,128)(2,1)} %copy.41), calls=%async_computation.2 | async-start | bytes 262144 | tf_op jit(solution)/shard_map/all_to_all | solution.py:152
  14.7 6.2 %copy-start.1 = (bf16[1,128,4096]{2,1,0:T(8,128)(2,1)S(1)}, bf16[1,128,4096]{2,1,0:T(8,128)(2,1)}, u32[]{:S(2)}) copy-start(bf16[1,128,4096]{2,1,0:T(8,128)(2,1)} %param.10) | copy-start | bytes 3145732
  17.4 18.2 %all-to-all-start = ((bf16[128,2,2048]{2,0,1:T(8,128)(2,1)}), bf16[128,2,2048]{2,0,1:T(8,128)(2,1)S(1)}, u32[]{:S(2)}, u32[]{:S(2)}) async-start(bf16[128,2,2048]{2,0,1:T(8,128)(2,1)} %copy.39), calls=%async_computation | async-start | bytes 2097152 | tf_op jit(solution)/shard_map/all_to_all | solution.py:150
  21.8 18.0 %copy-start.2 = (s32[1,256]{1,0:T(1,128)S(1)}, s32[1,256]{1,0:T(1,128)}, u32[]{:S(2)}) copy-start(s32[1,256]{1,0:T(1,128)} %param.11) | copy-start | bytes 3076
  35.5 20.2 %all-to-all-start.1 = ((bf16[128,2,2048]{2,0,1:T(8,128)(2,1)}), bf16[128,2,2048]{2,0,1:T(8,128)(2,1)S(1)}, u32[]{:S(2)}, u32[]{:S(2)}) async-start(bf16[128,2,2048]{2,0,1:T(8,128)(2,1)} %copy.40), calls=%async_computation.1 | async-start | bytes 2097152 | tf_op jit(solution)/shard_map/all_to_all | solution.py:151
  72.9 10.7 %all-to-all-start.6 = ((bf16[2,128,256]{1,2,0:T(8,128)(2,1)}), bf16[2,128,256]{1,2,0:T(8,128)(2,1)S(1)}, u32[]{:S(2)}, u32[]{:S(2)}) async-start(bf16[2,128,256]{1,2,0:T(8,128)(2,1)} %copy.47), calls=%async_computation.6 | async-start | bytes 262144 | tf_op jit(solution)/shard_map/all_to_all | solution.py:159
  83.7 53.8 %all-to-all-start.8 = ((bf16[128,2,16,256]{0,3,1,2:T(8,128)(2,1)}), bf16[128,2,16,256]{0,3,1,2:T(8,128)(2,1)}, u32[]{:S(2)}, u32[]{:S(2)}) async-start(bf16[128,2,16,256]{0,3,1,2:T(8,128)(2,1)} %copy.50), calls=%async_computation.8 | async-start | bytes 4194304 | tf_op jit(solution)/shard_map/all_to_all | solution.py:139
  139.0 52.4 %all-to-all-start.7 = ((bf16[16,128,512]{2,1,0:T(8,128)(2,1)}), bf16[16,128,512]{2,1,0:T(8,128)(2,1)}, u32[]{:S(2)}, u32[]{:S(2)}) async-start(bf16[16,128,512]{2,1,0:T(8,128)(2,1)} %broadcast_in_dim.15), calls=%async_computation.7 | async-start | bytes 4194304 | tf_op jit(solution)/shard_map/all_to_all | solution.py:167
  194.9 1.0 copy-start
  196.8 38.7 %collective-permute-start = (f32[256,512]{1,0:T(8,128)}, f32[256,512]{1,0:T(8,128)S(1)}, u32[]{:S(2)}, u32[]{:S(2)}) collective-permute-start(f32[256,512]{1,0:T(8,128)} %dynamic-slice_bitcast_fusion), channel_id=1, source_target_pairs={{0,16},{16,0},{1,17},{17,1},{2,18},{18,2},{3,19},{19,3},{4,20},{20... | collective-permute-start | bytes 1572872 | tf_op jit(solution)/shard_map/ppermute | solution.py:183
  204.5 8.0 %all-to-all-start.3 = ((bf16[128,2,256]{2,0,1:T(8,128)(2,1)}), bf16[128,2,256]{2,0,1:T(8,128)(2,1)S(1)}, u32[]{:S(2)}, u32[]{:S(2)}) async-start(bf16[128,2,256]{2,0,1:T(8,128)(2,1)} %bitcast.58), calls=%async_computation.3 | async-start | bytes 262144 | tf_op jit(solution)/shard_map/all_to_all | solution.py:194
  232.1 7.8 %all-to-all-start.5 = ((bf16[2,128,256]{2,1,0:T(8,128)(2,1)}), bf16[2,128,256]{2,1,0:T(8,128)(2,1)S(1)}, u32[]{:S(2)}, u32[]{:S(2)}) async-start(bf16[2,128,256]{2,1,0:T(8,128)(2,1)} %bitcast.12), calls=%async_computation.5 | async-start | bytes 262144 | tf_op jit(solution)/shard_map/all_to_all | solution.py:197
  239.9 16.1 %all-to-all-start.4 = ((bf16[2,128,2048]{2,1,0:T(8,128)(2,1)}), bf16[2,128,2048]{2,1,0:T(8,128)(2,1)S(1)}, u32[]{:S(2)}, u32[]{:S(2)}) async-start(bf16[2,128,2048]{2,1,0:T(8,128)(2,1)} %bitcast.10), calls=%async_computation.4 | async-start | bytes 2097152 | tf_op jit(solution)/shard_map/all_to_all | solution.py:196
Sparse Core Ops, SparseCore 0:
  10.8 81.7 all-gather.1

commit v4 on v3

--- a/solution.py
+++ b/solution.py
@@ -12,6 +12,7 @@
 QH = 32
 KVH = 4
 ROWS = 128
+FSDP = ("zx", "core")
 
 
 drop_cut = 1677722
@@ -123,9 +124,11 @@
 
 def per_device(layer_input, queries, key_states, out_grad, doc_positions, drop_seed, value_weight):
     seq_devices = lax.axis_size("seq")
-    fsdp_devices = lax.axis_size("fsdp")
+    zx_devices = lax.axis_size("zx")
+    fsdp_devices = zx_devices * 2
+    core_index = lax.axis_index("core")
     seq_index = lax.axis_index("seq")
-    batch_index = lax.axis_index("fsdp")
+    batch_index = lax.axis_index(FSDP)
     tok_rows = layer_input.shape[1]
     seq_len = tok_rows * seq_devices
     local_input = layer_input[0]
@@ -134,15 +137,24 @@
     per_copy = QH // copies_total
     heads_dev = QH // seq_devices
     repeat_count = copies_total // KVH
-    full_weight = lax.all_gather(value_weight, ("seq", "fsdp"), axis=0, tiled=True)
     block_rows = value_weight.shape[0]
+    swap = [(0, 1), (1, 0)]
+    weight_own = lax.all_gather(value_weight, ("seq", "zx"), axis=0, tiled=True)
+    weight_other = lax.ppermute(weight_own, "core", swap)
+    input_view = local_input.reshape(tok_rows, seq_devices * zx_devices, 2, block_rows)
+    input_own = lax.dynamic_index_in_dim(input_view, core_index, 2, keepdims=False).reshape(
+        tok_rows, -1
+    )
+    input_other = lax.dynamic_index_in_dim(input_view, 1 - core_index, 2, keepdims=False).reshape(
+        tok_rows, -1
+    )
     input_cols = lax.all_to_all(
         local_input.reshape(tok_rows, seq_devices, fsdp_devices, block_rows),
-        "fsdp",
+        FSDP,
         split_axis=2,
         concat_axis=0,
         tiled=True,
-    ).reshape(fsdp_devices * tok_rows, seq_devices * block_rows)
+    ).reshape(zx_devices, 2, tok_rows, seq_devices * block_rows)
     key_rep = jnp.repeat(key_states[0].reshape(tok_rows, KVH, HD), repeat_count, axis=1).reshape(
         tok_rows, copies_total * HD
     )
@@ -164,16 +176,24 @@
         .reshape(tok_rows, KVH * HD)
         .astype(jnp.bfloat16)
     )
-    value_grads = lax.all_to_all(
-        jnp.broadcast_to(value_grad[None], (fsdp_devices,) + value_grad.shape),
-        "fsdp",
+    grads_own = lax.all_to_all(
+        jnp.broadcast_to(value_grad[None], (zx_devices,) + value_grad.shape),
+        "zx",
         split_axis=0,
         concat_axis=0,
         tiled=True,
-    ).reshape(fsdp_devices * tok_rows, KVH * HD)
-
-    partial = lax.dot_general(
-        input_cols, value_grads, (((0,), (0,)), ((), ())), preferred_element_type=jnp.float32
+    ).reshape(zx_devices * tok_rows, KVH * HD)
+    grads_other = lax.ppermute(grads_own, "core", swap)
+    cols_own = lax.dynamic_index_in_dim(input_cols, core_index, 1, keepdims=False).reshape(
+        zx_devices * tok_rows, -1
+    )
+    cols_other = lax.dynamic_index_in_dim(input_cols, 1 - core_index, 1, keepdims=False).reshape(
+        zx_devices * tok_rows, -1
+    )
+    first_dims = (((0,), (0,)), ((), ()))
+    partial = (
+        lax.dot_general(cols_own, grads_own, first_dims, preferred_element_type=jnp.float32)
+        + lax.dot_general(cols_other, grads_other, first_dims, preferred_element_type=jnp.float32)
     ).reshape(seq_devices, block_rows, KVH * HD)
     summed = lax.dynamic_index_in_dim(partial, seq_index, 0, keepdims=False)
     for shift in range(1, seq_devices):
@@ -185,9 +205,10 @@
         )
     weight_grad = (summed * (1.0 / math.sqrt(fsdp_devices * seq_len))).astype(jnp.bfloat16)
 
-    values_loc = jnp.dot(local_input, full_weight, preferred_element_type=jnp.float32).astype(
-        jnp.bfloat16
-    )
+    values_loc = (
+        jnp.dot(input_own, weight_own, preferred_element_type=jnp.float32)
+        + jnp.dot(input_other, weight_other, preferred_element_type=jnp.float32)
+    ).astype(jnp.bfloat16)
     value_rep = jnp.repeat(values_loc.reshape(tok_rows, KVH, HD), repeat_count, axis=1).reshape(
         tok_rows, copies_total * HD
     )
@@ -203,30 +224,42 @@
         .astype(jnp.bfloat16)
     )
     last_dims = (((1,), (1,)), ((), ()))
-    input_grad = lax.dot_general(
-        value_grad, full_weight, last_dims, preferred_element_type=jnp.float32
-    ).astype(jnp.bfloat16)
+    grad_own = lax.dot_general(
+        value_grad, weight_own, last_dims, preferred_element_type=jnp.float32
+    ).astype(jnp.bfloat16).reshape(tok_rows, seq_devices * zx_devices, 1, block_rows)
+    grad_other = lax.dot_general(
+        value_grad, weight_other, last_dims, preferred_element_type=jnp.float32
+    ).astype(jnp.bfloat16).reshape(tok_rows, seq_devices * zx_devices, 1, block_rows)
+    input_grad = jnp.where(
+        core_index == 0,
+        jnp.concatenate([grad_own, grad_other], axis=2),
+        jnp.concatenate([grad_other, grad_own], axis=2),
+    ).reshape(tok_rows, -1)
     return (query_grad[None], key_grad[None], input_grad[None], weight_grad)
 
 
 def solution(mesh):
+    seq_devices, fsdp_devices = mesh.devices.shape
+    chips = jax.sharding.Mesh(
+        mesh.devices.reshape(seq_devices, fsdp_devices // 2, 2), ("seq",) + FSDP
+    )
     return jax.shard_map(
         per_device,
-        mesh=mesh,
+        mesh=chips,
         in_specs=(
-            P("fsdp", "seq", None),
-            P("fsdp", "seq", None),
-            P("fsdp", "seq", None),
-            P("fsdp", "seq", None),
-            P("fsdp", None),
+            P(FSDP, "seq", None),
+            P(FSDP, "seq", None),
+            P(FSDP, "seq", None),
+            P(FSDP, "seq", None),
+            P(FSDP, None),
             P(),
-            P(("seq", "fsdp"), None),
+            P(("seq",) + FSDP, None),
         ),
         out_specs=(
-            P("fsdp", "seq", None),
-            P("fsdp", "seq", None),
-            P("fsdp", "seq", None),
-            P(("seq", "fsdp"), None),
+            P(FSDP, "seq", None),
+            P(FSDP, "seq", None),
+            P(FSDP, "seq", None),
+            P(("seq",) + FSDP, None),
         ),
         check_vma=False,
     )

time: 267 us -> 254 us (0.951)
  waiting for transfers between devices: 132 us -> 96.8 us
  local copies, waits for them, and re-layouts: 27.1 us -> 41.4 us
  blocking collectives: 0 us -> 8.29 us
    all_to_all x2 -> x1, waiting for transfers between devices: 43.1 us -> 16.4 us  [per_device(): lax.all_to_all(jnp.broadcast_to(value_grad[None], (zx_devices,) + value_g...]
    dynamic_slice x0 -> x4, local copies, waits for them, and re-layouts: none -> 9.33 us  [the longest x2 3.95 us: per_device(): lax.dynamic_index_in_dim(input_cols, 1 - core_index, 1, keepdims=False)]
    select_n x0 -> x2, local copies, waits for them, and re-layouts: none -> 9.11 us  [per_device(): jnp.where(core_index == 0, jnp.concatenate([grad_own, grad_other], axis=2...]
    all_to_all x0 -> x1, blocking collectives: none -> 8.29 us  [per_device(): lax.all_to_all(dv.astype(jnp.bfloat16), 'seq', split_axis=0, concat_axis=...]
    ppermute x1, waiting for transfers between devices: 0.01 us -> 5.97 us  [per_device(): lax.ppermute(piece, 'seq', [(i, (i + shift) % seq_devices) for i in range...]
    all_to_all x1, waiting for transfers between devices: 4.66 us -> 0.01 us  [per_device(): lax.all_to_all(value_rep, 'seq', split_axis=1, concat_axis=0, tiled=True)]
    all_to_all x1 -> x0, local copies, waits for them, and re-layouts: 4.26 us -> none  [per_device(): lax.all_to_all(local_input.reshape(tok_rows, seq_devices, fsdp_devices, b...]
    all_to_all x1, waiting for transfers between devices: 3.83 us -> 0.01 us  [per_device(): lax.all_to_all(dq, 'seq', split_axis=0, concat_axis=1, tiled=True)]
  transfers between devices with their start and end apart: 11 -> 12, of which waited for: 8 -> 7; matrix products, arithmetic and copies ran while one was open for 14% -> 20% of each run, Pallas kernels for 13% -> 7%
where the time goes in v4:
time: 254 us; the launch traced here: 252 us
  waiting for transfers between devices  96.8 us (38%)
  local copies, waits for them, and re-layouts  41.4 us (16%)
  starting transfers between devices  36.8 us (14%)
  Pallas kernels  35.2 us (14%)
  matrix products  15.6 us (6%)
  between operations  15 us (6%)
  blocking collectives  8.29 us (3%)
  other arithmetic  2.91 us (1%)
    all_to_all x1, waiting for transfers between devices, per_device(): lax.all_to_all(local_input.reshape(tok_rows, seq_devices, fsdp_devices, b...  43.7 us
    pallas_call x2, Pallas kernels, attention(): pl.pallas_call(kernel, grid_spec=pltpu.PrefetchScalarGridSpec(num_scalar_...  35.2 us
    all_to_all x1, waiting for transfers between devices, per_device(): lax.all_to_all(jnp.broadcast_to(value_grad[None], (zx_devices,) + value_g...  16.4 us
    all_to_all x1, waiting for transfers between devices, per_device(): lax.all_to_all(out_grad[0], 'seq', split_axis=1, concat_axis=0, tiled=True)  15.8 us
    all_to_all x1, waiting for transfers between devices, per_device(): lax.all_to_all(queries[0], 'seq', split_axis=1, concat_axis=0, tiled=True)  12.4 us
    select_n x2, local copies, waits for them, and re-layouts, per_device(): jnp.where(core_index == 0, jnp.concatenate([grad_own, grad_other], axis=2...  9.11 us
    all_to_all x1, blocking collectives, per_device(): lax.all_to_all(dv.astype(jnp.bfloat16), 'seq', split_axis=0, concat_axis=...  8.29 us
    all_to_all x1, starting transfers between devices, per_device(): lax.all_to_all(local_input.reshape(tok_rows, seq_devices, fsdp_devices, b...  7.47 us
  transfers between devices with their start and end apart: 12, of which 7 were waited for; matrix products, arithmetic and copies ran while one was open for 20% of the time, Pallas kernels for 7%

profile of v4, /device:TPU:10, one launch (start us, length us, event | category | flops | bytes accessed | tf_op | source)
XLA Modules:
  0.0 252.0 jit_solution(11145065176997520274)
XLA Ops:
  7.2 0.0 all-gather.2.cloned.1.call-start
  7.2 0.7 all-gather.2.cloned.1.call-update
  7.9 0.9 all_to_all.118
  8.8 0.7 copy.47
  9.5 3.4 %all-to-all-start.2 = ((bf16[128,2,256]{2,0,1:T(8,128)(2,1)}), bf16[128,2,256]{2,0,1:T(8,128)(2,1)S(1)}, u32[]{:S(2)}, u32[]{:S(2)}) async-start(bf16[128,2,256]{2,0,1:T(8,128)(2,1)} %copy.47), calls=%async_computation.2 | async-start | bytes 262144 | tf_op jit(solution)/shard_map/all_to_all | solution.py:164
  12.9 1.8 all_to_all.110
  14.7 0.0 copy-start.4
  14.8 1.3 copy.45
  16.1 1.3 all-to-all-done.2
  17.4 3.6 %all-to-all-start = ((bf16[128,2,2048]{2,0,1:T(8,128)(2,1)}), bf16[128,2,2048]{2,0,1:T(8,128)(2,1)S(1)}, u32[]{:S(2)}, u32[]{:S(2)}) async-start(bf16[128,2,2048]{2,0,1:T(8,128)(2,1)} %copy.45), calls=%async_computation | async-start | bytes 2097152 | tf_op jit(solution)/shard_map/all_to_all | solution.py:162
  21.0 0.8 all_to_all.114
  21.8 0.0 copy-start.6
  21.8 1.3 copy.46
  23.1 12.4 %all-to-all-done = bf16[128,2,2048]{2,0,1:T(8,128)(2,1)S(1)} async-done(((bf16[128,2,2048]{2,0,1:T(8,128)(2,1)}), bf16[128,2,2048]{2,0,1:T(8,128)(2,1)S(1)}, u32[]{:S(2)}, u32[]{:S(2)}) %all-to-all-start) | async-done | bytes 1048608 | tf_op jit(solution)/shard_map/all_to_all | solution.py:162
  35.5 3.6 %all-to-all-start.1 = ((bf16[128,2,2048]{2,0,1:T(8,128)(2,1)}), bf16[128,2,2048]{2,0,1:T(8,128)(2,1)S(1)}, u32[]{:S(2)}, u32[]{:S(2)}) async-start(bf16[128,2,2048]{2,0,1:T(8,128)(2,1)} %copy.46), calls=%async_computation.1 | async-start | bytes 2097152 | tf_op jit(solution)/shard_map/all_to_all | solution.py:163
  39.8 0.1 copy.50.pos_ref
  39.9 15.8 %all-to-all-done.1 = bf16[128,2,2048]{2,0,1:T(8,128)(2,1)S(1)} async-done(((bf16[128,2,2048]{2,0,1:T(8,128)(2,1)}), bf16[128,2,2048]{2,0,1:T(8,128)(2,1)S(1)}, u32[]{:S(2)}, u32[]{:S(2)}) %all-to-all-start.1) | async-done | bytes 1048608 | tf_op jit(solution)/shard_map/all_to_all | solution.py:163
  55.8 16.4 %shard_map.103 = f32[256,256]{1,0:T(8,128)S(1)} custom-call(s32[16]{0:T(128)S(1)} %shift-right-logical_xor_fusion.seeds_ref, s32[256,1]{1,0:T(8,128)S(1)} %copy.50.pos_ref, bf16[256,2048]{1,0:T(8,128)(2,1)S(1)} %bitcast.66, bf16[256,2048]{1,0:T(8,128)(2,1)S(1)} %bitcast.68, bf16[256,256]{1,0:T(8,128)(2,1)S(1)} %bitcast.70), custom_call_target="tpu_custom_call" | custom-call | tf_op jit(solution)/shard_map/pallas_call | solution.py:109
  72.2 0.1 copy.54
  72.3 8.3 %all_to_all.150 = bf16[2,128,256]{1,2,0:T(8,128)(2,1)S(1)} all-to-all(bf16[2,128,256]{1,2,0:T(8,128)(2,1)S(1)} %copy.54), channel_id=1, replica_groups=mesh['seq'=2,'zx'=8,'core'=2] {'seq'}, dimensions={0} | all-to-all | bytes 262144 | tf_op jit(solution)/shard_map/all_to_all | solution.py:171
  80.6 0.1 copy.59
  80.7 1.1 broadcast_in_dim.5
  81.8 6.1 %all-to-all-start.8 = ((bf16[8,128,512]{2,1,0:T(8,128)(2,1)}), bf16[8,128,512]{2,1,0:T(8,128)(2,1)}, u32[]{:S(2)}, u32[]{:S(2)}) async-start(bf16[8,128,512]{2,1,0:T(8,128)(2,1)} %broadcast_in_dim.5), calls=%async_computation.8 | async-start | bytes 2097152 | tf_op jit(solution)/shard_map/all_to_all | solution.py:179
  87.9 4.1 %copy.48 = bf16[1,128,8192]{1,2,0:T(8,128)(2,1)} copy(bf16[1,128,8192]{2,1,0:T(8,128)(2,1)} %param.7) | data formatting | bytes 4194304 | tf_op args[0]
  91.9 3.2 %copy.57 = bf16[128,2,16,256]{0,3,1,2:T(8,128)(2,1)} copy(bf16[128,2,16,256]{0,3,2,1:T(8,128)(2,1)} %bitcast.73) | data formatting | bytes 4194304 | tf_op jit(solution)/shard_map/reshape;squeeze | solution.py:152
  95.1 16.4 %all-to-all-done.8 = bf16[8,128,512]{2,1,0:T(8,128)(2,1)} async-done(((bf16[8,128,512]{2,1,0:T(8,128)(2,1)}), bf16[8,128,512]{2,1,0:T(8,128)(2,1)}, u32[]{:S(2)}, u32[]{:S(2)}) %all-to-all-start.8) | async-done | bytes 1048608 | tf_op jit(solution)/shard_map/all_to_all | solution.py:179
  111.5 7.5 %all-to-all-start.7 = ((bf16[128,2,16,256]{0,3,1,2:T(8,128)(2,1)}), bf16[128,2,16,256]{0,3,1,2:T(8,128)(2,1)}, u32[]{:S(2)}, u32[]{:S(2)}) async-start(bf16[128,2,16,256]{0,3,1,2:T(8,128)(2,1)} %copy.57), calls=%async_computation.7 | async-start | bytes 4194304 | tf_op jit(solution)/shard_map/all_to_all | solution.py:151
  119.0 0.0 all-gather.2.cloned.1.call-done
  119.0 0.2 collective-permute-start
  119.2 0.4 collective-permute-start.1
  119.6 3.1 %constant_dynamic-slice_fusion.2 = (bf16[128,16,1,256]{0,3,2,1:T(8,128)(2,1)}, bf16[128,16,1,256]{0,3,2,1:T(8,128)(2,1)}) fusion(bf16[128,16,2,256]{0,3,2,1:T(8,128)(2,1)} %bitcast.74, s32[]{:T(128)S(6)} %select_n.43, s32[]{:T(128)S(6)} %select_n.42), kind=kLoop, calls=%fused_computation.13 | loop fusion | bytes 4194312 | tf_op jit(solution)/shard_map/jit(dynamic_index_in_dim)/dynamic_slice | solution.py:148
  122.7 43.7 %all-to-all-done.7 = bf16[128,2,16,256]{0,3,1,2:T(8,128)(2,1)} async-done(((bf16[128,2,16,256]{0,3,1,2:T(8,128)(2,1)}), bf16[128,2,16,256]{0,3,1,2:T(8,128)(2,1)}, u32[]{:S(2)}, u32[]{:S(2)}) %all-to-all-start.7) | async-done | bytes 2097184 | tf_op jit(solution)/shard_map/all_to_all | solution.py:151
  166.4 2.6 %constant_dynamic-slice_fusion = (bf16[8,1,128,512]{2,3,1,0:T(8,128)(2,1)S(1)}, bf16[8,1,128,512]{2,3,1,0:T(8,128)(2,1)}) fusion(bf16[8,2,128,512]{2,3,1,0:T(8,128)(2,1)} %bitcast.26, s32[]{:T(128)S(6)} %select_n.43, s32[]{:T(128)S(6)} %select_n.42), kind=kLoop, calls=%fused_computation.11 | loop fusion | bytes 4194312 | tf_op jit(solution)/shard_map/jit(dynamic_index_in_dim)/dynamic_slice | solution.py:190
  169.0 2.3 copy.58
  171.3 1.3 copy.60
  172.6 2.4 fusion.6
  175.0 2.1 convolution_add_fusion
  177.2 0.0 copy-start.3
  177.2 1.0 dynamic-slice_bitcast_fusion
  178.1 0.7 collective-permute-start.2
  178.9 0.7 fusion.5
  179.6 0.0 collective-permute-done
  179.6 0.5 copy-done.1
  180.1 3.0 %fusion = bf16[128,512]{1,0:T(8,128)(2,1)S(1)} fusion(f32[128,512]{1,0:T(8,128)S(1)} %fusion.5, bf16[128,4096]{0,1:T(8,128)(2,1)S(1)} %bitcast.77, bf16[4096,512]{1,0:T(8,128)(2,1)} %collective-permute-done), kind=kOutput, calls=%fused_computation.5 | convolution fusion | flops 537001984 | bytes 5636096 | tf_op jit(solution)/shard_map/dot_general | solution.py:210
  183.1 0.7 copy.65
  183.8 3.4 %all-to-all-start.3 = ((bf16[128,2,256]{2,0,1:T(8,128)(2,1)}), bf16[128,2,256]{2,0,1:T(8,128)(2,1)S(1)}, u32[]{:S(2)}, u32[]{:S(2)}) async-start(bf16[128,2,256]{2,0,1:T(8,128)(2,1)} %bitcast.65), calls=%async_computation.3 | async-start | bytes 262144 | tf_op jit(solution)/shard_map/all_to_all | solution.py:215
  187.1 6.0 %collective-permute-done.2 = f32[256,512]{1,0:T(8,128)S(1)} collective-permute-done((f32[256,512]{1,0:T(8,128)}, f32[256,512]{1,0:T(8,128)S(1)}, u32[]{:S(2)}, u32[]{:S(2)}) %collective-permute-start.2) | collective-permute-done | bytes 524320 | tf_op jit(solution)/shard_map/ppermute | solution.py:203
  193.1 1.9 fusion.2
  195.0 18.8 %shard_map.102 = (bf16[256,2048]{1,0:T(8,128)(2,1)}, f32[256,256]{1,0:T(8,128)S(1)}) custom-call(s32[16]{0:T(128)S(1)} %shift-right-logical_xor_fusion.seeds_ref, s32[256,1]{1,0:T(8,128)S(1)} %copy.50.pos_ref, bf16[256,2048]{1,0:T(8,128)(2,1)S(1)} %bitcast.67, bf16[256,2048]{1,0:T(8,128)(2,1)S(1)} %bitcast.69, bf16[256,256]{1,0:T(8,128)(2,1)S(1)} %bitcast.71, ...), custom_call_target="tpu_custom_call" | custom-call | tf_op jit(solution)/shard_map/pallas_call | solution.py:109
  213.8 0.7 convert_element_type.31
  214.5 3.4 %all-to-all-start.5 = ((bf16[2,128,256]{2,1,0:T(8,128)(2,1)}), bf16[2,128,256]{2,1,0:T(8,128)(2,1)S(1)}, u32[]{:S(2)}, u32[]{:S(2)}) async-start(bf16[2,128,256]{2,1,0:T(8,128)(2,1)} %bitcast.14), calls=%async_computation.5 | async-start | bytes 262144 | tf_op jit(solution)/shard_map/all_to_all | solution.py:218
  217.8 3.7 %convolution_convert_fusion.1 = bf16[128,4096]{1,0:T(8,128)(2,1)S(1)} fusion(bf16[128,512]{0,1:T(8,128)(2,1)S(1)} %bitcast.82, bf16[4096,512]{1,0:T(8,128)(2,1)} %all-gather.2.cloned.1.call-done), kind=kOutput, calls=%fused_computation.1 | convolution fusion | flops 537395200 | bytes 5373952 | tf_op jit(solution)/shard_map/dot_general | solution.py:227
  221.6 0.2 copy.62
  221.8 0.5 all-to-all-done.5
  222.3 4.6 %all-to-all-start.4 = ((bf16[2,128,2048]{2,1,0:T(8,128)(2,1)}), bf16[2,128,2048]{2,1,0:T(8,128)(2,1)}, u32[]{:S(2)}, u32[]{:S(2)}) async-start(bf16[2,128,2048]{2,1,0:T(8,128)(2,1)} %bitcast.12), calls=%async_computation.4 | async-start | bytes 2097152 | tf_op jit(solution)/shard_map/all_to_all | solution.py:217
  226.9 3.7 %convolution_convert_fusion = bf16[128,4096]{1,0:T(8,128)(2,1)S(1)} fusion(bf16[128,512]{0,1:T(8,128)(2,1)S(1)} %bitcast.83, bf16[4096,512]{1,0:T(8,128)(2,1)} %collective-permute-done), kind=kOutput, calls=%fused_computation | convolution fusion | flops 537395200 | bytes 5373952 | tf_op jit(solution)/shard_map/dot_general | solution.py:230
  230.6 0.2 copy.63
  230.9 0.3 maximum_select_fusion
  231.3 4.6 %copy.55 = bf16[128,16,2,256]{3,2,1,0:T(2,128)(2,1)} copy(bf16[128,16,2,256]{3,1,0,2:T(8,128)(2,1)S(1)} %maximum_select_fusion) | data formatting | bytes 4194304 | tf_op jit(solution)/shard_map/jit(_where)/select_n | solution.py:233
  235.9 4.5 %select_n.46 = bf16[1,128,8192]{2,1,0:T(8,128)(2,1)} reshape(bf16[128,16,2,256]{3,2,1,0:T(2,128)(2,1)} %copy.55) | data formatting | bytes 4194304 | tf_op jit(solution)/shard_map/jit(_where)/select_n | solution.py:233
  240.4 0.1 copy.52
  240.5 0.7 all_to_all.132
  241.2 2.3 copy.51
  243.6 1.6 broadcast_in_dim.4
  (15 shorter events, 0.1 us)
Async XLA Ops:
  7.2 111.8 %all-gather.2.cloned.1.call-start = ((), (), s32[]{:S(2)}) async-start(), calls=%async_computation.9 | async-start | bytes 4456448 | tf_op jit(solution)/shard_map/all_gather | solution.py:142
  9.5 7.8 %all-to-all-start.2 = ((bf16[128,2,256]{2,0,1:T(8,128)(2,1)}), bf16[128,2,256]{2,0,1:T(8,128)(2,1)S(1)}, u32[]{:S(2)}, u32[]{:S(2)}) async-start(bf16[128,2,256]{2,0,1:T(8,128)(2,1)} %copy.47), calls=%async_computation.2 | async-start | bytes 262144 | tf_op jit(solution)/shard_map/all_to_all | solution.py:164
  14.7 6.2 %copy-start.4 = (bf16[1,128,4096]{2,1,0:T(8,128)(2,1)S(1)}, bf16[1,128,4096]{2,1,0:T(8,128)(2,1)}, u32[]{:S(2)}) copy-start(bf16[1,128,4096]{2,1,0:T(8,128)(2,1)} %param.10) | copy-start | bytes 3145732
  17.4 18.2 %all-to-all-start = ((bf16[128,2,2048]{2,0,1:T(8,128)(2,1)}), bf16[128,2,2048]{2,0,1:T(8,128)(2,1)S(1)}, u32[]{:S(2)}, u32[]{:S(2)}) async-start(bf16[128,2,2048]{2,0,1:T(8,128)(2,1)} %copy.45), calls=%async_computation | async-start | bytes 2097152 | tf_op jit(solution)/shard_map/all_to_all | solution.py:162
  21.8 18.0 %copy-start.6 = (s32[1,256]{1,0:T(1,128)S(1)}, s32[1,256]{1,0:T(1,128)}, u32[]{:S(2)}) copy-start(s32[1,256]{1,0:T(1,128)} %param.11) | copy-start | bytes 3076
  35.5 20.3 %all-to-all-start.1 = ((bf16[128,2,2048]{2,0,1:T(8,128)(2,1)}), bf16[128,2,2048]{2,0,1:T(8,128)(2,1)S(1)}, u32[]{:S(2)}, u32[]{:S(2)}) async-start(bf16[128,2,2048]{2,0,1:T(8,128)(2,1)} %copy.46), calls=%async_computation.1 | async-start | bytes 2097152 | tf_op jit(solution)/shard_map/all_to_all | solution.py:163
  81.8 29.7 %all-to-all-start.8 = ((bf16[8,128,512]{2,1,0:T(8,128)(2,1)}), bf16[8,128,512]{2,1,0:T(8,128)(2,1)}, u32[]{:S(2)}, u32[]{:S(2)}) async-start(bf16[8,128,512]{2,1,0:T(8,128)(2,1)} %broadcast_in_dim.5), calls=%async_computation.8 | async-start | bytes 2097152 | tf_op jit(solution)/shard_map/all_to_all | solution.py:179
  111.5 54.9 %all-to-all-start.7 = ((bf16[128,2,16,256]{0,3,1,2:T(8,128)(2,1)}), bf16[128,2,16,256]{0,3,1,2:T(8,128)(2,1)}, u32[]{:S(2)}, u32[]{:S(2)}) async-start(bf16[128,2,16,256]{0,3,1,2:T(8,128)(2,1)} %copy.57), calls=%async_computation.7 | async-start | bytes 4194304 | tf_op jit(solution)/shard_map/all_to_all | solution.py:151
  119.0 60.6 %collective-permute-start = (bf16[4096,512]{1,0:T(8,128)(2,1)}, bf16[4096,512]{1,0:T(8,128)(2,1)}, u32[]{:S(2)}, u32[]{:S(2)}) collective-permute-start(bf16[4096,512]{1,0:T(8,128)(2,1)} %all-gather.2.cloned.1.call-done), channel_id=1, source_target_pairs={{0,1},{1,0},{2,3},{3,2},{4,5},{5,4},{6,7},{7,6},{8,9},{9,8},{10,11... | collective-permute-start | bytes 12582920 | tf_op jit(solution)/shard_map/ppermute | solution.py:143
  119.2 55.8 %collective-permute-start.1 = (bf16[1024,512]{1,0:T(8,128)(2,1)}, bf16[1024,512]{1,0:T(8,128)(2,1)}, u32[]{:S(2)}, u32[]{:S(2)}) collective-permute-start(bf16[1024,512]{1,0:T(8,128)(2,1)} %bitcast.28), channel_id=1, source_target_pairs={{0,1},{1,0},{2,3},{3,2},{4,5},{5,4},{6,7},{7,6},{8,9},{9,8},{10,11... | collective-permute-start | bytes 3145736 | tf_op jit(solution)/shard_map/ppermute | solution.py:186
  172.6 2.4 copy-start.5
  175.0 3.9 %copy-start = (bf16[4096,512]{1,0:T(8,128)(2,1)S(1)}, bf16[4096,512]{1,0:T(8,128)(2,1)}, u32[]{:S(2)}) copy-start(bf16[4096,512]{1,0:T(8,128)(2,1)} %all-gather.2.cloned.1.call-done) | copy-start | bytes 12582916
  175.0 3.9 %copy-start.2 = (bf16[128,16,1,256]{0,3,2,1:T(8,128)(2,1)S(1)}, bf16[128,16,1,256]{0,3,2,1:T(8,128)(2,1)}, u32[]{:S(2)}) copy-start(bf16[128,16,1,256]{0,3,2,1:T(8,128)(2,1)} %get-tuple-element.11) | copy-start | bytes 3145732
  177.2 1.7 copy-start.3
  178.1 15.0 %collective-permute-start.2 = (f32[256,512]{1,0:T(8,128)}, f32[256,512]{1,0:T(8,128)S(1)}, u32[]{:S(2)}, u32[]{:S(2)}) collective-permute-start(f32[256,512]{1,0:T(8,128)} %dynamic-slice_bitcast_fusion), channel_id=1, source_target_pairs={{0,16},{16,0},{1,17},{17,1},{2,18},{18,2},{3,19},{19,3},{4,20},{20... | collective-permute-start | bytes 1572872 | tf_op jit(solution)/shard_map/ppermute | solution.py:203
  178.9 1.2 copy-start.1
  183.8 11.2 %all-to-all-start.3 = ((bf16[128,2,256]{2,0,1:T(8,128)(2,1)}), bf16[128,2,256]{2,0,1:T(8,128)(2,1)S(1)}, u32[]{:S(2)}, u32[]{:S(2)}) async-start(bf16[128,2,256]{2,0,1:T(8,128)(2,1)} %bitcast.65), calls=%async_computation.3 | async-start | bytes 262144 | tf_op jit(solution)/shard_map/all_to_all | solution.py:215
  214.5 7.8 %all-to-all-start.5 = ((bf16[2,128,256]{2,1,0:T(8,128)(2,1)}), bf16[2,128,256]{2,1,0:T(8,128)(2,1)S(1)}, u32[]{:S(2)}, u32[]{:S(2)}) async-start(bf16[2,128,256]{2,1,0:T(8,128)(2,1)} %bitcast.14), calls=%async_computation.5 | async-start | bytes 262144 | tf_op jit(solution)/shard_map/all_to_all | solution.py:218
  222.3 18.9 %all-to-all-start.4 = ((bf16[2,128,2048]{2,1,0:T(8,128)(2,1)}), bf16[2,128,2048]{2,1,0:T(8,128)(2,1)}, u32[]{:S(2)}, u32[]{:S(2)}) async-start(bf16[2,128,2048]{2,1,0:T(8,128)(2,1)} %bitcast.12), calls=%async_computation.4 | async-start | bytes 2097152 | tf_op jit(solution)/shard_map/all_to_all | solution.py:217
Sparse Core Ops, SparseCore 0:
  10.8 84.8 all-gather.1

commit v5 on v4

v5 whole, which is shorter than its diff:
```python
import functools
import math

import jax
import jax.numpy as jnp
from jax import lax
from jax.experimental import pallas as pl
from jax.experimental.pallas import tpu as pltpu
from jax.sharding import PartitionSpec as P

HD = 128
QH = 32
KVH = 4
ROWS = 128
FSDP = ("zx", "core")


drop_cut = 1677722
keep_scale = 1.0 / 0.9


def mixing(state):
    state = state ^ lax.shift_right_logical(state, jnp.full_like(state, 16))
    state = state * 2146121005
    state = state ^ lax.shift_right_logical(state, jnp.full_like(state, 15))
    state = state * 739982445
    state = state ^ lax.shift_right_logical(state, jnp.full_like(state, 16))
    return state


def attention_kernel(seeds_ref, offset_ref, pos_ref, q_ref, do_ref, k_ref, *refs, seq_len,
                     per_group, first):
    if first:
        (dv_ref,) = refs
    else:
        v_ref, dq_ref, dk_ref = refs
    g = pl.program_id(0)
    h = pl.program_id(1)
    head_seed = seeds_ref[g * per_group + h]
    inverse_root = 1.0 / math.sqrt(HD)
    last_dims = (((1,), (1,)), ((), ()))
    first_dims = (((0,), (0,)), ((), ()))
    acc_ref = dv_ref if first else dk_ref

    @pl.when(h == 0)
    def _():
        acc_ref[...] = jnp.zeros_like(acc_ref)

    q = q_ref[...]
    do = do_ref[...]
    k = k_ref[...]
    pos = pos_ref[...]
    rows_here = q.shape[0]
    scores = lax.dot_general(q, k, last_dims, preferred_element_type=jnp.float32) * inverse_root
    rows = lax.broadcasted_iota(jnp.int32, (rows_here, seq_len), 0) + offset_ref[0]
    cols = lax.broadcasted_iota(jnp.int32, (rows_here, seq_len), 1)
    visible = (cols <= rows) & (rows - cols <= pos)
    masked = jnp.where(visible, scores, -jnp.inf)
    row_max = jnp.max(masked, axis=1, keepdims=True)
    exp_terms = jnp.where(visible, jnp.exp(scores - row_max), 0.0)
    probs = exp_terms / jnp.sum(exp_terms, axis=1, keepdims=True)
    kept = (mixing(rows * seq_len + cols + head_seed) & 16777215) >= drop_cut
    if first:
        dropped = jnp.where(kept, probs * keep_scale, 0.0).astype(jnp.bfloat16)
        dv_ref[...] += lax.dot_general(dropped, do, first_dims, preferred_element_type=jnp.float32)
        return
    v = v_ref[...]
    raw = lax.dot_general(do, v, last_dims, preferred_element_type=jnp.float32)
    prob_grad = jnp.where(kept, raw * keep_scale, 0.0)
    row_delta = jnp.sum(probs * prob_grad, axis=1, keepdims=True)
    score_grad = (probs * (prob_grad - row_delta)).astype(jnp.bfloat16)
    dq = jnp.dot(score_grad, k, preferred_element_type=jnp.float32) * inverse_root
    dq_ref[...] = dq.astype(dq_ref.dtype)
    dk_ref[...] += (
        lax.dot_general(score_grad, q, first_dims, preferred_element_type=jnp.float32)
        * inverse_root
    )


def attention(seeds, offset, pos, queries, grads, keys, values):
    rows_here = queries.shape[0]
    seq_len = keys.shape[0]
    groups = keys.shape[1] // HD
    per_group = queries.shape[1] // HD // groups
    head_map = lambda g, h, s, o: (0, g * per_group + h)
    group_map = lambda g, h, s, o: (0, g)
    whole_map = lambda g, h, s, o: (0, 0)
    first = values is None
    kernel = functools.partial(
        attention_kernel, seq_len=seq_len, per_group=per_group, first=first
    )
    in_specs = [
        pl.BlockSpec((rows_here, 1), whole_map),
        pl.BlockSpec((rows_here, HD), head_map),
        pl.BlockSpec((rows_here, HD), head_map),
        pl.BlockSpec((seq_len, HD), group_map),
    ]
    operands = [seeds, offset, pos, queries, grads, keys]
    acc = jax.ShapeDtypeStruct(keys.shape, jnp.float32)
    if first:
        out_specs = [pl.BlockSpec((seq_len, HD), group_map)]
        out_shape = [acc]
    else:
        in_specs.append(pl.BlockSpec((seq_len, HD), group_map))
        operands.append(values)
        out_specs = [pl.BlockSpec((rows_here, HD), head_map), pl.BlockSpec((seq_len, HD), group_map)]
        out_shape = [jax.ShapeDtypeStruct(queries.shape, jnp.bfloat16), acc]
    return pl.pallas_call(
        kernel,
        grid_spec=pltpu.PrefetchScalarGridSpec(
            num_scalar_prefetch=2,
            grid=(groups, per_group),
            in_specs=in_specs,
            out_specs=out_specs,
        ),
        out_shape=out_shape,
        compiler_params=pltpu.CompilerParams(
            dimension_semantics=("arbitrary", "arbitrary"),
            vmem_limit_bytes=48 * 1024 * 1024,
        ),
    )(*operands)


def gather_seq(piece, seq_index, seq_devices):
    received = [piece]
    for shift in range(1, seq_devices):
        received.append(
            lax.ppermute(piece, "seq", [(i, (i + shift) % seq_devices) for i in range(seq_devices)])
        )
    order = (seq_index - jnp.arange(seq_devices, dtype=jnp.int32)) % seq_devices
    stacked = jnp.take(jnp.stack(received), order, axis=0)
    return stacked.reshape((seq_devices * piece.shape[0],) + piece.shape[1:])


def reduce_seq(partial, seq_index, seq_devices):
    blocks = partial.reshape((seq_devices, partial.shape[0] // seq_devices) + partial.shape[1:])
    summed = lax.dynamic_index_in_dim(blocks, seq_index, 0, keepdims=False)
    for shift in range(1, seq_devices):
        piece = lax.dynamic_index_in_dim(blocks, (seq_index + shift) % seq_devices, 0, keepdims=False)
        summed = summed + lax.ppermute(
            piece, "seq", [(i, (i + shift) % seq_devices) for i in range(seq_devices)]
        )
    return summed


def per_device(layer_input, queries, key_states, out_grad, doc_positions, drop_seed, value_weight):
    seq_devices = lax.axis_size("seq")
    zx_devices = lax.axis_size("zx")
    fsdp_devices = zx_devices * 2
    core_index = lax.axis_index("core")
    seq_index = lax.axis_index("seq")
    batch_index = lax.axis_index(FSDP)
    tok_rows = layer_input.shape[1]
    seq_len = tok_rows * seq_devices
    local_input = layer_input[0]
    block_rows = value_weight.shape[0]
    swap = [(0, 1), (1, 0)]
    weight_own = lax.all_gather(value_weight, ("seq", "zx"), axis=0, tiled=True)
    weight_other = lax.ppermute(weight_own, "core", swap)
    input_view = local_input.reshape(tok_rows, seq_devices * zx_devices, 2, block_rows)
    input_own = lax.dynamic_index_in_dim(input_view, core_index, 2, keepdims=False).reshape(
        tok_rows, -1
    )
    input_other = lax.dynamic_index_in_dim(input_view, 1 - core_index, 2, keepdims=False).reshape(
        tok_rows, -1
    )
    input_cols = lax.all_to_all(
        local_input.reshape(tok_rows, seq_devices, fsdp_devices, block_rows),
        FSDP,
        split_axis=2,
        concat_axis=0,
        tiled=True,
    ).reshape(zx_devices, 2, tok_rows, seq_devices * block_rows)
    base_seed = mixing(drop_seed + batch_index * 1000003)
    seeds = mixing(base_seed ^ jnp.arange(QH, dtype=jnp.int32) * 1640531527)
    offset = (seq_index * tok_rows).reshape(1).astype(jnp.int32)
    pos = lax.dynamic_slice_in_dim(doc_positions[0], seq_index * tok_rows, tok_rows)[:, None]
    query_loc, grad_loc = queries[0], out_grad[0]
    key_full = gather_seq(key_states[0], seq_index, seq_devices)
    (dv,) = attention(seeds, offset, pos, query_loc, grad_loc, key_full, None)
    value_grad = reduce_seq(dv, seq_index, seq_devices).astype(jnp.bfloat16)
    grads_own = lax.all_to_all(
        jnp.broadcast_to(value_grad[None], (zx_devices,) + value_grad.shape),
        "zx",
        split_axis=0,
        concat_axis=0,
        tiled=True,
    ).reshape(zx_devices * tok_rows, KVH * HD)
    grads_other = lax.ppermute(grads_own, "core", swap)
    cols_own = lax.dynamic_index_in_dim(input_cols, core_index, 1, keepdims=False).reshape(
        zx_devices * tok_rows, -1
    )
    cols_other = lax.dynamic_index_in_dim(input_cols, 1 - core_index, 1, keepdims=False).reshape(
        zx_devices * tok_rows, -1
    )
    first_dims = (((0,), (0,)), ((), ()))
    partial = (
        lax.dot_general(cols_own, grads_own, first_dims, preferred_element_type=jnp.float32)
        + lax.dot_general(cols_other, grads_other, first_dims, preferred_element_type=jnp.float32)
    ).reshape(seq_devices, block_rows, KVH * HD)
    summed = lax.dynamic_index_in_dim(partial, seq_index, 0, keepdims=False)
    for shift in range(1, seq_devices):
        piece = lax.dynamic_index_in_dim(
            partial, (seq_index + shift) % seq_devices, 0, keepdims=False
        )
        summed = summed + lax.ppermute(
            piece, "seq", [(i, (i + shift) % seq_devices) for i in range(seq_devices)]
        )
    weight_grad = (summed * (1.0 / math.sqrt(fsdp_devices * seq_len))).astype(jnp.bfloat16)

    values_loc = (
        jnp.dot(input_own, weight_own, preferred_element_type=jnp.float32)
        + jnp.dot(input_other, weight_other, preferred_element_type=jnp.float32)
    ).astype(jnp.bfloat16)
    value_full = gather_seq(values_loc, seq_index, seq_devices)
    dq, dk = attention(seeds, offset, pos, query_loc, grad_loc, key_full, value_full)
    query_grad = dq
    key_grad = reduce_seq(dk, seq_index, seq_devices).astype(jnp.bfloat16)
    last_dims = (((1,), (1,)), ((), ()))
    grad_own = lax.dot_general(
        value_grad, weight_own, last_dims, preferred_element_type=jnp.float32
    ).astype(jnp.bfloat16).reshape(tok_rows, seq_devices * zx_devices, 1, block_rows)
    grad_other = lax.dot_general(
        value_grad, weight_other, last_dims, preferred_element_type=jnp.float32
    ).astype(jnp.bfloat16).reshape(tok_rows, seq_devices * zx_devices, 1, block_rows)
    input_grad = jnp.where(
        core_index == 0,
        jnp.concatenate([grad_own, grad_other], axis=2),
        jnp.concatenate([grad_other, grad_own], axis=2),
    ).reshape(tok_rows, -1)
    return (query_grad[None], key_grad[None], input_grad[None], weight_grad)


def solution(mesh):
    seq_devices, fsdp_devices = mesh.devices.shape
    chips = jax.sharding.Mesh(
        mesh.devices.reshape(seq_devices, fsdp_devices // 2, 2), ("seq",) + FSDP
    )
    return jax.shard_map(
        per_device,
        mesh=chips,
        in_specs=(
            P(FSDP, "seq", None),
            P(FSDP, "seq", None),
            P(FSDP, "seq", None),
            P(FSDP, "seq", None),
            P(FSDP, None),
            P(),
            P(("seq",) + FSDP, None),
        ),
        out_specs=(
            P(FSDP, "seq", None),
            P(FSDP, "seq", None),
            P(FSDP, "seq", None),
            P(("seq",) + FSDP, None),
        ),
        check_vma=False,
    )
```

time: 254 us -> 282 us (1.11)
  waiting for transfers between devices: 96.8 us -> 158 us
  starting transfers between devices: 36.8 us -> 19.3 us
  local copies, waits for them, and re-layouts: 41.4 us -> 27.8 us
  blocking collectives: 8.29 us -> 0 us
  Pallas kernels: 35.2 us -> 43.1 us
    all_gather x1, waiting for transfers between devices: 0.01 us -> 79.9 us  [per_device(): weight_own = lax.all_gather(value_weight, ('seq', 'zx'), axis=0, tiled=True)]
    all_to_all x6 -> x0, waiting for transfers between devices: 30 us -> none  [the longest x1 15.8 us: per_device(): lax.all_to_all(out_grad[0], 'seq', split_axis=1, concat_axis=0, tiled=True)]
    all_to_all x6 -> x0, starting transfers between devices: 21.9 us -> none  [the longest x1 4.61 us: per_device(): lax.all_to_all(dq, 'seq', split_axis=0, concat_axis=1, tiled=True)]
    all_to_all x12 -> x0, local copies, waits for them, and re-layouts: 11 us -> none  [the longest x2 3.17 us: per_device(): lax.all_to_all(queries[0], 'seq', split_axis=1, concat_axis=0, tiled=True)]
    ppermute x0 -> x4, waiting for transfers between devices: none -> 9.72 us  [the longest x2 6.28 us: reduce_seq(): lax.ppermute(piece, 'seq', [(i, (i + shift) % seq_devices) for i in range...]
    all_to_all x1 -> x0, blocking collectives: 8.29 us -> none  [per_device(): lax.all_to_all(dv.astype(jnp.bfloat16), 'seq', split_axis=0, concat_axis=...]
    pallas_call x2, Pallas kernels: 35.2 us -> 43.1 us  [attention(): pl.pallas_call(kernel, grid_spec=pltpu.PrefetchScalarGridSpec(num_scalar_...]
    ppermute x0 -> x4, starting transfers between devices: none -> 4.13 us  [the longest x2 2.1 us: gather_seq(): lax.ppermute(piece, 'seq', [(i, (i + shift) % seq_devices) for i in range...]
  transfers between devices with their start and end apart: 12 -> 10, of which waited for: 7 -> 6; matrix products, arithmetic and copies ran while one was open for 20% -> 14% of each run, Pallas kernels for 7% -> 8%
where the time goes in v5:
time: 282 us
  waiting for transfers between devices  158 us (56%)
  Pallas kernels  43.1 us (15%)
  local copies, waits for them, and re-layouts  27.8 us (10%)
  starting transfers between devices  19.3 us (7%)
  between operations  15 us (5%)
  matrix products  13.1 us (5%)
  other arithmetic  5.07 us (2%)
    all_gather x1, waiting for transfers between devices, per_device(): weight_own = lax.all_gather(value_weight, ('seq', 'zx'), axis=0, tiled=True)  79.9 us
    all_to_all x1, waiting for transfers between devices, per_device(): lax.all_to_all(local_input.reshape(tok_rows, seq_devices, fsdp_devices, b...  47.2 us
    pallas_call x2, Pallas kernels, attention(): pl.pallas_call(kernel, grid_spec=pltpu.PrefetchScalarGridSpec(num_scalar_...  43.1 us
    all_to_all x1, waiting for transfers between devices, per_device(): lax.all_to_all(jnp.broadcast_to(value_grad[None], (zx_devices,) + value_g...  18.3 us
    all_to_all x1, starting transfers between devices, per_device(): lax.all_to_all(local_input.reshape(tok_rows, seq_devices, fsdp_devices, b...  7.79 us
    unnamed x23, local copies, waits for them, and re-layouts  6.69 us
    ppermute x2, waiting for transfers between devices, reduce_seq(): lax.ppermute(piece, 'seq', [(i, (i + shift) % seq_devices) for i in range...  6.28 us
    select_n x2, local copies, waits for them, and re-layouts, per_device(): jnp.where(core_index == 0, jnp.concatenate([grad_own, grad_other], axis=2...  6.09 us
  transfers between devices with their start and end apart: 10, of which 6 were waited for; matrix products, arithmetic and copies ran while one was open for 14% of the time, Pallas kernels for 8%

profile of v5, /device:TPU:10, one launch (start us, length us, event | category | flops | bytes accessed | tf_op | source)
XLA Modules:
  0.0 281.6 jit_solution(13312736853855972251)
XLA Ops:
  7.2 0.0 copy-start
  7.2 0.0 all-gather.2.cloned.1.call-start
  7.2 0.7 all-gather.2.cloned.1.call-update
  7.9 79.9 %all-gather.2.cloned.1.call-done = bf16[4096,512]{1,0:T(8,128)(2,1)} async-done(((bf16[256,512]{1,0:T(8,128)(2,1)}), bf16[4096,512]{1,0:T(8,128)(2,1)}) %all-gather.2.cloned.1.call-update) | async-done | bytes 4194320 | tf_op jit(solution)/shard_map/all_gather | solution.py:158
  87.8 0.0 collective-permute-start.1
  87.8 0.6 collective-permute-start
  89.1 3.2 %copy.25 = bf16[1,128,8192]{1,2,0:T(8,128)(2,1)S(1)} copy(bf16[1,128,8192]{2,1,0:T(8,128)(2,1)} %param.9) | data formatting | bytes 4194304 | tf_op args[0]
  92.3 0.0 copy-start.3
  92.4 0.0 copy-start.4
  92.4 0.2 constant_dynamic-slice_fusion.2
  92.7 1.0 copy-done.3
  93.7 1.6 copy-done.4
  95.3 0.7 fusion.10
  96.0 0.0 collective-permute-done.1
  96.1 0.0 copy-start.9
  96.1 3.0 %fusion = bf16[128,512]{1,0:T(8,128)(2,1)S(1)} fusion(f32[128,512]{1,0:T(8,128)S(1)} %fusion.10, bf16[128,4096]{0,1:T(8,128)(2,1)S(1)} %bitcast.86, bf16[4096,512]{1,0:T(8,128)(2,1)} %collective-permute-done.1), kind=kOutput, calls=%fused_computation.7 | convolution fusion | flops 537001984 | bytes 5636096 | tf_op jit(solution)/shard_map/dot_general | solution.py:213
  99.1 0.0 copy-start.1
  99.1 0.0 copy-start.2
  99.1 1.5 collective-permute-start.2
  100.6 0.0 copy-done
  100.6 0.1 copy.26.pos_ref
  100.7 0.0 collective-permute-done
  100.7 0.0 copy-done.9
  100.8 0.6 gather_fusion
  101.4 3.4 %collective-permute-done.2 = bf16[128,512]{1,0:T(8,128)(2,1)S(1)} collective-permute-done((bf16[128,512]{1,0:T(8,128)(2,1)S(1)}, bf16[128,512]{1,0:T(8,128)(2,1)S(1)}, u32[]{:S(2)}, u32[]{:S(2)}) %collective-permute-start.2) | collective-permute-done | bytes 131104 | tf_op jit(solution)/shard_map/ppermute | solution.py:128
  104.8 0.6 gather_fusion.1
  105.4 0.1 broadcast_select_fusion
  105.5 0.0 copy-done.1
  105.5 0.0 copy-done.2
  105.5 19.6 %shard_map.103 = f32[256,512]{1,0:T(8,128)S(1)} custom-call(s32[32]{0:T(128)S(1)} %shift-right-logical_xor_fusion.seeds_ref, s32[1]{0:T(128)} %bitcast.offset_ref, s32[128,1]{1,0:T(8,128)S(1)} %copy.26.pos_ref, bf16[128,4096]{1,0:T(8,128)(2,1)S(1)} %bitcast.71, bf16[128,4096]{1,0:T(8,128)(2,1)S(1)} %bitcast.73, bf16[256,512]{1,0:T(8,128)(2,1)S(1)} %bitcast.75), custom_call_target="tpu_custom_call" | custom-call | tf_op jit(solution)/shard_map/pallas_call | solution.py:108
  125.1 1.5 collective-permute-start.4
  126.6 6.3 %collective-permute-done.4 = f32[128,512]{1,0:T(8,128)} collective-permute-done((f32[128,512]{1,0:T(8,128)S(1)}, f32[128,512]{1,0:T(8,128)}, u32[]{:S(2)}, u32[]{:S(2)}) %collective-permute-start.4) | collective-permute-done | bytes 262176 | tf_op jit(solution)/shard_map/ppermute | solution.py:140
  132.9 1.0 fusion.3
  133.9 1.1 broadcast_in_dim.31
  135.0 5.6 %all-to-all-start.1 = ((bf16[8,128,512]{2,1,0:T(8,128)(2,1)}), bf16[8,128,512]{2,1,0:T(8,128)(2,1)}, u32[]{:S(2)}, u32[]{:S(2)}) async-start(bf16[8,128,512]{2,1,0:T(8,128)(2,1)} %broadcast_in_dim.31), calls=%async_computation.1 | async-start | bytes 2097152 | tf_op jit(solution)/shard_map/all_to_all | solution.py:182
  140.6 3.1 %copy.30 = bf16[128,2,16,256]{0,3,1,2:T(8,128)(2,1)} copy(bf16[128,2,16,256]{0,3,2,1:T(8,128)(2,1)} %bitcast.83) | data formatting | bytes 4194304 | tf_op jit(solution)/shard_map/reshape;squeeze | solution.py:168
  143.7 18.3 %all-to-all-done.1 = bf16[8,128,512]{2,1,0:T(8,128)(2,1)} async-done(((bf16[8,128,512]{2,1,0:T(8,128)(2,1)}), bf16[8,128,512]{2,1,0:T(8,128)(2,1)}, u32[]{:S(2)}, u32[]{:S(2)}) %all-to-all-start.1) | async-done | bytes 1048608 | tf_op jit(solution)/shard_map/all_to_all | solution.py:182
  162.0 7.8 %all-to-all-start = ((bf16[128,2,16,256]{0,3,1,2:T(8,128)(2,1)}), bf16[128,2,16,256]{0,3,1,2:T(8,128)(2,1)}, u32[]{:S(2)}, u32[]{:S(2)}) async-start(bf16[128,2,16,256]{0,3,1,2:T(8,128)(2,1)} %copy.30), calls=%async_computation | async-start | bytes 4194304 | tf_op jit(solution)/shard_map/all_to_all | solution.py:167
  169.8 0.2 collective-permute-start.5
  170.0 47.2 %all-to-all-done = bf16[128,2,16,256]{0,3,1,2:T(8,128)(2,1)} async-done(((bf16[128,2,16,256]{0,3,1,2:T(8,128)(2,1)}), bf16[128,2,16,256]{0,3,1,2:T(8,128)(2,1)}, u32[]{:S(2)}, u32[]{:S(2)}) %all-to-all-start) | async-done | bytes 2097184 | tf_op jit(solution)/shard_map/all_to_all | solution.py:167
  217.2 3.1 %constant_dynamic-slice_fusion = (bf16[8,1,128,512]{2,3,1,0:T(8,128)(2,1)}, bf16[8,1,128,512]{2,3,1,0:T(8,128)(2,1)}) fusion(bf16[8,2,128,512]{2,3,1,0:T(8,128)(2,1)} %bitcast.24, s32[]{:T(128)S(6)} %select_n.72, s32[]{:T(128)S(6)} %select_n.71), kind=kLoop, calls=%fused_computation.25 | loop fusion | bytes 4194312 | tf_op jit(solution)/shard_map/jit(dynamic_index_in_dim)/dynamic_slice | solution.py:193
  220.2 2.3 copy.32
  222.6 2.3 copy.31
  224.8 23.6 %shard_map.102 = (bf16[128,4096]{1,0:T(8,128)(2,1)}, f32[256,512]{1,0:T(8,128)S(1)}) custom-call(s32[32]{0:T(128)S(1)} %shift-right-logical_xor_fusion.seeds_ref, s32[1]{0:T(128)} %bitcast.offset_ref, s32[128,1]{1,0:T(8,128)S(1)} %copy.26.pos_ref, bf16[128,4096]{1,0:T(8,128)(2,1)S(1)} %bitcast.72, bf16[128,4096]{1,0:T(8,128)(2,1)S(1)} %bitcast.74, ...), custom_call_target="tpu_custom_call" | custom-call | tf_op jit(solution)/shard_map/pallas_call | solution.py:108
  248.4 0.7 dynamic-slice_bitcast_fusion.2
  249.1 0.5 collective-permute-start.3
  249.7 3.7 %convolution_convert_fusion = bf16[128,4096]{1,0:T(8,128)(2,1)S(1)} fusion(bf16[128,512]{1,0:T(8,128)(2,1)S(1)} %fusion.3, bf16[4096,512]{1,0:T(8,128)(2,1)} %collective-permute-done.1), kind=kOutput, calls=%fused_computation.2 | convolution fusion | flops 537395200 | bytes 5373952 | tf_op jit(solution)/shard_map/dot_general | solution.py:223
  253.3 0.0 copy-done.8
  253.4 2.1 fusion.11
  255.4 0.0 collective-permute-done.5
  255.5 2.1 convolution_add_fusion
  257.6 0.9 dynamic-slice_bitcast_fusion
  258.5 0.3 copy-done.6
  258.8 1.5 collective-permute-start.6
  260.3 1.5 convolution_convert_fusion.1
  261.7 0.2 copy.33
  262.0 0.2 copy.34
  262.3 0.3 maximum_select_fusion
  262.6 3.3 %copy.28 = bf16[128,16,2,256]{3,2,1,0:T(2,128)(2,1)S(1)} copy(bf16[128,16,2,256]{3,1,0,2:T(8,128)(2,1)S(1)} %maximum_select_fusion) | data formatting | bytes 4194304 | tf_op jit(solution)/shard_map/jit(_where)/select_n | solution.py:226
  265.9 2.8 select_n.78
  268.7 0.0 collective-permute-done.3
  268.7 1.6 fusion.5
  270.4 2.5 collective-permute-done.6
  272.9 1.9 fusion.2
  (14 shorter events, 0.1 us)
Async XLA Ops:
  7.2 93.4 %copy-start = (s32[1,256]{1,0:T(1,128)S(1)}, s32[1,256]{1,0:T(1,128)}, u32[]{:S(2)}) copy-start(s32[1,256]{1,0:T(1,128)} %param.13) | copy-start | bytes 3076
  7.2 80.7 %all-gather.2.cloned.1.call-start = ((), (), s32[]{:S(2)}) async-start(), calls=%async_computation.2 | async-start | bytes 4456448 | tf_op jit(solution)/shard_map/all_gather | solution.py:158
  87.8 8.2 %collective-permute-start.1 = (bf16[4096,512]{1,0:T(8,128)(2,1)}, bf16[4096,512]{1,0:T(8,128)(2,1)}, u32[]{:S(2)}, u32[]{:S(2)}) collective-permute-start(bf16[4096,512]{1,0:T(8,128)(2,1)} %all-gather.2.cloned.1.call-done), channel_id=1, source_target_pairs={{0,1},{1,0},{2,3},{3,2},{4,5},{5,4},{6,7},{7,6},{8,9},{9,8},{10,11... | collective-permute-start | bytes 12582920 | tf_op jit(solution)/shard_map/ppermute | solution.py:159
  87.8 12.9 %collective-permute-start = (bf16[128,512]{1,0:T(8,128)(2,1)}, bf16[128,512]{1,0:T(8,128)(2,1)S(1)}, u32[]{:S(2)}, u32[]{:S(2)}) collective-permute-start(bf16[128,512]{1,0:T(8,128)(2,1)} %bitcast.95), channel_id=1, source_target_pairs={{0,16},{16,0},{1,17},{17,1},{2,18},{18,2},{3,19},{19,3},{4,20},{20... | collective-permute-start | bytes 393224 | tf_op jit(solution)/shard_map/ppermute | solution.py:128
  92.3 1.3 copy-start.3
  92.4 2.9 %copy-start.4 = (bf16[4096,512]{1,0:T(8,128)(2,1)S(1)}, bf16[4096,512]{1,0:T(8,128)(2,1)}, u32[]{:S(2)}) copy-start(bf16[4096,512]{1,0:T(8,128)(2,1)} %all-gather.2.cloned.1.call-done) | copy-start | bytes 12582916
  96.1 4.7 %copy-start.9 = (bf16[1,128,512]{2,1,0:T(8,128)(2,1)S(1)}, bf16[1,128,512]{2,1,0:T(8,128)(2,1)}, u32[]{:S(2)}) copy-start(bf16[1,128,512]{2,1,0:T(8,128)(2,1)} %param.11) | copy-start | bytes 393220
  99.1 6.4 %copy-start.1 = (bf16[1,128,4096]{2,1,0:T(8,128)(2,1)S(1)}, bf16[1,128,4096]{2,1,0:T(8,128)(2,1)}, u32[]{:S(2)}) copy-start(bf16[1,128,4096]{2,1,0:T(8,128)(2,1)} %param.10) | copy-start | bytes 3145732
  99.1 6.4 %copy-start.2 = (bf16[1,128,4096]{2,1,0:T(8,128)(2,1)S(1)}, bf16[1,128,4096]{2,1,0:T(8,128)(2,1)}, u32[]{:S(2)}) copy-start(bf16[1,128,4096]{2,1,0:T(8,128)(2,1)} %param.12) | copy-start | bytes 3145732
  99.1 5.7 %collective-permute-start.2 = (bf16[128,512]{1,0:T(8,128)(2,1)S(1)}, bf16[128,512]{1,0:T(8,128)(2,1)S(1)}, u32[]{:S(2)}, u32[]{:S(2)}) collective-permute-start(bf16[128,512]{1,0:T(8,128)(2,1)S(1)} %fusion), channel_id=1, source_target_pairs={{0,16},{16,0},{1,17},{17,1},{2,18},{18,2},{3,19},{19,3},{4,20},{20... | collective-permute-start | bytes 393224 | tf_op jit(solution)/shard_map/ppermute | solution.py:128
  125.1 7.8 %collective-permute-start.4 = (f32[128,512]{1,0:T(8,128)S(1)}, f32[128,512]{1,0:T(8,128)}, u32[]{:S(2)}, u32[]{:S(2)}) collective-permute-start(f32[128,512]{1,0:T(8,128)S(1)} %dynamic-slice_bitcast_fusion.1), channel_id=1, source_target_pairs={{0,16},{16,0},{1,17},{17,1},{2,18},{18,2},{3,19},{19,3},{4,20},{20... | collective-permute-start | bytes 786440 | tf_op jit(solution)/shard_map/ppermute | solution.py:140
  135.0 27.0 %all-to-all-start.1 = ((bf16[8,128,512]{2,1,0:T(8,128)(2,1)}), bf16[8,128,512]{2,1,0:T(8,128)(2,1)}, u32[]{:S(2)}, u32[]{:S(2)}) async-start(bf16[8,128,512]{2,1,0:T(8,128)(2,1)} %broadcast_in_dim.31), calls=%async_computation.1 | async-start | bytes 2097152 | tf_op jit(solution)/shard_map/all_to_all | solution.py:182
  162.0 55.2 %all-to-all-start = ((bf16[128,2,16,256]{0,3,1,2:T(8,128)(2,1)}), bf16[128,2,16,256]{0,3,1,2:T(8,128)(2,1)}, u32[]{:S(2)}, u32[]{:S(2)}) async-start(bf16[128,2,16,256]{0,3,1,2:T(8,128)(2,1)} %copy.30), calls=%async_computation | async-start | bytes 4194304 | tf_op jit(solution)/shard_map/all_to_all | solution.py:167
  169.8 85.6 %collective-permute-start.5 = (bf16[1024,512]{1,0:T(8,128)(2,1)}, bf16[1024,512]{1,0:T(8,128)(2,1)}, u32[]{:S(2)}, u32[]{:S(2)}) collective-permute-start(bf16[1024,512]{1,0:T(8,128)(2,1)} %bitcast.26), channel_id=1, source_target_pairs={{0,1},{1,0},{2,3},{3,2},{4,5},{5,4},{6,7},{7,6},{8,9},{9,8},{10,11... | collective-permute-start | bytes 3145736 | tf_op jit(solution)/shard_map/ppermute | solution.py:189
  249.1 4.2 %copy-start.8 = (bf16[8,1,128,512]{3,2,0,1:T(8,128)(2,1)S(1)}, bf16[8,1,128,512]{3,2,0,1:T(8,128)(2,1)}, u32[]{:S(2)}) copy-start(bf16[8,1,128,512]{3,2,0,1:T(8,128)(2,1)} %copy.31) | copy-start | bytes 3145732
  249.1 19.6 %collective-permute-start.3 = (f32[128,512]{1,0:T(8,128)}, f32[128,512]{1,0:T(8,128)}, u32[]{:S(2)}, u32[]{:S(2)}) collective-permute-start(f32[128,512]{1,0:T(8,128)} %dynamic-slice_bitcast_fusion.2), channel_id=1, source_target_pairs={{0,16},{16,0},{1,17},{17,1},{2,18},{18,2},{3,19},{19,3},{4,20},{20... | collective-permute-start | bytes 786440 | tf_op jit(solution)/shard_map/ppermute | solution.py:140
  253.4 2.1 copy-start.7
  255.4 4.8 %copy-start.5 = (bf16[4096,512]{1,0:T(8,128)(2,1)S(1)}, bf16[4096,512]{1,0:T(8,128)(2,1)}, u32[]{:S(2)}) copy-start(bf16[4096,512]{1,0:T(8,128)(2,1)} %all-gather.2.cloned.1.call-done) | copy-start | bytes 12582916
  257.6 1.2 copy-start.6
  258.8 14.1 %collective-permute-start.6 = (f32[256,512]{1,0:T(8,128)}, f32[256,512]{1,0:T(8,128)S(1)}, u32[]{:S(2)}, u32[]{:S(2)}) collective-permute-start(f32[256,512]{1,0:T(8,128)} %dynamic-slice_bitcast_fusion), channel_id=1, source_target_pairs={{0,16},{16,0},{1,17},{17,1},{2,18},{18,2},{3,19},{19,3},{4,20},{20... | collective-permute-start | bytes 1572872 | tf_op jit(solution)/shard_map/ppermute | solution.py:206
Sparse Core Ops, SparseCore 0:
  10.8 76.9 all-gather.1

commit v6 on v5

--- a/solution.py
+++ b/solution.py
@@ -178,6 +178,7 @@
     query_loc, grad_loc = queries[0], out_grad[0]
     key_full = gather_seq(key_states[0], seq_index, seq_devices)
     (dv,) = attention(seeds, offset, pos, query_loc, grad_loc, key_full, None)
+    dv, input_cols, weight_own = lax.optimization_barrier((dv, input_cols, weight_own))
     value_grad = reduce_seq(dv, seq_index, seq_devices).astype(jnp.bfloat16)
     grads_own = lax.all_to_all(
         jnp.broadcast_to(value_grad[None], (zx_devices,) + value_grad.shape),

time: 282 us -> 233 us (0.83); the launches traced: 282 us -> 229 us
  waiting for transfers between devices: 158 us -> 84.9 us
  blocking collectives: 0 us -> 28.5 us
  starting transfers between devices: 19.3 us -> 11.4 us
  other arithmetic: 5.07 us -> 2.18 us
    all_gather x1, waiting for transfers between devices: 79.9 us -> 27.9 us  [per_device(): weight_own = lax.all_gather(value_weight, ('seq', 'zx'), axis=0, tiled=True)]
    all_to_all x0 -> x1, blocking collectives: none -> 28.5 us  [per_device(): lax.all_to_all(jnp.broadcast_to(value_grad[None], (zx_devices,) + value_g...]
    all_to_all x1 -> x0, waiting for transfers between devices: 18.3 us -> none  [per_device(): lax.all_to_all(jnp.broadcast_to(value_grad[None], (zx_devices,) + value_g...]
    all_to_all x1, waiting for transfers between devices: 47.2 us -> 36.5 us  [per_device(): lax.all_to_all(local_input.reshape(tok_rows, seq_devices, fsdp_devices, b...]
    all_to_all x1 -> x0, starting transfers between devices: 5.6 us -> none  [per_device(): lax.all_to_all(jnp.broadcast_to(value_grad[None], (zx_devices,) + value_g...]
    ppermute x1, waiting for transfers between devices: 2.52 us -> 6.88 us  [per_device(): lax.ppermute(piece, 'seq', [(i, (i + shift) % seq_devices) for i in range...]
    ppermute x2, waiting for transfers between devices: 3.44 us -> 6.64 us  [gather_seq(): lax.ppermute(piece, 'seq', [(i, (i + shift) % seq_devices) for i in range...]
    select_n x2, local copies, waits for them, and re-layouts: 6.09 us -> 9.09 us  [per_device(): jnp.where(core_index == 0, jnp.concatenate([grad_own, grad_other], axis=2...]
  transfers between devices with their start and end apart: 10 -> 9, of which waited for: 6 -> 6; matrix products, arithmetic and copies ran while one was open for 14% -> 19% of each run, Pallas kernels for 8% -> 9%
where the time goes in v6:
time: 233 us; the launch traced here: 229 us
  waiting for transfers between devices  84.9 us (36%)
  Pallas kernels  43.1 us (18%)
  local copies, waits for them, and re-layouts  28.6 us (12%)
  blocking collectives  28.5 us (12%)
  matrix products  15.6 us (7%)
  between operations  15 us (6%)
  starting transfers between devices  11.4 us (5%)
    pallas_call x2, Pallas kernels, attention(): pl.pallas_call(kernel, grid_spec=pltpu.PrefetchScalarGridSpec(num_scalar_...  43.1 us
    all_to_all x1, waiting for transfers between devices, per_device(): lax.all_to_all(local_input.reshape(tok_rows, seq_devices, fsdp_devices, b...  36.5 us
    all_to_all x1, blocking collectives, per_device(): lax.all_to_all(jnp.broadcast_to(value_grad[None], (zx_devices,) + value_g...  28.5 us
    all_gather x1, waiting for transfers between devices, per_device(): weight_own = lax.all_gather(value_weight, ('seq', 'zx'), axis=0, tiled=True)  27.9 us
    select_n x2, local copies, waits for them, and re-layouts, per_device(): jnp.where(core_index == 0, jnp.concatenate([grad_own, grad_other], axis=2...  9.09 us
    unnamed x27, local copies, waits for them, and re-layouts  7.09 us
    ppermute x1, waiting for transfers between devices, per_device(): lax.ppermute(piece, 'seq', [(i, (i + shift) % seq_devices) for i in range...  6.88 us
    ppermute x2, waiting for transfers between devices, gather_seq(): lax.ppermute(piece, 'seq', [(i, (i + shift) % seq_devices) for i in range...  6.64 us
  transfers between devices with their start and end apart: 9, of which 6 were waited for; matrix products, arithmetic and copies ran while one was open for 19% of the time, Pallas kernels for 9%

profile of v6, /device:TPU:10, one launch (start us, length us, event | category | flops | bytes accessed | tf_op | source)
XLA Modules:
  0.0 229.3 jit_solution(14358635789814015416)
XLA Ops:
  7.2 0.0 copy-start
  7.2 0.0 all-gather.2.cloned.1.call-start
  7.2 0.7 all-gather.2.cloned.1.call-update
  7.9 3.2 %copy.25 = bf16[1,128,8192]{1,2,0:T(8,128)(2,1)S(1)} copy(bf16[1,128,8192]{2,1,0:T(8,128)(2,1)} %param.9) | data formatting | bytes 4194304 | tf_op args[0]
  11.1 0.0 copy-start.3
  11.2 1.3 copy-done.3
  12.5 1.6 copy.28
  14.1 6.4 %all-to-all-start = ((bf16[128,2,16,256]{0,3,1,2:T(8,128)(2,1)}), bf16[128,2,16,256]{0,3,1,2:T(8,128)(2,1)}, u32[]{:S(2)}, u32[]{:S(2)}) async-start(bf16[128,2,16,256]{0,3,1,2:T(8,128)(2,1)} %copy.28), calls=%async_computation | async-start | bytes 4194304 | tf_op jit(solution)/shard_map/all_to_all | solution.py:167
  20.4 0.0 copy-done.11
  20.4 1.6 collective-permute-start
  22.8 0.1 copy.29.pos_ref
  22.9 5.0 %collective-permute-done = bf16[128,512]{1,0:T(8,128)(2,1)S(1)} collective-permute-done((bf16[128,512]{1,0:T(8,128)(2,1)S(1)}, bf16[128,512]{1,0:T(8,128)(2,1)S(1)}, u32[]{:S(2)}, u32[]{:S(2)}) %collective-permute-start) | collective-permute-done | bytes 131104 | tf_op jit(solution)/shard_map/ppermute | solution.py:128
  28.0 0.6 gather_fusion
  28.5 0.1 broadcast_select_fusion.1
  28.6 0.0 copy-done.1
  28.6 0.0 copy-done.2
  28.6 19.6 %shard_map.102 = f32[256,512]{1,0:T(8,128)S(1)} custom-call(s32[32]{0:T(128)S(1)} %shift-right-logical_xor_fusion.seeds_ref, s32[1]{0:T(128)} %bitcast.offset_ref, s32[128,1]{1,0:T(8,128)S(1)} %copy.29.pos_ref, bf16[128,4096]{1,0:T(8,128)(2,1)S(1)} %bitcast.71, bf16[128,4096]{1,0:T(8,128)(2,1)S(1)} %bitcast.73, bf16[256,512]{1,0:T(8,128)(2,1)S(1)} %bitcast.75), custom_call_target="tpu_custom_call" | custom-call | tf_op jit(solution)/shard_map/pallas_call | solution.py:108
  48.2 36.5 %all-to-all-done = bf16[128,2,16,256]{0,3,1,2:T(8,128)(2,1)} async-done(((bf16[128,2,16,256]{0,3,1,2:T(8,128)(2,1)}), bf16[128,2,16,256]{0,3,1,2:T(8,128)(2,1)}, u32[]{:S(2)}, u32[]{:S(2)}) %all-to-all-start) | async-done | bytes 2097184 | tf_op jit(solution)/shard_map/all_to_all | solution.py:167
  84.7 27.9 %all-gather.2.cloned.1.call-done = bf16[4096,512]{1,0:T(8,128)(2,1)} async-done(((bf16[256,512]{1,0:T(8,128)(2,1)}), bf16[4096,512]{1,0:T(8,128)(2,1)}) %all-gather.2.cloned.1.call-update) | async-done | bytes 4194320 | tf_op jit(solution)/shard_map/all_gather | solution.py:158
  112.6 0.7 collective-permute-start.4
  113.3 0.0 collective-permute-start.1
  113.3 6.3 %collective-permute-done.4 = f32[128,512]{1,0:T(8,128)S(1)} collective-permute-done((f32[128,512]{1,0:T(8,128)S(1)}, f32[128,512]{1,0:T(8,128)S(1)}, u32[]{:S(2)}, u32[]{:S(2)}) %collective-permute-start.4) | collective-permute-done | bytes 262176 | tf_op jit(solution)/shard_map/ppermute | solution.py:140
  119.6 0.0 copy-start.7
  119.6 0.1 broadcast_in_dim.31
  119.7 28.5 %all_to_all.20 = bf16[8,128,512]{2,1,0:T(8,128)(2,1)} all-to-all(bf16[8,128,512]{2,1,0:T(8,128)(2,1)S(1)} %broadcast_in_dim.31), channel_id=1, replica_groups=mesh['seq'=2,'zx'=8,'core'=2] {'zx'}, dimensions={0} | all-to-all | bytes 2097152 | tf_op jit(solution)/shard_map/all_to_all | solution.py:183
  148.2 0.0 copy-done.7
  148.2 0.0 collective-permute-start.5
  148.2 3.1 %constant_dynamic-slice_fusion.2 = (bf16[128,16,1,256]{0,3,2,1:T(8,128)(2,1)}, bf16[128,16,1,256]{0,3,2,1:T(8,128)(2,1)}) fusion(bf16[128,16,2,256]{0,3,2,1:T(8,128)(2,1)} %bitcast.83, s32[]{:T(128)S(6)} %select_n.72, s32[]{:T(128)S(6)} %select_n.71), kind=kLoop, calls=%fused_computation.27 | loop fusion | bytes 4194312 | tf_op jit(solution)/shard_map/jit(dynamic_index_in_dim)/dynamic_slice | solution.py:164
  151.3 2.7 %constant_dynamic-slice_fusion = (bf16[8,1,128,512]{2,3,1,0:T(8,128)(2,1)S(1)}, bf16[8,1,128,512]{2,3,1,0:T(8,128)(2,1)}) fusion(bf16[8,2,128,512]{2,3,1,0:T(8,128)(2,1)} %bitcast.12, s32[]{:T(128)S(6)} %select_n.72, s32[]{:T(128)S(6)} %select_n.71), kind=kLoop, calls=%fused_computation.25 | loop fusion | bytes 4194312 | tf_op jit(solution)/shard_map/jit(dynamic_index_in_dim)/dynamic_slice | solution.py:194
  154.0 2.3 %copy.31 = bf16[8,1,128,512]{3,2,0,1:T(8,128)(2,1)} copy(bf16[8,1,128,512]{2,3,1,0:T(8,128)(2,1)} %get-tuple-element.16) | data formatting | bytes 2097152 | tf_op jit(solution)/shard_map/jit(dynamic_index_in_dim)/dynamic_slice | solution.py:191
  156.3 1.3 copy.32
  157.6 3.3 %fusion.10 = f32[128,512]{1,0:T(8,128)S(1)} fusion(bf16[128,4096]{0,1:T(8,128)(2,1)} %bitcast.87, bf16[4096,512]{1,0:T(8,128)(2,1)} %all-gather.2.cloned.1.call-done), kind=kOutput, calls=%fused_computation.41 | convolution fusion | flops 536870912 | bytes 5505024 | tf_op jit(solution)/shard_map/dot_general | solution.py:213
  161.0 0.0 copy-start.9
  161.0 2.1 fusion.11
  163.0 0.0 collective-permute-done.5
  163.1 0.0 copy-done.9
  163.1 0.0 copy-start.4
  163.1 0.0 copy-start.8
  163.1 2.1 convolution_add_fusion
  165.3 0.7 collective-permute-start.6
  165.9 0.0 copy-done.8
  165.9 1.5 convolution_convert_fusion.1
  167.4 0.0 copy-start.6
  167.4 1.2 copy.33
  168.6 0.0 collective-permute-done.1
  168.7 0.1 copy-done.6
  168.7 3.0 %fusion = bf16[128,512]{1,0:T(8,128)(2,1)S(1)} fusion(f32[128,512]{1,0:T(8,128)S(1)} %fusion.10, bf16[128,4096]{0,1:T(8,128)(2,1)S(1)} %bitcast.86, bf16[4096,512]{1,0:T(8,128)(2,1)} %collective-permute-done.1), kind=kOutput, calls=%fused_computation.7 | convolution fusion | flops 537001984 | bytes 5636096 | tf_op jit(solution)/shard_map/dot_general | solution.py:214
  171.7 1.5 collective-permute-start.2
  173.2 6.9 %collective-permute-done.6 = f32[256,512]{1,0:T(8,128)S(1)} collective-permute-done((f32[256,512]{1,0:T(8,128)S(1)}, f32[256,512]{1,0:T(8,128)S(1)}, u32[]{:S(2)}, u32[]{:S(2)}) %collective-permute-start.6) | collective-permute-done | bytes 524320 | tf_op jit(solution)/shard_map/ppermute | solution.py:207
  180.0 0.8 fusion.2
  180.9 1.6 collective-permute-done.2
  182.5 0.6 gather_fusion.1
  183.1 0.1 broadcast_select_fusion
  183.2 23.6 %shard_map.103 = (bf16[128,4096]{1,0:T(8,128)(2,1)}, f32[256,512]{1,0:T(8,128)S(1)}) custom-call(s32[32]{0:T(128)S(1)} %shift-right-logical_xor_fusion.seeds_ref, s32[1]{0:T(128)} %bitcast.offset_ref, s32[128,1]{1,0:T(8,128)S(1)} %copy.29.pos_ref, bf16[128,4096]{1,0:T(8,128)(2,1)S(1)} %bitcast.72, bf16[128,4096]{1,0:T(8,128)(2,1)S(1)} %bitcast.74, ...), custom_call_target="tpu_custom_call" | custom-call | tf_op jit(solution)/shard_map/pallas_call | solution.py:108
  206.8 0.6 collective-permute-start.3
  207.4 3.7 %convolution_convert_fusion = bf16[128,4096]{1,0:T(8,128)(2,1)S(1)} fusion(bf16[128,512]{1,0:T(8,128)(2,1)S(1)} %copy-done.8, bf16[4096,512]{1,0:T(8,128)(2,1)} %collective-permute-done.1), kind=kOutput, calls=%fused_computation.2 | convolution fusion | flops 537395200 | bytes 5373952 | tf_op jit(solution)/shard_map/dot_general | solution.py:224
  211.1 0.0 copy-start.5
  211.1 0.2 copy.34
  211.4 1.0 copy-done.5
  212.3 0.3 maximum_select_fusion
  212.7 4.6 %copy.30 = bf16[128,16,2,256]{3,2,1,0:T(2,128)(2,1)} copy(bf16[128,16,2,256]{3,1,0,2:T(8,128)(2,1)S(1)} %maximum_select_fusion) | data formatting | bytes 4194304 | tf_op jit(solution)/shard_map/jit(_where)/select_n | solution.py:227
  217.3 4.5 %select_n.78 = bf16[1,128,8192]{2,1,0:T(8,128)(2,1)} reshape(bf16[128,16,2,256]{3,2,1,0:T(2,128)(2,1)} %copy.30) | data formatting | bytes 4194304 | tf_op jit(solution)/shard_map/jit(_where)/select_n | solution.py:227
  221.8 0.0 collective-permute-done.3
  221.8 0.7 fusion.5
  (18 shorter events, 0.2 us)
Async XLA Ops:
  7.2 15.6 %copy-start = (s32[1,256]{1,0:T(1,128)S(1)}, s32[1,256]{1,0:T(1,128)}, u32[]{:S(2)}) copy-start(s32[1,256]{1,0:T(1,128)} %param.13) | copy-start | bytes 3076
  7.2 105.4 %all-gather.2.cloned.1.call-start = ((), (), s32[]{:S(2)}) async-start(), calls=%async_computation.2 | async-start | bytes 4456448 | tf_op jit(solution)/shard_map/all_gather | solution.py:158
  11.1 1.3 copy-start.3
  14.1 6.4 %copy-start.11 = (bf16[1,128,512]{2,1,0:T(8,128)(2,1)S(1)}, bf16[1,128,512]{2,1,0:T(8,128)(2,1)}, u32[]{:S(2)}) copy-start(bf16[1,128,512]{2,1,0:T(8,128)(2,1)} %param.11) | copy-start | bytes 393220
  14.1 14.6 %copy-start.1 = (bf16[1,128,4096]{2,1,0:T(8,128)(2,1)S(1)}, bf16[1,128,4096]{2,1,0:T(8,128)(2,1)}, u32[]{:S(2)}) copy-start(bf16[1,128,4096]{2,1,0:T(8,128)(2,1)} %param.10) | copy-start | bytes 3145732
  14.1 14.6 %copy-start.2 = (bf16[1,128,4096]{2,1,0:T(8,128)(2,1)S(1)}, bf16[1,128,4096]{2,1,0:T(8,128)(2,1)}, u32[]{:S(2)}) copy-start(bf16[1,128,4096]{2,1,0:T(8,128)(2,1)} %param.12) | copy-start | bytes 3145732
  14.1 70.6 %all-to-all-start = ((bf16[128,2,16,256]{0,3,1,2:T(8,128)(2,1)}), bf16[128,2,16,256]{0,3,1,2:T(8,128)(2,1)}, u32[]{:S(2)}, u32[]{:S(2)}) async-start(bf16[128,2,16,256]{0,3,1,2:T(8,128)(2,1)} %copy.28), calls=%async_computation | async-start | bytes 4194304 | tf_op jit(solution)/shard_map/all_to_all | solution.py:167
  20.4 7.5 %collective-permute-start = (bf16[128,512]{1,0:T(8,128)(2,1)S(1)}, bf16[128,512]{1,0:T(8,128)(2,1)S(1)}, u32[]{:S(2)}, u32[]{:S(2)}) collective-permute-start(bf16[128,512]{1,0:T(8,128)(2,1)S(1)} %bitcast.95), channel_id=1, source_target_pairs={{0,16},{16,0},{1,17},{17,1},{2,18},{18,2},{3,19},{19,3},{4,20},{20... | collective-permute-start | bytes 393224 | tf_op jit(solution)/shard_map/ppermute | solution.py:128
  112.6 7.0 %collective-permute-start.4 = (f32[128,512]{1,0:T(8,128)S(1)}, f32[128,512]{1,0:T(8,128)S(1)}, u32[]{:S(2)}, u32[]{:S(2)}) collective-permute-start(f32[128,512]{1,0:T(8,128)S(1)} %dynamic-slice_bitcast_fusion.1), channel_id=1, source_target_pairs={{0,16},{16,0},{1,17},{17,1},{2,18},{18,2},{3,19},{19,3},{4,20},{20... | collective-permute-start | bytes 786440 | tf_op jit(solution)/shard_map/ppermute | solution.py:140
  113.3 55.4 %collective-permute-start.1 = (bf16[4096,512]{1,0:T(8,128)(2,1)}, bf16[4096,512]{1,0:T(8,128)(2,1)}, u32[]{:S(2)}, u32[]{:S(2)}) collective-permute-start(bf16[4096,512]{1,0:T(8,128)(2,1)} %all-gather.2.cloned.1.call-done), channel_id=1, source_target_pairs={{0,1},{1,0},{2,3},{3,2},{4,5},{5,4},{6,7},{7,6},{8,9},{9,8},{10,11... | collective-permute-start | bytes 12582920 | tf_op jit(solution)/shard_map/ppermute | solution.py:159
  119.6 28.6 %copy-start.7 = (bf16[128,512]{1,0:T(8,128)(2,1)}, bf16[128,512]{1,0:T(8,128)(2,1)S(1)}, u32[]{:S(2)}) copy-start(bf16[128,512]{1,0:T(8,128)(2,1)S(1)} %fusion.3) | copy-start | bytes 393220
  148.2 14.9 %collective-permute-start.5 = (bf16[1024,512]{1,0:T(8,128)(2,1)}, bf16[1024,512]{1,0:T(8,128)(2,1)}, u32[]{:S(2)}, u32[]{:S(2)}) collective-permute-start(bf16[1024,512]{1,0:T(8,128)(2,1)} %bitcast.26), channel_id=1, source_target_pairs={{0,1},{1,0},{2,3},{3,2},{4,5},{5,4},{6,7},{7,6},{8,9},{9,8},{10,11... | collective-permute-start | bytes 3145736 | tf_op jit(solution)/shard_map/ppermute | solution.py:190
  157.6 3.3 %copy-start.10 = (bf16[8,1,128,512]{3,2,0,1:T(8,128)(2,1)S(1)}, bf16[8,1,128,512]{3,2,0,1:T(8,128)(2,1)}, u32[]{:S(2)}) copy-start(bf16[8,1,128,512]{3,2,0,1:T(8,128)(2,1)} %copy.31) | copy-start | bytes 3145732
  161.0 2.1 copy-start.9
  163.1 2.9 %copy-start.4 = (bf16[4096,512]{1,0:T(8,128)(2,1)S(1)}, bf16[4096,512]{1,0:T(8,128)(2,1)}, u32[]{:S(2)}) copy-start(bf16[4096,512]{1,0:T(8,128)(2,1)} %all-gather.2.cloned.1.call-done) | copy-start | bytes 12582916
  163.1 2.8 %copy-start.8 = (bf16[128,512]{1,0:T(8,128)(2,1)S(1)}, bf16[128,512]{1,0:T(8,128)(2,1)}, u32[]{:S(2)}) copy-start(bf16[128,512]{1,0:T(8,128)(2,1)} %copy-done.7) | copy-start | bytes 393220
  165.3 14.8 %collective-permute-start.6 = (f32[256,512]{1,0:T(8,128)S(1)}, f32[256,512]{1,0:T(8,128)S(1)}, u32[]{:S(2)}, u32[]{:S(2)}) collective-permute-start(f32[256,512]{1,0:T(8,128)S(1)} %dynamic-slice_bitcast_fusion), channel_id=1, source_target_pairs={{0,16},{16,0},{1,17},{17,1},{2,18},{18,2},{3,19},{19,3},{4,20},{20... | collective-permute-start | bytes 1572872 | tf_op jit(solution)/shard_map/ppermute | solution.py:207
  167.4 1.3 copy-start.6
  171.7 10.8 %collective-permute-start.2 = (bf16[128,512]{1,0:T(8,128)(2,1)S(1)}, bf16[128,512]{1,0:T(8,128)(2,1)S(1)}, u32[]{:S(2)}, u32[]{:S(2)}) collective-permute-start(bf16[128,512]{1,0:T(8,128)(2,1)S(1)} %fusion), channel_id=1, source_target_pairs={{0,16},{16,0},{1,17},{17,1},{2,18},{18,2},{3,19},{19,3},{4,20},{20... | collective-permute-start | bytes 393224 | tf_op jit(solution)/shard_map/ppermute | solution.py:128
  206.8 15.0 %collective-permute-start.3 = (f32[128,512]{1,0:T(8,128)S(1)}, f32[128,512]{1,0:T(8,128)S(1)}, u32[]{:S(2)}, u32[]{:S(2)}) collective-permute-start(f32[128,512]{1,0:T(8,128)S(1)} %dynamic-slice_bitcast_fusion.2), channel_id=1, source_target_pairs={{0,16},{16,0},{1,17},{17,1},{2,18},{18,2},{3,19},{19,3},{4,20},{20... | collective-permute-start | bytes 786440 | tf_op jit(solution)/shard_map/ppermute | solution.py:140
  211.1 1.2 copy-start.5
Sparse Core Ops, SparseCore 0:
  10.8 101.7 all-gather.1

commit v7 on v5

--- a/solution.py
+++ b/solution.py
@@ -156,7 +156,6 @@
     block_rows = value_weight.shape[0]
     swap = [(0, 1), (1, 0)]
     weight_own = lax.all_gather(value_weight, ("seq", "zx"), axis=0, tiled=True)
-    weight_other = lax.ppermute(weight_own, "core", swap)
     input_view = local_input.reshape(tok_rows, seq_devices * zx_devices, 2, block_rows)
     input_own = lax.dynamic_index_in_dim(input_view, core_index, 2, keepdims=False).reshape(
         tok_rows, -1
@@ -164,13 +163,6 @@
     input_other = lax.dynamic_index_in_dim(input_view, 1 - core_index, 2, keepdims=False).reshape(
         tok_rows, -1
     )
-    input_cols = lax.all_to_all(
-        local_input.reshape(tok_rows, seq_devices, fsdp_devices, block_rows),
-        FSDP,
-        split_axis=2,
-        concat_axis=0,
-        tiled=True,
-    ).reshape(zx_devices, 2, tok_rows, seq_devices * block_rows)
     base_seed = mixing(drop_seed + batch_index * 1000003)
     seeds = mixing(base_seed ^ jnp.arange(QH, dtype=jnp.int32) * 1640531527)
     offset = (seq_index * tok_rows).reshape(1).astype(jnp.int32)
@@ -178,14 +170,26 @@
     query_loc, grad_loc = queries[0], out_grad[0]
     key_full = gather_seq(key_states[0], seq_index, seq_devices)
     (dv,) = attention(seeds, offset, pos, query_loc, grad_loc, key_full, None)
-    value_grad = reduce_seq(dv, seq_index, seq_devices).astype(jnp.bfloat16)
-    grads_own = lax.all_to_all(
-        jnp.broadcast_to(value_grad[None], (zx_devices,) + value_grad.shape),
-        "zx",
-        split_axis=0,
+    dv, weight_own, input_late = lax.optimization_barrier((dv, weight_own, local_input))
+    weight_other = lax.ppermute(weight_own, "core", swap)
+    input_cols = lax.all_to_all(
+        input_late.reshape(tok_rows, seq_devices, fsdp_devices, block_rows),
+        FSDP,
+        split_axis=2,
         concat_axis=0,
         tiled=True,
-    ).reshape(zx_devices * tok_rows, KVH * HD)
+    ).reshape(zx_devices, 2, tok_rows, seq_devices * block_rows)
+    value_grad = reduce_seq(dv, seq_index, seq_devices).astype(jnp.bfloat16)
+    grads_own = lax.all_gather(value_grad, "zx", axis=0, tiled=True)
+    values_loc = (
+        jnp.dot(input_own, weight_own, preferred_element_type=jnp.float32)
+        + jnp.dot(input_other, weight_other, preferred_element_type=jnp.float32)
+    ).astype(jnp.bfloat16)
+    value_full = gather_seq(values_loc, seq_index, seq_devices)
+    dq, dk = attention(seeds, offset, pos, query_loc, grad_loc, key_full, value_full)
+    grads_own, input_cols, dq, dk = lax.optimization_barrier((grads_own, input_cols, dq, dk))
+    query_grad = dq
+    key_grad = reduce_seq(dk, seq_index, seq_devices).astype(jnp.bfloat16)
     grads_other = lax.ppermute(grads_own, "core", swap)
     cols_own = lax.dynamic_index_in_dim(input_cols, core_index, 1, keepdims=False).reshape(
         zx_devices * tok_rows, -1
@@ -208,14 +212,6 @@
         )
     weight_grad = (summed * (1.0 / math.sqrt(fsdp_devices * seq_len))).astype(jnp.bfloat16)
 
-    values_loc = (
-        jnp.dot(input_own, weight_own, preferred_element_type=jnp.float32)
-        + jnp.dot(input_other, weight_other, preferred_element_type=jnp.float32)
-    ).astype(jnp.bfloat16)
-    value_full = gather_seq(values_loc, seq_index, seq_devices)
-    dq, dk = attention(seeds, offset, pos, query_loc, grad_loc, key_full, value_full)
-    query_grad = dq
-    key_grad = reduce_seq(dk, seq_index, seq_devices).astype(jnp.bfloat16)
     last_dims = (((1,), (1,)), ((), ()))
     grad_own = lax.dot_general(
         value_grad, weight_own, last_dims, preferred_element_type=jnp.float32

time: 282 us -> 201 us (0.71)
  waiting for transfers between devices: 158 us -> 84.9 us
  starting transfers between devices: 19.3 us -> 11.6 us
    all_to_all x2 -> x1, waiting for transfers between devices: 65.5 us -> 0.01 us  [per_device(): lax.all_to_all(input_late.reshape(tok_rows, seq_devices, fsdp_devices, bl...]
    all_gather x1, waiting for transfers between devices: 79.9 us -> 53.1 us  [per_device(): weight_own = lax.all_gather(value_weight, ('seq', 'zx'), axis=0, tiled=True)]
    all_gather x0 -> x1, waiting for transfers between devices: none -> 18.2 us  [per_device(): grads_own = lax.all_gather(value_grad, 'zx', axis=0, tiled=True)]
    all_to_all x2 -> x1, starting transfers between devices: 13.4 us -> 4.77 us  [per_device(): lax.all_to_all(input_late.reshape(tok_rows, seq_devices, fsdp_devices, bl...]
    reshape x0 -> x1, local copies, waits for them, and re-layouts: none -> 3.16 us  [per_device(): input_late.reshape(tok_rows, seq_devices, fsdp_devices, block_rows)]
    another operation x1 -> x0, local copies, waits for them, and re-layouts: 3.15 us -> none  [per_device(): local_input.reshape(tok_rows, seq_devices, fsdp_devices, block_rows)]
    unnamed x23 -> x19, local copies, waits for them, and re-layouts: 6.69 us -> 5.72 us
  transfers between devices with their start and end apart: 10 -> 10, of which waited for: 6 -> 5; matrix products, arithmetic and copies ran while one was open for 14% -> 21% of each run, Pallas kernels for 8% -> 22%
where the time goes in v7:
time: 201 us; the launch traced here: 199 us
  waiting for transfers between devices  84.9 us (42%)
  Pallas kernels  43.1 us (21%)
  local copies, waits for them, and re-layouts  25.3 us (13%)
  matrix products  15.4 us (8%)
  between operations  15 us (7%)
  starting transfers between devices  11.6 us (6%)
  other arithmetic  4.03 us (2%)
    all_gather x1, waiting for transfers between devices, per_device(): weight_own = lax.all_gather(value_weight, ('seq', 'zx'), axis=0, tiled=True)  53.1 us
    pallas_call x2, Pallas kernels, attention(): pl.pallas_call(kernel, grid_spec=pltpu.PrefetchScalarGridSpec(num_scalar_...  43.1 us
    all_gather x1, waiting for transfers between devices, per_device(): grads_own = lax.all_gather(value_grad, 'zx', axis=0, tiled=True)  18.2 us
    ppermute x2, waiting for transfers between devices, reduce_seq(): lax.ppermute(piece, 'seq', [(i, (i + shift) % seq_devices) for i in range...  6.9 us
    select_n x2, local copies, waits for them, and re-layouts, per_device(): jnp.where(core_index == 0, jnp.concatenate([grad_own, grad_other], axis=2...  6.09 us
    unnamed x19, local copies, waits for them, and re-layouts  5.72 us
    all_to_all x1, starting transfers between devices, per_device(): lax.all_to_all(input_late.reshape(tok_rows, seq_devices, fsdp_devices, bl...  4.77 us
  transfers between devices with their start and end apart: 10, of which 5 were waited for; matrix products, arithmetic and copies ran while one was open for 21% of the time, Pallas kernels for 22%

profile of v7, /device:TPU:10, one launch (start us, length us, event | category | flops | bytes accessed | tf_op | source)
XLA Modules:
  0.0 199.3 jit_solution(13875618102407946585)
XLA Ops:
  7.2 0.0 copy-start
  7.2 0.0 all-gather.3.cloned.1.call-start
  7.2 0.7 all-gather.3.cloned.1.call-update
  7.9 1.6 collective-permute-start
  10.2 0.0 copy-done
  10.2 0.1 copy.25.pos_ref
  10.4 0.0 copy-start.7
  10.4 0.0 copy-start.1
  10.4 0.0 copy-start.2
  10.4 4.2 %copy.26 = bf16[1,128,8192]{1,2,0:T(8,128)(2,1)} copy(bf16[1,128,8192]{2,1,0:T(8,128)(2,1)} %param.9) | data formatting | bytes 4194304 | tf_op args[0]
  14.6 0.0 collective-permute-done
  14.6 0.0 copy-done.7
  14.7 0.6 gather_fusion
  15.2 0.1 broadcast_select_fusion.1
  15.3 0.0 copy-done.1
  15.3 0.0 copy-done.2
  15.4 19.6 %shard_map.102 = f32[256,512]{1,0:T(8,128)S(1)} custom-call(s32[32]{0:T(128)S(1)} %shift-right-logical_xor_fusion.seeds_ref, s32[1]{0:T(128)} %bitcast.offset_ref, s32[128,1]{1,0:T(8,128)S(1)} %copy.25.pos_ref, bf16[128,4096]{1,0:T(8,128)(2,1)S(1)} %bitcast.71, bf16[128,4096]{1,0:T(8,128)(2,1)S(1)} %bitcast.73, bf16[256,512]{1,0:T(8,128)(2,1)S(1)} %bitcast.75), custom_call_target="tpu_custom_call" | custom-call | tf_op jit(solution)/shard_map/pallas_call | solution.py:108
  34.9 53.1 %all-gather.3.cloned.1.call-done = bf16[4096,512]{1,0:T(8,128)(2,1)} async-done(((bf16[256,512]{1,0:T(8,128)(2,1)}), bf16[4096,512]{1,0:T(8,128)(2,1)}) %all-gather.3.cloned.1.call-update) | async-done | bytes 4194320 | tf_op jit(solution)/shard_map/all_gather | solution.py:158
  88.0 0.0 collective-permute-start.2
  88.0 3.2 %copy.27 = bf16[128,2,16,256]{0,3,1,2:T(8,128)(2,1)} copy(bf16[128,2,16,256]{0,3,2,1:T(8,128)(2,1)} %bitcast.82) | data formatting | bytes 4194304 | tf_op jit(solution)/shard_map/reshape | solution.py:176
  91.2 4.8 %all-to-all-start = ((bf16[128,2,16,256]{0,3,1,2:T(8,128)(2,1)}), bf16[128,2,16,256]{0,3,1,2:T(8,128)(2,1)}, u32[]{:S(2)}, u32[]{:S(2)}) async-start(bf16[128,2,16,256]{0,3,1,2:T(8,128)(2,1)} %copy.27), calls=%async_computation | async-start | bytes 4194304 | tf_op jit(solution)/shard_map/all_to_all | solution.py:175
  95.9 0.0 all-gather.5.cloned.1.call-start
  96.0 1.5 collective-permute-start.1
  97.5 6.9 %collective-permute-done.1 = f32[128,512]{1,0:T(8,128)S(1)} collective-permute-done((f32[128,512]{1,0:T(8,128)S(1)}, f32[128,512]{1,0:T(8,128)S(1)}, u32[]{:S(2)}, u32[]{:S(2)}) %collective-permute-start.1) | collective-permute-done | bytes 262176 | tf_op jit(solution)/shard_map/ppermute | solution.py:140
  104.4 0.7 fusion.4
  105.1 0.0 all-gather.5.cloned.1.call-update
  105.2 0.0 copy-start.3
  105.2 1.8 constant_dynamic-slice_fusion.2
  107.0 1.0 copy-done.3
  108.0 0.7 fusion.10
  108.7 0.0 collective-permute-done.2
  108.7 3.0 %fusion = bf16[128,512]{1,0:T(8,128)(2,1)S(1)} fusion(f32[128,512]{1,0:T(8,128)S(1)} %fusion.10, bf16[128,4096]{0,1:T(8,128)(2,1)S(1)} %bitcast.86, bf16[4096,512]{1,0:T(8,128)(2,1)} %collective-permute-done.2), kind=kOutput, calls=%fused_computation.7 | convolution fusion | flops 537001984 | bytes 5636096 | tf_op jit(solution)/shard_map/dot_general | solution.py:186
  111.7 1.5 collective-permute-start.3
  113.2 3.5 %collective-permute-done.3 = bf16[128,512]{1,0:T(8,128)(2,1)S(1)} collective-permute-done((bf16[128,512]{1,0:T(8,128)(2,1)S(1)}, bf16[128,512]{1,0:T(8,128)(2,1)S(1)}, u32[]{:S(2)}, u32[]{:S(2)}) %collective-permute-start.3) | collective-permute-done | bytes 131104 | tf_op jit(solution)/shard_map/ppermute | solution.py:128
  116.8 0.6 gather_fusion.1
  117.3 0.1 broadcast_select_fusion
  117.4 23.6 %shard_map.103 = (bf16[128,4096]{1,0:T(8,128)(2,1)}, f32[256,512]{1,0:T(8,128)S(1)}) custom-call(s32[32]{0:T(128)S(1)} %shift-right-logical_xor_fusion.seeds_ref, s32[1]{0:T(128)} %bitcast.offset_ref, s32[128,1]{1,0:T(8,128)S(1)} %copy.25.pos_ref, bf16[128,4096]{1,0:T(8,128)(2,1)S(1)} %bitcast.72, bf16[128,4096]{1,0:T(8,128)(2,1)S(1)} %bitcast.74, ...), custom_call_target="tpu_custom_call" | custom-call | tf_op jit(solution)/shard_map/pallas_call | solution.py:108
  141.0 18.2 %all-gather.5.cloned.1.call-done = bf16[1024,512]{1,0:T(8,128)(2,1)} async-done(((bf16[128,512]{1,0:T(8,128)(2,1)}), bf16[1024,512]{1,0:T(8,128)(2,1)}) %all-gather.5.cloned.1.call-update) | async-done | bytes 1048592 | tf_op jit(solution)/shard_map/all_gather | solution.py:183
  159.2 0.0 all-to-all-done
  159.2 0.0 collective-permute-start.5
  159.2 0.0 copy-done.4
  159.2 3.7 %convolution_convert_fusion.1 = bf16[128,4096]{1,0:T(8,128)(2,1)S(1)} fusion(bf16[128,512]{1,0:T(8,128)(2,1)S(1)} %copy-done.4, bf16[4096,512]{1,0:T(8,128)(2,1)} %all-gather.3.cloned.1.call-done), kind=kOutput, calls=%fused_computation.3 | convolution fusion | flops 537395200 | bytes 5373952 | tf_op jit(solution)/shard_map/dot_general | solution.py:216
  162.9 0.2 copy.33
  163.2 1.4 collective-permute-start.4
  164.5 2.7 %constant_dynamic-slice_fusion = (bf16[8,1,128,512]{2,3,1,0:T(8,128)(2,1)S(1)}, bf16[8,1,128,512]{2,3,1,0:T(8,128)(2,1)}) fusion(bf16[8,2,128,512]{2,3,1,0:T(8,128)(2,1)} %bitcast.14, s32[]{:T(128)S(6)} %select_n.75, s32[]{:T(128)S(6)} %select_n.74), kind=kLoop, calls=%fused_computation.25 | loop fusion | bytes 4194312 | tf_op jit(solution)/shard_map/jit(dynamic_index_in_dim)/dynamic_slice | solution.py:197
  167.2 2.3 %copy.31 = bf16[8,1,128,512]{3,2,0,1:T(8,128)(2,1)} copy(bf16[8,1,128,512]{2,3,1,0:T(8,128)(2,1)} %get-tuple-element.24) | data formatting | bytes 2097152 | tf_op jit(solution)/shard_map/jit(dynamic_index_in_dim)/dynamic_slice | solution.py:194
  169.5 1.3 copy.32
  170.8 2.4 %fusion.11 = f32[512,512]{1,0:T(8,128)S(1)} fusion(bf16[1024,512]{1,0:T(8,128)(2,1)} %bitcast.93, bf16[1024,512]{1,0:T(8,128)(2,1)} %all-gather.5.cloned.1.call-done), kind=kOutput, calls=%fused_computation.42 | convolution fusion | flops 536870912 | bytes 3145728 | tf_op jit(solution)/shard_map/dot_general | solution.py:202
  173.2 0.0 collective-permute-done.5
  173.2 0.0 copy-done.6
  173.2 2.0 convolution_add_fusion
  175.2 0.0 copy-start.5
  175.2 0.9 dynamic-slice_bitcast_fusion
  176.1 0.7 collective-permute-start.6
  176.8 3.7 %convolution_convert_fusion = bf16[128,4096]{1,0:T(8,128)(2,1)S(1)} fusion(bf16[128,512]{1,0:T(8,128)(2,1)S(1)} %copy-done.4, bf16[4096,512]{1,0:T(8,128)(2,1)} %collective-permute-done.2), kind=kOutput, calls=%fused_computation.2 | convolution fusion | flops 537395200 | bytes 5373952 | tf_op jit(solution)/shard_map/dot_general | solution.py:219
  180.5 0.0 copy-done.5
  180.5 0.2 copy.34
  180.8 0.3 maximum_select_fusion
  181.1 3.3 %copy.30 = bf16[128,16,2,256]{3,2,1,0:T(2,128)(2,1)S(1)} copy(bf16[128,16,2,256]{3,1,0,2:T(8,128)(2,1)S(1)} %maximum_select_fusion) | data formatting | bytes 4194304 | tf_op jit(solution)/shard_map/jit(_where)/select_n | solution.py:222
  184.4 2.8 %select_n.78 = bf16[1,128,8192]{2,1,0:T(8,128)(2,1)} reshape(bf16[128,16,2,256]{3,2,1,0:T(2,128)(2,1)S(1)} %copy.30) | data formatting | bytes 4194304 | tf_op jit(solution)/shard_map/jit(_where)/select_n | solution.py:222
  187.2 0.0 collective-permute-done.4
  187.2 0.7 fusion.5
  187.9 2.6 %collective-permute-done.6 = f32[256,512]{1,0:T(8,128)} collective-permute-done((f32[256,512]{1,0:T(8,128)}, f32[256,512]{1,0:T(8,128)}, u32[]{:S(2)}, u32[]{:S(2)}) %collective-permute-start.6) | collective-permute-done | bytes 524320 | tf_op jit(solution)/shard_map/ppermute | solution.py:210
  190.5 2.0 %fusion.2 = bf16[256,512]{1,0:T(8,128)(2,1)} fusion(f32[256,512]{1,0:T(8,128)} %collective-permute-done.6, f32[2,256,512]{2,1,0:T(8,128)} %bitcast.91, s32[]{:T(128)S(6)} %select_n.71), kind=kLoop, calls=%fused_computation.10 | loop fusion | flops 393216 | bytes 1310724 | tf_op jit(solution)/shard_map/convert_element_type | solution.py:213
  (11 shorter events, 0.2 us)
Async XLA Ops:
  7.2 3.1 %copy-start = (s32[1,256]{1,0:T(1,128)S(1)}, s32[1,256]{1,0:T(1,128)}, u32[]{:S(2)}) copy-start(s32[1,256]{1,0:T(1,128)} %param.13) | copy-start | bytes 3076
  7.2 80.8 %all-gather.3.cloned.1.call-start = ((), (), s32[]{:S(2)}) async-start(), calls=%async_computation.1 | async-start | bytes 4456448 | tf_op jit(solution)/shard_map/all_gather | solution.py:158
  7.9 6.7 %collective-permute-start = (bf16[128,512]{1,0:T(8,128)(2,1)}, bf16[128,512]{1,0:T(8,128)(2,1)S(1)}, u32[]{:S(2)}, u32[]{:S(2)}) collective-permute-start(bf16[128,512]{1,0:T(8,128)(2,1)} %bitcast.95), channel_id=1, source_target_pairs={{0,16},{16,0},{1,17},{17,1},{2,18},{18,2},{3,19},{19,3},{4,20},{20... | collective-permute-start | bytes 393224 | tf_op jit(solution)/shard_map/ppermute | solution.py:128
  10.4 4.3 %copy-start.7 = (bf16[1,128,512]{2,1,0:T(8,128)(2,1)S(1)}, bf16[1,128,512]{2,1,0:T(8,128)(2,1)}, u32[]{:S(2)}) copy-start(bf16[1,128,512]{2,1,0:T(8,128)(2,1)} %param.11) | copy-start | bytes 393220
  10.4 5.0 %copy-start.1 = (bf16[1,128,4096]{2,1,0:T(8,128)(2,1)S(1)}, bf16[1,128,4096]{2,1,0:T(8,128)(2,1)}, u32[]{:S(2)}) copy-start(bf16[1,128,4096]{2,1,0:T(8,128)(2,1)} %param.10) | copy-start | bytes 3145732
  10.4 5.0 %copy-start.2 = (bf16[1,128,4096]{2,1,0:T(8,128)(2,1)S(1)}, bf16[1,128,4096]{2,1,0:T(8,128)(2,1)}, u32[]{:S(2)}) copy-start(bf16[1,128,4096]{2,1,0:T(8,128)(2,1)} %param.12) | copy-start | bytes 3145732
  88.0 20.7 %collective-permute-start.2 = (bf16[4096,512]{1,0:T(8,128)(2,1)}, bf16[4096,512]{1,0:T(8,128)(2,1)}, u32[]{:S(2)}, u32[]{:S(2)}) collective-permute-start(bf16[4096,512]{1,0:T(8,128)(2,1)} %all-gather.3.cloned.1.call-done), channel_id=1, source_target_pairs={{0,1},{1,0},{2,3},{3,2},{4,5},{5,4},{6,7},{7,6},{8,9},{9,8},{10,11... | collective-permute-start | bytes 12582920 | tf_op jit(solution)/shard_map/ppermute | solution.py:174
  91.2 68.0 %all-to-all-start = ((bf16[128,2,16,256]{0,3,1,2:T(8,128)(2,1)}), bf16[128,2,16,256]{0,3,1,2:T(8,128)(2,1)}, u32[]{:S(2)}, u32[]{:S(2)}) async-start(bf16[128,2,16,256]{0,3,1,2:T(8,128)(2,1)} %copy.27), calls=%async_computation | async-start | bytes 4194304 | tf_op jit(solution)/shard_map/all_to_all | solution.py:175
  95.9 63.3 %all-gather.5.cloned.1.call-start = ((), (), s32[]{:S(2)}) async-start(), calls=%async_computation.2 | async-start | bytes 1179648 | tf_op jit(solution)/shard_map/all_gather | solution.py:183
  96.0 8.4 %collective-permute-start.1 = (f32[128,512]{1,0:T(8,128)S(1)}, f32[128,512]{1,0:T(8,128)S(1)}, u32[]{:S(2)}, u32[]{:S(2)}) collective-permute-start(f32[128,512]{1,0:T(8,128)S(1)} %dynamic-slice_bitcast_fusion.2), channel_id=1, source_target_pairs={{0,16},{16,0},{1,17},{17,1},{2,18},{18,2},{3,19},{19,3},{4,20},{20... | collective-permute-start | bytes 786440 | tf_op jit(solution)/shard_map/ppermute | solution.py:140
  105.2 2.8 %copy-start.3 = (bf16[4096,512]{1,0:T(8,128)(2,1)S(1)}, bf16[4096,512]{1,0:T(8,128)(2,1)}, u32[]{:S(2)}) copy-start(bf16[4096,512]{1,0:T(8,128)(2,1)} %all-gather.3.cloned.1.call-done) | copy-start | bytes 12582916
  111.7 5.0 %collective-permute-start.3 = (bf16[128,512]{1,0:T(8,128)(2,1)S(1)}, bf16[128,512]{1,0:T(8,128)(2,1)S(1)}, u32[]{:S(2)}, u32[]{:S(2)}) collective-permute-start(bf16[128,512]{1,0:T(8,128)(2,1)S(1)} %fusion), channel_id=1, source_target_pairs={{0,16},{16,0},{1,17},{17,1},{2,18},{18,2},{3,19},{19,3},{4,20},{20... | collective-permute-start | bytes 393224 | tf_op jit(solution)/shard_map/ppermute | solution.py:128
  116.7 42.5 %copy-start.4 = (bf16[128,512]{1,0:T(8,128)(2,1)S(1)}, bf16[128,512]{1,0:T(8,128)(2,1)}, u32[]{:S(2)}) copy-start(bf16[128,512]{1,0:T(8,128)(2,1)} %fusion.4) | copy-start | bytes 393220
  159.2 14.0 %collective-permute-start.5 = (bf16[1024,512]{1,0:T(8,128)(2,1)}, bf16[1024,512]{1,0:T(8,128)(2,1)}, u32[]{:S(2)}, u32[]{:S(2)}) collective-permute-start(bf16[1024,512]{1,0:T(8,128)(2,1)} %all-gather.5.cloned.1.call-done), channel_id=1, source_target_pairs={{0,1},{1,0},{2,3},{3,2},{4,5},{5,4},{6,7},{7,6},{8,9},{9,8},{10,11... | collective-permute-start | bytes 3145736 | tf_op jit(solution)/shard_map/ppermute | solution.py:193
  163.2 24.0 %collective-permute-start.4 = (f32[128,512]{1,0:T(8,128)S(1)}, f32[128,512]{1,0:T(8,128)S(1)}, u32[]{:S(2)}, u32[]{:S(2)}) collective-permute-start(f32[128,512]{1,0:T(8,128)S(1)} %dynamic-slice_bitcast_fusion.1), channel_id=1, source_target_pairs={{0,16},{16,0},{1,17},{17,1},{2,18},{18,2},{3,19},{19,3},{4,20},{20... | collective-permute-start | bytes 786440 | tf_op jit(solution)/shard_map/ppermute | solution.py:140
  170.8 2.4 %copy-start.6 = (bf16[8,1,128,512]{3,2,0,1:T(8,128)(2,1)S(1)}, bf16[8,1,128,512]{3,2,0,1:T(8,128)(2,1)}, u32[]{:S(2)}) copy-start(bf16[8,1,128,512]{3,2,0,1:T(8,128)(2,1)} %copy.32) | copy-start | bytes 3145732
  175.2 5.3 %copy-start.5 = (f32[512,512]{1,0:T(8,128)}, f32[512,512]{1,0:T(8,128)S(1)}, u32[]{:S(2)}) copy-start(f32[512,512]{1,0:T(8,128)S(1)} %convolution_add_fusion) | copy-start | bytes 3145732
  176.1 14.4 %collective-permute-start.6 = (f32[256,512]{1,0:T(8,128)}, f32[256,512]{1,0:T(8,128)}, u32[]{:S(2)}, u32[]{:S(2)}) collective-permute-start(f32[256,512]{1,0:T(8,128)} %dynamic-slice_bitcast_fusion), channel_id=1, source_target_pairs={{0,16},{16,0},{1,17},{17,1},{2,18},{18,2},{3,19},{19,3},{4,20},{20... | collective-permute-start | bytes 1572872 | tf_op jit(solution)/shard_map/ppermute | solution.py:210
Sparse Core Ops, SparseCore 0:
  10.8 77.1 all-gather.2
  105.3 53.8 all-gather.4

commit v8 on v7

--- a/solution.py
+++ b/solution.py
@@ -170,7 +170,11 @@
     query_loc, grad_loc = queries[0], out_grad[0]
     key_full = gather_seq(key_states[0], seq_index, seq_devices)
     (dv,) = attention(seeds, offset, pos, query_loc, grad_loc, key_full, None)
-    dv, weight_own, input_late = lax.optimization_barrier((dv, weight_own, local_input))
+    value_grad = reduce_seq(dv, seq_index, seq_devices).astype(jnp.bfloat16)
+    grads_own = lax.all_gather(value_grad, "zx", axis=0, tiled=True)
+    value_grad, weight_own, input_late = lax.optimization_barrier(
+        (value_grad, weight_own, local_input)
+    )
     weight_other = lax.ppermute(weight_own, "core", swap)
     input_cols = lax.all_to_all(
         input_late.reshape(tok_rows, seq_devices, fsdp_devices, block_rows),
@@ -179,39 +183,10 @@
         concat_axis=0,
         tiled=True,
     ).reshape(zx_devices, 2, tok_rows, seq_devices * block_rows)
-    value_grad = reduce_seq(dv, seq_index, seq_devices).astype(jnp.bfloat16)
-    grads_own = lax.all_gather(value_grad, "zx", axis=0, tiled=True)
     values_loc = (
         jnp.dot(input_own, weight_own, preferred_element_type=jnp.float32)
         + jnp.dot(input_other, weight_other, preferred_element_type=jnp.float32)
     ).astype(jnp.bfloat16)
-    value_full = gather_seq(values_loc, seq_index, seq_devices)
-    dq, dk = attention(seeds, offset, pos, query_loc, grad_loc, key_full, value_full)
-    grads_own, input_cols, dq, dk = lax.optimization_barrier((grads_own, input_cols, dq, dk))
-    query_grad = dq
-    key_grad = reduce_seq(dk, seq_index, seq_devices).astype(jnp.bfloat16)
-    grads_other = lax.ppermute(grads_own, "core", swap)
-    cols_own = lax.dynamic_index_in_dim(input_cols, core_index, 1, keepdims=False).reshape(
-        zx_devices * tok_rows, -1
-    )
-    cols_other = lax.dynamic_index_in_dim(input_cols, 1 - core_index, 1, keepdims=False).reshape(
-        zx_devices * tok_rows, -1
-    )
-    first_dims = (((0,), (0,)), ((), ()))
-    partial = (
-        lax.dot_general(cols_own, grads_own, first_dims, preferred_element_type=jnp.float32)
-        + lax.dot_general(cols_other, grads_other, first_dims, preferred_element_type=jnp.float32)
-    ).reshape(seq_devices, block_rows, KVH * HD)
-    summed = lax.dynamic_index_in_dim(partial, seq_index, 0, keepdims=False)
-    for shift in range(1, seq_devices):
-        piece = lax.dynamic_index_in_dim(
-            partial, (seq_index + shift) % seq_devices, 0, keepdims=False
-        )
-        summed = summed + lax.ppermute(
-            piece, "seq", [(i, (i + shift) % seq_devices) for i in range(seq_devices)]
-        )
-    weight_grad = (summed * (1.0 / math.sqrt(fsdp_devices * seq_len))).astype(jnp.bfloat16)
-
     last_dims = (((1,), (1,)), ((), ()))
     grad_own = lax.dot_general(
         value_grad, weight_own, last_dims, preferred_element_type=jnp.float32
@@ -224,6 +199,34 @@
         jnp.concatenate([grad_own, grad_other], axis=2),
         jnp.concatenate([grad_other, grad_own], axis=2),
     ).reshape(tok_rows, -1)
+    value_full = gather_seq(values_loc, seq_index, seq_devices)
+    input_grad, value_full = lax.optimization_barrier((input_grad, value_full))
+    dq, dk = attention(seeds, offset, pos, query_loc, grad_loc, key_full, value_full)
+    grads_own, input_cols, dq, dk = lax.optimization_barrier((grads_own, input_cols, dq, dk))
+    query_grad = dq
+    key_grad = reduce_seq(dk, seq_index, seq_devices).astype(jnp.bfloat16)
+    grads_other = lax.ppermute(grads_own, "core", swap)
+    cols_own = lax.dynamic_index_in_dim(input_cols, core_index, 1, keepdims=False).reshape(
+        zx_devices * tok_rows, -1
+    )
+    cols_other = lax.dynamic_index_in_dim(input_cols, 1 - core_index, 1, keepdims=False).reshape(
+        zx_devices * tok_rows, -1
+    )
+    first_dims = (((0,), (0,)), ((), ()))
+    partial = (
+        lax.dot_general(cols_own, grads_own, first_dims, preferred_element_type=jnp.float32)
+        + lax.dot_general(cols_other, grads_other, first_dims, preferred_element_type=jnp.float32)
+    ).reshape(seq_devices, block_rows, KVH * HD)
+    summed = lax.dynamic_index_in_dim(partial, seq_index, 0, keepdims=False)
+    for shift in range(1, seq_devices):
+        piece = lax.dynamic_index_in_dim(
+            partial, (seq_index + shift) % seq_devices, 0, keepdims=False
+        )
+        summed = summed + lax.ppermute(
+            piece, "seq", [(i, (i + shift) % seq_devices) for i in range(seq_devices)]
+        )
+    weight_grad = (summed * (1.0 / math.sqrt(fsdp_devices * seq_len))).astype(jnp.bfloat16)
+
     return (query_grad[None], key_grad[None], input_grad[None], weight_grad)
 
 

time: 201 us -> 197 us (0.980)
  waiting for transfers between devices: 84.9 us -> 77.4 us
    ppermute x2, waiting for transfers between devices: 6.9 us -> 22.9 us  [reduce_seq(): lax.ppermute(piece, 'seq', [(i, (i + shift) % seq_devices) for i in range...]
    all_gather x1, waiting for transfers between devices: 53.1 us -> 40.9 us  [per_device(): weight_own = lax.all_gather(value_weight, ('seq', 'zx'), axis=0, tiled=True)]
    all_gather x1, waiting for transfers between devices: 18.2 us -> 8.67 us  [per_device(): grads_own = lax.all_gather(value_grad, 'zx', axis=0, tiled=True)]
    select_n x2, local copies, waits for them, and re-layouts: 6.09 us -> 9.18 us  [per_device(): jnp.where(core_index == 0, jnp.concatenate([grad_own, grad_other], axis=2...]
    ppermute x1, waiting for transfers between devices: 2.55 us -> 0.01 us  [per_device(): lax.ppermute(piece, 'seq', [(i, (i + shift) % seq_devices) for i in range...]
    unnamed x19 -> x21, local copies, waits for them, and re-layouts: 5.72 us -> 7.19 us
  transfers between devices with their start and end apart: 10 -> 10, of which waited for: 5 -> 6; matrix products, arithmetic and copies ran while one was open for 21% -> 20% of each run, Pallas kernels for 22% -> 22%
where the time goes in v8:
time: 197 us; the launch traced here: 194 us
  waiting for transfers between devices  77.4 us (39%)
  Pallas kernels  43.1 us (22%)
  local copies, waits for them, and re-layouts  25.9 us (13%)
  between operations  16.4 us (8%)
  matrix products  15.6 us (8%)
  starting transfers between devices  12.1 us (6%)
  other arithmetic  3.74 us (2%)
    pallas_call x2, Pallas kernels, attention(): pl.pallas_call(kernel, grid_spec=pltpu.PrefetchScalarGridSpec(num_scalar_...  43.1 us
    all_gather x1, waiting for transfers between devices, per_device(): weight_own = lax.all_gather(value_weight, ('seq', 'zx'), axis=0, tiled=True)  40.9 us
    ppermute x2, waiting for transfers between devices, reduce_seq(): lax.ppermute(piece, 'seq', [(i, (i + shift) % seq_devices) for i in range...  22.9 us
    select_n x2, local copies, waits for them, and re-layouts, per_device(): jnp.where(core_index == 0, jnp.concatenate([grad_own, grad_other], axis=2...  9.18 us
    all_gather x1, waiting for transfers between devices, per_device(): grads_own = lax.all_gather(value_grad, 'zx', axis=0, tiled=True)  8.67 us
    unnamed x21, local copies, waits for them, and re-layouts  7.19 us
    all_to_all x1, starting transfers between devices, per_device(): lax.all_to_all(input_late.reshape(tok_rows, seq_devices, fsdp_devices, bl...  4.9 us
  transfers between devices with their start and end apart: 10, of which 6 were waited for; matrix products, arithmetic and copies ran while one was open for 20% of the time, Pallas kernels for 22%

profile of v8, /device:TPU:10, one launch (start us, length us, event | category | flops | bytes accessed | tf_op | source)
XLA Modules:
  0.0 194.3 jit_solution(3420150205291248345)
XLA Ops:
  8.0 0.0 copy-start
  8.0 0.0 copy-start.1
  8.0 0.0 all-gather.5.cloned.1.call-start
  8.1 0.7 all-gather.5.cloned.1.call-update
  8.8 1.6 collective-permute-start
  11.1 0.0 copy-done
  11.1 0.1 copy.25.pos_ref
  11.2 3.0 %collective-permute-done = bf16[128,512]{1,0:T(8,128)(2,1)S(1)} collective-permute-done((bf16[128,512]{1,0:T(8,128)(2,1)}, bf16[128,512]{1,0:T(8,128)(2,1)S(1)}, u32[]{:S(2)}, u32[]{:S(2)}) %collective-permute-start) | collective-permute-done | bytes 131104 | tf_op jit(solution)/shard_map/ppermute | solution.py:128
  14.3 0.9 pad_maximum_fusion
  15.2 0.6 gather_fusion
  15.8 0.1 broadcast_select_fusion.1
  15.9 0.0 copy-done.1
  15.9 0.0 copy-start.2
  15.9 1.2 copy-done.2
  17.1 19.6 %shard_map.102 = f32[256,512]{1,0:T(8,128)S(1)} custom-call(s32[32]{0:T(128)S(1)} %shift-right-logical_xor_fusion.seeds_ref, s32[1]{0:T(128)} %bitcast.offset_ref, s32[128,1]{1,0:T(8,128)S(1)} %copy.25.pos_ref, bf16[128,4096]{1,0:T(8,128)(2,1)S(1)} %bitcast.72, bf16[128,4096]{1,0:T(8,128)(2,1)S(1)} %bitcast.74, bf16[256,512]{1,0:T(8,128)(2,1)S(1)} %bitcast.76), custom_call_target="tpu_custom_call" | custom-call | tf_op jit(solution)/shard_map/pallas_call | solution.py:108
  36.7 1.6 collective-permute-start.1
  38.3 4.1 %copy.26 = bf16[1,128,8192]{1,2,0:T(8,128)(2,1)} copy(bf16[1,128,8192]{2,1,0:T(8,128)(2,1)} %param.9) | data formatting | bytes 4194304 | tf_op args[0]
  42.4 5.4 %collective-permute-done.1 = f32[128,512]{1,0:T(8,128)S(1)} collective-permute-done((f32[128,512]{1,0:T(8,128)S(1)}, f32[128,512]{1,0:T(8,128)S(1)}, u32[]{:S(2)}, u32[]{:S(2)}) %collective-permute-start.1) | collective-permute-done | bytes 262176 | tf_op jit(solution)/shard_map/ppermute | solution.py:140
  47.7 0.7 fusion.4
  48.4 40.9 %all-gather.5.cloned.1.call-done = bf16[4096,512]{1,0:T(8,128)(2,1)} async-done(((bf16[256,512]{1,0:T(8,128)(2,1)}), bf16[4096,512]{1,0:T(8,128)(2,1)}) %all-gather.5.cloned.1.call-update) | async-done | bytes 4194320 | tf_op jit(solution)/shard_map/all_gather | solution.py:158
  89.4 0.0 collective-permute-start.2
  89.4 3.2 %copy.27 = bf16[128,2,16,256]{0,3,1,2:T(8,128)(2,1)} copy(bf16[128,2,16,256]{0,3,2,1:T(8,128)(2,1)} %bitcast.83) | data formatting | bytes 4194304 | tf_op jit(solution)/shard_map/reshape | solution.py:180
  92.5 4.9 %all-to-all-start = ((bf16[128,2,16,256]{0,3,1,2:T(8,128)(2,1)}), bf16[128,2,16,256]{0,3,1,2:T(8,128)(2,1)}, u32[]{:S(2)}, u32[]{:S(2)}) async-start(bf16[128,2,16,256]{0,3,1,2:T(8,128)(2,1)} %copy.27), calls=%async_computation | async-start | bytes 4194304 | tf_op jit(solution)/shard_map/all_to_all | solution.py:179
  97.4 0.0 all-gather.3.cloned.1.call-start
  97.5 0.0 copy-done.4
  97.5 1.5 constant_dynamic-slice_fusion.2
  99.0 0.0 all-gather.3.cloned.1.call-update
  99.0 0.0 copy-start.5
  99.0 3.9 %convolution_convert_fusion.1 = bf16[128,4096]{1,0:T(8,128)(2,1)S(1)} fusion(bf16[128,512]{1,0:T(8,128)(2,1)} %fusion.4, bf16[4096,512]{1,0:T(8,128)(2,1)} %all-gather.5.cloned.1.call-done), kind=kOutput, calls=%fused_computation.3 | convolution fusion | flops 537395200 | bytes 5373952 | tf_op jit(solution)/shard_map/dot_general | solution.py:191
  102.9 0.0 copy-start.7
  102.9 0.2 copy.33
  103.1 0.0 copy-done.5
  103.2 0.9 copy-done.7
  104.1 0.8 fusion.10
  104.9 0.0 collective-permute-done.2
  104.9 0.4 copy-done.6
  105.3 3.0 %fusion = bf16[128,512]{1,0:T(8,128)(2,1)S(1)} fusion(f32[128,512]{1,0:T(8,128)S(1)} %fusion.10, bf16[128,4096]{0,1:T(8,128)(2,1)S(1)} %bitcast.87, bf16[4096,512]{1,0:T(8,128)(2,1)} %collective-permute-done.2), kind=kOutput, calls=%fused_computation.7 | convolution fusion | flops 537001984 | bytes 5636096 | tf_op jit(solution)/shard_map/dot_general | solution.py:188
  108.3 1.5 collective-permute-start.3
  109.9 0.0 copy-done.8
  109.9 3.7 %convolution_convert_fusion = bf16[128,4096]{1,0:T(8,128)(2,1)S(1)} fusion(bf16[128,512]{1,0:T(8,128)(2,1)S(1)} %copy-done.8, bf16[4096,512]{1,0:T(8,128)(2,1)} %collective-permute-done.2), kind=kOutput, calls=%fused_computation.2 | convolution fusion | flops 537395200 | bytes 5373952 | tf_op jit(solution)/shard_map/dot_general | solution.py:194
  113.6 0.2 copy.34
  113.8 0.3 maximum_select_fusion
  114.2 4.6 %copy.28 = bf16[128,16,2,256]{3,2,1,0:T(2,128)(2,1)} copy(bf16[128,16,2,256]{3,1,0,2:T(8,128)(2,1)S(1)} %maximum_select_fusion) | data formatting | bytes 4194304 | tf_op jit(solution)/shard_map/jit(_where)/select_n | solution.py:197
  118.8 4.6 %select_n.70 = bf16[128,8192]{1,0:T(8,128)(2,1)} reshape(bf16[128,16,2,256]{3,2,1,0:T(2,128)(2,1)} %copy.28) | data formatting | bytes 4194304 | tf_op jit(solution)/shard_map/jit(_where)/select_n | solution.py:197
  123.4 0.0 collective-permute-done.3
  123.4 0.6 gather_fusion.1
  124.0 0.1 broadcast_select_fusion
  124.1 0.0 copy-done.3
  124.1 23.6 %shard_map.103 = (bf16[128,4096]{1,0:T(8,128)(2,1)}, f32[256,512]{1,0:T(8,128)S(1)}) custom-call(s32[32]{0:T(128)S(1)} %shift-right-logical_xor_fusion.seeds_ref, s32[1]{0:T(128)} %bitcast.offset_ref, s32[128,1]{1,0:T(8,128)S(1)} %copy.25.pos_ref, bf16[128,4096]{1,0:T(8,128)(2,1)S(1)} %bitcast.73, bf16[128,4096]{1,0:T(8,128)(2,1)S(1)} %bitcast.75, ...), custom_call_target="tpu_custom_call" | custom-call | tf_op jit(solution)/shard_map/pallas_call | solution.py:108
  147.7 8.7 %all-gather.3.cloned.1.call-done = bf16[1024,512]{1,0:T(8,128)(2,1)} async-done(((bf16[128,512]{1,0:T(8,128)(2,1)}), bf16[1024,512]{1,0:T(8,128)(2,1)}) %all-gather.3.cloned.1.call-update) | async-done | bytes 1048592 | tf_op jit(solution)/shard_map/all_gather | solution.py:174
  156.3 1.1 all-to-all-done
  157.5 0.3 collective-permute-start.5
  157.8 1.7 constant_dynamic-slice_fusion
  159.4 1.3 copy.31
  160.8 0.5 copy.32
  161.3 2.3 %fusion.11 = f32[512,512]{1,0:T(8,128)S(1)} fusion(bf16[1024,512]{1,0:T(8,128)(2,1)} %bitcast.95, bf16[1024,512]{1,0:T(8,128)(2,1)} %all-gather.3.cloned.1.call-done), kind=kOutput, calls=%fused_computation.42 | convolution fusion | flops 536870912 | bytes 3145728 | tf_op jit(solution)/shard_map/dot_general | solution.py:217
  163.6 0.0 collective-permute-done.5
  163.6 2.0 %convolution_add_fusion = f32[512,512]{1,0:T(8,128)S(1)} fusion(f32[512,512]{1,0:T(8,128)S(1)} %fusion.11, bf16[1024,512]{1,0:T(8,128)(2,1)S(1)} %bitcast.94, bf16[1024,512]{1,0:T(8,128)(2,1)} %collective-permute-done.5), kind=kOutput, calls=%fused_computation.5 | convolution fusion | flops 537133056 | bytes 4194304 | tf_op jit(solution)/shard_map/dot_general | solution.py:218
  165.6 1.5 collective-permute-start.6
  167.2 0.6 collective-permute-start.4
  167.8 17.5 %collective-permute-done.4 = f32[128,512]{1,0:T(8,128)S(1)} collective-permute-done((f32[128,512]{1,0:T(8,128)S(1)}, f32[128,512]{1,0:T(8,128)S(1)}, u32[]{:S(2)}, u32[]{:S(2)}) %collective-permute-start.4) | collective-permute-done | bytes 262176 | tf_op jit(solution)/shard_map/ppermute | solution.py:140
  185.3 0.7 fusion.5
  186.0 0.0 collective-permute-done.6
  186.0 0.8 fusion.2
  (13 shorter events, 0.2 us)
Async XLA Ops:
  8.0 3.1 %copy-start = (s32[1,256]{1,0:T(1,128)S(1)}, s32[1,256]{1,0:T(1,128)}, u32[]{:S(2)}) copy-start(s32[1,256]{1,0:T(1,128)} %param.13) | copy-start | bytes 3076
  8.0 7.9 %copy-start.1 = (bf16[1,128,4096]{2,1,0:T(8,128)(2,1)S(1)}, bf16[1,128,4096]{2,1,0:T(8,128)(2,1)}, u32[]{:S(2)}) copy-start(bf16[1,128,4096]{2,1,0:T(8,128)(2,1)} %param.10) | copy-start | bytes 3145732
  8.0 81.3 %all-gather.5.cloned.1.call-start = ((), (), s32[]{:S(2)}) async-start(), calls=%async_computation.2 | async-start | bytes 4456448 | tf_op jit(solution)/shard_map/all_gather | solution.py:158
  8.8 5.5 %collective-permute-start = (bf16[128,512]{1,0:T(8,128)(2,1)}, bf16[128,512]{1,0:T(8,128)(2,1)S(1)}, u32[]{:S(2)}, u32[]{:S(2)}) collective-permute-start(bf16[128,512]{1,0:T(8,128)(2,1)} %bitcast.97), channel_id=1, source_target_pairs={{0,16},{16,0},{1,17},{17,1},{2,18},{18,2},{3,19},{19,3},{4,20},{20... | collective-permute-start | bytes 393224 | tf_op jit(solution)/shard_map/ppermute | solution.py:128
  15.9 1.2 copy-start.2
  36.7 11.0 %collective-permute-start.1 = (f32[128,512]{1,0:T(8,128)S(1)}, f32[128,512]{1,0:T(8,128)S(1)}, u32[]{:S(2)}, u32[]{:S(2)}) collective-permute-start(f32[128,512]{1,0:T(8,128)S(1)} %dynamic-slice_bitcast_fusion.2), channel_id=1, source_target_pairs={{0,16},{16,0},{1,17},{17,1},{2,18},{18,2},{3,19},{19,3},{4,20},{20... | collective-permute-start | bytes 786440 | tf_op jit(solution)/shard_map/ppermute | solution.py:140
  89.4 15.5 %collective-permute-start.2 = (bf16[4096,512]{1,0:T(8,128)(2,1)}, bf16[4096,512]{1,0:T(8,128)(2,1)}, u32[]{:S(2)}, u32[]{:S(2)}) collective-permute-start(bf16[4096,512]{1,0:T(8,128)(2,1)} %all-gather.5.cloned.1.call-done), channel_id=1, source_target_pairs={{0,1},{1,0},{2,3},{3,2},{4,5},{5,4},{6,7},{7,6},{8,9},{9,8},{10,11... | collective-permute-start | bytes 12582920 | tf_op jit(solution)/shard_map/ppermute | solution.py:178
  92.5 5.0 %copy-start.4 = (bf16[1,128,8192]{1,2,0:T(8,128)(2,1)S(1)}, bf16[1,128,8192]{1,2,0:T(8,128)(2,1)}, u32[]{:S(2)}) copy-start(bf16[1,128,8192]{1,2,0:T(8,128)(2,1)} %copy.26) | copy-start | bytes 6291460
  92.5 64.9 %all-to-all-start = ((bf16[128,2,16,256]{0,3,1,2:T(8,128)(2,1)}), bf16[128,2,16,256]{0,3,1,2:T(8,128)(2,1)}, u32[]{:S(2)}, u32[]{:S(2)}) async-start(bf16[128,2,16,256]{0,3,1,2:T(8,128)(2,1)} %copy.27), calls=%async_computation | async-start | bytes 4194304 | tf_op jit(solution)/shard_map/all_to_all | solution.py:179
  97.4 58.9 %all-gather.3.cloned.1.call-start = ((), (), s32[]{:S(2)}) async-start(), calls=%async_computation.1 | async-start | bytes 1179648 | tf_op jit(solution)/shard_map/all_gather | solution.py:174
  99.0 4.2 %copy-start.5 = (bf16[4096,512]{1,0:T(8,128)(2,1)S(1)}, bf16[4096,512]{1,0:T(8,128)(2,1)}, u32[]{:S(2)}) copy-start(bf16[4096,512]{1,0:T(8,128)(2,1)} %all-gather.5.cloned.1.call-done) | copy-start | bytes 12582916
  102.9 1.2 copy-start.7
  104.1 1.2 copy-start.6
  105.3 4.6 %copy-start.8 = (bf16[128,512]{1,0:T(8,128)(2,1)S(1)}, bf16[128,512]{1,0:T(8,128)(2,1)}, u32[]{:S(2)}) copy-start(bf16[128,512]{1,0:T(8,128)(2,1)} %fusion.4) | copy-start | bytes 393220
  108.3 15.0 %collective-permute-start.3 = (bf16[128,512]{1,0:T(8,128)(2,1)S(1)}, bf16[128,512]{1,0:T(8,128)(2,1)S(1)}, u32[]{:S(2)}, u32[]{:S(2)}) collective-permute-start(bf16[128,512]{1,0:T(8,128)(2,1)S(1)} %fusion), channel_id=1, source_target_pairs={{0,16},{16,0},{1,17},{17,1},{2,18},{18,2},{3,19},{19,3},{4,20},{20... | collective-permute-start | bytes 393224 | tf_op jit(solution)/shard_map/ppermute | solution.py:128
  118.8 5.3 %copy-start.3 = (bf16[1,128,4096]{2,1,0:T(8,128)(2,1)S(1)}, bf16[1,128,4096]{2,1,0:T(8,128)(2,1)}, u32[]{:S(2)}) copy-start(bf16[1,128,4096]{2,1,0:T(8,128)(2,1)} %param.12) | copy-start | bytes 3145732
  157.5 6.1 %collective-permute-start.5 = (bf16[1024,512]{1,0:T(8,128)(2,1)}, bf16[1024,512]{1,0:T(8,128)(2,1)}, u32[]{:S(2)}, u32[]{:S(2)}) collective-permute-start(bf16[1024,512]{1,0:T(8,128)(2,1)} %all-gather.3.cloned.1.call-done), channel_id=1, source_target_pairs={{0,1},{1,0},{2,3},{3,2},{4,5},{5,4},{6,7},{7,6},{8,9},{9,8},{10,11... | collective-permute-start | bytes 3145736 | tf_op jit(solution)/shard_map/ppermute | solution.py:208
  165.6 20.4 %collective-permute-start.6 = (f32[256,512]{1,0:T(8,128)S(1)}, f32[256,512]{1,0:T(8,128)S(1)}, u32[]{:S(2)}, u32[]{:S(2)}) collective-permute-start(f32[256,512]{1,0:T(8,128)S(1)} %dynamic-slice_bitcast_fusion), channel_id=1, source_target_pairs={{0,16},{16,0},{1,17},{17,1},{2,18},{18,2},{3,19},{19,3},{4,20},{20... | collective-permute-start | bytes 1572872 | tf_op jit(solution)/shard_map/ppermute | solution.py:225
  167.2 18.2 %collective-permute-start.4 = (f32[128,512]{1,0:T(8,128)S(1)}, f32[128,512]{1,0:T(8,128)S(1)}, u32[]{:S(2)}, u32[]{:S(2)}) collective-permute-start(f32[128,512]{1,0:T(8,128)S(1)} %dynamic-slice_bitcast_fusion.1), channel_id=1, source_target_pairs={{0,16},{16,0},{1,17},{17,1},{2,18},{18,2},{3,19},{19,3},{4,20},{20... | collective-permute-start | bytes 786440 | tf_op jit(solution)/shard_map/ppermute | solution.py:140
Sparse Core Ops, SparseCore 0:
  11.7 77.6 all-gather.4
Sparse Core Ops, SparseCore 1:
  100.6 55.7 all-gather.2

commit v9 on v8

--- a/solution.py
+++ b/solution.py
@@ -121,15 +121,19 @@
     )(*operands)
 
 
+def gather_axis(piece, index, devices, axis):
+    received = [piece]
+    for shift in range(1, devices):
+        received.append(
+            lax.ppermute(piece, axis, [(i, (i + shift) % devices) for i in range(devices)])
+        )
+    order = (index - jnp.arange(devices, dtype=jnp.int32)) % devices
+    stacked = jnp.take(jnp.stack(received), order, axis=0)
+    return stacked.reshape((devices * piece.shape[0],) + piece.shape[1:])
+
+
 def gather_seq(piece, seq_index, seq_devices):
-    received = [piece]
-    for shift in range(1, seq_devices):
-        received.append(
-            lax.ppermute(piece, "seq", [(i, (i + shift) % seq_devices) for i in range(seq_devices)])
-        )
-    order = (seq_index - jnp.arange(seq_devices, dtype=jnp.int32)) % seq_devices
-    stacked = jnp.take(jnp.stack(received), order, axis=0)
-    return stacked.reshape((seq_devices * piece.shape[0],) + piece.shape[1:])
+    return gather_axis(piece, seq_index, seq_devices, "seq")
 
 
 def reduce_seq(partial, seq_index, seq_devices):
@@ -171,7 +175,7 @@
     key_full = gather_seq(key_states[0], seq_index, seq_devices)
     (dv,) = attention(seeds, offset, pos, query_loc, grad_loc, key_full, None)
     value_grad = reduce_seq(dv, seq_index, seq_devices).astype(jnp.bfloat16)
-    grads_own = lax.all_gather(value_grad, "zx", axis=0, tiled=True)
+    grads_own = gather_axis(value_grad, lax.axis_index("zx"), zx_devices, "zx")
     value_grad, weight_own, input_late = lax.optimization_barrier(
         (value_grad, weight_own, local_input)
     )
@@ -202,7 +206,7 @@
     value_full = gather_seq(values_loc, seq_index, seq_devices)
     input_grad, value_full = lax.optimization_barrier((input_grad, value_full))
     dq, dk = attention(seeds, offset, pos, query_loc, grad_loc, key_full, value_full)
-    grads_own, input_cols, dq, dk = lax.optimization_barrier((grads_own, input_cols, dq, dk))
+    grads_own, input_cols, dq = lax.optimization_barrier((grads_own, input_cols, dq))
     query_grad = dq
     key_grad = reduce_seq(dk, seq_index, seq_devices).astype(jnp.bfloat16)
     grads_other = lax.ppermute(grads_own, "core", swap)

time: 197 us -> 252 us (1.28)
  waiting for transfers between devices: 77.4 us -> 119 us
  starting transfers between devices: 12.1 us -> 22.6 us
  local copies, waits for them, and re-layouts: 25.9 us -> 30.4 us
    ppermute x2 -> x9, waiting for transfers between devices: 3.05 us -> 54.3 us  [gather_axis(): lax.ppermute(piece, axis, [(i, (i + shift) % devices) for i in range(devi...]
    ppermute x2 -> x9, starting transfers between devices: 3.12 us -> 12.5 us  [gather_axis(): lax.ppermute(piece, axis, [(i, (i + shift) % devices) for i in range(devi...]
    all_gather x1 -> x0, waiting for transfers between devices: 8.67 us -> none  [per_device(): grads_own = lax.all_gather(value_grad, 'zx', axis=0, tiled=True)]
    unnamed x21 -> x27, local copies, waits for them, and re-layouts: 7.19 us -> 10.9 us
  transfers between devices with their start and end apart: 10 -> 16, of which waited for: 6 -> 8; matrix products, arithmetic and copies ran while one was open for 20% -> 18% of each run, Pallas kernels for 22% -> 17%
where the time goes in v9:
time: 252 us; the launch traced here: 251 us
  waiting for transfers between devices  119 us (47%)
  Pallas kernels  43.1 us (17%)
  local copies, waits for them, and re-layouts  30.4 us (12%)
  starting transfers between devices  22.6 us (9%)
  matrix products  15.6 us (6%)
  between operations  15 us (6%)
  other arithmetic  5.01 us (2%)
    ppermute x9, waiting for transfers between devices, gather_axis(): lax.ppermute(piece, axis, [(i, (i + shift) % devices) for i in range(devi...  54.3 us
    pallas_call x2, Pallas kernels, attention(): pl.pallas_call(kernel, grid_spec=pltpu.PrefetchScalarGridSpec(num_scalar_...  43.1 us
    all_gather x1, waiting for transfers between devices, per_device(): weight_own = lax.all_gather(value_weight, ('seq', 'zx'), axis=0, tiled=True)  40.9 us
    ppermute x2, waiting for transfers between devices, reduce_seq(): lax.ppermute(piece, 'seq', [(i, (i + shift) % seq_devices) for i in range...  23.2 us
    ppermute x9, starting transfers between devices, gather_axis(): lax.ppermute(piece, axis, [(i, (i + shift) % devices) for i in range(devi...  12.5 us
    unnamed x27, local copies, waits for them, and re-layouts  10.9 us
    select_n x2, local copies, waits for them, and re-layouts, per_device(): jnp.where(core_index == 0, jnp.concatenate([grad_own, grad_other], axis=2...  9.2 us
    all_to_all x1, starting transfers between devices, per_device(): lax.all_to_all(input_late.reshape(tok_rows, seq_devices, fsdp_devices, bl...  6.28 us
  transfers between devices with their start and end apart: 16, of which 8 were waited for; matrix products, arithmetic and copies ran while one was open for 18% of the time, Pallas kernels for 17%

profile of v9, /device:TPU:10, one launch (start us, length us, event | category | flops | bytes accessed | tf_op | source)
XLA Modules:
  0.0 250.8 jit_solution(3913721278481691061)
XLA Ops:
  7.2 0.0 copy-start
  7.2 0.0 all-gather.2.cloned.1.call-start
  7.2 0.7 all-gather.2.cloned.1.call-update
  7.9 1.6 collective-permute-start
  10.3 0.1 copy.25.pos_ref
  10.4 3.0 %collective-permute-done = bf16[128,512]{1,0:T(8,128)(2,1)S(1)} collective-permute-done((bf16[128,512]{1,0:T(8,128)(2,1)}, bf16[128,512]{1,0:T(8,128)(2,1)S(1)}, u32[]{:S(2)}, u32[]{:S(2)}) %collective-permute-start) | collective-permute-done | bytes 131104 | tf_op jit(solution)/shard_map/ppermute | solution.py:128
  13.4 0.9 pad_maximum_fusion
  14.4 0.6 gather_fusion.1
  14.9 0.1 broadcast_select_fusion.1
  15.1 0.0 copy-start.2
  15.1 1.2 copy-done.2
  16.3 19.6 %shard_map.102 = f32[256,512]{1,0:T(8,128)S(1)} custom-call(s32[32]{0:T(128)S(1)} %shift-right-logical_xor_fusion.seeds_ref, s32[1]{0:T(128)} %bitcast.1.offset_ref, s32[128,1]{1,0:T(8,128)S(1)} %copy.25.pos_ref, bf16[128,4096]{1,0:T(8,128)(2,1)S(1)} %bitcast.95, bf16[128,4096]{1,0:T(8,128)(2,1)S(1)} %bitcast.97, bf16[256,512]{1,0:T(8,128)(2,1)S(1)} %bitcast.99), custom_call_target="tpu_custom_call" | custom-call | tf_op jit(solution)/shard_map/pallas_call | solution.py:108
  35.9 1.6 collective-permute-start.1
  37.5 4.1 %copy.26 = bf16[1,128,8192]{1,2,0:T(8,128)(2,1)} copy(bf16[1,128,8192]{2,1,0:T(8,128)(2,1)} %param.9) | data formatting | bytes 4194304 | tf_op args[0]
  41.5 5.4 %collective-permute-done.1 = f32[128,512]{1,0:T(8,128)S(1)} collective-permute-done((f32[128,512]{1,0:T(8,128)S(1)}, f32[128,512]{1,0:T(8,128)S(1)}, u32[]{:S(2)}, u32[]{:S(2)}) %collective-permute-start.1) | collective-permute-done | bytes 262176 | tf_op jit(solution)/shard_map/ppermute | solution.py:144
  46.9 0.7 bitcast_dynamic-update-slice_fusion.7
  47.6 40.9 %all-gather.2.cloned.1.call-done = bf16[4096,512]{1,0:T(8,128)(2,1)} async-done(((bf16[256,512]{1,0:T(8,128)(2,1)}), bf16[4096,512]{1,0:T(8,128)(2,1)}) %all-gather.2.cloned.1.call-update) | async-done | bytes 4194320 | tf_op jit(solution)/shard_map/all_gather | solution.py:162
  88.5 0.0 copy-start.4
  88.6 3.3 %constant_dynamic-slice_fusion.2 = (bf16[128,16,1,256]{0,3,2,1:T(8,128)(2,1)}, bf16[128,16,1,256]{0,3,2,1:T(8,128)(2,1)}) fusion(bf16[128,16,2,256]{0,3,2,1:T(8,128)(2,1)} %bitcast.106, s32[]{:T(128)S(6)} %select_n.115, s32[]{:T(128)S(6)} %select_n.114), kind=kLoop, calls=%fused_computation.40 | loop fusion | bytes 4194312 | tf_op jit(solution)/shard_map/jit(dynamic_index_in_dim)/dynamic_slice | solution.py:167
  91.8 0.1 broadcast_bitcast_fusion
  91.9 1.0 collective-permute-start.2
  93.0 0.6 collective-permute-start.3
  93.6 2.8 %collective-permute-start.4 = (bf16[128,512]{1,0:T(8,128)(2,1)}, bf16[128,512]{1,0:T(8,128)(2,1)}, u32[]{:S(2)}, u32[]{:S(2)}) collective-permute-start(bf16[128,512]{1,0:T(8,128)(2,1)} %get-tuple-element.16), channel_id=1, source_target_pairs={{0,6},{2,8},{4,10},{6,12},{8,14},{10,0},{12,2},{14,4},{1,7},{3,9},... | collective-permute-start | bytes 393224 | tf_op jit(solution)/shard_map/ppermute | solution.py:128
  96.3 1.0 collective-permute-start.5
  97.4 1.5 copy.27
  98.9 6.3 %all-to-all-start = ((bf16[128,2,16,256]{0,3,1,2:T(8,128)(2,1)}), bf16[128,2,16,256]{0,3,1,2:T(8,128)(2,1)}, u32[]{:S(2)}, u32[]{:S(2)}) async-start(bf16[128,2,16,256]{0,3,1,2:T(8,128)(2,1)} %copy.27), calls=%async_computation | async-start | bytes 4194304 | tf_op jit(solution)/shard_map/all_to_all | solution.py:183
  105.2 0.3 collective-permute-start.6
  105.5 0.9 bitcast_dynamic-update-slice_fusion.6
  106.4 3.7 %collective-permute-start.7 = (bf16[128,512]{1,0:T(8,128)(2,1)}, bf16[128,512]{1,0:T(8,128)(2,1)S(1)}, u32[]{:S(2)}, u32[]{:S(2)}) collective-permute-start(bf16[128,512]{1,0:T(8,128)(2,1)} %get-tuple-element.16), channel_id=1, source_target_pairs={{0,12},{2,14},{4,0},{6,2},{8,4},{10,6},{12,8},{14,10},{1,13},{3,15... | collective-permute-start | bytes 393224 | tf_op jit(solution)/shard_map/ppermute | solution.py:128
  110.1 0.9 bitcast_dynamic-update-slice_fusion.5
  111.0 0.8 collective-permute-start.8
  111.8 0.9 bitcast_dynamic-update-slice_fusion.4
  112.7 9.7 %collective-permute-done.5 = bf16[128,512]{1,0:T(8,128)(2,1)} collective-permute-done((bf16[128,512]{1,0:T(8,128)(2,1)}, bf16[128,512]{1,0:T(8,128)(2,1)}, u32[]{:S(2)}, u32[]{:S(2)}) %collective-permute-start.5) | collective-permute-done | bytes 131104 | tf_op jit(solution)/shard_map/ppermute | solution.py:128
  122.4 0.9 bitcast_dynamic-update-slice_fusion.3
  123.3 22.5 %collective-permute-done.6 = bf16[128,512]{1,0:T(8,128)(2,1)S(1)} collective-permute-done((bf16[128,512]{1,0:T(8,128)(2,1)}, bf16[128,512]{1,0:T(8,128)(2,1)S(1)}, u32[]{:S(2)}, u32[]{:S(2)}) %collective-permute-start.6) | collective-permute-done | bytes 131104 | tf_op jit(solution)/shard_map/ppermute | solution.py:128
  145.9 17.8 %collective-permute-done.7 = bf16[128,512]{1,0:T(8,128)(2,1)S(1)} collective-permute-done((bf16[128,512]{1,0:T(8,128)(2,1)}, bf16[128,512]{1,0:T(8,128)(2,1)S(1)}, u32[]{:S(2)}, u32[]{:S(2)}) %collective-permute-start.7) | collective-permute-done | bytes 131104 | tf_op jit(solution)/shard_map/ppermute | solution.py:128
  163.7 1.1 collective-permute-done.8
  164.9 0.6 gather_fusion
  165.5 1.2 bitcast_select_fusion
  166.7 3.9 %convolution_convert_fusion.1 = bf16[128,4096]{1,0:T(8,128)(2,1)S(1)} fusion(bf16[128,512]{1,0:T(8,128)(2,1)} %get-tuple-element.16, bf16[4096,512]{1,0:T(8,128)(2,1)} %all-gather.2.cloned.1.call-done), kind=kOutput, calls=%fused_computation.4 | convolution fusion | flops 537395200 | bytes 5373952 | tf_op jit(solution)/shard_map/dot_general | solution.py:195
  170.6 0.2 copy.33
  170.8 0.9 copy-done.7
  171.8 0.8 fusion.14
  172.6 0.4 copy-done.6
  173.0 2.9 %fusion = bf16[128,512]{1,0:T(8,128)(2,1)S(1)} fusion(f32[128,512]{1,0:T(8,128)S(1)} %fusion.14, bf16[128,4096]{0,1:T(8,128)(2,1)S(1)} %bitcast.110, bf16[4096,512]{1,0:T(8,128)(2,1)} %collective-permute-done.9), kind=kOutput, calls=%fused_computation.8 | convolution fusion | flops 537001984 | bytes 5636096 | tf_op jit(solution)/shard_map/dot_general | solution.py:192
  176.0 0.7 collective-permute-start.10
  176.7 3.7 %convolution_convert_fusion = bf16[128,4096]{1,0:T(8,128)(2,1)S(1)} fusion(bf16[128,512]{1,0:T(8,128)(2,1)} %get-tuple-element.16, bf16[4096,512]{1,0:T(8,128)(2,1)} %collective-permute-done.9), kind=kOutput, calls=%fused_computation.3 | convolution fusion | flops 537395200 | bytes 5373952 | tf_op jit(solution)/shard_map/dot_general | solution.py:198
  180.5 0.2 copy.34
  180.7 0.3 maximum_select_fusion
  181.1 4.6 %copy.28 = bf16[128,16,2,256]{3,2,1,0:T(2,128)(2,1)} copy(bf16[128,16,2,256]{3,1,0,2:T(8,128)(2,1)S(1)} %maximum_select_fusion) | data formatting | bytes 4194304 | tf_op jit(solution)/shard_map/jit(_where)/select_n | solution.py:201
  185.7 4.6 %select_n.113 = bf16[128,8192]{1,0:T(8,128)(2,1)} reshape(bf16[128,16,2,256]{3,2,1,0:T(2,128)(2,1)} %copy.28) | data formatting | bytes 4194304 | tf_op jit(solution)/shard_map/jit(_where)/select_n | solution.py:201
  190.3 0.6 gather_fusion.2
  190.9 0.1 broadcast_select_fusion
  191.0 23.6 %shard_map.103 = (bf16[128,4096]{1,0:T(8,128)(2,1)}, f32[256,512]{1,0:T(8,128)S(1)}) custom-call(s32[32]{0:T(128)S(1)} %shift-right-logical_xor_fusion.seeds_ref, s32[1]{0:T(128)} %bitcast.1.offset_ref, s32[128,1]{1,0:T(8,128)S(1)} %copy.25.pos_ref, bf16[128,4096]{1,0:T(8,128)(2,1)S(1)} %bitcast.96, bf16[128,4096]{1,0:T(8,128)(2,1)S(1)} %bitcast.98, ...), custom_call_target="tpu_custom_call" | custom-call | tf_op jit(solution)/shard_map/pallas_call | solution.py:108
  214.6 1.7 constant_dynamic-slice_fusion
  216.3 1.3 copy.31
  217.6 0.5 copy.32
  218.1 2.3 fusion.15
  220.4 2.0 convolution_add_fusion
  222.4 1.4 collective-permute-start.13
  223.9 0.8 collective-permute-start.11
  224.6 17.8 %collective-permute-done.11 = f32[128,512]{1,0:T(8,128)S(1)} collective-permute-done((f32[128,512]{1,0:T(8,128)S(1)}, f32[128,512]{1,0:T(8,128)S(1)}, u32[]{:S(2)}, u32[]{:S(2)}) %collective-permute-start.11) | collective-permute-done | bytes 262176 | tf_op jit(solution)/shard_map/ppermute | solution.py:144
  242.5 0.7 fusion.5
  243.2 0.8 fusion.2
  (37 shorter events, 0.3 us)
Async XLA Ops:
  7.2 3.1 %copy-start = (s32[1,256]{1,0:T(1,128)S(1)}, s32[1,256]{1,0:T(1,128)}, u32[]{:S(2)}) copy-start(s32[1,256]{1,0:T(1,128)} %param.13) | copy-start | bytes 3076
  7.2 7.9 %copy-start.1 = (bf16[1,128,4096]{2,1,0:T(8,128)(2,1)S(1)}, bf16[1,128,4096]{2,1,0:T(8,128)(2,1)}, u32[]{:S(2)}) copy-start(bf16[1,128,4096]{2,1,0:T(8,128)(2,1)} %param.10) | copy-start | bytes 3145732
  7.2 81.3 %all-gather.2.cloned.1.call-start = ((), (), s32[]{:S(2)}) async-start(), calls=%async_computation.1 | async-start | bytes 4456448 | tf_op jit(solution)/shard_map/all_gather | solution.py:162
  7.9 5.5 %collective-permute-start = (bf16[128,512]{1,0:T(8,128)(2,1)}, bf16[128,512]{1,0:T(8,128)(2,1)S(1)}, u32[]{:S(2)}, u32[]{:S(2)}) collective-permute-start(bf16[128,512]{1,0:T(8,128)(2,1)} %bitcast.120), channel_id=1, source_target_pairs={{0,16},{16,0},{1,17},{17,1},{2,18},{18,2},{3,19},{19,3},{4,20},{20... | collective-permute-start | bytes 393224 | tf_op jit(solution)/shard_map/ppermute | solution.py:128
  15.1 1.2 copy-start.2
  35.9 11.0 %collective-permute-start.1 = (f32[128,512]{1,0:T(8,128)S(1)}, f32[128,512]{1,0:T(8,128)S(1)}, u32[]{:S(2)}, u32[]{:S(2)}) collective-permute-start(f32[128,512]{1,0:T(8,128)S(1)} %dynamic-slice_bitcast_fusion.2), channel_id=1, source_target_pairs={{0,16},{16,0},{1,17},{17,1},{2,18},{18,2},{3,19},{19,3},{4,20},{20... | collective-permute-start | bytes 786440 | tf_op jit(solution)/shard_map/ppermute | solution.py:144
  88.5 84.1 %collective-permute-start.9 = (bf16[4096,512]{1,0:T(8,128)(2,1)}, bf16[4096,512]{1,0:T(8,128)(2,1)}, u32[]{:S(2)}, u32[]{:S(2)}) collective-permute-start(bf16[4096,512]{1,0:T(8,128)(2,1)} %all-gather.2.cloned.1.call-done), channel_id=1, source_target_pairs={{0,1},{1,0},{2,3},{3,2},{4,5},{5,4},{6,7},{7,6},{8,9},{9,8},{10,11... | collective-permute-start | bytes 12582920 | tf_op jit(solution)/shard_map/ppermute | solution.py:182
  88.5 8.8 %copy-start.4 = (bf16[1,128,8192]{1,2,0:T(8,128)(2,1)S(1)}, bf16[1,128,8192]{1,2,0:T(8,128)(2,1)}, u32[]{:S(2)}) copy-start(bf16[1,128,8192]{1,2,0:T(8,128)(2,1)} %copy.26) | copy-start | bytes 6291460
  91.9 13.3 %collective-permute-start.2 = (bf16[128,512]{1,0:T(8,128)(2,1)}, bf16[128,512]{1,0:T(8,128)(2,1)}, u32[]{:S(2)}, u32[]{:S(2)}) collective-permute-start(bf16[128,512]{1,0:T(8,128)(2,1)} %get-tuple-element.16), channel_id=1, source_target_pairs={{0,2},{2,4},{4,6},{6,8},{8,10},{10,12},{12,14},{14,0},{1,3},{3,5},... | collective-permute-start | bytes 393224 | tf_op jit(solution)/shard_map/ppermute | solution.py:128
  93.0 13.4 %collective-permute-start.3 = (bf16[128,512]{1,0:T(8,128)(2,1)}, bf16[128,512]{1,0:T(8,128)(2,1)}, u32[]{:S(2)}, u32[]{:S(2)}) collective-permute-start(bf16[128,512]{1,0:T(8,128)(2,1)} %get-tuple-element.16), channel_id=1, source_target_pairs={{0,4},{2,6},{4,8},{6,10},{8,12},{10,14},{12,0},{14,2},{1,5},{3,7},... | collective-permute-start | bytes 393224 | tf_op jit(solution)/shard_map/ppermute | solution.py:128
  93.6 17.4 %collective-permute-start.4 = (bf16[128,512]{1,0:T(8,128)(2,1)}, bf16[128,512]{1,0:T(8,128)(2,1)}, u32[]{:S(2)}, u32[]{:S(2)}) collective-permute-start(bf16[128,512]{1,0:T(8,128)(2,1)} %get-tuple-element.16), channel_id=1, source_target_pairs={{0,6},{2,8},{4,10},{6,12},{8,14},{10,0},{12,2},{14,4},{1,7},{3,9},... | collective-permute-start | bytes 393224 | tf_op jit(solution)/shard_map/ppermute | solution.py:128
  96.3 26.1 %collective-permute-start.5 = (bf16[128,512]{1,0:T(8,128)(2,1)}, bf16[128,512]{1,0:T(8,128)(2,1)}, u32[]{:S(2)}, u32[]{:S(2)}) collective-permute-start(bf16[128,512]{1,0:T(8,128)(2,1)} %get-tuple-element.16), channel_id=1, source_target_pairs={{0,8},{2,10},{4,12},{6,14},{8,0},{10,2},{12,4},{14,6},{1,9},{3,11}... | collective-permute-start | bytes 393224 | tf_op jit(solution)/shard_map/ppermute | solution.py:128
  98.9 6.6 %copy-start.8 = (bf16[8,128,512]{2,1,0:T(8,128)(2,1)S(1)}, bf16[8,128,512]{2,1,0:T(8,128)(2,1)}, u32[]{:S(2)}) copy-start(bf16[8,128,512]{2,1,0:T(8,128)(2,1)} %get-tuple-element.25) | copy-start | bytes 3145732
  98.9 115.7 %all-to-all-start = ((bf16[128,2,16,256]{0,3,1,2:T(8,128)(2,1)}), bf16[128,2,16,256]{0,3,1,2:T(8,128)(2,1)}, u32[]{:S(2)}, u32[]{:S(2)}) async-start(bf16[128,2,16,256]{0,3,1,2:T(8,128)(2,1)} %copy.27), calls=%async_computation | async-start | bytes 4194304 | tf_op jit(solution)/shard_map/all_to_all | solution.py:183
  105.2 40.7 %collective-permute-start.6 = (bf16[128,512]{1,0:T(8,128)(2,1)}, bf16[128,512]{1,0:T(8,128)(2,1)S(1)}, u32[]{:S(2)}, u32[]{:S(2)}) collective-permute-start(bf16[128,512]{1,0:T(8,128)(2,1)} %get-tuple-element.16), channel_id=1, source_target_pairs={{0,10},{2,12},{4,14},{6,0},{8,2},{10,4},{12,6},{14,8},{1,11},{3,13... | collective-permute-start | bytes 393224 | tf_op jit(solution)/shard_map/ppermute | solution.py:128
  106.4 57.3 %collective-permute-start.7 = (bf16[128,512]{1,0:T(8,128)(2,1)}, bf16[128,512]{1,0:T(8,128)(2,1)S(1)}, u32[]{:S(2)}, u32[]{:S(2)}) collective-permute-start(bf16[128,512]{1,0:T(8,128)(2,1)} %get-tuple-element.16), channel_id=1, source_target_pairs={{0,12},{2,14},{4,0},{6,2},{8,4},{10,6},{12,8},{14,10},{1,13},{3,15... | collective-permute-start | bytes 393224 | tf_op jit(solution)/shard_map/ppermute | solution.py:128
  111.0 53.9 %collective-permute-start.8 = (bf16[128,512]{1,0:T(8,128)(2,1)}, bf16[128,512]{1,0:T(8,128)(2,1)S(1)}, u32[]{:S(2)}, u32[]{:S(2)}) collective-permute-start(bf16[128,512]{1,0:T(8,128)(2,1)} %get-tuple-element.16), channel_id=1, source_target_pairs={{0,14},{2,0},{4,2},{6,4},{8,6},{10,8},{12,10},{14,12},{1,15},{3,1}... | collective-permute-start | bytes 393224 | tf_op jit(solution)/shard_map/ppermute | solution.py:128
  166.7 4.2 %copy-start.5 = (bf16[4096,512]{1,0:T(8,128)(2,1)S(1)}, bf16[4096,512]{1,0:T(8,128)(2,1)}, u32[]{:S(2)}) copy-start(bf16[4096,512]{1,0:T(8,128)(2,1)} %all-gather.2.cloned.1.call-done) | copy-start | bytes 12582916
  170.6 1.2 copy-start.7
  171.8 1.2 copy-start.6
  176.0 14.3 %collective-permute-start.10 = (bf16[128,512]{1,0:T(8,128)(2,1)S(1)}, bf16[128,512]{1,0:T(8,128)(2,1)S(1)}, u32[]{:S(2)}, u32[]{:S(2)}) collective-permute-start(bf16[128,512]{1,0:T(8,128)(2,1)S(1)} %fusion), channel_id=1, source_target_pairs={{0,16},{16,0},{1,17},{17,1},{2,18},{18,2},{3,19},{19,3},{4,20},{20... | collective-permute-start | bytes 393224 | tf_op jit(solution)/shard_map/ppermute | solution.py:128
  185.7 5.3 %copy-start.3 = (bf16[1,128,4096]{2,1,0:T(8,128)(2,1)S(1)}, bf16[1,128,4096]{2,1,0:T(8,128)(2,1)}, u32[]{:S(2)}) copy-start(bf16[1,128,4096]{2,1,0:T(8,128)(2,1)} %param.12) | copy-start | bytes 3145732
  214.6 5.9 %collective-permute-start.12 = (bf16[1024,512]{1,0:T(8,128)(2,1)}, bf16[1024,512]{1,0:T(8,128)(2,1)}, u32[]{:S(2)}, u32[]{:S(2)}) collective-permute-start(bf16[1024,512]{1,0:T(8,128)(2,1)} %bitcast_select_fusion), channel_id=1, source_target_pairs={{0,1},{1,0},{2,3},{3,2},{4,5},{5,4},{6,7},{7,6},{8,9},{9,8},{10,11... | collective-permute-start | bytes 3145736 | tf_op jit(solution)/shard_map/ppermute | solution.py:212
  222.4 20.7 %collective-permute-start.13 = (f32[256,512]{1,0:T(8,128)S(1)}, f32[256,512]{1,0:T(8,128)S(1)}, u32[]{:S(2)}, u32[]{:S(2)}) collective-permute-start(f32[256,512]{1,0:T(8,128)S(1)} %dynamic-slice_bitcast_fusion), channel_id=1, source_target_pairs={{0,16},{16,0},{1,17},{17,1},{2,18},{18,2},{3,19},{19,3},{4,20},{20... | collective-permute-start | bytes 1572872 | tf_op jit(solution)/shard_map/ppermute | solution.py:229
  223.9 18.6 %collective-permute-start.11 = (f32[128,512]{1,0:T(8,128)S(1)}, f32[128,512]{1,0:T(8,128)S(1)}, u32[]{:S(2)}, u32[]{:S(2)}) collective-permute-start(f32[128,512]{1,0:T(8,128)S(1)} %dynamic-slice_bitcast_fusion.1), channel_id=1, source_target_pairs={{0,16},{16,0},{1,17},{17,1},{2,18},{18,2},{3,19},{19,3},{4,20},{20... | collective-permute-start | bytes 786440 | tf_op jit(solution)/shard_map/ppermute | solution.py:144
Sparse Core Ops, SparseCore 0:
  10.8 77.6 all-gather.1

commit v10 on v8

--- a/solution.py
+++ b/solution.py
@@ -202,9 +202,11 @@
     value_full = gather_seq(values_loc, seq_index, seq_devices)
     input_grad, value_full = lax.optimization_barrier((input_grad, value_full))
     dq, dk = attention(seeds, offset, pos, query_loc, grad_loc, key_full, value_full)
-    grads_own, input_cols, dq, dk = lax.optimization_barrier((grads_own, input_cols, dq, dk))
+    key_grad = reduce_seq(dk, seq_index, seq_devices).astype(jnp.bfloat16)
+    grads_own, input_cols, dq, key_grad = lax.optimization_barrier(
+        (grads_own, input_cols, dq, key_grad)
+    )
     query_grad = dq
-    key_grad = reduce_seq(dk, seq_index, seq_devices).astype(jnp.bfloat16)
     grads_other = lax.ppermute(grads_own, "core", swap)
     cols_own = lax.dynamic_index_in_dim(input_cols, core_index, 1, keepdims=False).reshape(
         zx_devices * tok_rows, -1

time: 197 us -> 189 us (0.959)
  waiting for transfers between devices: 77.4 us -> 71 us
    ppermute x1, waiting for transfers between devices: 0.01 us -> 12.6 us  [per_device(): lax.ppermute(piece, 'seq', [(i, (i + shift) % seq_devices) for i in range...]
    ppermute x2, waiting for transfers between devices: 22.9 us -> 12.8 us  [reduce_seq(): lax.ppermute(piece, 'seq', [(i, (i + shift) % seq_devices) for i in range...]
    all_gather x1, waiting for transfers between devices: 8.67 us -> 0.01 us  [per_device(): grads_own = lax.all_gather(value_grad, 'zx', axis=0, tiled=True)]
  transfers between devices with their start and end apart: 10 -> 10, of which waited for: 6 -> 6; matrix products, arithmetic and copies ran while one was open for 20% -> 21% of each run, Pallas kernels for 22% -> 23%
where the time goes in v10:
time: 189 us; the launch traced here: 187 us
  waiting for transfers between devices  71 us (38%)
  Pallas kernels  43.1 us (23%)
  local copies, waits for them, and re-layouts  25.1 us (13%)
  between operations  16.4 us (9%)
  matrix products  15.3 us (8%)
  starting transfers between devices  12.2 us (6%)
  other arithmetic  3.74 us (2%)
    pallas_call x2, Pallas kernels, attention(): pl.pallas_call(kernel, grid_spec=pltpu.PrefetchScalarGridSpec(num_scalar_...  43.1 us
    all_gather x1, waiting for transfers between devices, per_device(): weight_own = lax.all_gather(value_weight, ('seq', 'zx'), axis=0, tiled=True)  40.9 us
    ppermute x2, waiting for transfers between devices, reduce_seq(): lax.ppermute(piece, 'seq', [(i, (i + shift) % seq_devices) for i in range...  12.8 us
    ppermute x1, waiting for transfers between devices, per_device(): lax.ppermute(piece, 'seq', [(i, (i + shift) % seq_devices) for i in range...  12.6 us
    select_n x2, local copies, waits for them, and re-layouts, per_device(): jnp.where(core_index == 0, jnp.concatenate([grad_own, grad_other], axis=2...  9.18 us
    unnamed x21, local copies, waits for them, and re-layouts  7.19 us
    all_to_all x1, starting transfers between devices, per_device(): lax.all_to_all(input_late.reshape(tok_rows, seq_devices, fsdp_devices, bl...  4.9 us
    dot_general x1, matrix products, per_device(): lax.dot_general(value_grad, weight_own, last_dims, preferred_element_type...  3.88 us
  transfers between devices with their start and end apart: 10, of which 6 were waited for; matrix products, arithmetic and copies ran while one was open for 21% of the time, Pallas kernels for 23%

profile of v10, /device:TPU:10, one launch (start us, length us, event | category | flops | bytes accessed | tf_op | source)
XLA Modules:
  0.0 186.9 jit_solution(15641111937823298671)
XLA Ops:
  8.0 0.0 copy-start
  8.0 0.0 copy-start.1
  8.0 0.0 all-gather.5.cloned.1.call-start
  8.1 0.7 all-gather.5.cloned.1.call-update
  8.8 1.6 collective-permute-start
  11.1 0.0 copy-done
  11.1 0.1 copy.25.pos_ref
  11.2 3.0 %collective-permute-done = bf16[128,512]{1,0:T(8,128)(2,1)S(1)} collective-permute-done((bf16[128,512]{1,0:T(8,128)(2,1)}, bf16[128,512]{1,0:T(8,128)(2,1)S(1)}, u32[]{:S(2)}, u32[]{:S(2)}) %collective-permute-start) | collective-permute-done | bytes 131104 | tf_op jit(solution)/shard_map/ppermute | solution.py:128
  14.3 0.9 pad_maximum_fusion
  15.2 0.6 gather_fusion
  15.8 0.1 broadcast_select_fusion.1
  15.9 0.0 copy-done.1
  15.9 0.0 copy-start.2
  15.9 1.2 copy-done.2
  17.1 19.6 %shard_map.102 = f32[256,512]{1,0:T(8,128)S(1)} custom-call(s32[32]{0:T(128)S(1)} %shift-right-logical_xor_fusion.seeds_ref, s32[1]{0:T(128)} %bitcast.offset_ref, s32[128,1]{1,0:T(8,128)S(1)} %copy.25.pos_ref, bf16[128,4096]{1,0:T(8,128)(2,1)S(1)} %bitcast.69, bf16[128,4096]{1,0:T(8,128)(2,1)S(1)} %bitcast.71, bf16[256,512]{1,0:T(8,128)(2,1)S(1)} %bitcast.73), custom_call_target="tpu_custom_call" | custom-call | tf_op jit(solution)/shard_map/pallas_call | solution.py:108
  36.7 1.6 collective-permute-start.1
  38.3 4.1 %copy.26 = bf16[1,128,8192]{1,2,0:T(8,128)(2,1)} copy(bf16[1,128,8192]{2,1,0:T(8,128)(2,1)} %param.9) | data formatting | bytes 4194304 | tf_op args[0]
  42.4 5.4 %collective-permute-done.1 = f32[128,512]{1,0:T(8,128)S(1)} collective-permute-done((f32[128,512]{1,0:T(8,128)S(1)}, f32[128,512]{1,0:T(8,128)S(1)}, u32[]{:S(2)}, u32[]{:S(2)}) %collective-permute-start.1) | collective-permute-done | bytes 262176 | tf_op jit(solution)/shard_map/ppermute | solution.py:140
  47.7 0.7 fusion.4
  48.4 40.9 %all-gather.5.cloned.1.call-done = bf16[4096,512]{1,0:T(8,128)(2,1)} async-done(((bf16[256,512]{1,0:T(8,128)(2,1)}), bf16[4096,512]{1,0:T(8,128)(2,1)}) %all-gather.5.cloned.1.call-update) | async-done | bytes 4194320 | tf_op jit(solution)/shard_map/all_gather | solution.py:158
  89.4 0.0 collective-permute-start.2
  89.4 3.2 %copy.27 = bf16[128,2,16,256]{0,3,1,2:T(8,128)(2,1)} copy(bf16[128,2,16,256]{0,3,2,1:T(8,128)(2,1)} %bitcast.80) | data formatting | bytes 4194304 | tf_op jit(solution)/shard_map/reshape | solution.py:180
  92.5 0.0 copy-start.4
  92.5 4.9 %all-to-all-start = ((bf16[128,2,16,256]{0,3,1,2:T(8,128)(2,1)}), bf16[128,2,16,256]{0,3,1,2:T(8,128)(2,1)}, u32[]{:S(2)}, u32[]{:S(2)}) async-start(bf16[128,2,16,256]{0,3,1,2:T(8,128)(2,1)} %copy.27), calls=%async_computation | async-start | bytes 4194304 | tf_op jit(solution)/shard_map/all_to_all | solution.py:179
  97.4 0.0 all-gather.3.cloned.1.call-start
  97.5 0.0 copy-done.4
  97.5 1.5 constant_dynamic-slice_fusion.2
  99.0 0.0 all-gather.3.cloned.1.call-update
  99.0 0.0 copy-start.5
  99.0 3.9 %convolution_convert_fusion.1 = bf16[128,4096]{1,0:T(8,128)(2,1)S(1)} fusion(bf16[128,512]{1,0:T(8,128)(2,1)} %fusion.4, bf16[4096,512]{1,0:T(8,128)(2,1)} %all-gather.5.cloned.1.call-done), kind=kOutput, calls=%fused_computation.3 | convolution fusion | flops 537395200 | bytes 5373952 | tf_op jit(solution)/shard_map/dot_general | solution.py:191
  102.9 0.0 copy-start.7
  102.9 0.2 copy.33
  103.1 0.0 copy-done.5
  103.2 0.9 copy-done.7
  104.1 0.8 fusion.9
  104.9 0.0 collective-permute-done.2
  104.9 0.4 copy-done.6
  105.3 3.0 %fusion = bf16[128,512]{1,0:T(8,128)(2,1)S(1)} fusion(f32[128,512]{1,0:T(8,128)S(1)} %fusion.9, bf16[128,4096]{0,1:T(8,128)(2,1)S(1)} %bitcast.84, bf16[4096,512]{1,0:T(8,128)(2,1)} %collective-permute-done.2), kind=kOutput, calls=%fused_computation.7 | convolution fusion | flops 537001984 | bytes 5636096 | tf_op jit(solution)/shard_map/dot_general | solution.py:188
  108.3 1.5 collective-permute-start.3
  109.9 0.0 copy-done.8
  109.9 3.7 %convolution_convert_fusion = bf16[128,4096]{1,0:T(8,128)(2,1)S(1)} fusion(bf16[128,512]{1,0:T(8,128)(2,1)S(1)} %copy-done.8, bf16[4096,512]{1,0:T(8,128)(2,1)} %collective-permute-done.2), kind=kOutput, calls=%fused_computation.2 | convolution fusion | flops 537395200 | bytes 5373952 | tf_op jit(solution)/shard_map/dot_general | solution.py:194
  113.6 0.2 copy.34
  113.8 0.3 maximum_select_fusion
  114.2 4.6 %copy.28 = bf16[128,16,2,256]{3,2,1,0:T(2,128)(2,1)} copy(bf16[128,16,2,256]{3,1,0,2:T(8,128)(2,1)S(1)} %maximum_select_fusion) | data formatting | bytes 4194304 | tf_op jit(solution)/shard_map/jit(_where)/select_n | solution.py:197
  118.8 4.6 %select_n.70 = bf16[128,8192]{1,0:T(8,128)(2,1)} reshape(bf16[128,16,2,256]{3,2,1,0:T(2,128)(2,1)} %copy.28) | data formatting | bytes 4194304 | tf_op jit(solution)/shard_map/jit(_where)/select_n | solution.py:197
  123.4 0.0 collective-permute-done.3
  123.4 0.6 gather_fusion.1
  124.0 0.1 broadcast_select_fusion
  124.1 0.0 copy-done.3
  124.1 23.6 %shard_map.103 = (bf16[128,4096]{1,0:T(8,128)(2,1)}, f32[256,512]{1,0:T(8,128)S(1)}) custom-call(s32[32]{0:T(128)S(1)} %shift-right-logical_xor_fusion.seeds_ref, s32[1]{0:T(128)} %bitcast.offset_ref, s32[128,1]{1,0:T(8,128)S(1)} %copy.25.pos_ref, bf16[128,4096]{1,0:T(8,128)(2,1)S(1)} %bitcast.70, bf16[128,4096]{1,0:T(8,128)(2,1)S(1)} %bitcast.72, ...), custom_call_target="tpu_custom_call" | custom-call | tf_op jit(solution)/shard_map/pallas_call | solution.py:108
  147.7 0.7 collective-permute-start.4
  148.4 7.5 %collective-permute-done.4 = f32[128,512]{1,0:T(8,128)S(1)} collective-permute-done((f32[128,512]{1,0:T(8,128)S(1)}, f32[128,512]{1,0:T(8,128)S(1)}, u32[]{:S(2)}, u32[]{:S(2)}) %collective-permute-start.4) | collective-permute-done | bytes 262176 | tf_op jit(solution)/shard_map/ppermute | solution.py:140
  155.9 0.7 fusion.3
  156.6 0.9 all-to-all-done
  157.5 0.3 collective-permute-start.5
  157.8 1.7 constant_dynamic-slice_fusion
  159.4 0.5 copy.31
  160.0 0.5 copy.32
  160.5 2.0 %fusion.10 = f32[512,512]{1,0:T(8,128)S(1)} fusion(bf16[1024,512]{1,0:T(8,128)(2,1)S(1)} %bitcast.92, bf16[1024,512]{1,0:T(8,128)(2,1)} %all-gather.3.cloned.1.call-done), kind=kOutput, calls=%fused_computation.41 | convolution fusion | flops 536870912 | bytes 3145728 | tf_op jit(solution)/shard_map/dot_general | solution.py:219
  162.5 0.0 collective-permute-done.5
  162.5 2.0 %convolution_add_fusion = f32[512,512]{1,0:T(8,128)S(1)} fusion(f32[512,512]{1,0:T(8,128)S(1)} %fusion.10, bf16[1024,512]{1,0:T(8,128)(2,1)S(1)} %bitcast.91, bf16[1024,512]{1,0:T(8,128)(2,1)} %collective-permute-done.5), kind=kOutput, calls=%fused_computation.5 | convolution fusion | flops 537133056 | bytes 4194304 | tf_op jit(solution)/shard_map/dot_general | solution.py:220
  164.5 1.5 collective-permute-start.6
  166.0 12.6 %collective-permute-done.6 = f32[256,512]{1,0:T(8,128)S(1)} collective-permute-done((f32[256,512]{1,0:T(8,128)S(1)}, f32[256,512]{1,0:T(8,128)S(1)}, u32[]{:S(2)}, u32[]{:S(2)}) %collective-permute-start.6) | collective-permute-done | bytes 524320 | tf_op jit(solution)/shard_map/ppermute | solution.py:227
  178.6 0.8 fusion.2
  (13 shorter events, 0.2 us)
Async XLA Ops:
  8.0 3.1 %copy-start = (s32[1,256]{1,0:T(1,128)S(1)}, s32[1,256]{1,0:T(1,128)}, u32[]{:S(2)}) copy-start(s32[1,256]{1,0:T(1,128)} %param.13) | copy-start | bytes 3076
  8.0 7.9 %copy-start.1 = (bf16[1,128,4096]{2,1,0:T(8,128)(2,1)S(1)}, bf16[1,128,4096]{2,1,0:T(8,128)(2,1)}, u32[]{:S(2)}) copy-start(bf16[1,128,4096]{2,1,0:T(8,128)(2,1)} %param.10) | copy-start | bytes 3145732
  8.0 81.3 %all-gather.5.cloned.1.call-start = ((), (), s32[]{:S(2)}) async-start(), calls=%async_computation.2 | async-start | bytes 4456448 | tf_op jit(solution)/shard_map/all_gather | solution.py:158
  8.8 5.5 %collective-permute-start = (bf16[128,512]{1,0:T(8,128)(2,1)}, bf16[128,512]{1,0:T(8,128)(2,1)S(1)}, u32[]{:S(2)}, u32[]{:S(2)}) collective-permute-start(bf16[128,512]{1,0:T(8,128)(2,1)} %bitcast.94), channel_id=1, source_target_pairs={{0,16},{16,0},{1,17},{17,1},{2,18},{18,2},{3,19},{19,3},{4,20},{20... | collective-permute-start | bytes 393224 | tf_op jit(solution)/shard_map/ppermute | solution.py:128
  15.9 1.2 copy-start.2
  36.7 11.0 %collective-permute-start.1 = (f32[128,512]{1,0:T(8,128)S(1)}, f32[128,512]{1,0:T(8,128)S(1)}, u32[]{:S(2)}, u32[]{:S(2)}) collective-permute-start(f32[128,512]{1,0:T(8,128)S(1)} %dynamic-slice_bitcast_fusion.2), channel_id=1, source_target_pairs={{0,16},{16,0},{1,17},{17,1},{2,18},{18,2},{3,19},{19,3},{4,20},{20... | collective-permute-start | bytes 786440 | tf_op jit(solution)/shard_map/ppermute | solution.py:140
  89.4 15.5 %collective-permute-start.2 = (bf16[4096,512]{1,0:T(8,128)(2,1)}, bf16[4096,512]{1,0:T(8,128)(2,1)}, u32[]{:S(2)}, u32[]{:S(2)}) collective-permute-start(bf16[4096,512]{1,0:T(8,128)(2,1)} %all-gather.5.cloned.1.call-done), channel_id=1, source_target_pairs={{0,1},{1,0},{2,3},{3,2},{4,5},{5,4},{6,7},{7,6},{8,9},{9,8},{10,11... | collective-permute-start | bytes 12582920 | tf_op jit(solution)/shard_map/ppermute | solution.py:178
  92.5 5.0 %copy-start.4 = (bf16[1,128,8192]{1,2,0:T(8,128)(2,1)S(1)}, bf16[1,128,8192]{1,2,0:T(8,128)(2,1)}, u32[]{:S(2)}) copy-start(bf16[1,128,8192]{1,2,0:T(8,128)(2,1)} %copy.26) | copy-start | bytes 6291460
  92.5 64.9 %all-to-all-start = ((bf16[128,2,16,256]{0,3,1,2:T(8,128)(2,1)}), bf16[128,2,16,256]{0,3,1,2:T(8,128)(2,1)}, u32[]{:S(2)}, u32[]{:S(2)}) async-start(bf16[128,2,16,256]{0,3,1,2:T(8,128)(2,1)} %copy.27), calls=%async_computation | async-start | bytes 4194304 | tf_op jit(solution)/shard_map/all_to_all | solution.py:179
  97.4 59.1 %all-gather.3.cloned.1.call-start = ((), (), s32[]{:S(2)}) async-start(), calls=%async_computation.1 | async-start | bytes 1179648 | tf_op jit(solution)/shard_map/all_gather | solution.py:174
  99.0 4.2 %copy-start.5 = (bf16[4096,512]{1,0:T(8,128)(2,1)S(1)}, bf16[4096,512]{1,0:T(8,128)(2,1)}, u32[]{:S(2)}) copy-start(bf16[4096,512]{1,0:T(8,128)(2,1)} %all-gather.5.cloned.1.call-done) | copy-start | bytes 12582916
  102.9 1.2 copy-start.7
  104.1 1.2 copy-start.6
  105.3 4.6 %copy-start.8 = (bf16[128,512]{1,0:T(8,128)(2,1)S(1)}, bf16[128,512]{1,0:T(8,128)(2,1)}, u32[]{:S(2)}) copy-start(bf16[128,512]{1,0:T(8,128)(2,1)} %fusion.4) | copy-start | bytes 393220
  108.3 15.0 %collective-permute-start.3 = (bf16[128,512]{1,0:T(8,128)(2,1)S(1)}, bf16[128,512]{1,0:T(8,128)(2,1)S(1)}, u32[]{:S(2)}, u32[]{:S(2)}) collective-permute-start(bf16[128,512]{1,0:T(8,128)(2,1)S(1)} %fusion), channel_id=1, source_target_pairs={{0,16},{16,0},{1,17},{17,1},{2,18},{18,2},{3,19},{19,3},{4,20},{20... | collective-permute-start | bytes 393224 | tf_op jit(solution)/shard_map/ppermute | solution.py:128
  118.8 5.3 %copy-start.3 = (bf16[1,128,4096]{2,1,0:T(8,128)(2,1)S(1)}, bf16[1,128,4096]{2,1,0:T(8,128)(2,1)}, u32[]{:S(2)}) copy-start(bf16[1,128,4096]{2,1,0:T(8,128)(2,1)} %param.12) | copy-start | bytes 3145732
  147.7 8.2 %collective-permute-start.4 = (f32[128,512]{1,0:T(8,128)S(1)}, f32[128,512]{1,0:T(8,128)S(1)}, u32[]{:S(2)}, u32[]{:S(2)}) collective-permute-start(f32[128,512]{1,0:T(8,128)S(1)} %dynamic-slice_bitcast_fusion.1), channel_id=1, source_target_pairs={{0,16},{16,0},{1,17},{17,1},{2,18},{18,2},{3,19},{19,3},{4,20},{20... | collective-permute-start | bytes 786440 | tf_op jit(solution)/shard_map/ppermute | solution.py:140
  157.5 5.0 %collective-permute-start.5 = (bf16[1024,512]{1,0:T(8,128)(2,1)}, bf16[1024,512]{1,0:T(8,128)(2,1)}, u32[]{:S(2)}, u32[]{:S(2)}) collective-permute-start(bf16[1024,512]{1,0:T(8,128)(2,1)} %all-gather.3.cloned.1.call-done), channel_id=1, source_target_pairs={{0,1},{1,0},{2,3},{3,2},{4,5},{5,4},{6,7},{7,6},{8,9},{9,8},{10,11... | collective-permute-start | bytes 3145736 | tf_op jit(solution)/shard_map/ppermute | solution.py:210
  164.5 14.1 %collective-permute-start.6 = (f32[256,512]{1,0:T(8,128)S(1)}, f32[256,512]{1,0:T(8,128)S(1)}, u32[]{:S(2)}, u32[]{:S(2)}) collective-permute-start(f32[256,512]{1,0:T(8,128)S(1)} %dynamic-slice_bitcast_fusion), channel_id=1, source_target_pairs={{0,16},{16,0},{1,17},{17,1},{2,18},{18,2},{3,19},{19,3},{4,20},{20... | collective-permute-start | bytes 1572872 | tf_op jit(solution)/shard_map/ppermute | solution.py:227
Sparse Core Ops, SparseCore 0:
  11.7 77.6 all-gather.4
Sparse Core Ops, SparseCore 1:
  100.6 55.7 all-gather.2

commit v11 on v10

--- a/solution.py
+++ b/solution.py
@@ -171,18 +171,21 @@
     key_full = gather_seq(key_states[0], seq_index, seq_devices)
     (dv,) = attention(seeds, offset, pos, query_loc, grad_loc, key_full, None)
     value_grad = reduce_seq(dv, seq_index, seq_devices).astype(jnp.bfloat16)
-    grads_own = lax.all_gather(value_grad, "zx", axis=0, tiled=True)
+    grads_pair = gather_seq(value_grad, seq_index, seq_devices)
+    grads_own = lax.all_gather(grads_pair, "zx", axis=0, tiled=True).reshape(
+        zx_devices, seq_devices, tok_rows, KVH * HD
+    )
     value_grad, weight_own, input_late = lax.optimization_barrier(
         (value_grad, weight_own, local_input)
     )
     weight_other = lax.ppermute(weight_own, "core", swap)
     input_cols = lax.all_to_all(
-        input_late.reshape(tok_rows, seq_devices, fsdp_devices, block_rows),
-        FSDP,
-        split_axis=2,
+        input_late.reshape(tok_rows, seq_devices * fsdp_devices, block_rows),
+        ("seq",) + FSDP,
+        split_axis=1,
         concat_axis=0,
         tiled=True,
-    ).reshape(zx_devices, 2, tok_rows, seq_devices * block_rows)
+    ).reshape(seq_devices, zx_devices, 2, tok_rows, block_rows)
     values_loc = (
         jnp.dot(input_own, weight_own, preferred_element_type=jnp.float32)
         + jnp.dot(input_other, weight_other, preferred_element_type=jnp.float32)
@@ -208,25 +211,12 @@
     )
     query_grad = dq
     grads_other = lax.ppermute(grads_own, "core", swap)
-    cols_own = lax.dynamic_index_in_dim(input_cols, core_index, 1, keepdims=False).reshape(
-        zx_devices * tok_rows, -1
-    )
-    cols_other = lax.dynamic_index_in_dim(input_cols, 1 - core_index, 1, keepdims=False).reshape(
-        zx_devices * tok_rows, -1
-    )
-    first_dims = (((0,), (0,)), ((), ()))
-    partial = (
-        lax.dot_general(cols_own, grads_own, first_dims, preferred_element_type=jnp.float32)
-        + lax.dot_general(cols_other, grads_other, first_dims, preferred_element_type=jnp.float32)
-    ).reshape(seq_devices, block_rows, KVH * HD)
-    summed = lax.dynamic_index_in_dim(partial, seq_index, 0, keepdims=False)
-    for shift in range(1, seq_devices):
-        piece = lax.dynamic_index_in_dim(
-            partial, (seq_index + shift) % seq_devices, 0, keepdims=False
-        )
-        summed = summed + lax.ppermute(
-            piece, "seq", [(i, (i + shift) % seq_devices) for i in range(seq_devices)]
-        )
+    cols_own = lax.dynamic_index_in_dim(input_cols, core_index, 2, keepdims=False)
+    cols_other = lax.dynamic_index_in_dim(input_cols, 1 - core_index, 2, keepdims=False)
+    token_dims = (((0, 1, 2), (1, 0, 2)), ((), ()))
+    summed = lax.dot_general(
+        cols_own, grads_own, token_dims, preferred_element_type=jnp.float32
+    ) + lax.dot_general(cols_other, grads_other, token_dims, preferred_element_type=jnp.float32)
     weight_grad = (summed * (1.0 / math.sqrt(fsdp_devices * seq_len))).astype(jnp.bfloat16)
 
     return (query_grad[None], key_grad[None], input_grad[None], weight_grad)

time: 189 us -> 190 us (level)
  waiting for transfers between devices: 71 us -> 72.9 us
    ppermute x1 -> x0, waiting for transfers between devices: 12.6 us -> none  [per_device(): lax.ppermute(piece, 'seq', [(i, (i + shift) % seq_devices) for i in range...]
    all_gather x1, waiting for transfers between devices: 0.01 us -> 8.47 us  [per_device(): lax.all_gather(grads_pair, 'zx', axis=0, tiled=True)]
    ppermute x2 -> x3, waiting for transfers between devices: 3.05 us -> 10.9 us  [gather_seq(): lax.ppermute(piece, 'seq', [(i, (i + shift) % seq_devices) for i in range...]
    all_to_all x0 -> x1, local copies, waits for them, and re-layouts: none -> 4.08 us  [per_device(): lax.all_to_all(input_late.reshape(tok_rows, seq_devices * fsdp_devices, b...]
    ppermute x2, waiting for transfers between devices: 12.8 us -> 9.02 us  [reduce_seq(): lax.ppermute(piece, 'seq', [(i, (i + shift) % seq_devices) for i in range...]
    reshape x1 -> x0, local copies, waits for them, and re-layouts: 3.16 us -> none  [per_device(): input_late.reshape(tok_rows, seq_devices, fsdp_devices, block_rows)]
    dynamic_slice x3 -> x0, local copies, waits for them, and re-layouts: 2.75 us -> none  [the longest x2 2.21 us: per_device(): lax.dynamic_index_in_dim(input_cols, 1 - core_index, 1, keepdims=False)]
    ppermute x1, waiting for transfers between devices: 0.01 us -> 2.58 us  [per_device(): grads_other = lax.ppermute(grads_own, 'core', swap)]
  transfers between devices with their start and end apart: 10 -> 10, of which waited for: 6 -> 7; matrix products, arithmetic and copies ran while one was open for 21% -> 21% of each run, Pallas kernels for 23% -> 23%
where the time goes in v11:
time: 190 us; the launch traced here: 187 us
  waiting for transfers between devices  72.9 us (38%)
  Pallas kernels  43.1 us (23%)
  local copies, waits for them, and re-layouts  25.4 us (13%)
  matrix products  15.5 us (8%)
  between operations  15 us (8%)
  starting transfers between devices  10.7 us (6%)
  other arithmetic  4.63 us (2%)
    pallas_call x2, Pallas kernels, attention(): pl.pallas_call(kernel, grid_spec=pltpu.PrefetchScalarGridSpec(num_scalar_...  43.1 us
    all_gather x1, waiting for transfers between devices, per_device(): weight_own = lax.all_gather(value_weight, ('seq', 'zx'), axis=0, tiled=True)  41.2 us
    ppermute x3, waiting for transfers between devices, gather_seq(): lax.ppermute(piece, 'seq', [(i, (i + shift) % seq_devices) for i in range...  10.9 us
    select_n x2, local copies, waits for them, and re-layouts, per_device(): jnp.where(core_index == 0, jnp.concatenate([grad_own, grad_other], axis=2...  9.17 us
    ppermute x2, waiting for transfers between devices, reduce_seq(): lax.ppermute(piece, 'seq', [(i, (i + shift) % seq_devices) for i in range...  9.02 us
    all_gather x1, waiting for transfers between devices, per_device(): lax.all_gather(grads_pair, 'zx', axis=0, tiled=True)  8.47 us
    unnamed x15, local copies, waits for them, and re-layouts  6.65 us
    all_to_all x1, starting transfers between devices, per_device(): lax.all_to_all(input_late.reshape(tok_rows, seq_devices * fsdp_devices, b...  4.53 us
  transfers between devices with their start and end apart: 10, of which 7 were waited for; matrix products, arithmetic and copies ran while one was open for 21% of the time, Pallas kernels for 23%

profile of v11, /device:TPU:10, one launch (start us, length us, event | category | flops | bytes accessed | tf_op | source)
XLA Modules:
  0.0 187.2 jit_solution(5973986428243239735)
XLA Ops:
  7.2 0.0 copy-start
  7.2 0.0 copy-start.1
  7.2 0.0 all-gather.5.cloned.1.call-start
  7.2 0.7 all-gather.5.cloned.1.call-update
  7.9 1.6 collective-permute-start
  10.2 0.0 copy-done
  10.3 0.1 copy.21.pos_ref
  10.4 3.0 %collective-permute-done = bf16[128,512]{1,0:T(8,128)(2,1)S(1)} collective-permute-done((bf16[128,512]{1,0:T(8,128)(2,1)}, bf16[128,512]{1,0:T(8,128)(2,1)S(1)}, u32[]{:S(2)}, u32[]{:S(2)}) %collective-permute-start) | collective-permute-done | bytes 131104 | tf_op jit(solution)/shard_map/ppermute | solution.py:128
  13.4 0.9 pad_maximum_fusion
  14.4 0.6 gather_fusion
  14.9 0.1 broadcast_select_fusion.1
  15.0 0.0 copy-done.1
  15.1 0.0 copy-start.2
  15.1 1.2 copy-done.2
  16.3 19.6 %shard_map.102 = f32[256,512]{1,0:T(8,128)S(1)} custom-call(s32[32]{0:T(128)S(1)} %shift-right-logical_xor_fusion.seeds_ref, s32[1]{0:T(128)} %bitcast.offset_ref, s32[128,1]{1,0:T(8,128)S(1)} %copy.21.pos_ref, bf16[128,4096]{1,0:T(8,128)(2,1)S(1)} %bitcast.80, bf16[128,4096]{1,0:T(8,128)(2,1)S(1)} %bitcast.82, bf16[256,512]{1,0:T(8,128)(2,1)S(1)} %bitcast.84), custom_call_target="tpu_custom_call" | custom-call | tf_op jit(solution)/shard_map/pallas_call | solution.py:108
  35.9 1.6 collective-permute-start.1
  37.5 4.1 %copy.22 = bf16[1,128,8192]{1,2,0:T(8,128)(2,1)} copy(bf16[1,128,8192]{2,1,0:T(8,128)(2,1)} %param.9) | data formatting | bytes 4194304 | tf_op args[0]
  41.6 5.3 %collective-permute-done.1 = f32[128,512]{1,0:T(8,128)S(1)} collective-permute-done((f32[128,512]{1,0:T(8,128)S(1)}, f32[128,512]{1,0:T(8,128)S(1)}, u32[]{:S(2)}, u32[]{:S(2)}) %collective-permute-start.1) | collective-permute-done | bytes 262176 | tf_op jit(solution)/shard_map/ppermute | solution.py:140
  46.9 0.7 fusion.9
  47.6 41.2 %all-gather.5.cloned.1.call-done = bf16[4096,512]{1,0:T(8,128)(2,1)} async-done(((bf16[256,512]{1,0:T(8,128)(2,1)}), bf16[4096,512]{1,0:T(8,128)(2,1)}) %all-gather.5.cloned.1.call-update) | async-done | bytes 4194320 | tf_op jit(solution)/shard_map/all_gather | solution.py:158
  88.7 0.0 collective-permute-start.3
  88.8 1.7 constant_dynamic-slice_fusion
  90.4 0.7 collective-permute-start.2
  91.1 4.5 %all-to-all-start = ((bf16[128,32,256]{0,2,1:T(8,128)(2,1)}), bf16[128,32,256]{0,2,1:T(8,128)(2,1)}, u32[]{:S(2)}, u32[]{:S(2)}) async-start(bf16[128,32,256]{0,2,1:T(8,128)(2,1)} %bitcast.15), calls=%async_computation | async-start | bytes 4194304 | tf_op jit(solution)/shard_map/all_to_all | solution.py:182
  95.6 0.0 all-gather.3.cloned.1.call-start
  95.7 2.9 %fusion.17 = f32[128,512]{1,0:T(8,128)S(1)} fusion(bf16[128,4096]{0,1:T(8,128)(2,1)S(1)} %bitcast.98, bf16[4096,512]{1,0:T(8,128)(2,1)} %all-gather.5.cloned.1.call-done), kind=kOutput, calls=%fused_computation.48 | convolution fusion | flops 536870912 | bytes 5505024 | tf_op jit(solution)/shard_map/dot_general | solution.py:190
  98.6 0.0 collective-permute-done.3
  98.6 2.9 %fusion.3 = bf16[128,512]{1,0:T(8,128)(2,1)S(1)} fusion(f32[128,512]{1,0:T(8,128)S(1)} %fusion.17, bf16[128,4096]{0,1:T(8,128)(2,1)S(1)} %bitcast.97, bf16[4096,512]{1,0:T(8,128)(2,1)} %collective-permute-done.3), kind=kOutput, calls=%fused_computation.12 | convolution fusion | flops 537001984 | bytes 5636096 | tf_op jit(solution)/shard_map/dot_general | solution.py:191
  101.6 1.6 collective-permute-start.4
  103.1 0.0 collective-permute-done.2
  103.1 1.0 pad_maximum_fusion.1
  104.1 0.6 gather_fusion.1
  104.7 7.9 %collective-permute-done.4 = bf16[128,512]{1,0:T(8,128)(2,1)S(1)} collective-permute-done((bf16[128,512]{1,0:T(8,128)(2,1)S(1)}, bf16[128,512]{1,0:T(8,128)(2,1)S(1)}, u32[]{:S(2)}, u32[]{:S(2)}) %collective-permute-start.4) | collective-permute-done | bytes 131104 | tf_op jit(solution)/shard_map/ppermute | solution.py:128
  112.6 0.6 gather_fusion.2
  113.2 0.8 broadcast_select_fusion
  114.0 0.0 all-gather.3.cloned.1.call-update
  114.0 3.7 %convolution_convert_fusion.1 = bf16[128,4096]{1,0:T(8,128)(2,1)S(1)} fusion(bf16[128,512]{1,0:T(8,128)(2,1)} %fusion.9, bf16[4096,512]{1,0:T(8,128)(2,1)} %all-gather.5.cloned.1.call-done), kind=kOutput, calls=%fused_computation.4 | convolution fusion | flops 537395200 | bytes 5373952 | tf_op jit(solution)/shard_map/dot_general | solution.py:194
  117.8 0.2 copy.33
  118.0 3.8 %convolution_convert_fusion = bf16[128,4096]{1,0:T(8,128)(2,1)S(1)} fusion(bf16[128,512]{1,0:T(8,128)(2,1)} %fusion.9, bf16[4096,512]{1,0:T(8,128)(2,1)} %collective-permute-done.3), kind=kOutput, calls=%fused_computation.3 | convolution fusion | flops 537395200 | bytes 5373952 | tf_op jit(solution)/shard_map/dot_general | solution.py:197
  121.8 0.2 copy.34
  122.0 0.3 maximum_select_fusion
  122.4 4.6 %copy.24 = bf16[128,16,2,256]{3,2,1,0:T(2,128)(2,1)} copy(bf16[128,16,2,256]{3,1,0,2:T(8,128)(2,1)S(1)} %maximum_select_fusion) | data formatting | bytes 4194304 | tf_op jit(solution)/shard_map/jit(_where)/select_n | solution.py:200
  127.0 0.0 copy-start.3
  127.0 4.6 %select_n.67 = bf16[128,8192]{1,0:T(8,128)(2,1)} reshape(bf16[128,16,2,256]{3,2,1,0:T(2,128)(2,1)} %copy.24) | data formatting | bytes 4194304 | tf_op jit(solution)/shard_map/jit(_where)/select_n | solution.py:200
  131.6 0.0 copy-done.3
  131.6 23.6 %shard_map.103 = (bf16[128,4096]{1,0:T(8,128)(2,1)}, f32[256,512]{1,0:T(8,128)S(1)}) custom-call(s32[32]{0:T(128)S(1)} %shift-right-logical_xor_fusion.seeds_ref, s32[1]{0:T(128)} %bitcast.offset_ref, s32[128,1]{1,0:T(8,128)S(1)} %copy.21.pos_ref, bf16[128,4096]{1,0:T(8,128)(2,1)S(1)} %bitcast.81, bf16[128,4096]{1,0:T(8,128)(2,1)S(1)} %bitcast.83, ...), custom_call_target="tpu_custom_call" | custom-call | tf_op jit(solution)/shard_map/pallas_call | solution.py:108
  155.2 0.6 collective-permute-start.5
  155.8 0.0 all-to-all-done
  155.8 4.1 %copy.23 = bf16[32,128,1,256]{3,1,0,2:T(8,128)(2,1)} copy(bf16[32,128,1,256]{1,3,0,2:T(8,128)(2,1)} %bitcast.17) | data formatting | bytes 4194304 | tf_op jit(solution)/shard_map/all_to_all | solution.py:182
  159.9 3.7 %collective-permute-done.5 = f32[128,512]{1,0:T(8,128)S(1)} collective-permute-done((f32[128,512]{1,0:T(8,128)S(1)}, f32[128,512]{1,0:T(8,128)S(1)}, u32[]{:S(2)}, u32[]{:S(2)}) %collective-permute-start.5) | collective-permute-done | bytes 262176 | tf_op jit(solution)/shard_map/ppermute | solution.py:140
  163.5 0.7 fusion.8
  164.2 8.5 %all-gather.3.cloned.1.call-done = bf16[2048,512]{1,0:T(8,128)(2,1)} async-done(((bf16[256,512]{1,0:T(8,128)(2,1)}), bf16[2048,512]{1,0:T(8,128)(2,1)}) %all-gather.3.cloned.1.call-update) | async-done | bytes 2097168 | tf_op jit(solution)/shard_map/all_gather | solution.py:175
  172.7 0.0 copy-start.4
  172.7 0.0 copy-start.5
  172.7 1.9 %copy.28 = bf16[8,2,128,512]{3,2,0,1:T(8,128)(2,1)S(1)} copy(bf16[8,2,128,512]{3,2,1,0:T(8,128)(2,1)} %bitcast.91) | data formatting | bytes 4194304 | tf_op jit(solution)/shard_map/optimization_barrier | solution.py:209
  174.7 0.1 collective-permute-start.6
  174.7 0.2 copy-done.4
  174.9 0.6 copy-done.5
  175.6 0.7 convolution_bitcast_fusion.1
  176.3 2.6 %collective-permute-done.6 = bf16[8,2,128,512]{3,2,0,1:T(8,128)(2,1)S(1)} collective-permute-done((bf16[8,2,128,512]{3,2,0,1:T(8,128)(2,1)S(1)}, bf16[8,2,128,512]{3,2,0,1:T(8,128)(2,1)S(1)}, u32[]{:S(2)}, u32[]{:S(2)}) %collective-permute-start.6) | collective-permute-done | bytes 2097184 | tf_op jit(solution)/shard_map/ppermute | solution.py:213
  178.9 1.4 fusion.2
  (8 shorter events, 0.1 us)
Async XLA Ops:
  7.2 3.1 %copy-start = (s32[1,256]{1,0:T(1,128)S(1)}, s32[1,256]{1,0:T(1,128)}, u32[]{:S(2)}) copy-start(s32[1,256]{1,0:T(1,128)} %param.13) | copy-start | bytes 3076
  7.2 7.9 %copy-start.1 = (bf16[1,128,4096]{2,1,0:T(8,128)(2,1)S(1)}, bf16[1,128,4096]{2,1,0:T(8,128)(2,1)}, u32[]{:S(2)}) copy-start(bf16[1,128,4096]{2,1,0:T(8,128)(2,1)} %param.10) | copy-start | bytes 3145732
  7.2 81.6 %all-gather.5.cloned.1.call-start = ((), (), s32[]{:S(2)}) async-start(), calls=%async_computation.2 | async-start | bytes 4456448 | tf_op jit(solution)/shard_map/all_gather | solution.py:158
  7.9 5.5 %collective-permute-start = (bf16[128,512]{1,0:T(8,128)(2,1)}, bf16[128,512]{1,0:T(8,128)(2,1)S(1)}, u32[]{:S(2)}, u32[]{:S(2)}) collective-permute-start(bf16[128,512]{1,0:T(8,128)(2,1)} %bitcast.104), channel_id=1, source_target_pairs={{0,16},{16,0},{1,17},{17,1},{2,18},{18,2},{3,19},{19,3},{4,20},{20... | collective-permute-start | bytes 393224 | tf_op jit(solution)/shard_map/ppermute | solution.py:128
  15.1 1.2 copy-start.2
  35.9 11.0 %collective-permute-start.1 = (f32[128,512]{1,0:T(8,128)S(1)}, f32[128,512]{1,0:T(8,128)S(1)}, u32[]{:S(2)}, u32[]{:S(2)}) collective-permute-start(f32[128,512]{1,0:T(8,128)S(1)} %dynamic-slice_bitcast_fusion.1), channel_id=1, source_target_pairs={{0,16},{16,0},{1,17},{17,1},{2,18},{18,2},{3,19},{19,3},{4,20},{20... | collective-permute-start | bytes 786440 | tf_op jit(solution)/shard_map/ppermute | solution.py:140
  88.7 9.9 %collective-permute-start.3 = (bf16[4096,512]{1,0:T(8,128)(2,1)}, bf16[4096,512]{1,0:T(8,128)(2,1)}, u32[]{:S(2)}, u32[]{:S(2)}) collective-permute-start(bf16[4096,512]{1,0:T(8,128)(2,1)} %all-gather.5.cloned.1.call-done), channel_id=1, source_target_pairs={{0,1},{1,0},{2,3},{3,2},{4,5},{5,4},{6,7},{7,6},{8,9},{9,8},{10,11... | collective-permute-start | bytes 12582920 | tf_op jit(solution)/shard_map/ppermute | solution.py:181
  90.4 12.7 %collective-permute-start.2 = (bf16[128,512]{1,0:T(8,128)(2,1)}, bf16[128,512]{1,0:T(8,128)(2,1)}, u32[]{:S(2)}, u32[]{:S(2)}) collective-permute-start(bf16[128,512]{1,0:T(8,128)(2,1)} %fusion.9), channel_id=1, source_target_pairs={{0,16},{16,0},{1,17},{17,1},{2,18},{18,2},{3,19},{19,3},{4,20},{20... | collective-permute-start | bytes 393224 | tf_op jit(solution)/shard_map/ppermute | solution.py:128
  91.1 64.7 %all-to-all-start = ((bf16[128,32,256]{0,2,1:T(8,128)(2,1)}), bf16[128,32,256]{0,2,1:T(8,128)(2,1)}, u32[]{:S(2)}, u32[]{:S(2)}) async-start(bf16[128,32,256]{0,2,1:T(8,128)(2,1)} %bitcast.15), calls=%async_computation | async-start | bytes 4194304 | tf_op jit(solution)/shard_map/all_to_all | solution.py:182
  95.6 77.1 %all-gather.3.cloned.1.call-start = ((), (), s32[]{:S(2)}) async-start(), calls=%async_computation.1 | async-start | bytes 2359296 | tf_op jit(solution)/shard_map/all_gather | solution.py:175
  101.6 11.0 %collective-permute-start.4 = (bf16[128,512]{1,0:T(8,128)(2,1)S(1)}, bf16[128,512]{1,0:T(8,128)(2,1)S(1)}, u32[]{:S(2)}, u32[]{:S(2)}) collective-permute-start(bf16[128,512]{1,0:T(8,128)(2,1)S(1)} %fusion.3), channel_id=1, source_target_pairs={{0,16},{16,0},{1,17},{17,1},{2,18},{18,2},{3,19},{19,3},{4,20},{20... | collective-permute-start | bytes 393224 | tf_op jit(solution)/shard_map/ppermute | solution.py:128
  127.0 4.6 %copy-start.3 = (bf16[1,128,4096]{2,1,0:T(8,128)(2,1)S(1)}, bf16[1,128,4096]{2,1,0:T(8,128)(2,1)}, u32[]{:S(2)}) copy-start(bf16[1,128,4096]{2,1,0:T(8,128)(2,1)} %param.12) | copy-start | bytes 3145732
  155.2 8.4 %collective-permute-start.5 = (f32[128,512]{1,0:T(8,128)S(1)}, f32[128,512]{1,0:T(8,128)S(1)}, u32[]{:S(2)}, u32[]{:S(2)}) collective-permute-start(f32[128,512]{1,0:T(8,128)S(1)} %dynamic-slice_bitcast_fusion), channel_id=1, source_target_pairs={{0,16},{16,0},{1,17},{17,1},{2,18},{18,2},{3,19},{19,3},{4,20},{20... | collective-permute-start | bytes 786440 | tf_op jit(solution)/shard_map/ppermute | solution.py:140
  172.7 2.2 %copy-start.4 = (bf16[2048,512]{1,0:T(8,128)(2,1)S(1)}, bf16[2048,512]{1,0:T(8,128)(2,1)}, u32[]{:S(2)}) copy-start(bf16[2048,512]{1,0:T(8,128)(2,1)} %all-gather.3.cloned.1.call-done) | copy-start | bytes 6291460
  172.7 2.9 %copy-start.5 = (bf16[32,128,1,256]{3,1,0,2:T(8,128)(2,1)S(1)}, bf16[32,128,1,256]{3,1,0,2:T(8,128)(2,1)}, u32[]{:S(2)}) copy-start(bf16[32,128,1,256]{3,1,0,2:T(8,128)(2,1)} %copy.23) | copy-start | bytes 6291460
  174.7 4.2 %collective-permute-start.6 = (bf16[8,2,128,512]{3,2,0,1:T(8,128)(2,1)S(1)}, bf16[8,2,128,512]{3,2,0,1:T(8,128)(2,1)S(1)}, u32[]{:S(2)}, u32[]{:S(2)}) collective-permute-start(bf16[8,2,128,512]{3,2,0,1:T(8,128)(2,1)S(1)} %copy.28), channel_id=1, source_target_pairs={{0,1},{1,0},{2,3},{3,2},{4,5},{5,4},{6,7},{7,6},{8,9},{9,8},{10,11... | collective-permute-start | bytes 6291464 | tf_op jit(solution)/shard_map/ppermute | solution.py:213
Sparse Core Ops, SparseCore 0:
  10.8 77.8 all-gather.4
  114.1 58.5 all-gather.2

commit v12 on v11

--- a/solution.py
+++ b/solution.py
@@ -172,20 +172,24 @@
     (dv,) = attention(seeds, offset, pos, query_loc, grad_loc, key_full, None)
     value_grad = reduce_seq(dv, seq_index, seq_devices).astype(jnp.bfloat16)
     grads_pair = gather_seq(value_grad, seq_index, seq_devices)
-    grads_own = lax.all_gather(grads_pair, "zx", axis=0, tiled=True).reshape(
-        zx_devices, seq_devices, tok_rows, KVH * HD
-    )
-    value_grad, weight_own, input_late = lax.optimization_barrier(
-        (value_grad, weight_own, local_input)
-    )
-    weight_other = lax.ppermute(weight_own, "core", swap)
+    grads_own = lax.all_to_all(
+        jnp.broadcast_to(grads_pair[None], (zx_devices,) + grads_pair.shape),
+        "zx",
+        split_axis=0,
+        concat_axis=0,
+        tiled=True,
+    ).reshape(zx_devices, seq_devices, tok_rows, KVH * HD)
     input_cols = lax.all_to_all(
-        input_late.reshape(tok_rows, seq_devices * fsdp_devices, block_rows),
+        local_input.reshape(tok_rows, seq_devices * fsdp_devices, block_rows),
         ("seq",) + FSDP,
         split_axis=1,
         concat_axis=0,
         tiled=True,
     ).reshape(seq_devices, zx_devices, 2, tok_rows, block_rows)
+    value_grad, weight_own, input_cols = lax.optimization_barrier(
+        (value_grad, weight_own, input_cols)
+    )
+    weight_other = lax.ppermute(weight_own, "core", swap)
     values_loc = (
         jnp.dot(input_own, weight_own, preferred_element_type=jnp.float32)
         + jnp.dot(input_other, weight_other, preferred_element_type=jnp.float32)

time: 190 us -> 199 us (1.047)
  waiting for transfers between devices: 72.9 us -> 79.6 us
  starting transfers between devices: 10.7 us -> 16.2 us
  other arithmetic: 4.63 us -> 2.37 us
    all_gather x1, waiting for transfers between devices: 41.2 us -> 24.4 us  [per_device(): weight_own = lax.all_gather(value_weight, ('seq', 'zx'), axis=0, tiled=True)]
    all_to_all x1 -> x2, waiting for transfers between devices: 0.01 us -> 15.8 us  [the longest x1 15.7 us: per_device(): lax.all_to_all(local_input.reshape(tok_rows, seq_devices * fsdp_devices,...]
    all_gather x1 -> x0, waiting for transfers between devices: 8.47 us -> none  [per_device(): lax.all_gather(grads_pair, 'zx', axis=0, tiled=True)]
    ppermute x2, waiting for transfers between devices: 9.02 us -> 16 us  [reduce_seq(): lax.ppermute(piece, 'seq', [(i, (i + shift) % seq_devices) for i in range...]
    all_to_all x1 -> x2, starting transfers between devices: 4.53 us -> 10.9 us  [the longest x1 6.07 us: per_device(): lax.all_to_all(local_input.reshape(tok_rows, seq_devices * fsdp_devices,...]
    ppermute x3, waiting for transfers between devices: 10.9 us -> 17.2 us  [gather_seq(): lax.ppermute(piece, 'seq', [(i, (i + shift) % seq_devices) for i in range...]
    ppermute x1, waiting for transfers between devices: 0.01 us -> 3.93 us  [per_device(): weight_other = lax.ppermute(weight_own, 'core', swap)]
    dot_general x1, matrix products: 2.93 us -> 0.74 us  [per_device(): jnp.dot(input_own, weight_own, preferred_element_type=jnp.float32)]
  transfers between devices with their start and end apart: 10 -> 10, of which waited for: 7 -> 8; matrix products, arithmetic and copies ran while one was open for 21% -> 18% of each run, Pallas kernels for 23% -> 22%
where the time goes in v12:
time: 199 us; the launch traced here: 197 us
  waiting for transfers between devices  79.6 us (40%)
  Pallas kernels  43.1 us (22%)
  local copies, waits for them, and re-layouts  26.2 us (13%)
  starting transfers between devices  16.2 us (8%)
  between operations  14.9 us (7%)
  matrix products  14.8 us (7%)
  other arithmetic  2.37 us (1%)
    pallas_call x2, Pallas kernels, attention(): pl.pallas_call(kernel, grid_spec=pltpu.PrefetchScalarGridSpec(num_scalar_...  43.1 us
    all_gather x1, waiting for transfers between devices, per_device(): weight_own = lax.all_gather(value_weight, ('seq', 'zx'), axis=0, tiled=True)  24.4 us
    ppermute x3, waiting for transfers between devices, gather_seq(): lax.ppermute(piece, 'seq', [(i, (i + shift) % seq_devices) for i in range...  17.2 us
    ppermute x2, waiting for transfers between devices, reduce_seq(): lax.ppermute(piece, 'seq', [(i, (i + shift) % seq_devices) for i in range...  16 us
    all_to_all x1, waiting for transfers between devices, per_device(): lax.all_to_all(local_input.reshape(tok_rows, seq_devices * fsdp_devices,...  15.7 us
    select_n x2, local copies, waits for them, and re-layouts, per_device(): jnp.where(core_index == 0, jnp.concatenate([grad_own, grad_other], axis=2...  9.09 us
    all_to_all x1, starting transfers between devices, per_device(): lax.all_to_all(local_input.reshape(tok_rows, seq_devices * fsdp_devices,...  6.07 us
    unnamed x15, local copies, waits for them, and re-layouts  5.11 us
  transfers between devices with their start and end apart: 10, of which 8 were waited for; matrix products, arithmetic and copies ran while one was open for 18% of the time, Pallas kernels for 22%

profile of v12, /device:TPU:10, one launch (start us, length us, event | category | flops | bytes accessed | tf_op | source)
XLA Modules:
  0.0 197.2 jit_solution(1436666387734366328)
XLA Ops:
  7.2 0.0 copy-start
  7.2 0.0 all-gather.2.cloned.1.call-start
  7.2 0.7 all-gather.2.cloned.1.call-update
  7.9 4.1 %copy.22 = bf16[1,128,8192]{1,2,0:T(8,128)(2,1)} copy(bf16[1,128,8192]{2,1,0:T(8,128)(2,1)} %param.9) | data formatting | bytes 4194304 | tf_op args[0]
  12.0 0.0 copy-start.5
  12.0 0.0 copy-start.1
  12.0 0.0 copy-start.2
  12.0 6.1 %all-to-all-start.1 = ((bf16[128,32,256]{0,2,1:T(8,128)(2,1)}), bf16[128,32,256]{0,2,1:T(8,128)(2,1)}, u32[]{:S(2)}, u32[]{:S(2)}) async-start(bf16[128,32,256]{0,2,1:T(8,128)(2,1)} %bitcast.90), calls=%async_computation.1 | async-start | bytes 4194304 | tf_op jit(solution)/shard_map/all_to_all | solution.py:182
  18.1 0.0 copy-done.5
  18.1 1.5 collective-permute-start
  20.3 0.0 copy-done
  20.4 0.1 copy.21.pos_ref
  20.5 12.9 %collective-permute-done = bf16[128,512]{1,0:T(8,128)(2,1)S(1)} collective-permute-done((bf16[128,512]{1,0:T(8,128)(2,1)S(1)}, bf16[128,512]{1,0:T(8,128)(2,1)S(1)}, u32[]{:S(2)}, u32[]{:S(2)}) %collective-permute-start) | collective-permute-done | bytes 131104 | tf_op jit(solution)/shard_map/ppermute | solution.py:128
  33.4 0.6 gather_fusion
  34.0 0.1 broadcast_select_fusion.1
  34.1 0.0 copy-done.1
  34.1 0.0 copy-done.2
  34.1 19.6 %shard_map.102 = f32[256,512]{1,0:T(8,128)S(1)} custom-call(s32[32]{0:T(128)S(1)} %shift-right-logical_xor_fusion.seeds_ref, s32[1]{0:T(128)} %bitcast.offset_ref, s32[128,1]{1,0:T(8,128)S(1)} %copy.21.pos_ref, bf16[128,4096]{1,0:T(8,128)(2,1)S(1)} %bitcast.79, bf16[128,4096]{1,0:T(8,128)(2,1)S(1)} %bitcast.81, bf16[256,512]{1,0:T(8,128)(2,1)S(1)} %bitcast.83), custom_call_target="tpu_custom_call" | custom-call | tf_op jit(solution)/shard_map/pallas_call | solution.py:108
  53.7 0.8 collective-permute-start.1
  54.5 10.2 %collective-permute-done.1 = f32[128,512]{1,0:T(8,128)S(1)} collective-permute-done((f32[128,512]{1,0:T(8,128)S(1)}, f32[128,512]{1,0:T(8,128)S(1)}, u32[]{:S(2)}, u32[]{:S(2)}) %collective-permute-start.1) | collective-permute-done | bytes 262176 | tf_op jit(solution)/shard_map/ppermute | solution.py:140
  64.8 15.7 %all-to-all-done.1 = bf16[128,32,256]{0,2,1:T(8,128)(2,1)} async-done(((bf16[128,32,256]{0,2,1:T(8,128)(2,1)}), bf16[128,32,256]{0,2,1:T(8,128)(2,1)}, u32[]{:S(2)}, u32[]{:S(2)}) %all-to-all-start.1) | async-done | bytes 2097184 | tf_op jit(solution)/shard_map/all_to_all | solution.py:182
  80.5 4.2 %copy.23 = bf16[32,128,1,256]{3,1,0,2:T(8,128)(2,1)} copy(bf16[32,128,1,256]{1,3,0,2:T(8,128)(2,1)} %bitcast.16) | data formatting | bytes 4194304 | tf_op jit(solution)/shard_map/all_to_all | solution.py:182
  84.7 24.4 %all-gather.2.cloned.1.call-done = bf16[4096,512]{1,0:T(8,128)(2,1)} async-done(((bf16[256,512]{1,0:T(8,128)(2,1)}), bf16[4096,512]{1,0:T(8,128)(2,1)}) %all-gather.2.cloned.1.call-update) | async-done | bytes 4194320 | tf_op jit(solution)/shard_map/all_gather | solution.py:158
  109.1 0.0 collective-permute-start.3
  109.1 0.0 copy-start.3
  109.1 1.8 constant_dynamic-slice_fusion
  111.0 0.7 collective-permute-start.2
  111.6 0.3 copy-done.3
  112.0 0.7 fusion.17
  112.7 3.9 %collective-permute-done.3 = bf16[4096,512]{1,0:T(8,128)(2,1)} collective-permute-done((bf16[4096,512]{1,0:T(8,128)(2,1)}, bf16[4096,512]{1,0:T(8,128)(2,1)}, u32[]{:S(2)}, u32[]{:S(2)}) %collective-permute-start.3) | collective-permute-done | bytes 4194336 | tf_op jit(solution)/shard_map/ppermute | solution.py:192
  116.6 2.9 %fusion.3 = bf16[128,512]{1,0:T(8,128)(2,1)S(1)} fusion(f32[128,512]{1,0:T(8,128)S(1)} %fusion.17, bf16[128,4096]{0,1:T(8,128)(2,1)S(1)} %bitcast.96, bf16[4096,512]{1,0:T(8,128)(2,1)} %collective-permute-done.3), kind=kOutput, calls=%fused_computation.12 | convolution fusion | flops 537001984 | bytes 5636096 | tf_op jit(solution)/shard_map/dot_general | solution.py:195
  119.6 0.7 collective-permute-start.4
  120.2 0.0 collective-permute-done.2
  120.3 0.6 gather_fusion.1
  120.8 4.3 %collective-permute-done.4 = bf16[128,512]{1,0:T(8,128)(2,1)S(1)} collective-permute-done((bf16[128,512]{1,0:T(8,128)(2,1)S(1)}, bf16[128,512]{1,0:T(8,128)(2,1)S(1)}, u32[]{:S(2)}, u32[]{:S(2)}) %collective-permute-start.4) | collective-permute-done | bytes 131104 | tf_op jit(solution)/shard_map/ppermute | solution.py:128
  125.2 1.3 gather_fusion.2
  126.5 1.1 broadcast_select_fusion
  127.6 1.5 broadcast_in_dim.34
  129.1 4.8 %all-to-all-start = ((bf16[8,256,512]{2,1,0:T(8,128)(2,1)}), bf16[8,256,512]{2,1,0:T(8,128)(2,1)}, u32[]{:S(2)}, u32[]{:S(2)}) async-start(bf16[8,256,512]{2,1,0:T(8,128)(2,1)} %broadcast_in_dim.34), calls=%async_computation | async-start | bytes 4194304 | tf_op jit(solution)/shard_map/all_to_all | solution.py:175
  133.9 3.7 %convolution_convert_fusion.1 = bf16[128,4096]{1,0:T(8,128)(2,1)S(1)} fusion(bf16[128,512]{1,0:T(8,128)(2,1)S(1)} %fusion.9, bf16[4096,512]{1,0:T(8,128)(2,1)} %all-gather.2.cloned.1.call-done), kind=kOutput, calls=%fused_computation.4 | convolution fusion | flops 537395200 | bytes 5373952 | tf_op jit(solution)/shard_map/dot_general | solution.py:198
  137.5 0.2 copy.33
  137.8 3.7 %convolution_convert_fusion = bf16[128,4096]{1,0:T(8,128)(2,1)S(1)} fusion(bf16[128,512]{1,0:T(8,128)(2,1)S(1)} %fusion.9, bf16[4096,512]{1,0:T(8,128)(2,1)} %collective-permute-done.3), kind=kOutput, calls=%fused_computation.3 | convolution fusion | flops 537395200 | bytes 5373952 | tf_op jit(solution)/shard_map/dot_general | solution.py:201
  141.5 0.2 copy.34
  141.7 0.3 maximum_select_fusion
  142.1 4.6 %copy.24 = bf16[128,16,2,256]{3,2,1,0:T(2,128)(2,1)} copy(bf16[128,16,2,256]{3,1,0,2:T(8,128)(2,1)S(1)} %maximum_select_fusion) | data formatting | bytes 4194304 | tf_op jit(solution)/shard_map/jit(_where)/select_n | solution.py:204
  146.7 4.5 %select_n.67 = bf16[128,8192]{1,0:T(8,128)(2,1)} reshape(bf16[128,16,2,256]{3,2,1,0:T(2,128)(2,1)} %copy.24) | data formatting | bytes 4194304 | tf_op jit(solution)/shard_map/jit(_where)/select_n | solution.py:204
  151.2 23.6 %shard_map.103 = (bf16[128,4096]{1,0:T(8,128)(2,1)}, f32[256,512]{1,0:T(8,128)S(1)}) custom-call(s32[32]{0:T(128)S(1)} %shift-right-logical_xor_fusion.seeds_ref, s32[1]{0:T(128)} %bitcast.offset_ref, s32[128,1]{1,0:T(8,128)S(1)} %copy.21.pos_ref, bf16[128,4096]{1,0:T(8,128)(2,1)S(1)} %bitcast.80, bf16[128,4096]{1,0:T(8,128)(2,1)S(1)} %bitcast.82, ...), custom_call_target="tpu_custom_call" | custom-call | tf_op jit(solution)/shard_map/pallas_call | solution.py:108
  174.8 1.5 collective-permute-start.5
  176.3 5.7 %collective-permute-done.5 = f32[128,512]{1,0:T(8,128)S(1)} collective-permute-done((f32[128,512]{1,0:T(8,128)S(1)}, f32[128,512]{1,0:T(8,128)S(1)}, u32[]{:S(2)}, u32[]{:S(2)}) %collective-permute-start.5) | collective-permute-done | bytes 262176 | tf_op jit(solution)/shard_map/ppermute | solution.py:140
  182.1 0.7 fusion.8
  182.7 0.0 all-to-all-done
  182.8 0.0 copy-start.4
  182.8 1.9 copy.28
  184.7 0.1 collective-permute-start.6
  184.8 0.2 copy-done.4
  185.0 2.3 %convolution_bitcast_fusion.1 = f32[256,512]{1,0:T(8,128)S(1)} fusion(bf16[2,8,2,128,256]{4,3,2,1,0:T(8,128)(2,1)S(1)} %bitcast.92, s32[]{:T(128)S(6)} %select_n.68, bf16[8,2,128,512]{3,2,1,0:T(8,128)(2,1)} %bitcast.13), kind=kOutput, calls=%fused_computation.7 | convolution fusion | flops 536870912 | bytes 3670020 | tf_op jit(solution)/shard_map/dot_general | solution.py:221
  187.3 1.6 collective-permute-done.6
  188.9 1.4 fusion.2
  (11 shorter events, 0.2 us)
Async XLA Ops:
  7.2 13.2 %copy-start = (s32[1,256]{1,0:T(1,128)S(1)}, s32[1,256]{1,0:T(1,128)}, u32[]{:S(2)}) copy-start(s32[1,256]{1,0:T(1,128)} %param.13) | copy-start | bytes 3076
  7.2 102.0 %all-gather.2.cloned.1.call-start = ((), (), s32[]{:S(2)}) async-start(), calls=%async_computation.2 | async-start | bytes 4456448 | tf_op jit(solution)/shard_map/all_gather | solution.py:158
  12.0 6.1 %copy-start.5 = (bf16[1,128,512]{2,1,0:T(8,128)(2,1)S(1)}, bf16[1,128,512]{2,1,0:T(8,128)(2,1)}, u32[]{:S(2)}) copy-start(bf16[1,128,512]{2,1,0:T(8,128)(2,1)} %param.11) | copy-start | bytes 393220
  12.0 22.1 %copy-start.1 = (bf16[1,128,4096]{2,1,0:T(8,128)(2,1)S(1)}, bf16[1,128,4096]{2,1,0:T(8,128)(2,1)}, u32[]{:S(2)}) copy-start(bf16[1,128,4096]{2,1,0:T(8,128)(2,1)} %param.10) | copy-start | bytes 3145732
  12.0 22.1 %copy-start.2 = (bf16[1,128,4096]{2,1,0:T(8,128)(2,1)S(1)}, bf16[1,128,4096]{2,1,0:T(8,128)(2,1)}, u32[]{:S(2)}) copy-start(bf16[1,128,4096]{2,1,0:T(8,128)(2,1)} %param.12) | copy-start | bytes 3145732
  12.0 68.5 %all-to-all-start.1 = ((bf16[128,32,256]{0,2,1:T(8,128)(2,1)}), bf16[128,32,256]{0,2,1:T(8,128)(2,1)}, u32[]{:S(2)}, u32[]{:S(2)}) async-start(bf16[128,32,256]{0,2,1:T(8,128)(2,1)} %bitcast.90), calls=%async_computation.1 | async-start | bytes 4194304 | tf_op jit(solution)/shard_map/all_to_all | solution.py:182
  18.1 15.3 %collective-permute-start = (bf16[128,512]{1,0:T(8,128)(2,1)S(1)}, bf16[128,512]{1,0:T(8,128)(2,1)S(1)}, u32[]{:S(2)}, u32[]{:S(2)}) collective-permute-start(bf16[128,512]{1,0:T(8,128)(2,1)S(1)} %bitcast.104), channel_id=1, source_target_pairs={{0,16},{16,0},{1,17},{17,1},{2,18},{18,2},{3,19},{19,3},{4,20},{20... | collective-permute-start | bytes 393224 | tf_op jit(solution)/shard_map/ppermute | solution.py:128
  53.7 11.1 %collective-permute-start.1 = (f32[128,512]{1,0:T(8,128)S(1)}, f32[128,512]{1,0:T(8,128)S(1)}, u32[]{:S(2)}, u32[]{:S(2)}) collective-permute-start(f32[128,512]{1,0:T(8,128)S(1)} %dynamic-slice_bitcast_fusion.1), channel_id=1, source_target_pairs={{0,16},{16,0},{1,17},{17,1},{2,18},{18,2},{3,19},{19,3},{4,20},{20... | collective-permute-start | bytes 786440 | tf_op jit(solution)/shard_map/ppermute | solution.py:140
  109.1 7.5 %collective-permute-start.3 = (bf16[4096,512]{1,0:T(8,128)(2,1)}, bf16[4096,512]{1,0:T(8,128)(2,1)}, u32[]{:S(2)}, u32[]{:S(2)}) collective-permute-start(bf16[4096,512]{1,0:T(8,128)(2,1)} %all-gather.2.cloned.1.call-done), channel_id=1, source_target_pairs={{0,1},{1,0},{2,3},{3,2},{4,5},{5,4},{6,7},{7,6},{8,9},{9,8},{10,11... | collective-permute-start | bytes 12582920 | tf_op jit(solution)/shard_map/ppermute | solution.py:192
  109.1 2.8 %copy-start.3 = (bf16[4096,512]{1,0:T(8,128)(2,1)S(1)}, bf16[4096,512]{1,0:T(8,128)(2,1)}, u32[]{:S(2)}) copy-start(bf16[4096,512]{1,0:T(8,128)(2,1)} %all-gather.2.cloned.1.call-done) | copy-start | bytes 12582916
  111.0 9.3 %collective-permute-start.2 = (bf16[128,512]{1,0:T(8,128)(2,1)S(1)}, bf16[128,512]{1,0:T(8,128)(2,1)S(1)}, u32[]{:S(2)}, u32[]{:S(2)}) collective-permute-start(bf16[128,512]{1,0:T(8,128)(2,1)S(1)} %fusion.9), channel_id=1, source_target_pairs={{0,16},{16,0},{1,17},{17,1},{2,18},{18,2},{3,19},{19,3},{4,20},{20... | collective-permute-start | bytes 393224 | tf_op jit(solution)/shard_map/ppermute | solution.py:128
  119.6 5.6 %collective-permute-start.4 = (bf16[128,512]{1,0:T(8,128)(2,1)S(1)}, bf16[128,512]{1,0:T(8,128)(2,1)S(1)}, u32[]{:S(2)}, u32[]{:S(2)}) collective-permute-start(bf16[128,512]{1,0:T(8,128)(2,1)S(1)} %fusion.3), channel_id=1, source_target_pairs={{0,16},{16,0},{1,17},{17,1},{2,18},{18,2},{3,19},{19,3},{4,20},{20... | collective-permute-start | bytes 393224 | tf_op jit(solution)/shard_map/ppermute | solution.py:128
  129.1 53.7 %all-to-all-start = ((bf16[8,256,512]{2,1,0:T(8,128)(2,1)}), bf16[8,256,512]{2,1,0:T(8,128)(2,1)}, u32[]{:S(2)}, u32[]{:S(2)}) async-start(bf16[8,256,512]{2,1,0:T(8,128)(2,1)} %broadcast_in_dim.34), calls=%async_computation | async-start | bytes 4194304 | tf_op jit(solution)/shard_map/all_to_all | solution.py:175
  174.8 7.3 %collective-permute-start.5 = (f32[128,512]{1,0:T(8,128)S(1)}, f32[128,512]{1,0:T(8,128)S(1)}, u32[]{:S(2)}, u32[]{:S(2)}) collective-permute-start(f32[128,512]{1,0:T(8,128)S(1)} %dynamic-slice_bitcast_fusion), channel_id=1, source_target_pairs={{0,16},{16,0},{1,17},{17,1},{2,18},{18,2},{3,19},{19,3},{4,20},{20... | collective-permute-start | bytes 786440 | tf_op jit(solution)/shard_map/ppermute | solution.py:140
  182.8 2.2 %copy-start.4 = (bf16[32,128,1,256]{3,1,0,2:T(8,128)(2,1)S(1)}, bf16[32,128,1,256]{3,1,0,2:T(8,128)(2,1)}, u32[]{:S(2)}) copy-start(bf16[32,128,1,256]{3,1,0,2:T(8,128)(2,1)} %copy.23) | copy-start | bytes 6291460
  184.7 4.2 %collective-permute-start.6 = (bf16[8,2,128,512]{3,2,0,1:T(8,128)(2,1)S(1)}, bf16[8,2,128,512]{3,2,0,1:T(8,128)(2,1)S(1)}, u32[]{:S(2)}, u32[]{:S(2)}) collective-permute-start(bf16[8,2,128,512]{3,2,0,1:T(8,128)(2,1)S(1)} %copy.28), channel_id=1, source_target_pairs={{0,1},{1,0},{2,3},{3,2},{4,5},{5,4},{6,7},{7,6},{8,9},{9,8},{10,11... | collective-permute-start | bytes 6291464 | tf_op jit(solution)/shard_map/ppermute | solution.py:217
Sparse Core Ops, SparseCore 0:
  10.8 98.2 all-gather.1

commit v13 on v10

--- a/solution.py
+++ b/solution.py
@@ -225,8 +225,10 @@
             partial, (seq_index + shift) % seq_devices, 0, keepdims=False
         )
         summed = summed + lax.ppermute(
-            piece, "seq", [(i, (i + shift) % seq_devices) for i in range(seq_devices)]
-        )
+            piece.astype(jnp.bfloat16),
+            "seq",
+            [(i, (i + shift) % seq_devices) for i in range(seq_devices)],
+        ).astype(jnp.float32)
     weight_grad = (summed * (1.0 / math.sqrt(fsdp_devices * seq_len))).astype(jnp.bfloat16)
 
     return (query_grad[None], key_grad[None], input_grad[None], weight_grad)

time: 189 us -> 184 us (0.974)
  waiting for transfers between devices: 71 us -> 65.4 us
    ppermute x1, waiting for transfers between devices: 12.6 us -> 6.95 us  [per_device(): lax.ppermute(piece.astype(jnp.bfloat16), 'seq', [(i, (i + shift) % seq_de...]
  transfers between devices with their start and end apart: 10 -> 10, of which waited for: 6 -> 6; matrix products, arithmetic and copies ran while one was open for 21% -> 21% of each run, Pallas kernels for 23% -> 24%
where the time goes in v13:
time: 184 us; the launch traced here: 181 us
  waiting for transfers between devices  65.4 us (36%)
  Pallas kernels  43.1 us (23%)
  local copies, waits for them, and re-layouts  25.1 us (14%)
  between operations  16.4 us (9%)
  matrix products  15.3 us (8%)
  starting transfers between devices  12.2 us (7%)
  other arithmetic  3.7 us (2%)
    pallas_call x2, Pallas kernels, attention(): pl.pallas_call(kernel, grid_spec=pltpu.PrefetchScalarGridSpec(num_scalar_...  43.1 us
    all_gather x1, waiting for transfers between devices, per_device(): weight_own = lax.all_gather(value_weight, ('seq', 'zx'), axis=0, tiled=True)  40.9 us
    ppermute x2, waiting for transfers between devices, reduce_seq(): lax.ppermute(piece, 'seq', [(i, (i + shift) % seq_devices) for i in range...  12.8 us
    select_n x2, local copies, waits for them, and re-layouts, per_device(): jnp.where(core_index == 0, jnp.concatenate([grad_own, grad_other], axis=2...  9.18 us
    unnamed x21, local copies, waits for them, and re-layouts  7.19 us
    ppermute x1, waiting for transfers between devices, per_device(): lax.ppermute(piece.astype(jnp.bfloat16), 'seq', [(i, (i + shift) % seq_de...  6.95 us
    all_to_all x1, starting transfers between devices, per_device(): lax.all_to_all(input_late.reshape(tok_rows, seq_devices, fsdp_devices, bl...  4.9 us
    dot_general x1, matrix products, per_device(): lax.dot_general(value_grad, weight_own, last_dims, preferred_element_type...  3.88 us
  transfers between devices with their start and end apart: 10, of which 6 were waited for; matrix products, arithmetic and copies ran while one was open for 21% of the time, Pallas kernels for 24%

profile of v13, /device:TPU:10, one launch (start us, length us, event | category | flops | bytes accessed | tf_op | source)
XLA Modules:
  0.0 181.2 jit_solution(732446707715072297)
XLA Ops:
  8.0 0.0 copy-start
  8.0 0.0 copy-start.1
  8.0 0.0 all-gather.5.cloned.1.call-start
  8.1 0.7 all-gather.5.cloned.1.call-update
  8.8 1.6 collective-permute-start
  11.1 0.0 copy-done
  11.1 0.1 copy.25.pos_ref
  11.2 3.0 %collective-permute-done = bf16[128,512]{1,0:T(8,128)(2,1)S(1)} collective-permute-done((bf16[128,512]{1,0:T(8,128)(2,1)}, bf16[128,512]{1,0:T(8,128)(2,1)S(1)}, u32[]{:S(2)}, u32[]{:S(2)}) %collective-permute-start) | collective-permute-done | bytes 131104 | tf_op jit(solution)/shard_map/ppermute | solution.py:128
  14.3 0.9 pad_maximum_fusion
  15.2 0.6 gather_fusion
  15.8 0.1 broadcast_select_fusion.1
  15.9 0.0 copy-done.1
  15.9 0.0 copy-start.2
  15.9 1.2 copy-done.2
  17.1 19.6 %shard_map.102 = f32[256,512]{1,0:T(8,128)S(1)} custom-call(s32[32]{0:T(128)S(1)} %shift-right-logical_xor_fusion.seeds_ref, s32[1]{0:T(128)} %bitcast.offset_ref, s32[128,1]{1,0:T(8,128)S(1)} %copy.25.pos_ref, bf16[128,4096]{1,0:T(8,128)(2,1)S(1)} %bitcast.69, bf16[128,4096]{1,0:T(8,128)(2,1)S(1)} %bitcast.71, bf16[256,512]{1,0:T(8,128)(2,1)S(1)} %bitcast.73), custom_call_target="tpu_custom_call" | custom-call | tf_op jit(solution)/shard_map/pallas_call | solution.py:108
  36.7 1.6 collective-permute-start.1
  38.3 4.1 %copy.26 = bf16[1,128,8192]{1,2,0:T(8,128)(2,1)} copy(bf16[1,128,8192]{2,1,0:T(8,128)(2,1)} %param.9) | data formatting | bytes 4194304 | tf_op args[0]
  42.4 5.4 %collective-permute-done.1 = f32[128,512]{1,0:T(8,128)S(1)} collective-permute-done((f32[128,512]{1,0:T(8,128)S(1)}, f32[128,512]{1,0:T(8,128)S(1)}, u32[]{:S(2)}, u32[]{:S(2)}) %collective-permute-start.1) | collective-permute-done | bytes 262176 | tf_op jit(solution)/shard_map/ppermute | solution.py:140
  47.7 0.7 fusion.5
  48.4 40.9 %all-gather.5.cloned.1.call-done = bf16[4096,512]{1,0:T(8,128)(2,1)} async-done(((bf16[256,512]{1,0:T(8,128)(2,1)}), bf16[4096,512]{1,0:T(8,128)(2,1)}) %all-gather.5.cloned.1.call-update) | async-done | bytes 4194320 | tf_op jit(solution)/shard_map/all_gather | solution.py:158
  89.4 0.0 collective-permute-start.2
  89.4 3.2 %copy.27 = bf16[128,2,16,256]{0,3,1,2:T(8,128)(2,1)} copy(bf16[128,2,16,256]{0,3,2,1:T(8,128)(2,1)} %bitcast.80) | data formatting | bytes 4194304 | tf_op jit(solution)/shard_map/reshape | solution.py:180
  92.5 0.0 copy-start.4
  92.5 4.9 %all-to-all-start = ((bf16[128,2,16,256]{0,3,1,2:T(8,128)(2,1)}), bf16[128,2,16,256]{0,3,1,2:T(8,128)(2,1)}, u32[]{:S(2)}, u32[]{:S(2)}) async-start(bf16[128,2,16,256]{0,3,1,2:T(8,128)(2,1)} %copy.27), calls=%async_computation | async-start | bytes 4194304 | tf_op jit(solution)/shard_map/all_to_all | solution.py:179
  97.4 0.0 all-gather.3.cloned.1.call-start
  97.5 0.0 copy-done.4
  97.5 1.5 constant_dynamic-slice_fusion.2
  99.0 0.0 all-gather.3.cloned.1.call-update
  99.0 0.0 copy-start.5
  99.0 3.9 %convolution_convert_fusion.1 = bf16[128,4096]{1,0:T(8,128)(2,1)S(1)} fusion(bf16[128,512]{1,0:T(8,128)(2,1)} %fusion.5, bf16[4096,512]{1,0:T(8,128)(2,1)} %all-gather.5.cloned.1.call-done), kind=kOutput, calls=%fused_computation.3 | convolution fusion | flops 537395200 | bytes 5373952 | tf_op jit(solution)/shard_map/dot_general | solution.py:191
  102.9 0.0 copy-start.7
  102.9 0.2 copy.33
  103.1 0.0 copy-done.5
  103.2 0.9 copy-done.7
  104.1 0.8 fusion.10
  104.9 0.0 collective-permute-done.2
  104.9 0.4 copy-done.6
  105.3 3.0 %fusion = bf16[128,512]{1,0:T(8,128)(2,1)S(1)} fusion(f32[128,512]{1,0:T(8,128)S(1)} %fusion.10, bf16[128,4096]{0,1:T(8,128)(2,1)S(1)} %bitcast.84, bf16[4096,512]{1,0:T(8,128)(2,1)} %collective-permute-done.2), kind=kOutput, calls=%fused_computation.7 | convolution fusion | flops 537001984 | bytes 5636096 | tf_op jit(solution)/shard_map/dot_general | solution.py:188
  108.3 1.5 collective-permute-start.3
  109.9 0.0 copy-done.8
  109.9 3.7 %convolution_convert_fusion = bf16[128,4096]{1,0:T(8,128)(2,1)S(1)} fusion(bf16[128,512]{1,0:T(8,128)(2,1)S(1)} %copy-done.8, bf16[4096,512]{1,0:T(8,128)(2,1)} %collective-permute-done.2), kind=kOutput, calls=%fused_computation.2 | convolution fusion | flops 537395200 | bytes 5373952 | tf_op jit(solution)/shard_map/dot_general | solution.py:194
  113.6 0.2 copy.34
  113.8 0.3 maximum_select_fusion
  114.2 4.6 %copy.28 = bf16[128,16,2,256]{3,2,1,0:T(2,128)(2,1)} copy(bf16[128,16,2,256]{3,1,0,2:T(8,128)(2,1)S(1)} %maximum_select_fusion) | data formatting | bytes 4194304 | tf_op jit(solution)/shard_map/jit(_where)/select_n | solution.py:197
  118.8 4.6 %select_n.70 = bf16[128,8192]{1,0:T(8,128)(2,1)} reshape(bf16[128,16,2,256]{3,2,1,0:T(2,128)(2,1)} %copy.28) | data formatting | bytes 4194304 | tf_op jit(solution)/shard_map/jit(_where)/select_n | solution.py:197
  123.4 0.0 collective-permute-done.3
  123.4 0.6 gather_fusion.1
  124.0 0.1 broadcast_select_fusion
  124.1 0.0 copy-done.3
  124.1 23.6 %shard_map.103 = (bf16[128,4096]{1,0:T(8,128)(2,1)}, f32[256,512]{1,0:T(8,128)S(1)}) custom-call(s32[32]{0:T(128)S(1)} %shift-right-logical_xor_fusion.seeds_ref, s32[1]{0:T(128)} %bitcast.offset_ref, s32[128,1]{1,0:T(8,128)S(1)} %copy.25.pos_ref, bf16[128,4096]{1,0:T(8,128)(2,1)S(1)} %bitcast.70, bf16[128,4096]{1,0:T(8,128)(2,1)S(1)} %bitcast.72, ...), custom_call_target="tpu_custom_call" | custom-call | tf_op jit(solution)/shard_map/pallas_call | solution.py:108
  147.7 0.7 collective-permute-start.4
  148.4 7.5 %collective-permute-done.4 = f32[128,512]{1,0:T(8,128)S(1)} collective-permute-done((f32[128,512]{1,0:T(8,128)S(1)}, f32[128,512]{1,0:T(8,128)S(1)}, u32[]{:S(2)}, u32[]{:S(2)}) %collective-permute-start.4) | collective-permute-done | bytes 262176 | tf_op jit(solution)/shard_map/ppermute | solution.py:140
  155.9 0.7 fusion.4
  156.6 0.9 all-to-all-done
  157.5 0.3 collective-permute-start.5
  157.8 1.7 constant_dynamic-slice_fusion
  159.4 0.5 copy.31
  160.0 0.5 copy.32
  160.5 2.0 %fusion.11 = f32[512,512]{1,0:T(8,128)S(1)} fusion(bf16[1024,512]{1,0:T(8,128)(2,1)S(1)} %bitcast.90, bf16[1024,512]{1,0:T(8,128)(2,1)} %all-gather.3.cloned.1.call-done), kind=kOutput, calls=%fused_computation.42 | convolution fusion | flops 536870912 | bytes 3145728 | tf_op jit(solution)/shard_map/dot_general | solution.py:219
  162.5 0.0 collective-permute-done.5
  162.5 2.0 %convolution_add_fusion = f32[512,512]{1,0:T(8,128)S(1)} fusion(f32[512,512]{1,0:T(8,128)S(1)} %fusion.11, bf16[1024,512]{1,0:T(8,128)(2,1)S(1)} %bitcast.89, bf16[1024,512]{1,0:T(8,128)(2,1)} %collective-permute-done.5), kind=kOutput, calls=%fused_computation.5 | convolution fusion | flops 537133056 | bytes 4194304 | tf_op jit(solution)/shard_map/dot_general | solution.py:220
  164.5 1.5 collective-permute-start.6
  166.0 7.0 %collective-permute-done.6 = bf16[256,512]{1,0:T(8,128)(2,1)S(1)} collective-permute-done((bf16[256,512]{1,0:T(8,128)(2,1)S(1)}, bf16[256,512]{1,0:T(8,128)(2,1)S(1)}, u32[]{:S(2)}, u32[]{:S(2)}) %collective-permute-start.6) | collective-permute-done | bytes 262176 | tf_op jit(solution)/shard_map/ppermute | solution.py:227
  173.0 0.8 fusion.2
  (13 shorter events, 0.2 us)
Async XLA Ops:
  8.0 3.1 %copy-start = (s32[1,256]{1,0:T(1,128)S(1)}, s32[1,256]{1,0:T(1,128)}, u32[]{:S(2)}) copy-start(s32[1,256]{1,0:T(1,128)} %param.13) | copy-start | bytes 3076
  8.0 7.9 %copy-start.1 = (bf16[1,128,4096]{2,1,0:T(8,128)(2,1)S(1)}, bf16[1,128,4096]{2,1,0:T(8,128)(2,1)}, u32[]{:S(2)}) copy-start(bf16[1,128,4096]{2,1,0:T(8,128)(2,1)} %param.10) | copy-start | bytes 3145732
  8.0 81.3 %all-gather.5.cloned.1.call-start = ((), (), s32[]{:S(2)}) async-start(), calls=%async_computation.2 | async-start | bytes 4456448 | tf_op jit(solution)/shard_map/all_gather | solution.py:158
  8.8 5.5 %collective-permute-start = (bf16[128,512]{1,0:T(8,128)(2,1)}, bf16[128,512]{1,0:T(8,128)(2,1)S(1)}, u32[]{:S(2)}, u32[]{:S(2)}) collective-permute-start(bf16[128,512]{1,0:T(8,128)(2,1)} %bitcast.94), channel_id=1, source_target_pairs={{0,16},{16,0},{1,17},{17,1},{2,18},{18,2},{3,19},{19,3},{4,20},{20... | collective-permute-start | bytes 393224 | tf_op jit(solution)/shard_map/ppermute | solution.py:128
  15.9 1.2 copy-start.2
  36.7 11.0 %collective-permute-start.1 = (f32[128,512]{1,0:T(8,128)S(1)}, f32[128,512]{1,0:T(8,128)S(1)}, u32[]{:S(2)}, u32[]{:S(2)}) collective-permute-start(f32[128,512]{1,0:T(8,128)S(1)} %dynamic-slice_bitcast_fusion.1), channel_id=1, source_target_pairs={{0,16},{16,0},{1,17},{17,1},{2,18},{18,2},{3,19},{19,3},{4,20},{20... | collective-permute-start | bytes 786440 | tf_op jit(solution)/shard_map/ppermute | solution.py:140
  89.4 15.5 %collective-permute-start.2 = (bf16[4096,512]{1,0:T(8,128)(2,1)}, bf16[4096,512]{1,0:T(8,128)(2,1)}, u32[]{:S(2)}, u32[]{:S(2)}) collective-permute-start(bf16[4096,512]{1,0:T(8,128)(2,1)} %all-gather.5.cloned.1.call-done), channel_id=1, source_target_pairs={{0,1},{1,0},{2,3},{3,2},{4,5},{5,4},{6,7},{7,6},{8,9},{9,8},{10,11... | collective-permute-start | bytes 12582920 | tf_op jit(solution)/shard_map/ppermute | solution.py:178
  92.5 5.0 %copy-start.4 = (bf16[1,128,8192]{1,2,0:T(8,128)(2,1)S(1)}, bf16[1,128,8192]{1,2,0:T(8,128)(2,1)}, u32[]{:S(2)}) copy-start(bf16[1,128,8192]{1,2,0:T(8,128)(2,1)} %copy.26) | copy-start | bytes 6291460
  92.5 64.9 %all-to-all-start = ((bf16[128,2,16,256]{0,3,1,2:T(8,128)(2,1)}), bf16[128,2,16,256]{0,3,1,2:T(8,128)(2,1)}, u32[]{:S(2)}, u32[]{:S(2)}) async-start(bf16[128,2,16,256]{0,3,1,2:T(8,128)(2,1)} %copy.27), calls=%async_computation | async-start | bytes 4194304 | tf_op jit(solution)/shard_map/all_to_all | solution.py:179
  97.4 59.1 %all-gather.3.cloned.1.call-start = ((), (), s32[]{:S(2)}) async-start(), calls=%async_computation.1 | async-start | bytes 1179648 | tf_op jit(solution)/shard_map/all_gather | solution.py:174
  99.0 4.2 %copy-start.5 = (bf16[4096,512]{1,0:T(8,128)(2,1)S(1)}, bf16[4096,512]{1,0:T(8,128)(2,1)}, u32[]{:S(2)}) copy-start(bf16[4096,512]{1,0:T(8,128)(2,1)} %all-gather.5.cloned.1.call-done) | copy-start | bytes 12582916
  102.9 1.2 copy-start.7
  104.1 1.2 copy-start.6
  105.3 4.6 %copy-start.8 = (bf16[128,512]{1,0:T(8,128)(2,1)S(1)}, bf16[128,512]{1,0:T(8,128)(2,1)}, u32[]{:S(2)}) copy-start(bf16[128,512]{1,0:T(8,128)(2,1)} %fusion.5) | copy-start | bytes 393220
  108.3 15.0 %collective-permute-start.3 = (bf16[128,512]{1,0:T(8,128)(2,1)S(1)}, bf16[128,512]{1,0:T(8,128)(2,1)S(1)}, u32[]{:S(2)}, u32[]{:S(2)}) collective-permute-start(bf16[128,512]{1,0:T(8,128)(2,1)S(1)} %fusion), channel_id=1, source_target_pairs={{0,16},{16,0},{1,17},{17,1},{2,18},{18,2},{3,19},{19,3},{4,20},{20... | collective-permute-start | bytes 393224 | tf_op jit(solution)/shard_map/ppermute | solution.py:128
  118.8 5.3 %copy-start.3 = (bf16[1,128,4096]{2,1,0:T(8,128)(2,1)S(1)}, bf16[1,128,4096]{2,1,0:T(8,128)(2,1)}, u32[]{:S(2)}) copy-start(bf16[1,128,4096]{2,1,0:T(8,128)(2,1)} %param.12) | copy-start | bytes 3145732
  147.7 8.2 %collective-permute-start.4 = (f32[128,512]{1,0:T(8,128)S(1)}, f32[128,512]{1,0:T(8,128)S(1)}, u32[]{:S(2)}, u32[]{:S(2)}) collective-permute-start(f32[128,512]{1,0:T(8,128)S(1)} %dynamic-slice_bitcast_fusion), channel_id=1, source_target_pairs={{0,16},{16,0},{1,17},{17,1},{2,18},{18,2},{3,19},{19,3},{4,20},{20... | collective-permute-start | bytes 786440 | tf_op jit(solution)/shard_map/ppermute | solution.py:140
  157.5 5.0 %collective-permute-start.5 = (bf16[1024,512]{1,0:T(8,128)(2,1)}, bf16[1024,512]{1,0:T(8,128)(2,1)}, u32[]{:S(2)}, u32[]{:S(2)}) collective-permute-start(bf16[1024,512]{1,0:T(8,128)(2,1)} %all-gather.3.cloned.1.call-done), channel_id=1, source_target_pairs={{0,1},{1,0},{2,3},{3,2},{4,5},{5,4},{6,7},{7,6},{8,9},{9,8},{10,11... | collective-permute-start | bytes 3145736 | tf_op jit(solution)/shard_map/ppermute | solution.py:210
  164.5 8.5 %collective-permute-start.6 = (bf16[256,512]{1,0:T(8,128)(2,1)S(1)}, bf16[256,512]{1,0:T(8,128)(2,1)S(1)}, u32[]{:S(2)}, u32[]{:S(2)}) collective-permute-start(bf16[256,512]{1,0:T(8,128)(2,1)S(1)} %fusion.3), channel_id=1, source_target_pairs={{0,16},{16,0},{1,17},{17,1},{2,18},{18,2},{3,19},{19,3},{4,20},{20... | collective-permute-start | bytes 786440 | tf_op jit(solution)/shard_map/ppermute | solution.py:227
Sparse Core Ops, SparseCore 0:
  11.7 77.6 all-gather.4
Sparse Core Ops, SparseCore 1:
  100.6 55.7 all-gather.2

commit v14 on v10

--- a/solution.py
+++ b/solution.py
@@ -215,18 +215,34 @@
         zx_devices * tok_rows, -1
     )
     first_dims = (((0,), (0,)), ((), ()))
-    partial = (
-        lax.dot_general(cols_own, grads_own, first_dims, preferred_element_type=jnp.float32)
-        + lax.dot_general(cols_other, grads_other, first_dims, preferred_element_type=jnp.float32)
-    ).reshape(seq_devices, block_rows, KVH * HD)
-    summed = lax.dynamic_index_in_dim(partial, seq_index, 0, keepdims=False)
+
+    def block_partial(block):
+        start = block * block_rows
+        return lax.dot_general(
+            lax.dynamic_slice_in_dim(cols_own, start, block_rows, 1),
+            grads_own,
+            first_dims,
+            preferred_element_type=jnp.float32,
+        ) + lax.dot_general(
+            lax.dynamic_slice_in_dim(cols_other, start, block_rows, 1),
+            grads_other,
+            first_dims,
+            preferred_element_type=jnp.float32,
+        )
+
+    received = []
     for shift in range(1, seq_devices):
-        piece = lax.dynamic_index_in_dim(
-            partial, (seq_index + shift) % seq_devices, 0, keepdims=False
-        )
-        summed = summed + lax.ppermute(
-            piece, "seq", [(i, (i + shift) % seq_devices) for i in range(seq_devices)]
-        )
+        piece = block_partial((seq_index + shift) % seq_devices)
+        received.append(
+            lax.ppermute(
+                piece.astype(jnp.bfloat16),
+                "seq",
+                [(i, (i + shift) % seq_devices) for i in range(seq_devices)],
+            )
+        )
+    summed = lax.optimization_barrier(block_partial(seq_index))
+    for piece in received:
+        summed = summed + piece.astype(jnp.float32)
     weight_grad = (summed * (1.0 / math.sqrt(fsdp_devices * seq_len))).astype(jnp.bfloat16)
 
     return (query_grad[None], key_grad[None], input_grad[None], weight_grad)

time: 189 us -> 185 us (0.979)
  waiting for transfers between devices: 71 us -> 63.9 us
    ppermute x1, waiting for transfers between devices: 12.6 us -> 5.25 us  [per_device(): lax.ppermute(piece.astype(jnp.bfloat16), 'seq', [(i, (i + shift) % seq_de...]
    dot_general x2 -> x4, matrix products: 3.91 us -> 4.33 us  [the longest x2 3.37 us: block_partial(): lax.dot_general(lax.dynamic_slice_in_dim(cols_other, start, block_rows, 1...]
    unnamed x21 -> x27, local copies, waits for them, and re-layouts: 7.19 us -> 7.43 us
  transfers between devices with their start and end apart: 10 -> 10, of which waited for: 6 -> 6; matrix products, arithmetic and copies ran while one was open for 21% -> 22% of each run, Pallas kernels for 23% -> 24%
where the time goes in v14:
time: 185 us; the launch traced here: 182 us
  waiting for transfers between devices  63.9 us (35%)
  Pallas kernels  43.1 us (23%)
  local copies, waits for them, and re-layouts  26.9 us (15%)
  between operations  16.4 us (9%)
  matrix products  15.6 us (8%)
  starting transfers between devices  12.2 us (7%)
  other arithmetic  3.69 us (2%)
    pallas_call x2, Pallas kernels, attention(): pl.pallas_call(kernel, grid_spec=pltpu.PrefetchScalarGridSpec(num_scalar_...  43.1 us
    all_gather x1, waiting for transfers between devices, per_device(): weight_own = lax.all_gather(value_weight, ('seq', 'zx'), axis=0, tiled=True)  41.2 us
    ppermute x2, waiting for transfers between devices, reduce_seq(): lax.ppermute(piece, 'seq', [(i, (i + shift) % seq_devices) for i in range...  12.8 us
    select_n x2, local copies, waits for them, and re-layouts, per_device(): jnp.where(core_index == 0, jnp.concatenate([grad_own, grad_other], axis=2...  9.19 us
    unnamed x27, local copies, waits for them, and re-layouts  7.43 us
    ppermute x1, waiting for transfers between devices, per_device(): lax.ppermute(piece.astype(jnp.bfloat16), 'seq', [(i, (i + shift) % seq_de...  5.25 us
    all_to_all x1, starting transfers between devices, per_device(): lax.all_to_all(input_late.reshape(tok_rows, seq_devices, fsdp_devices, bl...  4.9 us
    dot_general x1, matrix products, per_device(): lax.dot_general(value_grad, weight_own, last_dims, preferred_element_type...  3.88 us
  transfers between devices with their start and end apart: 10, of which 6 were waited for; matrix products, arithmetic and copies ran while one was open for 22% of the time, Pallas kernels for 24%

profile of v14, /device:TPU:10, one launch (start us, length us, event | category | flops | bytes accessed | tf_op | source)
XLA Modules:
  0.0 182.0 jit_solution(15765589784921193621)
XLA Ops:
  8.0 0.0 copy-start
  8.0 0.0 copy-start.1
  8.0 0.0 all-gather.5.cloned.1.call-start
  8.1 0.7 all-gather.5.cloned.1.call-update
  8.8 1.6 collective-permute-start
  11.1 0.0 copy-done
  11.1 0.1 copy.25.pos_ref
  11.2 3.0 %collective-permute-done = bf16[128,512]{1,0:T(8,128)(2,1)S(1)} collective-permute-done((bf16[128,512]{1,0:T(8,128)(2,1)}, bf16[128,512]{1,0:T(8,128)(2,1)S(1)}, u32[]{:S(2)}, u32[]{:S(2)}) %collective-permute-start) | collective-permute-done | bytes 131104 | tf_op jit(solution)/shard_map/ppermute | solution.py:128
  14.3 0.9 pad_maximum_fusion
  15.2 0.6 gather_fusion
  15.8 0.1 broadcast_select_fusion.1
  15.9 0.0 copy-done.1
  15.9 0.0 copy-start.2
  15.9 1.2 copy-done.2
  17.1 19.6 %shard_map.102 = f32[256,512]{1,0:T(8,128)S(1)} custom-call(s32[32]{0:T(128)S(1)} %shift-right-logical_xor_fusion.seeds_ref, s32[1]{0:T(128)} %bitcast.offset_ref, s32[128,1]{1,0:T(8,128)S(1)} %copy.25.pos_ref, bf16[128,4096]{1,0:T(8,128)(2,1)S(1)} %bitcast.60, bf16[128,4096]{1,0:T(8,128)(2,1)S(1)} %bitcast.62, bf16[256,512]{1,0:T(8,128)(2,1)S(1)} %bitcast.64), custom_call_target="tpu_custom_call" | custom-call | tf_op jit(solution)/shard_map/pallas_call | solution.py:108
  36.7 1.6 collective-permute-start.1
  38.3 4.1 %copy.26 = bf16[1,128,8192]{1,2,0:T(8,128)(2,1)} copy(bf16[1,128,8192]{2,1,0:T(8,128)(2,1)} %param.9) | data formatting | bytes 4194304 | tf_op args[0]
  42.4 5.4 %collective-permute-done.1 = f32[128,512]{1,0:T(8,128)S(1)} collective-permute-done((f32[128,512]{1,0:T(8,128)S(1)}, f32[128,512]{1,0:T(8,128)S(1)}, u32[]{:S(2)}, u32[]{:S(2)}) %collective-permute-start.1) | collective-permute-done | bytes 262176 | tf_op jit(solution)/shard_map/ppermute | solution.py:140
  47.7 0.7 fusion.9
  48.4 41.2 %all-gather.5.cloned.1.call-done = bf16[4096,512]{1,0:T(8,128)(2,1)} async-done(((bf16[256,512]{1,0:T(8,128)(2,1)}), bf16[4096,512]{1,0:T(8,128)(2,1)}) %all-gather.5.cloned.1.call-update) | async-done | bytes 4194320 | tf_op jit(solution)/shard_map/all_gather | solution.py:158
  89.6 0.0 collective-permute-start.2
  89.6 3.2 %copy.27 = bf16[128,2,16,256]{0,3,1,2:T(8,128)(2,1)} copy(bf16[128,2,16,256]{0,3,2,1:T(8,128)(2,1)} %bitcast.71) | data formatting | bytes 4194304 | tf_op jit(solution)/shard_map/reshape | solution.py:180
  92.7 4.9 %all-to-all-start = ((bf16[128,2,16,256]{0,3,1,2:T(8,128)(2,1)}), bf16[128,2,16,256]{0,3,1,2:T(8,128)(2,1)}, u32[]{:S(2)}, u32[]{:S(2)}) async-start(bf16[128,2,16,256]{0,3,1,2:T(8,128)(2,1)} %copy.27), calls=%async_computation | async-start | bytes 4194304 | tf_op jit(solution)/shard_map/all_to_all | solution.py:179
  97.6 0.0 all-gather.3.cloned.1.call-start
  97.7 0.0 copy-done.4
  97.7 1.5 constant_dynamic-slice_fusion.2
  99.2 0.0 all-gather.3.cloned.1.call-update
  99.2 0.0 copy-start.5
  99.2 3.9 %convolution_convert_fusion.1 = bf16[128,4096]{1,0:T(8,128)(2,1)S(1)} fusion(bf16[128,512]{1,0:T(8,128)(2,1)} %fusion.9, bf16[4096,512]{1,0:T(8,128)(2,1)} %all-gather.5.cloned.1.call-done), kind=kOutput, calls=%fused_computation.3 | convolution fusion | flops 537395200 | bytes 5373952 | tf_op jit(solution)/shard_map/dot_general | solution.py:191
  103.1 0.0 copy-start.10
  103.1 0.2 copy.33
  103.4 0.9 copy-done.10
  104.3 0.8 fusion.18
  105.1 0.0 collective-permute-done.2
  105.1 0.4 copy-done.8
  105.5 3.0 %fusion.1 = bf16[128,512]{1,0:T(8,128)(2,1)S(1)} fusion(f32[128,512]{1,0:T(8,128)S(1)} %fusion.18, bf16[128,4096]{0,1:T(8,128)(2,1)S(1)} %bitcast.77, bf16[4096,512]{1,0:T(8,128)(2,1)} %collective-permute-done.2), kind=kOutput, calls=%fused_computation.9 | convolution fusion | flops 537001984 | bytes 5636096 | tf_op jit(solution)/shard_map/dot_general | solution.py:188
  108.5 1.5 collective-permute-start.3
  110.1 3.7 %convolution_convert_fusion = bf16[128,4096]{1,0:T(8,128)(2,1)S(1)} fusion(bf16[128,512]{1,0:T(8,128)(2,1)S(1)} %copy-done.11, bf16[4096,512]{1,0:T(8,128)(2,1)} %collective-permute-done.2), kind=kOutput, calls=%fused_computation.2 | convolution fusion | flops 537395200 | bytes 5373952 | tf_op jit(solution)/shard_map/dot_general | solution.py:194
  113.8 0.2 copy.34
  114.0 0.3 maximum_select_fusion
  114.4 4.6 %copy.28 = bf16[128,16,2,256]{3,2,1,0:T(2,128)(2,1)} copy(bf16[128,16,2,256]{3,1,0,2:T(8,128)(2,1)S(1)} %maximum_select_fusion) | data formatting | bytes 4194304 | tf_op jit(solution)/shard_map/jit(_where)/select_n | solution.py:197
  119.0 4.6 %select_n.75 = bf16[128,8192]{1,0:T(8,128)(2,1)} reshape(bf16[128,16,2,256]{3,2,1,0:T(2,128)(2,1)} %copy.28) | data formatting | bytes 4194304 | tf_op jit(solution)/shard_map/jit(_where)/select_n | solution.py:197
  123.6 0.0 collective-permute-done.3
  123.6 0.6 gather_fusion.1
  124.2 0.1 broadcast_select_fusion
  124.3 23.6 %shard_map.103 = (bf16[128,4096]{1,0:T(8,128)(2,1)}, f32[256,512]{1,0:T(8,128)S(1)}) custom-call(s32[32]{0:T(128)S(1)} %shift-right-logical_xor_fusion.seeds_ref, s32[1]{0:T(128)} %bitcast.offset_ref, s32[128,1]{1,0:T(8,128)S(1)} %copy.25.pos_ref, bf16[128,4096]{1,0:T(8,128)(2,1)S(1)} %bitcast.61, bf16[128,4096]{1,0:T(8,128)(2,1)S(1)} %bitcast.63, ...), custom_call_target="tpu_custom_call" | custom-call | tf_op jit(solution)/shard_map/pallas_call | solution.py:108
  147.9 0.7 collective-permute-start.4
  148.6 7.5 %collective-permute-done.4 = f32[128,512]{1,0:T(8,128)S(1)} collective-permute-done((f32[128,512]{1,0:T(8,128)S(1)}, f32[128,512]{1,0:T(8,128)S(1)}, u32[]{:S(2)}, u32[]{:S(2)}) %collective-permute-start.4) | collective-permute-done | bytes 262176 | tf_op jit(solution)/shard_map/ppermute | solution.py:140
  156.0 0.7 fusion.8
  156.7 0.9 all-to-all-done
  157.7 0.3 collective-permute-start.5
  158.0 1.7 constant_dynamic-slice_fusion
  159.7 1.3 copy.31
  161.0 1.3 copy.32
  162.4 0.0 copy-done.7
  162.4 0.5 fusion.3
  162.8 0.5 fusion.6
  163.3 0.0 collective-permute-done.5
  163.3 0.2 copy-done.9
  163.6 1.7 fusion
  165.3 1.5 collective-permute-start.6
  166.8 1.7 convolution_add_fusion.1
  168.5 5.2 %collective-permute-done.6 = bf16[256,512]{1,0:T(8,128)(2,1)S(1)} collective-permute-done((bf16[256,512]{1,0:T(8,128)(2,1)S(1)}, bf16[256,512]{1,0:T(8,128)(2,1)S(1)}, u32[]{:S(2)}, u32[]{:S(2)}) %collective-permute-start.6) | collective-permute-done | bytes 262176 | tf_op jit(solution)/shard_map/ppermute | solution.py:237
  173.8 0.8 multiply_convert_fusion
  (20 shorter events, 0.1 us)
Async XLA Ops:
  8.0 3.1 %copy-start = (s32[1,256]{1,0:T(1,128)S(1)}, s32[1,256]{1,0:T(1,128)}, u32[]{:S(2)}) copy-start(s32[1,256]{1,0:T(1,128)} %param.13) | copy-start | bytes 3076
  8.0 7.9 %copy-start.1 = (bf16[1,128,4096]{2,1,0:T(8,128)(2,1)S(1)}, bf16[1,128,4096]{2,1,0:T(8,128)(2,1)}, u32[]{:S(2)}) copy-start(bf16[1,128,4096]{2,1,0:T(8,128)(2,1)} %param.10) | copy-start | bytes 3145732
  8.0 81.6 %all-gather.5.cloned.1.call-start = ((), (), s32[]{:S(2)}) async-start(), calls=%async_computation.2 | async-start | bytes 4456448 | tf_op jit(solution)/shard_map/all_gather | solution.py:158
  8.8 5.5 %collective-permute-start = (bf16[128,512]{1,0:T(8,128)(2,1)}, bf16[128,512]{1,0:T(8,128)(2,1)S(1)}, u32[]{:S(2)}, u32[]{:S(2)}) collective-permute-start(bf16[128,512]{1,0:T(8,128)(2,1)} %bitcast.85), channel_id=1, source_target_pairs={{0,16},{16,0},{1,17},{17,1},{2,18},{18,2},{3,19},{19,3},{4,20},{20... | collective-permute-start | bytes 393224 | tf_op jit(solution)/shard_map/ppermute | solution.py:128
  15.9 1.2 copy-start.2
  36.7 11.0 %collective-permute-start.1 = (f32[128,512]{1,0:T(8,128)S(1)}, f32[128,512]{1,0:T(8,128)S(1)}, u32[]{:S(2)}, u32[]{:S(2)}) collective-permute-start(f32[128,512]{1,0:T(8,128)S(1)} %dynamic-slice_bitcast_fusion.1), channel_id=1, source_target_pairs={{0,16},{16,0},{1,17},{17,1},{2,18},{18,2},{3,19},{19,3},{4,20},{20... | collective-permute-start | bytes 786440 | tf_op jit(solution)/shard_map/ppermute | solution.py:140
  89.6 15.5 %collective-permute-start.2 = (bf16[4096,512]{1,0:T(8,128)(2,1)}, bf16[4096,512]{1,0:T(8,128)(2,1)}, u32[]{:S(2)}, u32[]{:S(2)}) collective-permute-start(bf16[4096,512]{1,0:T(8,128)(2,1)} %all-gather.5.cloned.1.call-done), channel_id=1, source_target_pairs={{0,1},{1,0},{2,3},{3,2},{4,5},{5,4},{6,7},{7,6},{8,9},{9,8},{10,11... | collective-permute-start | bytes 12582920 | tf_op jit(solution)/shard_map/ppermute | solution.py:178
  92.7 5.0 %copy-start.4 = (bf16[1,128,8192]{1,2,0:T(8,128)(2,1)S(1)}, bf16[1,128,8192]{1,2,0:T(8,128)(2,1)}, u32[]{:S(2)}) copy-start(bf16[1,128,8192]{1,2,0:T(8,128)(2,1)} %copy.26) | copy-start | bytes 6291460
  92.7 64.9 %all-to-all-start = ((bf16[128,2,16,256]{0,3,1,2:T(8,128)(2,1)}), bf16[128,2,16,256]{0,3,1,2:T(8,128)(2,1)}, u32[]{:S(2)}, u32[]{:S(2)}) async-start(bf16[128,2,16,256]{0,3,1,2:T(8,128)(2,1)} %copy.27), calls=%async_computation | async-start | bytes 4194304 | tf_op jit(solution)/shard_map/all_to_all | solution.py:179
  97.6 59.1 %all-gather.3.cloned.1.call-start = ((), (), s32[]{:S(2)}) async-start(), calls=%async_computation.1 | async-start | bytes 1179648 | tf_op jit(solution)/shard_map/all_gather | solution.py:174
  99.2 4.2 %copy-start.5 = (bf16[4096,512]{1,0:T(8,128)(2,1)S(1)}, bf16[4096,512]{1,0:T(8,128)(2,1)}, u32[]{:S(2)}) copy-start(bf16[4096,512]{1,0:T(8,128)(2,1)} %all-gather.5.cloned.1.call-done) | copy-start | bytes 12582916
  103.1 1.2 copy-start.10
  104.3 1.2 copy-start.8
  105.5 4.5 %copy-start.11 = (bf16[128,512]{1,0:T(8,128)(2,1)S(1)}, bf16[128,512]{1,0:T(8,128)(2,1)}, u32[]{:S(2)}) copy-start(bf16[128,512]{1,0:T(8,128)(2,1)} %fusion.9) | copy-start | bytes 393220
  108.5 15.0 %collective-permute-start.3 = (bf16[128,512]{1,0:T(8,128)(2,1)S(1)}, bf16[128,512]{1,0:T(8,128)(2,1)S(1)}, u32[]{:S(2)}, u32[]{:S(2)}) collective-permute-start(bf16[128,512]{1,0:T(8,128)(2,1)S(1)} %fusion.1), channel_id=1, source_target_pairs={{0,16},{16,0},{1,17},{17,1},{2,18},{18,2},{3,19},{19,3},{4,20},{20... | collective-permute-start | bytes 393224 | tf_op jit(solution)/shard_map/ppermute | solution.py:128
  119.0 5.3 %copy-start.3 = (bf16[1,128,4096]{2,1,0:T(8,128)(2,1)S(1)}, bf16[1,128,4096]{2,1,0:T(8,128)(2,1)}, u32[]{:S(2)}) copy-start(bf16[1,128,4096]{2,1,0:T(8,128)(2,1)} %param.12) | copy-start | bytes 3145732
  147.9 8.2 %collective-permute-start.4 = (f32[128,512]{1,0:T(8,128)S(1)}, f32[128,512]{1,0:T(8,128)S(1)}, u32[]{:S(2)}, u32[]{:S(2)}) collective-permute-start(f32[128,512]{1,0:T(8,128)S(1)} %dynamic-slice_bitcast_fusion), channel_id=1, source_target_pairs={{0,16},{16,0},{1,17},{17,1},{2,18},{18,2},{3,19},{19,3},{4,20},{20... | collective-permute-start | bytes 786440 | tf_op jit(solution)/shard_map/ppermute | solution.py:140
  157.7 5.7 %collective-permute-start.5 = (bf16[1024,512]{1,0:T(8,128)(2,1)}, bf16[1024,512]{1,0:T(8,128)(2,1)}, u32[]{:S(2)}, u32[]{:S(2)}) collective-permute-start(bf16[1024,512]{1,0:T(8,128)(2,1)} %all-gather.3.cloned.1.call-done), channel_id=1, source_target_pairs={{0,1},{1,0},{2,3},{3,2},{4,5},{5,4},{6,7},{7,6},{8,9},{9,8},{10,11... | collective-permute-start | bytes 3145736 | tf_op jit(solution)/shard_map/ppermute | solution.py:210
  159.7 2.7 %copy-start.6 = (bf16[1024,512]{1,0:T(8,128)(2,1)S(1)}, bf16[1024,512]{1,0:T(8,128)(2,1)}, u32[]{:S(2)}) copy-start(bf16[1024,512]{1,0:T(8,128)(2,1)} %all-gather.3.cloned.1.call-done) | copy-start | bytes 3145732
  161.0 1.3 copy-start.7
  162.4 1.2 copy-start.9
  165.3 8.5 %collective-permute-start.6 = (bf16[256,512]{1,0:T(8,128)(2,1)S(1)}, bf16[256,512]{1,0:T(8,128)(2,1)S(1)}, u32[]{:S(2)}, u32[]{:S(2)}) collective-permute-start(bf16[256,512]{1,0:T(8,128)(2,1)S(1)} %fusion), channel_id=1, source_target_pairs={{0,16},{16,0},{1,17},{17,1},{2,18},{18,2},{3,19},{19,3},{4,20},{20... | collective-permute-start | bytes 786440 | tf_op jit(solution)/shard_map/ppermute | solution.py:237
Sparse Core Ops, SparseCore 0:
  11.7 77.8 all-gather.4
Sparse Core Ops, SparseCore 1:
  100.8 55.7 all-gather.2

commit v15 on v13

--- a/solution.py
+++ b/solution.py
@@ -172,16 +172,15 @@
     (dv,) = attention(seeds, offset, pos, query_loc, grad_loc, key_full, None)
     value_grad = reduce_seq(dv, seq_index, seq_devices).astype(jnp.bfloat16)
     grads_own = lax.all_gather(value_grad, "zx", axis=0, tiled=True)
+    input_major = jnp.transpose(
+        local_input.reshape(tok_rows, seq_devices, fsdp_devices, block_rows), (2, 0, 1, 3)
+    )
     value_grad, weight_own, input_late = lax.optimization_barrier(
-        (value_grad, weight_own, local_input)
+        (value_grad, weight_own, input_major)
     )
     weight_other = lax.ppermute(weight_own, "core", swap)
     input_cols = lax.all_to_all(
-        input_late.reshape(tok_rows, seq_devices, fsdp_devices, block_rows),
-        FSDP,
-        split_axis=2,
-        concat_axis=0,
-        tiled=True,
+        input_late, FSDP, split_axis=0, concat_axis=0, tiled=True
     ).reshape(zx_devices, 2, tok_rows, seq_devices * block_rows)
     values_loc = (
         jnp.dot(input_own, weight_own, preferred_element_type=jnp.float32)

time: 184 us -> 184 us (level)
    optimization_barrier x0 -> x1, local copies, waits for them, and re-layouts: none -> 3.16 us  [per_device(): lax.optimization_barrier((value_grad, weight_own, input_major))]
    reshape x1 -> x0, local copies, waits for them, and re-layouts: 3.16 us -> none  [per_device(): input_late.reshape(tok_rows, seq_devices, fsdp_devices, block_rows)]
where the time goes in v15:
time: 184 us; the launch traced here: 181 us
  waiting for transfers between devices  65.4 us (36%)
  Pallas kernels  43.1 us (23%)
  local copies, waits for them, and re-layouts  25.1 us (14%)
  between operations  16.4 us (9%)
  matrix products  15.3 us (8%)
  starting transfers between devices  12.2 us (7%)
  other arithmetic  3.7 us (2%)
    pallas_call x2, Pallas kernels, attention(): pl.pallas_call(kernel, grid_spec=pltpu.PrefetchScalarGridSpec(num_scalar_...  43.1 us
    all_gather x1, waiting for transfers between devices, per_device(): weight_own = lax.all_gather(value_weight, ('seq', 'zx'), axis=0, tiled=True)  40.9 us
    ppermute x2, waiting for transfers between devices, reduce_seq(): lax.ppermute(piece, 'seq', [(i, (i + shift) % seq_devices) for i in range...  12.8 us
    select_n x2, local copies, waits for them, and re-layouts, per_device(): jnp.where(core_index == 0, jnp.concatenate([grad_own, grad_other], axis=2...  9.18 us
    unnamed x21, local copies, waits for them, and re-layouts  7.19 us
    ppermute x1, waiting for transfers between devices, per_device(): lax.ppermute(piece.astype(jnp.bfloat16), 'seq', [(i, (i + shift) % seq_de...  6.95 us
    all_to_all x1, starting transfers between devices, per_device(): lax.all_to_all(input_late, FSDP, split_axis=0, concat_axis=0, tiled=True)  4.9 us
    dot_general x1, matrix products, per_device(): lax.dot_general(value_grad, weight_own, last_dims, preferred_element_type...  3.88 us
  transfers between devices with their start and end apart: 10, of which 6 were waited for; matrix products, arithmetic and copies ran while one was open for 21% of the time, Pallas kernels for 24%

profile of v15, /device:TPU:10, one launch (start us, length us, event | category | flops | bytes accessed | tf_op | source)
XLA Modules:
  0.0 181.2 jit_solution(732446707715072297)
XLA Ops:
  8.0 0.0 copy-start
  8.0 0.0 copy-start.1
  8.0 0.0 all-gather.5.cloned.1.call-start
  8.1 0.7 all-gather.5.cloned.1.call-update
  8.8 1.6 collective-permute-start
  11.1 0.0 copy-done
  11.1 0.1 copy.25.pos_ref
  11.2 3.0 %collective-permute-done = bf16[128,512]{1,0:T(8,128)(2,1)S(1)} collective-permute-done((bf16[128,512]{1,0:T(8,128)(2,1)}, bf16[128,512]{1,0:T(8,128)(2,1)S(1)}, u32[]{:S(2)}, u32[]{:S(2)}) %collective-permute-start) | collective-permute-done | bytes 131104 | tf_op jit(solution)/shard_map/ppermute | solution.py:128
  14.3 0.9 pad_maximum_fusion
  15.2 0.6 gather_fusion
  15.8 0.1 broadcast_select_fusion.1
  15.9 0.0 copy-done.1
  15.9 0.0 copy-start.2
  15.9 1.2 copy-done.2
  17.1 19.6 %shard_map.102 = f32[256,512]{1,0:T(8,128)S(1)} custom-call(s32[32]{0:T(128)S(1)} %shift-right-logical_xor_fusion.seeds_ref, s32[1]{0:T(128)} %bitcast.offset_ref, s32[128,1]{1,0:T(8,128)S(1)} %copy.25.pos_ref, bf16[128,4096]{1,0:T(8,128)(2,1)S(1)} %bitcast.66, bf16[128,4096]{1,0:T(8,128)(2,1)S(1)} %bitcast.68, bf16[256,512]{1,0:T(8,128)(2,1)S(1)} %bitcast.70), custom_call_target="tpu_custom_call" | custom-call | tf_op jit(solution)/shard_map/pallas_call | solution.py:108
  36.7 1.6 collective-permute-start.1
  38.3 4.1 %copy.26 = bf16[1,128,8192]{1,2,0:T(8,128)(2,1)} copy(bf16[1,128,8192]{2,1,0:T(8,128)(2,1)} %param.9) | data formatting | bytes 4194304 | tf_op args[0]
  42.4 5.4 %collective-permute-done.1 = f32[128,512]{1,0:T(8,128)S(1)} collective-permute-done((f32[128,512]{1,0:T(8,128)S(1)}, f32[128,512]{1,0:T(8,128)S(1)}, u32[]{:S(2)}, u32[]{:S(2)}) %collective-permute-start.1) | collective-permute-done | bytes 262176 | tf_op jit(solution)/shard_map/ppermute | solution.py:140
  47.7 0.7 fusion.5
  48.4 40.9 %all-gather.5.cloned.1.call-done = bf16[4096,512]{1,0:T(8,128)(2,1)} async-done(((bf16[256,512]{1,0:T(8,128)(2,1)}), bf16[4096,512]{1,0:T(8,128)(2,1)}) %all-gather.5.cloned.1.call-update) | async-done | bytes 4194320 | tf_op jit(solution)/shard_map/all_gather | solution.py:158
  89.4 0.0 collective-permute-start.2
  89.4 3.2 %copy.27 = bf16[16,128,2,256]{1,3,2,0:T(8,128)(2,1)} copy(bf16[16,128,2,256]{1,3,0,2:T(8,128)(2,1)} %bitcast.77) | data formatting | bytes 4194304 | tf_op jit(solution)/shard_map/optimization_barrier | solution.py:178
  92.5 0.0 copy-start.4
  92.5 4.9 %all-to-all-start = ((bf16[16,128,2,256]{1,3,2,0:T(8,128)(2,1)}), bf16[16,128,2,256]{1,3,2,0:T(8,128)(2,1)}, u32[]{:S(2)}, u32[]{:S(2)}) async-start(bf16[16,128,2,256]{1,3,2,0:T(8,128)(2,1)} %copy.27), calls=%async_computation | async-start | bytes 4194304 | tf_op jit(solution)/shard_map/all_to_all | solution.py:182
  97.4 0.0 all-gather.3.cloned.1.call-start
  97.5 0.0 copy-done.4
  97.5 1.5 constant_dynamic-slice_fusion.2
  99.0 0.0 all-gather.3.cloned.1.call-update
  99.0 0.0 copy-start.5
  99.0 3.9 %convolution_convert_fusion.1 = bf16[128,4096]{1,0:T(8,128)(2,1)S(1)} fusion(bf16[128,512]{1,0:T(8,128)(2,1)} %fusion.5, bf16[4096,512]{1,0:T(8,128)(2,1)} %all-gather.5.cloned.1.call-done), kind=kOutput, calls=%fused_computation.3 | convolution fusion | flops 537395200 | bytes 5373952 | tf_op jit(solution)/shard_map/dot_general | solution.py:190
  102.9 0.0 copy-start.7
  102.9 0.2 copy.33
  103.1 0.0 copy-done.5
  103.2 0.9 copy-done.7
  104.1 0.8 fusion.10
  104.9 0.0 collective-permute-done.2
  104.9 0.4 copy-done.6
  105.3 3.0 %fusion = bf16[128,512]{1,0:T(8,128)(2,1)S(1)} fusion(f32[128,512]{1,0:T(8,128)S(1)} %fusion.10, bf16[128,4096]{0,1:T(8,128)(2,1)S(1)} %bitcast.81, bf16[4096,512]{1,0:T(8,128)(2,1)} %collective-permute-done.2), kind=kOutput, calls=%fused_computation.7 | convolution fusion | flops 537001984 | bytes 5636096 | tf_op jit(solution)/shard_map/dot_general | solution.py:187
  108.3 1.5 collective-permute-start.3
  109.9 0.0 copy-done.8
  109.9 3.7 %convolution_convert_fusion = bf16[128,4096]{1,0:T(8,128)(2,1)S(1)} fusion(bf16[128,512]{1,0:T(8,128)(2,1)S(1)} %copy-done.8, bf16[4096,512]{1,0:T(8,128)(2,1)} %collective-permute-done.2), kind=kOutput, calls=%fused_computation.2 | convolution fusion | flops 537395200 | bytes 5373952 | tf_op jit(solution)/shard_map/dot_general | solution.py:193
  113.6 0.2 copy.34
  113.8 0.3 maximum_select_fusion
  114.2 4.6 %copy.28 = bf16[128,16,2,256]{3,2,1,0:T(2,128)(2,1)} copy(bf16[128,16,2,256]{3,1,0,2:T(8,128)(2,1)S(1)} %maximum_select_fusion) | data formatting | bytes 4194304 | tf_op jit(solution)/shard_map/jit(_where)/select_n | solution.py:196
  118.8 4.6 %select_n.70 = bf16[128,8192]{1,0:T(8,128)(2,1)} reshape(bf16[128,16,2,256]{3,2,1,0:T(2,128)(2,1)} %copy.28) | data formatting | bytes 4194304 | tf_op jit(solution)/shard_map/jit(_where)/select_n | solution.py:196
  123.4 0.0 collective-permute-done.3
  123.4 0.6 gather_fusion.1
  124.0 0.1 broadcast_select_fusion
  124.1 0.0 copy-done.3
  124.1 23.6 %shard_map.103 = (bf16[128,4096]{1,0:T(8,128)(2,1)}, f32[256,512]{1,0:T(8,128)S(1)}) custom-call(s32[32]{0:T(128)S(1)} %shift-right-logical_xor_fusion.seeds_ref, s32[1]{0:T(128)} %bitcast.offset_ref, s32[128,1]{1,0:T(8,128)S(1)} %copy.25.pos_ref, bf16[128,4096]{1,0:T(8,128)(2,1)S(1)} %bitcast.67, bf16[128,4096]{1,0:T(8,128)(2,1)S(1)} %bitcast.69, ...), custom_call_target="tpu_custom_call" | custom-call | tf_op jit(solution)/shard_map/pallas_call | solution.py:108
  147.7 0.7 collective-permute-start.4
  148.4 7.5 %collective-permute-done.4 = f32[128,512]{1,0:T(8,128)S(1)} collective-permute-done((f32[128,512]{1,0:T(8,128)S(1)}, f32[128,512]{1,0:T(8,128)S(1)}, u32[]{:S(2)}, u32[]{:S(2)}) %collective-permute-start.4) | collective-permute-done | bytes 262176 | tf_op jit(solution)/shard_map/ppermute | solution.py:140
  155.9 0.7 fusion.4
  156.6 0.9 all-to-all-done
  157.5 0.3 collective-permute-start.5
  157.8 1.7 constant_dynamic-slice_fusion
  159.4 0.5 copy.31
  160.0 0.5 copy.32
  160.5 2.0 %fusion.11 = f32[512,512]{1,0:T(8,128)S(1)} fusion(bf16[1024,512]{1,0:T(8,128)(2,1)S(1)} %bitcast.87, bf16[1024,512]{1,0:T(8,128)(2,1)} %all-gather.3.cloned.1.call-done), kind=kOutput, calls=%fused_computation.42 | convolution fusion | flops 536870912 | bytes 3145728 | tf_op jit(solution)/shard_map/dot_general | solution.py:218
  162.5 0.0 collective-permute-done.5
  162.5 2.0 %convolution_add_fusion = f32[512,512]{1,0:T(8,128)S(1)} fusion(f32[512,512]{1,0:T(8,128)S(1)} %fusion.11, bf16[1024,512]{1,0:T(8,128)(2,1)S(1)} %bitcast.86, bf16[1024,512]{1,0:T(8,128)(2,1)} %collective-permute-done.5), kind=kOutput, calls=%fused_computation.5 | convolution fusion | flops 537133056 | bytes 4194304 | tf_op jit(solution)/shard_map/dot_general | solution.py:219
  164.5 1.5 collective-permute-start.6
  166.0 7.0 %collective-permute-done.6 = bf16[256,512]{1,0:T(8,128)(2,1)S(1)} collective-permute-done((bf16[256,512]{1,0:T(8,128)(2,1)S(1)}, bf16[256,512]{1,0:T(8,128)(2,1)S(1)}, u32[]{:S(2)}, u32[]{:S(2)}) %collective-permute-start.6) | collective-permute-done | bytes 262176 | tf_op jit(solution)/shard_map/ppermute | solution.py:226
  173.0 0.8 fusion.2
  (13 shorter events, 0.2 us)
Async XLA Ops:
  8.0 3.1 %copy-start = (s32[1,256]{1,0:T(1,128)S(1)}, s32[1,256]{1,0:T(1,128)}, u32[]{:S(2)}) copy-start(s32[1,256]{1,0:T(1,128)} %param.13) | copy-start | bytes 3076
  8.0 7.9 %copy-start.1 = (bf16[1,128,4096]{2,1,0:T(8,128)(2,1)S(1)}, bf16[1,128,4096]{2,1,0:T(8,128)(2,1)}, u32[]{:S(2)}) copy-start(bf16[1,128,4096]{2,1,0:T(8,128)(2,1)} %param.10) | copy-start | bytes 3145732
  8.0 81.3 %all-gather.5.cloned.1.call-start = ((), (), s32[]{:S(2)}) async-start(), calls=%async_computation.2 | async-start | bytes 4456448 | tf_op jit(solution)/shard_map/all_gather | solution.py:158
  8.8 5.5 %collective-permute-start = (bf16[128,512]{1,0:T(8,128)(2,1)}, bf16[128,512]{1,0:T(8,128)(2,1)S(1)}, u32[]{:S(2)}, u32[]{:S(2)}) collective-permute-start(bf16[128,512]{1,0:T(8,128)(2,1)} %bitcast.91), channel_id=1, source_target_pairs={{0,16},{16,0},{1,17},{17,1},{2,18},{18,2},{3,19},{19,3},{4,20},{20... | collective-permute-start | bytes 393224 | tf_op jit(solution)/shard_map/ppermute | solution.py:128
  15.9 1.2 copy-start.2
  36.7 11.0 %collective-permute-start.1 = (f32[128,512]{1,0:T(8,128)S(1)}, f32[128,512]{1,0:T(8,128)S(1)}, u32[]{:S(2)}, u32[]{:S(2)}) collective-permute-start(f32[128,512]{1,0:T(8,128)S(1)} %dynamic-slice_bitcast_fusion.1), channel_id=1, source_target_pairs={{0,16},{16,0},{1,17},{17,1},{2,18},{18,2},{3,19},{19,3},{4,20},{20... | collective-permute-start | bytes 786440 | tf_op jit(solution)/shard_map/ppermute | solution.py:140
  89.4 15.5 %collective-permute-start.2 = (bf16[4096,512]{1,0:T(8,128)(2,1)}, bf16[4096,512]{1,0:T(8,128)(2,1)}, u32[]{:S(2)}, u32[]{:S(2)}) collective-permute-start(bf16[4096,512]{1,0:T(8,128)(2,1)} %all-gather.5.cloned.1.call-done), channel_id=1, source_target_pairs={{0,1},{1,0},{2,3},{3,2},{4,5},{5,4},{6,7},{7,6},{8,9},{9,8},{10,11... | collective-permute-start | bytes 12582920 | tf_op jit(solution)/shard_map/ppermute | solution.py:181
  92.5 5.0 %copy-start.4 = (bf16[1,128,8192]{1,2,0:T(8,128)(2,1)S(1)}, bf16[1,128,8192]{1,2,0:T(8,128)(2,1)}, u32[]{:S(2)}) copy-start(bf16[1,128,8192]{1,2,0:T(8,128)(2,1)} %copy.26) | copy-start | bytes 6291460
  92.5 64.9 %all-to-all-start = ((bf16[16,128,2,256]{1,3,2,0:T(8,128)(2,1)}), bf16[16,128,2,256]{1,3,2,0:T(8,128)(2,1)}, u32[]{:S(2)}, u32[]{:S(2)}) async-start(bf16[16,128,2,256]{1,3,2,0:T(8,128)(2,1)} %copy.27), calls=%async_computation | async-start | bytes 4194304 | tf_op jit(solution)/shard_map/all_to_all | solution.py:182
  97.4 59.1 %all-gather.3.cloned.1.call-start = ((), (), s32[]{:S(2)}) async-start(), calls=%async_computation.1 | async-start | bytes 1179648 | tf_op jit(solution)/shard_map/all_gather | solution.py:174
  99.0 4.2 %copy-start.5 = (bf16[4096,512]{1,0:T(8,128)(2,1)S(1)}, bf16[4096,512]{1,0:T(8,128)(2,1)}, u32[]{:S(2)}) copy-start(bf16[4096,512]{1,0:T(8,128)(2,1)} %all-gather.5.cloned.1.call-done) | copy-start | bytes 12582916
  102.9 1.2 copy-start.7
  104.1 1.2 copy-start.6
  105.3 4.6 %copy-start.8 = (bf16[128,512]{1,0:T(8,128)(2,1)S(1)}, bf16[128,512]{1,0:T(8,128)(2,1)}, u32[]{:S(2)}) copy-start(bf16[128,512]{1,0:T(8,128)(2,1)} %fusion.5) | copy-start | bytes 393220
  108.3 15.0 %collective-permute-start.3 = (bf16[128,512]{1,0:T(8,128)(2,1)S(1)}, bf16[128,512]{1,0:T(8,128)(2,1)S(1)}, u32[]{:S(2)}, u32[]{:S(2)}) collective-permute-start(bf16[128,512]{1,0:T(8,128)(2,1)S(1)} %fusion), channel_id=1, source_target_pairs={{0,16},{16,0},{1,17},{17,1},{2,18},{18,2},{3,19},{19,3},{4,20},{20... | collective-permute-start | bytes 393224 | tf_op jit(solution)/shard_map/ppermute | solution.py:128
  118.8 5.3 %copy-start.3 = (bf16[1,128,4096]{2,1,0:T(8,128)(2,1)S(1)}, bf16[1,128,4096]{2,1,0:T(8,128)(2,1)}, u32[]{:S(2)}) copy-start(bf16[1,128,4096]{2,1,0:T(8,128)(2,1)} %param.12) | copy-start | bytes 3145732
  147.7 8.2 %collective-permute-start.4 = (f32[128,512]{1,0:T(8,128)S(1)}, f32[128,512]{1,0:T(8,128)S(1)}, u32[]{:S(2)}, u32[]{:S(2)}) collective-permute-start(f32[128,512]{1,0:T(8,128)S(1)} %dynamic-slice_bitcast_fusion), channel_id=1, source_target_pairs={{0,16},{16,0},{1,17},{17,1},{2,18},{18,2},{3,19},{19,3},{4,20},{20... | collective-permute-start | bytes 786440 | tf_op jit(solution)/shard_map/ppermute | solution.py:140
  157.5 5.0 %collective-permute-start.5 = (bf16[1024,512]{1,0:T(8,128)(2,1)}, bf16[1024,512]{1,0:T(8,128)(2,1)}, u32[]{:S(2)}, u32[]{:S(2)}) collective-permute-start(bf16[1024,512]{1,0:T(8,128)(2,1)} %all-gather.3.cloned.1.call-done), channel_id=1, source_target_pairs={{0,1},{1,0},{2,3},{3,2},{4,5},{5,4},{6,7},{7,6},{8,9},{9,8},{10,11... | collective-permute-start | bytes 3145736 | tf_op jit(solution)/shard_map/ppermute | solution.py:209
  164.5 8.5 %collective-permute-start.6 = (bf16[256,512]{1,0:T(8,128)(2,1)S(1)}, bf16[256,512]{1,0:T(8,128)(2,1)S(1)}, u32[]{:S(2)}, u32[]{:S(2)}) collective-permute-start(bf16[256,512]{1,0:T(8,128)(2,1)S(1)} %fusion.3), channel_id=1, source_target_pairs={{0,16},{16,0},{1,17},{17,1},{2,18},{18,2},{3,19},{19,3},{4,20},{20... | collective-permute-start | bytes 786440 | tf_op jit(solution)/shard_map/ppermute | solution.py:226
Sparse Core Ops, SparseCore 0:
  11.7 77.6 all-gather.4
Sparse Core Ops, SparseCore 1:
  100.6 55.7 all-gather.2

commit v16 on v13

--- a/solution.py
+++ b/solution.py
@@ -155,8 +155,10 @@
     local_input = layer_input[0]
     block_rows = value_weight.shape[0]
     swap = [(0, 1), (1, 0)]
-    weight_own = lax.all_gather(value_weight, ("seq", "zx"), axis=0, tiled=True)
-    input_view = local_input.reshape(tok_rows, seq_devices * zx_devices, 2, block_rows)
+    weight_own = lax.all_gather(value_weight, ("zx", "seq"), axis=0, tiled=True)
+    input_view = jnp.transpose(
+        local_input.reshape(tok_rows, seq_devices, zx_devices, 2, block_rows), (0, 2, 1, 3, 4)
+    ).reshape(tok_rows, zx_devices * seq_devices, 2, block_rows)
     input_own = lax.dynamic_index_in_dim(input_view, core_index, 2, keepdims=False).reshape(
         tok_rows, -1
     )
@@ -198,7 +200,8 @@
         core_index == 0,
         jnp.concatenate([grad_own, grad_other], axis=2),
         jnp.concatenate([grad_other, grad_own], axis=2),
-    ).reshape(tok_rows, -1)
+    ).reshape(tok_rows, zx_devices, seq_devices, 2, block_rows)
+    input_grad = jnp.transpose(input_grad, (0, 2, 1, 3, 4)).reshape(tok_rows, -1)
     value_full = gather_seq(values_loc, seq_index, seq_devices)
     input_grad, value_full = lax.optimization_barrier((input_grad, value_full))
     dq, dk = attention(seeds, offset, pos, query_loc, grad_loc, key_full, value_full)

time: 184 us -> 198 us (1.076)
  local copies, waits for them, and re-layouts: 25.1 us -> 32 us
  matrix products: 15.3 us -> 20.2 us
  other arithmetic: 3.7 us -> 7.42 us
    select_n x2 -> x0, local copies, waits for them, and re-layouts: 9.18 us -> none  [per_device(): jnp.where(core_index == 0, jnp.concatenate([grad_own, grad_other], axis=2...]
    transpose x0 -> x2, local copies, waits for them, and re-layouts: none -> 7.62 us  [the longest x1 5.03 us: per_device(): jnp.transpose(input_grad, (0, 2, 1, 3, 4)).reshape(tok_rows, -1)]
    reshape x0 -> x1, local copies, waits for them, and re-layouts: none -> 4.55 us  [per_device(): jnp.transpose(input_grad, (0, 2, 1, 3, 4)).reshape(tok_rows, -1)]
    concatenate x0 -> x2, local copies, waits for them, and re-layouts: none -> 3.66 us  [per_device(): jnp.concatenate([grad_own, grad_other], axis=2)]
    transpose x0 -> x1, other arithmetic: none -> 3.1 us  [per_device(): jnp.transpose(input_grad, (0, 2, 1, 3, 4)).reshape(tok_rows, -1)]
    dot_general x1, matrix products: 0.78 us -> 3.3 us  [per_device(): jnp.dot(input_own, weight_own, preferred_element_type=jnp.float32)]
    unnamed x21 -> x13, local copies, waits for them, and re-layouts: 7.19 us -> 5.31 us
  transfers between devices with their start and end apart: 10 -> 10, of which waited for: 6 -> 5; matrix products, arithmetic and copies ran while one was open for 21% -> 28% of each run, Pallas kernels for 24% -> 22%
where the time goes in v16:
time: 198 us; the launch traced here: 196 us
  waiting for transfers between devices  65.9 us (33%)
  Pallas kernels  43.1 us (22%)
  local copies, waits for them, and re-layouts  32 us (16%)
  matrix products  20.2 us (10%)
  between operations  16.4 us (8%)
  starting transfers between devices  10.9 us (6%)
  other arithmetic  7.42 us (4%)
    pallas_call x2, Pallas kernels, attention(): pl.pallas_call(kernel, grid_spec=pltpu.PrefetchScalarGridSpec(num_scalar_...  43.1 us
    all_gather x1, waiting for transfers between devices, per_device(): weight_own = lax.all_gather(value_weight, ('zx', 'seq'), axis=0, tiled=True)  41.2 us
    ppermute x2, waiting for transfers between devices, reduce_seq(): lax.ppermute(piece, 'seq', [(i, (i + shift) % seq_devices) for i in range...  12.9 us
    ppermute x1, waiting for transfers between devices, per_device(): lax.ppermute(piece.astype(jnp.bfloat16), 'seq', [(i, (i + shift) % seq_de...  8.13 us
    unnamed x13, local copies, waits for them, and re-layouts  5.31 us
    transpose x1, local copies, waits for them, and re-layouts, per_device(): jnp.transpose(input_grad, (0, 2, 1, 3, 4)).reshape(tok_rows, -1)  5.03 us
    all_to_all x1, starting transfers between devices, per_device(): lax.all_to_all(input_late.reshape(tok_rows, seq_devices, fsdp_devices, bl...  4.9 us
    dot_general x1, matrix products, per_device(): lax.dot_general(value_grad, weight_own, last_dims, preferred_element_type...  4.72 us
  transfers between devices with their start and end apart: 10, of which 5 were waited for; matrix products, arithmetic and copies ran while one was open for 28% of the time, Pallas kernels for 22%

profile of v16, /device:TPU:10, one launch (start us, length us, event | category | flops | bytes accessed | tf_op | source)
XLA Modules:
  0.0 196.0 jit_solution(17980266438030360833)
XLA Ops:
  8.0 0.0 copy-start
  8.0 0.0 copy-start.1
  8.0 0.0 all-gather.5.cloned.1.call-start
  8.1 0.7 all-gather.5.cloned.1.call-update
  8.8 1.6 collective-permute-start
  11.1 0.0 copy-done
  11.1 0.1 copy.30.pos_ref
  11.2 3.0 %collective-permute-done = bf16[128,512]{1,0:T(8,128)(2,1)S(1)} collective-permute-done((bf16[128,512]{1,0:T(8,128)(2,1)}, bf16[128,512]{1,0:T(8,128)(2,1)S(1)}, u32[]{:S(2)}, u32[]{:S(2)}) %collective-permute-start) | collective-permute-done | bytes 131104 | tf_op jit(solution)/shard_map/ppermute | solution.py:128
  14.3 0.9 pad_maximum_fusion
  15.2 0.6 gather_fusion
  15.8 0.1 broadcast_select_fusion.2
  15.9 0.0 copy-done.1
  15.9 0.0 copy-start.2
  15.9 1.2 copy-done.2
  17.1 19.6 %shard_map.102 = f32[256,512]{1,0:T(8,128)S(1)} custom-call(s32[32]{0:T(128)S(1)} %shift-right-logical_xor_fusion.seeds_ref, s32[1]{0:T(128)} %bitcast.offset_ref, s32[128,1]{1,0:T(8,128)S(1)} %copy.30.pos_ref, bf16[128,4096]{1,0:T(8,128)(2,1)S(1)} %bitcast.66, bf16[128,4096]{1,0:T(8,128)(2,1)S(1)} %bitcast.68, bf16[256,512]{1,0:T(8,128)(2,1)S(1)} %bitcast.70), custom_call_target="tpu_custom_call" | custom-call | tf_op jit(solution)/shard_map/pallas_call | solution.py:108
  36.7 1.6 collective-permute-start.1
  38.3 4.1 %copy.31 = bf16[1,128,8192]{1,2,0:T(8,128)(2,1)} copy(bf16[1,128,8192]{2,1,0:T(8,128)(2,1)} %param.9) | data formatting | bytes 4194304 | tf_op args[0]
  42.4 5.4 %collective-permute-done.1 = f32[128,512]{1,0:T(8,128)S(1)} collective-permute-done((f32[128,512]{1,0:T(8,128)S(1)}, f32[128,512]{1,0:T(8,128)S(1)}, u32[]{:S(2)}, u32[]{:S(2)}) %collective-permute-start.1) | collective-permute-done | bytes 262176 | tf_op jit(solution)/shard_map/ppermute | solution.py:140
  47.7 0.7 fusion.6
  48.4 41.2 %all-gather.5.cloned.1.call-done = bf16[4096,512]{1,0:T(8,128)(2,1)} async-done(((bf16[256,512]{1,0:T(8,128)(2,1)}), bf16[4096,512]{1,0:T(8,128)(2,1)}) %all-gather.5.cloned.1.call-update) | async-done | bytes 4194320 | tf_op jit(solution)/shard_map/all_gather | solution.py:158
  89.6 0.0 collective-permute-start.2
  89.6 3.2 %copy.32 = bf16[128,2,16,256]{0,3,1,2:T(8,128)(2,1)} copy(bf16[128,2,16,256]{0,3,2,1:T(8,128)(2,1)} %bitcast.77) | data formatting | bytes 4194304 | tf_op jit(solution)/shard_map/reshape | solution.py:182
  92.7 0.0 copy-start.4
  92.7 4.9 %all-to-all-start = ((bf16[128,2,16,256]{0,3,1,2:T(8,128)(2,1)}), bf16[128,2,16,256]{0,3,1,2:T(8,128)(2,1)}, u32[]{:S(2)}, u32[]{:S(2)}) async-start(bf16[128,2,16,256]{0,3,1,2:T(8,128)(2,1)} %copy.32), calls=%async_computation | async-start | bytes 4194304 | tf_op jit(solution)/shard_map/all_to_all | solution.py:181
  97.6 0.0 all-gather.3.cloned.1.call-start
  97.7 0.0 copy-done.4
  97.7 2.6 %copy.35 = bf16[128,8,2,2,256]{4,0,3,2,1:T(8,128)(2,1)} copy(bf16[128,8,2,2,256]{0,4,3,1,2:T(8,128)(2,1)S(1)} %bitcast.78) | data formatting | bytes 4194304 | tf_op jit(solution)/shard_map/transpose | solution.py:159
  100.3 1.7 constant_dynamic-slice_fusion.2
  102.0 1.3 copy.36
  103.3 0.7 copy.37
  103.9 0.0 all-gather.3.cloned.1.call-update
  104.0 4.7 %convolution_convert_fusion.1 = bf16[128,4096]{1,0:T(8,128)(2,1)} fusion(bf16[128,512]{1,0:T(8,128)(2,1)} %fusion.6, bf16[4096,512]{1,0:T(8,128)(2,1)} %all-gather.5.cloned.1.call-done), kind=kOutput, calls=%fused_computation.3 | convolution fusion | flops 537395200 | bytes 5373952 | tf_op jit(solution)/shard_map/dot_general | solution.py:193
  108.7 1.8 concatenate.12
  110.5 3.3 %fusion.11 = f32[128,512]{1,0:T(8,128)S(1)} fusion(bf16[128,4096]{0,1:T(8,128)(2,1)} %bitcast.81, bf16[4096,512]{1,0:T(8,128)(2,1)} %all-gather.5.cloned.1.call-done), kind=kOutput, calls=%fused_computation.42 | convolution fusion | flops 536870912 | bytes 5505024 | tf_op jit(solution)/shard_map/dot_general | solution.py:189
  113.8 0.0 collective-permute-done.2
  113.8 0.0 copy-start.5
  113.9 3.6 %fusion.1 = bf16[128,512]{1,0:T(8,128)(2,1)} fusion(f32[128,512]{1,0:T(8,128)S(1)} %fusion.11, bf16[128,4096]{0,1:T(8,128)(2,1)S(1)} %bitcast.80, bf16[4096,512]{1,0:T(8,128)(2,1)} %collective-permute-done.2), kind=kOutput, calls=%fused_computation.8 | convolution fusion | flops 537001984 | bytes 5636096 | tf_op jit(solution)/shard_map/dot_general | solution.py:190
  117.5 1.5 collective-permute-start.3
  118.9 0.0 copy-done.5
  118.9 4.6 %convolution_convert_fusion = bf16[128,4096]{1,0:T(8,128)(2,1)} fusion(bf16[128,512]{1,0:T(8,128)(2,1)S(1)} %copy-done.5, bf16[4096,512]{1,0:T(8,128)(2,1)} %collective-permute-done.2), kind=kOutput, calls=%fused_computation.2 | convolution fusion | flops 537395200 | bytes 5373952 | tf_op jit(solution)/shard_map/dot_general | solution.py:196
  123.6 1.8 concatenate.13
  125.4 3.1 %fusion = bf16[128,2,8,2,256]{4,1,2,0,3:T(2,128)(2,1)S(1)} fusion(pred[]{:T(512)S(6)} %eq.10, bf16[128,8,2,1,256]{4,2,1,0,3:T(2,128)(2,1)S(1)} %concatenate.13, bf16[128,8,2,1,256]{4,2,1,0,3:T(2,128)(2,1)S(1)} %concatenate.12), kind=kLoop, calls=%fused_computation.5 | loop fusion | flops 3145728 | bytes 4194305 | tf_op jit(solution)/shard_map/transpose | solution.py:204
  128.5 5.0 %copy.33 = bf16[128,2,8,2,256]{4,3,2,1,0:T(2,128)(2,1)} copy(bf16[128,2,8,2,256]{4,1,2,0,3:T(2,128)(2,1)S(1)} %fusion) | data formatting | bytes 4194304 | tf_op jit(solution)/shard_map/transpose | solution.py:204
  133.5 4.6 %reshape.79 = bf16[128,8192]{1,0:T(8,128)(2,1)} reshape(bf16[128,2,8,2,256]{4,3,2,1,0:T(2,128)(2,1)} %copy.33) | data formatting | bytes 4194304 | tf_op jit(solution)/shard_map/reshape | solution.py:204
  138.1 0.0 collective-permute-done.3
  138.1 1.0 pad_maximum_fusion.1
  139.1 0.6 gather_fusion.1
  139.7 0.1 broadcast_select_fusion.1
  139.8 0.0 copy-done.3
  139.8 23.6 %shard_map.103 = (bf16[128,4096]{1,0:T(8,128)(2,1)}, f32[256,512]{1,0:T(8,128)S(1)}) custom-call(s32[32]{0:T(128)S(1)} %shift-right-logical_xor_fusion.seeds_ref, s32[1]{0:T(128)} %bitcast.offset_ref, s32[128,1]{1,0:T(8,128)S(1)} %copy.30.pos_ref, bf16[128,4096]{1,0:T(8,128)(2,1)S(1)} %bitcast.67, bf16[128,4096]{1,0:T(8,128)(2,1)S(1)} %bitcast.69, ...), custom_call_target="tpu_custom_call" | custom-call | tf_op jit(solution)/shard_map/pallas_call | solution.py:108
  163.4 0.7 collective-permute-start.4
  164.0 7.5 %collective-permute-done.4 = f32[128,512]{1,0:T(8,128)S(1)} collective-permute-done((f32[128,512]{1,0:T(8,128)S(1)}, f32[128,512]{1,0:T(8,128)S(1)}, u32[]{:S(2)}, u32[]{:S(2)}) %collective-permute-start.4) | collective-permute-done | bytes 262176 | tf_op jit(solution)/shard_map/ppermute | solution.py:140
  171.5 0.7 fusion.5
  172.2 0.0 all-to-all-done
  172.3 0.0 collective-permute-start.5
  172.3 1.7 constant_dynamic-slice_fusion
  174.0 0.5 copy.39
  174.5 0.5 copy.40
  175.0 2.0 fusion.12
  177.0 0.0 collective-permute-done.5
  177.0 2.0 convolution_add_fusion
  179.0 0.6 collective-permute-start.6
  179.7 8.1 %collective-permute-done.6 = bf16[256,512]{1,0:T(8,128)(2,1)S(1)} collective-permute-done((bf16[256,512]{1,0:T(8,128)(2,1)S(1)}, bf16[256,512]{1,0:T(8,128)(2,1)S(1)}, u32[]{:S(2)}, u32[]{:S(2)}) %collective-permute-start.6) | collective-permute-done | bytes 262176 | tf_op jit(solution)/shard_map/ppermute | solution.py:230
  187.8 0.8 fusion.3
  (10 shorter events, 0.1 us)
Async XLA Ops:
  8.0 3.1 %copy-start = (s32[1,256]{1,0:T(1,128)S(1)}, s32[1,256]{1,0:T(1,128)}, u32[]{:S(2)}) copy-start(s32[1,256]{1,0:T(1,128)} %param.13) | copy-start | bytes 3076
  8.0 7.9 %copy-start.1 = (bf16[1,128,4096]{2,1,0:T(8,128)(2,1)S(1)}, bf16[1,128,4096]{2,1,0:T(8,128)(2,1)}, u32[]{:S(2)}) copy-start(bf16[1,128,4096]{2,1,0:T(8,128)(2,1)} %param.10) | copy-start | bytes 3145732
  8.0 81.5 %all-gather.5.cloned.1.call-start = ((), (), s32[]{:S(2)}) async-start(), calls=%async_computation.2 | async-start | bytes 4456448 | tf_op jit(solution)/shard_map/all_gather | solution.py:158
  8.8 5.5 %collective-permute-start = (bf16[128,512]{1,0:T(8,128)(2,1)}, bf16[128,512]{1,0:T(8,128)(2,1)S(1)}, u32[]{:S(2)}, u32[]{:S(2)}) collective-permute-start(bf16[128,512]{1,0:T(8,128)(2,1)} %bitcast.87), channel_id=1, source_target_pairs={{0,16},{16,0},{1,17},{17,1},{2,18},{18,2},{3,19},{19,3},{4,20},{20... | collective-permute-start | bytes 393224 | tf_op jit(solution)/shard_map/ppermute | solution.py:128
  15.9 1.2 copy-start.2
  36.7 11.0 %collective-permute-start.1 = (f32[128,512]{1,0:T(8,128)S(1)}, f32[128,512]{1,0:T(8,128)S(1)}, u32[]{:S(2)}, u32[]{:S(2)}) collective-permute-start(f32[128,512]{1,0:T(8,128)S(1)} %dynamic-slice_bitcast_fusion.1), channel_id=1, source_target_pairs={{0,16},{16,0},{1,17},{17,1},{2,18},{18,2},{3,19},{19,3},{4,20},{20... | collective-permute-start | bytes 786440 | tf_op jit(solution)/shard_map/ppermute | solution.py:140
  89.6 24.3 %collective-permute-start.2 = (bf16[4096,512]{1,0:T(8,128)(2,1)}, bf16[4096,512]{1,0:T(8,128)(2,1)}, u32[]{:S(2)}, u32[]{:S(2)}) collective-permute-start(bf16[4096,512]{1,0:T(8,128)(2,1)} %all-gather.5.cloned.1.call-done), channel_id=1, source_target_pairs={{0,1},{1,0},{2,3},{3,2},{4,5},{5,4},{6,7},{7,6},{8,9},{9,8},{10,11... | collective-permute-start | bytes 12582920 | tf_op jit(solution)/shard_map/ppermute | solution.py:180
  92.7 5.0 %copy-start.4 = (bf16[1,128,8192]{1,2,0:T(8,128)(2,1)S(1)}, bf16[1,128,8192]{1,2,0:T(8,128)(2,1)}, u32[]{:S(2)}) copy-start(bf16[1,128,8192]{1,2,0:T(8,128)(2,1)} %copy.31) | copy-start | bytes 6291460
  92.7 79.5 %all-to-all-start = ((bf16[128,2,16,256]{0,3,1,2:T(8,128)(2,1)}), bf16[128,2,16,256]{0,3,1,2:T(8,128)(2,1)}, u32[]{:S(2)}, u32[]{:S(2)}) async-start(bf16[128,2,16,256]{0,3,1,2:T(8,128)(2,1)} %copy.32), calls=%async_computation | async-start | bytes 4194304 | tf_op jit(solution)/shard_map/all_to_all | solution.py:181
  97.6 74.6 %all-gather.3.cloned.1.call-start = ((), (), s32[]{:S(2)}) async-start(), calls=%async_computation.1 | async-start | bytes 1179648 | tf_op jit(solution)/shard_map/all_gather | solution.py:176
  113.8 5.1 %copy-start.5 = (bf16[128,512]{1,0:T(8,128)(2,1)S(1)}, bf16[128,512]{1,0:T(8,128)(2,1)}, u32[]{:S(2)}) copy-start(bf16[128,512]{1,0:T(8,128)(2,1)} %fusion.6) | copy-start | bytes 393220
  117.5 20.6 %collective-permute-start.3 = (bf16[128,512]{1,0:T(8,128)(2,1)}, bf16[128,512]{1,0:T(8,128)(2,1)}, u32[]{:S(2)}, u32[]{:S(2)}) collective-permute-start(bf16[128,512]{1,0:T(8,128)(2,1)} %fusion.1), channel_id=1, source_target_pairs={{0,16},{16,0},{1,17},{17,1},{2,18},{18,2},{3,19},{19,3},{4,20},{20... | collective-permute-start | bytes 393224 | tf_op jit(solution)/shard_map/ppermute | solution.py:128
  133.5 6.2 %copy-start.3 = (bf16[1,128,4096]{2,1,0:T(8,128)(2,1)S(1)}, bf16[1,128,4096]{2,1,0:T(8,128)(2,1)}, u32[]{:S(2)}) copy-start(bf16[1,128,4096]{2,1,0:T(8,128)(2,1)} %param.12) | copy-start | bytes 3145732
  163.4 8.2 %collective-permute-start.4 = (f32[128,512]{1,0:T(8,128)S(1)}, f32[128,512]{1,0:T(8,128)S(1)}, u32[]{:S(2)}, u32[]{:S(2)}) collective-permute-start(f32[128,512]{1,0:T(8,128)S(1)} %dynamic-slice_bitcast_fusion), channel_id=1, source_target_pairs={{0,16},{16,0},{1,17},{17,1},{2,18},{18,2},{3,19},{19,3},{4,20},{20... | collective-permute-start | bytes 786440 | tf_op jit(solution)/shard_map/ppermute | solution.py:140
  172.3 4.8 %collective-permute-start.5 = (bf16[1024,512]{1,0:T(8,128)(2,1)}, bf16[1024,512]{1,0:T(8,128)(2,1)}, u32[]{:S(2)}, u32[]{:S(2)}) collective-permute-start(bf16[1024,512]{1,0:T(8,128)(2,1)} %all-gather.3.cloned.1.call-done), channel_id=1, source_target_pairs={{0,1},{1,0},{2,3},{3,2},{4,5},{5,4},{6,7},{7,6},{8,9},{9,8},{10,11... | collective-permute-start | bytes 3145736 | tf_op jit(solution)/shard_map/ppermute | solution.py:213
  179.0 8.8 %collective-permute-start.6 = (bf16[256,512]{1,0:T(8,128)(2,1)S(1)}, bf16[256,512]{1,0:T(8,128)(2,1)S(1)}, u32[]{:S(2)}, u32[]{:S(2)}) collective-permute-start(bf16[256,512]{1,0:T(8,128)(2,1)S(1)} %fusion.4), channel_id=1, source_target_pairs={{0,16},{16,0},{1,17},{17,1},{2,18},{18,2},{3,19},{19,3},{4,20},{20... | collective-permute-start | bytes 786440 | tf_op jit(solution)/shard_map/ppermute | solution.py:230
Sparse Core Ops, SparseCore 0:
  11.6 77.9 all-gather.4
Sparse Core Ops, SparseCore 1:
  104.1 53.8 all-gather.2

commit v17 on v13

--- a/solution.py
+++ b/solution.py
@@ -12,7 +12,7 @@
 QH = 32
 KVH = 4
 ROWS = 128
-FSDP = ("zx", "core")
+FSDP = ("z", "x", "core")
 
 
 drop_cut = 1677722
@@ -145,7 +145,9 @@
 
 def per_device(layer_input, queries, key_states, out_grad, doc_positions, drop_seed, value_weight):
     seq_devices = lax.axis_size("seq")
-    zx_devices = lax.axis_size("zx")
+    z_devices = lax.axis_size("z")
+    x_devices = lax.axis_size("x")
+    zx_devices = z_devices * x_devices
     fsdp_devices = zx_devices * 2
     core_index = lax.axis_index("core")
     seq_index = lax.axis_index("seq")
@@ -155,7 +157,7 @@
     local_input = layer_input[0]
     block_rows = value_weight.shape[0]
     swap = [(0, 1), (1, 0)]
-    weight_own = lax.all_gather(value_weight, ("seq", "zx"), axis=0, tiled=True)
+    weight_own = lax.all_gather(value_weight, ("seq", "z", "x"), axis=0, tiled=True)
     input_view = local_input.reshape(tok_rows, seq_devices * zx_devices, 2, block_rows)
     input_own = lax.dynamic_index_in_dim(input_view, core_index, 2, keepdims=False).reshape(
         tok_rows, -1
@@ -171,7 +173,10 @@
     key_full = gather_seq(key_states[0], seq_index, seq_devices)
     (dv,) = attention(seeds, offset, pos, query_loc, grad_loc, key_full, None)
     value_grad = reduce_seq(dv, seq_index, seq_devices).astype(jnp.bfloat16)
-    grads_own = lax.all_gather(value_grad, "zx", axis=0, tiled=True)
+    grads_own = lax.all_gather(value_grad, ("x", "z"), axis=0, tiled=True)
+    grads_own = jnp.transpose(
+        grads_own.reshape(x_devices, z_devices, tok_rows, KVH * HD), (1, 0, 2, 3)
+    ).reshape(zx_devices * tok_rows, KVH * HD)
     value_grad, weight_own, input_late = lax.optimization_barrier(
         (value_grad, weight_own, local_input)
     )
@@ -236,8 +241,10 @@
 
 def solution(mesh):
     seq_devices, fsdp_devices = mesh.devices.shape
+    z_devices = len({device.coords[2] for device in mesh.devices.flat})
     chips = jax.sharding.Mesh(
-        mesh.devices.reshape(seq_devices, fsdp_devices // 2, 2), ("seq",) + FSDP
+        mesh.devices.reshape(seq_devices, z_devices, fsdp_devices // 2 // z_devices, 2),
+        ("seq",) + FSDP,
     )
     return jax.shard_map(
         per_device,

time: 184 us -> 187 us (1.016)
  the two profiles are of different devices: /device:TPU:10 before, /device:TPU:0 now
where the time goes in v17:
time: 187 us; the launch traced here: 186 us
  waiting for transfers between devices  67.5 us (36%)
  Pallas kernels  43.1 us (23%)
  local copies, waits for them, and re-layouts  27.1 us (14%)
  between operations  16.5 us (9%)
  matrix products  15.4 us (8%)
  starting transfers between devices  13 us (7%)
  other arithmetic  3.71 us (2%)
    pallas_call x2, Pallas kernels, attention(): pl.pallas_call(kernel, grid_spec=pltpu.PrefetchScalarGridSpec(num_scalar_...  43.1 us
    all_gather x1, waiting for transfers between devices, per_device(): lax.all_gather(value_weight, ('seq', 'z', 'x'), axis=0, tiled=True)  41.2 us
    all_gather x1, waiting for transfers between devices, per_device(): grads_own = lax.all_gather(value_grad, ('x', 'z'), axis=0, tiled=True)  9.85 us
    select_n x2, local copies, waits for them, and re-layouts, per_device(): jnp.where(core_index == 0, jnp.concatenate([grad_own, grad_other], axis=2...  9.18 us
    ppermute x1, waiting for transfers between devices, per_device(): lax.ppermute(piece.astype(jnp.bfloat16), 'seq', [(i, (i + shift) % seq_de...  7.47 us
    unnamed x19, local copies, waits for them, and re-layouts  7.08 us
    ppermute x2, waiting for transfers between devices, reduce_seq(): lax.ppermute(piece, 'seq', [(i, (i + shift) % seq_devices) for i in range...  5.47 us
    ppermute x2, starting transfers between devices, gather_seq(): lax.ppermute(piece, 'seq', [(i, (i + shift) % seq_devices) for i in range...  4.61 us
  transfers between devices with their start and end apart: 10, of which 5 were waited for; matrix products, arithmetic and copies ran while one was open for 22% of the time, Pallas kernels for 23%

profile of v17, /device:TPU:0, one launch (start us, length us, event | category | flops | bytes accessed | tf_op | source)
XLA Modules:
  0.0 186.4 jit_solution(202159993637545283)
XLA Ops:
  8.0 0.0 copy-start
  8.0 0.0 copy-start.1
  8.0 0.0 all-gather.5.cloned.1.call-start
  8.1 0.7 all-gather.5.cloned.1.call-update
  8.8 3.0 %collective-permute-start = (bf16[128,512]{1,0:T(8,128)(2,1)}, bf16[128,512]{1,0:T(8,128)(2,1)S(1)}, u32[]{:S(2)}, u32[]{:S(2)}) collective-permute-start(bf16[128,512]{1,0:T(8,128)(2,1)} %bitcast.101), channel_id=1, source_target_pairs={{0,16},{16,0},{1,17},{17,1},{2,18},{18,2},{3,19},{19,3},{4,20},{20... | collective-permute-start | bytes 393224 | tf_op jit(solution)/shard_map/ppermute | solution.py:128
  12.5 0.0 copy-done
  12.5 0.1 copy.26.pos_ref
  12.7 2.8 %collective-permute-done = bf16[128,512]{1,0:T(8,128)(2,1)S(1)} collective-permute-done((bf16[128,512]{1,0:T(8,128)(2,1)}, bf16[128,512]{1,0:T(8,128)(2,1)S(1)}, u32[]{:S(2)}, u32[]{:S(2)}) %collective-permute-start) | collective-permute-done | bytes 131104 | tf_op jit(solution)/shard_map/ppermute | solution.py:128
  15.5 0.9 pad_maximum_fusion
  16.4 0.6 gather_fusion
  17.0 0.1 broadcast_select_fusion.1
  17.1 0.0 copy-done.1
  17.1 0.0 copy-start.2
  17.1 1.2 copy-done.2
  18.3 19.6 %shard_map.102 = f32[256,512]{1,0:T(8,128)S(1)} custom-call(s32[32]{0:T(128)S(1)} %shift-right-logical_xor_fusion.seeds_ref, s32[1]{0:T(128)} %bitcast.offset_ref, s32[128,1]{1,0:T(8,128)S(1)} %copy.26.pos_ref, bf16[128,4096]{1,0:T(8,128)(2,1)S(1)} %bitcast.73, bf16[128,4096]{1,0:T(8,128)(2,1)S(1)} %bitcast.75, bf16[256,512]{1,0:T(8,128)(2,1)S(1)} %bitcast.77), custom_call_target="tpu_custom_call" | custom-call | tf_op jit(solution)/shard_map/pallas_call | solution.py:108
  37.9 1.8 collective-permute-start.1
  39.7 4.1 %copy.28 = bf16[1,128,8192]{1,2,0:T(8,128)(2,1)} copy(bf16[1,128,8192]{2,1,0:T(8,128)(2,1)} %param.9) | data formatting | bytes 4194304 | tf_op args[0]
  43.8 5.5 %collective-permute-done.1 = f32[128,512]{1,0:T(8,128)S(1)} collective-permute-done((f32[128,512]{1,0:T(8,128)S(1)}, f32[128,512]{1,0:T(8,128)S(1)}, u32[]{:S(2)}, u32[]{:S(2)}) %collective-permute-start.1) | collective-permute-done | bytes 262176 | tf_op jit(solution)/shard_map/ppermute | solution.py:140
  49.3 0.7 fusion.5
  50.0 41.2 %all-gather.5.cloned.1.call-done = bf16[4096,512]{1,0:T(8,128)(2,1)} async-done(((bf16[256,512]{1,0:T(8,128)(2,1)}), bf16[4096,512]{1,0:T(8,128)(2,1)}) %all-gather.5.cloned.1.call-update) | async-done | bytes 4194320 | tf_op jit(solution)/shard_map/all_gather | solution.py:160
  91.2 0.0 collective-permute-start.2
  91.2 3.2 %copy.29 = bf16[128,2,16,256]{0,3,1,2:T(8,128)(2,1)} copy(bf16[128,2,16,256]{0,3,2,1:T(8,128)(2,1)} %bitcast.84) | data formatting | bytes 4194304 | tf_op jit(solution)/shard_map/reshape | solution.py:185
  94.3 4.6 %all-to-all-start = ((bf16[128,2,16,256]{0,3,1,2:T(8,128)(2,1)}), bf16[128,2,16,256]{0,3,1,2:T(8,128)(2,1)}, u32[]{:S(2)}, u32[]{:S(2)}) async-start(bf16[128,2,16,256]{0,3,1,2:T(8,128)(2,1)} %copy.29), calls=%async_computation | async-start | bytes 4194304 | tf_op jit(solution)/shard_map/all_to_all | solution.py:184
  98.9 0.0 all-gather.3.cloned.1.call-start
  99.0 0.0 copy-done.4
  99.0 1.5 constant_dynamic-slice_fusion.2
  100.4 0.0 all-gather.3.cloned.1.call-update
  100.5 0.0 copy-start.5
  100.5 0.0 copy-start.7
  100.5 3.4 %fusion.10 = f32[128,512]{1,0:T(8,128)S(1)} fusion(bf16[128,4096]{0,1:T(8,128)(2,1)} %bitcast.89, bf16[4096,512]{1,0:T(8,128)(2,1)} %all-gather.5.cloned.1.call-done), kind=kOutput, calls=%fused_computation.41 | convolution fusion | flops 536870912 | bytes 5505024 | tf_op jit(solution)/shard_map/dot_general | solution.py:192
  103.9 0.3 copy-done.5
  104.2 0.0 copy-done.7
  104.2 1.5 convolution_convert_fusion.1
  105.7 0.0 copy-start.6
  105.7 0.2 copy.35
  106.0 0.0 collective-permute-done.2
  106.0 0.9 copy-done.6
  106.9 2.9 %fusion = bf16[128,512]{1,0:T(8,128)(2,1)S(1)} fusion(f32[128,512]{1,0:T(8,128)S(1)} %fusion.10, bf16[128,4096]{0,1:T(8,128)(2,1)S(1)} %bitcast.88, bf16[4096,512]{1,0:T(8,128)(2,1)} %collective-permute-done.2), kind=kOutput, calls=%fused_computation.7 | convolution fusion | flops 537001984 | bytes 5636096 | tf_op jit(solution)/shard_map/dot_general | solution.py:193
  109.9 1.6 collective-permute-start.3
  111.5 3.7 %convolution_convert_fusion = bf16[128,4096]{1,0:T(8,128)(2,1)S(1)} fusion(bf16[128,512]{1,0:T(8,128)(2,1)S(1)} %copy-done.7, bf16[4096,512]{1,0:T(8,128)(2,1)} %collective-permute-done.2), kind=kOutput, calls=%fused_computation.2 | convolution fusion | flops 537395200 | bytes 5373952 | tf_op jit(solution)/shard_map/dot_general | solution.py:199
  115.1 0.2 copy.36
  115.4 0.3 maximum_select_fusion
  115.7 4.6 %copy.30 = bf16[128,16,2,256]{3,2,1,0:T(2,128)(2,1)} copy(bf16[128,16,2,256]{3,1,0,2:T(8,128)(2,1)S(1)} %maximum_select_fusion) | data formatting | bytes 4194304 | tf_op jit(solution)/shard_map/jit(_where)/select_n | solution.py:202
  120.4 4.6 %select_n.70 = bf16[128,8192]{1,0:T(8,128)(2,1)} reshape(bf16[128,16,2,256]{3,2,1,0:T(2,128)(2,1)} %copy.30) | data formatting | bytes 4194304 | tf_op jit(solution)/shard_map/jit(_where)/select_n | solution.py:202
  124.9 0.0 collective-permute-done.3
  125.0 0.6 gather_fusion.1
  125.5 0.1 broadcast_select_fusion
  125.6 23.6 %shard_map.103 = (bf16[128,4096]{1,0:T(8,128)(2,1)}, f32[256,512]{1,0:T(8,128)S(1)}) custom-call(s32[32]{0:T(128)S(1)} %shift-right-logical_xor_fusion.seeds_ref, s32[1]{0:T(128)} %bitcast.offset_ref, s32[128,1]{1,0:T(8,128)S(1)} %copy.26.pos_ref, bf16[128,4096]{1,0:T(8,128)(2,1)S(1)} %bitcast.74, bf16[128,4096]{1,0:T(8,128)(2,1)S(1)} %bitcast.76, ...), custom_call_target="tpu_custom_call" | custom-call | tf_op jit(solution)/shard_map/pallas_call | solution.py:108
  149.2 0.7 collective-permute-start.4
  149.9 9.8 %all-gather.3.cloned.1.call-done = bf16[1024,512]{1,0:T(8,128)(2,1)} async-done(((bf16[128,512]{1,0:T(8,128)(2,1)}), bf16[1024,512]{1,0:T(8,128)(2,1)}) %all-gather.3.cloned.1.call-update) | async-done | bytes 1048592 | tf_op jit(solution)/shard_map/all_gather | solution.py:176
  159.8 1.3 copy.27
  161.1 0.0 collective-permute-done.4
  161.1 0.7 fusion.4
  161.8 0.0 all-to-all-done
  161.8 0.0 collective-permute-start.5
  161.8 1.7 constant_dynamic-slice_fusion
  163.5 1.3 copy.33
  164.8 0.5 copy.34
  165.4 2.0 %fusion.11 = f32[512,512]{1,0:T(8,128)S(1)} fusion(bf16[1024,512]{1,0:T(8,128)(2,1)} %bitcast.97, bf16[1024,512]{1,0:T(8,128)(2,1)S(1)} %bitcast.95), kind=kOutput, calls=%fused_computation.42 | convolution fusion | flops 536870912 | bytes 3145728 | tf_op jit(solution)/shard_map/dot_general | solution.py:224
  167.3 0.0 collective-permute-done.5
  167.3 2.0 %convolution_add_fusion = f32[512,512]{1,0:T(8,128)S(1)} fusion(f32[512,512]{1,0:T(8,128)S(1)} %fusion.11, bf16[1024,512]{1,0:T(8,128)(2,1)S(1)} %bitcast.96, bf16[1024,512]{1,0:T(8,128)(2,1)} %collective-permute-done.5), kind=kOutput, calls=%fused_computation.5 | convolution fusion | flops 537133056 | bytes 4194304 | tf_op jit(solution)/shard_map/dot_general | solution.py:225
  169.4 1.3 collective-permute-start.6
  170.7 7.5 %collective-permute-done.6 = bf16[256,512]{1,0:T(8,128)(2,1)S(1)} collective-permute-done((bf16[256,512]{1,0:T(8,128)(2,1)S(1)}, bf16[256,512]{1,0:T(8,128)(2,1)S(1)}, u32[]{:S(2)}, u32[]{:S(2)}) %collective-permute-start.6) | collective-permute-done | bytes 262176 | tf_op jit(solution)/shard_map/ppermute | solution.py:232
  178.1 0.8 fusion.2
  (12 shorter events, 0.2 us)
Async XLA Ops:
  8.0 4.5 %copy-start = (s32[1,256]{1,0:T(1,128)S(1)}, s32[1,256]{1,0:T(1,128)}, u32[]{:S(2)}) copy-start(s32[1,256]{1,0:T(1,128)} %param.13) | copy-start | bytes 3076
  8.0 9.1 %copy-start.1 = (bf16[1,128,4096]{2,1,0:T(8,128)(2,1)S(1)}, bf16[1,128,4096]{2,1,0:T(8,128)(2,1)}, u32[]{:S(2)}) copy-start(bf16[1,128,4096]{2,1,0:T(8,128)(2,1)} %param.10) | copy-start | bytes 3145732
  8.0 83.1 %all-gather.5.cloned.1.call-start = ((), (), s32[]{:S(2)}) async-start(), calls=%async_computation.2 | async-start | bytes 4456448 | tf_op jit(solution)/shard_map/all_gather | solution.py:160
  8.8 6.7 %collective-permute-start = (bf16[128,512]{1,0:T(8,128)(2,1)}, bf16[128,512]{1,0:T(8,128)(2,1)S(1)}, u32[]{:S(2)}, u32[]{:S(2)}) collective-permute-start(bf16[128,512]{1,0:T(8,128)(2,1)} %bitcast.101), channel_id=1, source_target_pairs={{0,16},{16,0},{1,17},{17,1},{2,18},{18,2},{3,19},{19,3},{4,20},{20... | collective-permute-start | bytes 393224 | tf_op jit(solution)/shard_map/ppermute | solution.py:128
  17.1 1.2 copy-start.2
  37.9 11.3 %collective-permute-start.1 = (f32[128,512]{1,0:T(8,128)S(1)}, f32[128,512]{1,0:T(8,128)S(1)}, u32[]{:S(2)}, u32[]{:S(2)}) collective-permute-start(f32[128,512]{1,0:T(8,128)S(1)} %dynamic-slice_bitcast_fusion.1), channel_id=1, source_target_pairs={{0,16},{16,0},{1,17},{17,1},{2,18},{18,2},{3,19},{19,3},{4,20},{20... | collective-permute-start | bytes 786440 | tf_op jit(solution)/shard_map/ppermute | solution.py:140
  91.2 14.8 %collective-permute-start.2 = (bf16[4096,512]{1,0:T(8,128)(2,1)}, bf16[4096,512]{1,0:T(8,128)(2,1)}, u32[]{:S(2)}, u32[]{:S(2)}) collective-permute-start(bf16[4096,512]{1,0:T(8,128)(2,1)} %all-gather.5.cloned.1.call-done), channel_id=1, source_target_pairs={{0,1},{1,0},{2,3},{3,2},{4,5},{5,4},{6,7},{7,6},{8,9},{9,8},{10,11... | collective-permute-start | bytes 12582920 | tf_op jit(solution)/shard_map/ppermute | solution.py:183
  94.3 4.6 %copy-start.4 = (bf16[1,128,8192]{1,2,0:T(8,128)(2,1)S(1)}, bf16[1,128,8192]{1,2,0:T(8,128)(2,1)}, u32[]{:S(2)}) copy-start(bf16[1,128,8192]{1,2,0:T(8,128)(2,1)} %copy.28) | copy-start | bytes 6291460
  94.3 67.5 %all-to-all-start = ((bf16[128,2,16,256]{0,3,1,2:T(8,128)(2,1)}), bf16[128,2,16,256]{0,3,1,2:T(8,128)(2,1)}, u32[]{:S(2)}, u32[]{:S(2)}) async-start(bf16[128,2,16,256]{0,3,1,2:T(8,128)(2,1)} %copy.29), calls=%async_computation | async-start | bytes 4194304 | tf_op jit(solution)/shard_map/all_to_all | solution.py:184
  98.9 60.9 %all-gather.3.cloned.1.call-start = ((), (), s32[]{:S(2)}) async-start(), calls=%async_computation.1 | async-start | bytes 1179648 | tf_op jit(solution)/shard_map/all_gather | solution.py:176
  100.5 3.7 %copy-start.5 = (bf16[4096,512]{1,0:T(8,128)(2,1)S(1)}, bf16[4096,512]{1,0:T(8,128)(2,1)}, u32[]{:S(2)}) copy-start(bf16[4096,512]{1,0:T(8,128)(2,1)} %all-gather.5.cloned.1.call-done) | copy-start | bytes 12582916
  100.5 3.7 %copy-start.7 = (bf16[128,512]{1,0:T(8,128)(2,1)S(1)}, bf16[128,512]{1,0:T(8,128)(2,1)}, u32[]{:S(2)}) copy-start(bf16[128,512]{1,0:T(8,128)(2,1)} %fusion.5) | copy-start | bytes 393220
  105.7 1.2 copy-start.6
  109.9 15.1 %collective-permute-start.3 = (bf16[128,512]{1,0:T(8,128)(2,1)S(1)}, bf16[128,512]{1,0:T(8,128)(2,1)S(1)}, u32[]{:S(2)}, u32[]{:S(2)}) collective-permute-start(bf16[128,512]{1,0:T(8,128)(2,1)S(1)} %fusion), channel_id=1, source_target_pairs={{0,16},{16,0},{1,17},{17,1},{2,18},{18,2},{3,19},{19,3},{4,20},{20... | collective-permute-start | bytes 393224 | tf_op jit(solution)/shard_map/ppermute | solution.py:128
  120.4 5.3 %copy-start.3 = (bf16[1,128,4096]{2,1,0:T(8,128)(2,1)S(1)}, bf16[1,128,4096]{2,1,0:T(8,128)(2,1)}, u32[]{:S(2)}) copy-start(bf16[1,128,4096]{2,1,0:T(8,128)(2,1)} %param.12) | copy-start | bytes 3145732
  149.2 11.8 %collective-permute-start.4 = (f32[128,512]{1,0:T(8,128)S(1)}, f32[128,512]{1,0:T(8,128)S(1)}, u32[]{:S(2)}, u32[]{:S(2)}) collective-permute-start(f32[128,512]{1,0:T(8,128)S(1)} %dynamic-slice_bitcast_fusion), channel_id=1, source_target_pairs={{0,16},{16,0},{1,17},{17,1},{2,18},{18,2},{3,19},{19,3},{4,20},{20... | collective-permute-start | bytes 786440 | tf_op jit(solution)/shard_map/ppermute | solution.py:140
  161.8 5.5 %collective-permute-start.5 = (bf16[1024,512]{1,0:T(8,128)(2,1)S(1)}, bf16[1024,512]{1,0:T(8,128)(2,1)}, u32[]{:S(2)}, u32[]{:S(2)}) collective-permute-start(bf16[1024,512]{1,0:T(8,128)(2,1)S(1)} %bitcast.94), channel_id=1, source_target_pairs={{0,1},{1,0},{2,3},{3,2},{4,5},{5,4},{6,7},{7,6},{8,9},{9,8},{10,11... | collective-permute-start | bytes 3145736 | tf_op jit(solution)/shard_map/ppermute | solution.py:215
  169.4 8.8 %collective-permute-start.6 = (bf16[256,512]{1,0:T(8,128)(2,1)S(1)}, bf16[256,512]{1,0:T(8,128)(2,1)S(1)}, u32[]{:S(2)}, u32[]{:S(2)}) collective-permute-start(bf16[256,512]{1,0:T(8,128)(2,1)S(1)} %fusion.3), channel_id=1, source_target_pairs={{0,16},{16,0},{1,17},{17,1},{2,18},{18,2},{3,19},{19,3},{4,20},{20... | collective-permute-start | bytes 786440 | tf_op jit(solution)/shard_map/ppermute | solution.py:232
Sparse Core Ops, SparseCore 0:
  11.7 79.4 all-gather.4
Sparse Core Ops, SparseCore 1:
  102.1 57.6 all-gather.2
